TPU v7x, 256 devices: a whole 4x4x8 slice. The times are simulated.
256 devices in a mesh: row: 32 (over x, y, core), col: 8 (over z).
Axes of the slice: x: 4, y: 4, z: 8, core: 2. Of those that a mesh axis runs over, the one named last changes fastest.
Arguments:
- matrix: float32 [16384, 16384], P('row', 'col'), may hold values from -9 to 9
- vectors: float32 [16384, 128], P('row'), may hold values from -0.125 to 0.125
- tfactor: float32 [128, 128], replicated, may hold values from -1 to 2, as said below
Outputs:
- updated: float32 [16384, 16384], P('row', 'col')
Inputs may be any that keep to these rules, and one draw needn't show every extreme that they name: tfactor is upper triangular with its diagonal between 0.7 and 1.4.
All inputs are finite; a program needn't handle non-finite values.
Results may differ from a plain program's by a relative error of at most 0.000094.
Values sent between devices are 32-bit elements; how exact they have to be, the bound alone decides.
No kernel may reach another device: no remote copies, remote signals or barrier semaphores. Data moves between devices by JAX's collectives and lax.ppermute only.
A program may use at most 128 MiB of HBM per device.

v0:
```python
import jax
import jax.numpy as jnp
from jax import lax
from jax.sharding import PartitionSpec as P


def product(left, right):
    return jnp.dot(left, right, precision=lax.Precision.HIGHEST, preferred_element_type=jnp.float32)


def inner_product(left, right):
    return lax.dot_general(
        left,
        right,
        (((0,), (0,)), ((), ())),
        precision=lax.Precision.HIGHEST,
        preferred_element_type=jnp.float32,
    )


def outer_product(left, right):
    return lax.dot_general(
        left,
        right,
        (((1,), (1,)), ((), ())),
        precision=lax.Precision.HIGHEST,
        preferred_element_type=jnp.float32,
    )


def to_columns(panel_rows):
    rows_here = panel_rows.shape[0]
    row_count = lax.axis_size("row")
    blocks_per = row_count // lax.axis_size("col")
    col_index = lax.axis_index("col")
    gathered = lax.all_gather(panel_rows, "row", axis=0, tiled=True)
    return lax.dynamic_slice_in_dim(
        gathered, col_index * (blocks_per * rows_here), blocks_per * rows_here, 0
    )


def shards(matrix, vectors, tfactor):
    vec_cols = to_columns(vectors)
    x_rows = lax.psum(product(matrix, vec_cols), "col")
    y_rows = product(x_rows, tfactor)
    cross_terms = lax.psum(inner_product(vectors, y_rows), "row")
    coupling = inner_product(tfactor, cross_terms)
    w_rows = y_rows - 0.5 * product(vectors, coupling)
    w_cols = to_columns(w_rows)
    return matrix - outer_product(vectors, w_cols) - outer_product(w_rows, vec_cols)


def solution(mesh):
    in_specs = (P("row", "col"), P("row", None), P())
    out_specs = P("row", "col")
    return jax.shard_map(shards, mesh=mesh, in_specs=in_specs, out_specs=out_specs, check_vma=False)
```

profile of v0, /device:TPU:1, one launch (start us, length us, event | category | flops | bytes accessed | tf_op | source)
XLA Modules:
  0.0 338.5 jit_solution(5405151360092062463)
XLA Ops:
  6.5 0.0 copy-start
  6.5 0.0 all-gather.3.cloned.1.call-start
  6.5 0.7 all-gather.3.cloned.1.call-update
  7.3 0.0 all-reduce.3.cloned.1.call-start
  7.3 64.8 %all-gather.3.cloned.1.call-done = f32[16384,128]{1,0:T(8,128)} async-done(((f32[512,128]{1,0:T(8,128)}), f32[16384,128]{1,0:T(8,128)}) %all-gather.3.cloned.1.call-update) | async-done | bytes 8388624 | tf_op jit(solution)/shard_map/all_gather | solution.py:36
  72.1 7.7 %convolution_bitcast_fusion = f32[512,128]{0,1:T(8,128)} fusion(f32[512,2048]{1,0:T(8,128)} %param.3, f32[16384,128]{1,0:T(8,128)} %all-gather.3.cloned.1.call-done, s32[]{:T(128)S(6)} %select_n.4), kind=kOutput, calls=%fused_computation.5 | convolution fusion | flops 1610612736 | bytes 5505028 | tf_op jit(solution)/shard_map/dot_general | solution.py:8
  79.7 0.0 all-reduce.3.cloned.1.call-update
  79.8 0.0 all-reduce.5.cloned.1.call-start
  79.8 67.3 %all-reduce.3.cloned.1.call-done = f32[512,128]{0,1:T(8,128)} async-done(((f32[512,128]{0,1:T(8,128)}), f32[512,128]{0,1:T(8,128)}) %all-reduce.3.cloned.1.call-update) | async-done | bytes 262160 | tf_op jit(solution)/shard_map/psum | solution.py:44
  147.1 0.0 copy-done
  147.1 1.5 fusion.10
  148.6 0.0 copy-done.1
  148.7 1.2 convolution_bitcast_fusion.1
  149.9 0.0 all-reduce.5.cloned.1.call-update
  149.9 0.0 all-gather.5.cloned.1.call-start
  150.0 109.7 %all-reduce.5.cloned.1.call-done = f32[128,128]{0,1:T(8,128)} async-done(((f32[128,128]{0,1:T(8,128)}), f32[128,128]{0,1:T(8,128)}) %all-reduce.5.cloned.1.call-update) | async-done | bytes 65552 | tf_op jit(solution)/shard_map/psum | solution.py:46
  259.7 1.0 fusion.11
  260.7 1.1 fusion.2
  261.8 0.0 all-gather.5.cloned.1.call-update
  261.8 5.4 %copy.5 = f32[512,2048]{0,1:T(8,128)} copy(f32[512,2048]{1,0:T(8,128)} %param.3) | data formatting | bytes 8388608 | tf_op args[0]
  267.2 6.2 %fusion.4 = f32[512,2048]{0,1:T(8,128)} fusion(f32[512,128]{1,0:T(8,128)S(1)} %copy-done.2, f32[16384,128]{1,0:T(8,128)} %all-gather.3.cloned.1.call-done, s32[]{:T(128)S(6)} %select_n.4), kind=kOutput, calls=%fused_computation.8 | convolution fusion | flops 1610612736 | bytes 5505028 | tf_op jit(solution)/shard_map/dot_general | solution.py:22
  273.4 45.7 %all-gather.5.cloned.1.call-done = f32[16384,128]{1,0:T(8,128)} async-done(((f32[512,128]{1,0:T(8,128)}), f32[16384,128]{1,0:T(8,128)}) %all-gather.5.cloned.1.call-update) | async-done | bytes 8388624 | tf_op jit(solution)/shard_map/all_gather | solution.py:36
  319.1 7.5 %fusion = f32[512,2048]{0,1:T(8,128)} fusion(f32[512,2048]{0,1:T(8,128)} %fusion.4, f32[512,2048]{0,1:T(8,128)} %copy.5, f32[512,128]{1,0:T(8,128)S(1)} %copy-done.1, f32[16384,128]{1,0:T(8,128)} %all-gather.5.cloned.1.call-done, s32[]{:T(128)S(6)} %select_n.4), kind=kOutput, calls=%fused_computation.1 | convolution fusion | flops 1612709888 | bytes 13893636 | tf_op jit(solution)/shard_map/dot_general | solution.py:22
  326.6 5.3 %copy.7 = f32[512,2048]{1,0:T(8,128)} copy(f32[512,2048]{0,1:T(8,128)} %fusion) | data formatting | bytes 8388608 | tf_op jit(solution)/shard_map/sub | solution.py:50
  (3 shorter events, 0.0 us)
Async XLA Ops:
  6.5 140.6 %copy-start = (f32[128,128]{1,0:T(8,128)S(1)}, f32[128,128]{1,0:T(8,128)}, u32[]{:S(2)}) copy-start(f32[128,128]{1,0:T(8,128)} %param.5) | copy-start | bytes 196612
  6.5 142.1 %copy-start.1 = (f32[512,128]{1,0:T(8,128)S(1)}, f32[512,128]{1,0:T(8,128)}, u32[]{:S(2)}) copy-start(f32[512,128]{1,0:T(8,128)} %param.4) | copy-start | bytes 786436
  6.5 65.5 %all-gather.3.cloned.1.call-start = ((), (), s32[]{:S(2)}) async-start(), calls=%async_computation | async-start | bytes 8650752 | tf_op jit(solution)/shard_map/all_gather | solution.py:36
  7.3 139.8 %all-reduce.3.cloned.1.call-start = ((), (), s32[]{:S(2)}) async-start(), calls=%async_computation.1 | async-start | bytes 524288 | tf_op jit(solution)/shard_map/psum | solution.py:44
  79.8 179.9 %all-reduce.5.cloned.1.call-start = ((), (), s32[]{:S(2)}) async-start(), calls=%async_computation.2 | async-start | bytes 131072 | tf_op jit(solution)/shard_map/psum | solution.py:46
  149.9 169.2 %all-gather.5.cloned.1.call-start = ((), (), s32[]{:S(2)}) async-start(), calls=%async_computation.3 | async-start | bytes 8650752 | tf_op jit(solution)/shard_map/all_gather | solution.py:36
  261.8 5.4 %copy-start.2 = (f32[512,128]{1,0:T(8,128)S(1)}, f32[512,128]{1,0:T(8,128)}, u32[]{:S(2)}) copy-start(f32[512,128]{1,0:T(8,128)} %fusion.2) | copy-start | bytes 786436
Sparse Core Ops, SparseCore 0:
  9.9 62.1 all-gather.2
  79.9 67.1 all-reduce.2
  150.7 108.9 all-reduce.4
  262.1 56.9 all-gather.4
where the time goes:
time: 339 us
  waiting for transfers between devices  288 us (85%)
  matrix products  26.2 us (8%)
  between operations  13.2 us (4%)
  local copies, waits for them, and re-layouts  10.8 us (3%)
    all_gather x2, waiting for transfers between devices, to_columns(): gathered = lax.all_gather(panel_rows, 'row', axis=0, tiled=True)  110 us
    psum x1, waiting for transfers between devices, shards(): cross_terms = lax.psum(inner_product(vectors, y_rows), 'row')  110 us
    psum x1, waiting for transfers between devices, shards(): x_rows = lax.psum(product(matrix, vec_cols), 'col')  67.3 us
    dot_general x2, matrix products, outer_product(): lax.dot_general(left, right, (((1,), (1,)), ((), ())), precision=lax.Prec...  13.7 us
    dot_general x3, matrix products, product(): jnp.dot(left, right, precision=lax.Precision.HIGHEST, preferred_element_t...  10.3 us
  transfers between devices with their start and end apart: 4, of which 4 were waited for; matrix products, arithmetic and copies ran while one was open for 3% of the time, Pallas kernels for 0%

commit v1 on v0

v1 whole, which is shorter than its diff:
```python
import jax
import jax.numpy as jnp
from jax import lax
from jax.sharding import PartitionSpec as P


def product(left, right):
    return jnp.dot(left, right, precision=lax.Precision.HIGHEST, preferred_element_type=jnp.float32)


def inner_product(left, right):
    return lax.dot_general(
        left,
        right,
        (((0,), (0,)), ((), ())),
        precision=lax.Precision.HIGHEST,
        preferred_element_type=jnp.float32,
    )


def butterfly_sum(value, axis, size):
    step = 1
    while step < size:
        pairs = [(i, i ^ step) for i in range(size)]
        value = value + lax.ppermute(value, axis, pairs)
        step *= 2
    return value


def to_columns(panel_rows):
    rows_here = panel_rows.shape[0]
    row_count = lax.axis_size("row")
    col_count = lax.axis_size("col")
    per = row_count // col_count
    row = lax.axis_index("row")
    gathered = jnp.zeros((per * rows_here,) + panel_rows.shape[1:], panel_rows.dtype)
    for j in range(per):
        pairs = []
        for src_row in range(row_count):
            for src_col in range(col_count):
                dst_row = per * src_col + (src_row % per + j) % per
                dst_col = src_row // per
                pairs.append((src_row * col_count + src_col, dst_row * col_count + dst_col))
        block = lax.ppermute(panel_rows, ("row", "col"), pairs)
        slot = (row % per - j) % per
        gathered = lax.dynamic_update_slice_in_dim(gathered, block, slot * rows_here, 0)
    return gathered


def shards(matrix, vectors, tfactor):
    rows_here = matrix.shape[0]
    vec_cols = to_columns(vectors)
    x_part = product(matrix, vec_cols)
    s_part = inner_product(vectors, x_part)
    both = butterfly_sum(jnp.concatenate([x_part, s_part], axis=0), "col", lax.axis_size("col"))
    x_rows = both[:rows_here]
    s_full = butterfly_sum(both[rows_here:], "row", lax.axis_size("row"))
    x_cols = to_columns(x_rows)
    coupling = inner_product(tfactor, product(s_full, tfactor))
    w_rows = product(x_rows, tfactor) - 0.5 * product(vectors, coupling)
    w_cols = product(x_cols, tfactor) - 0.5 * product(vec_cols, coupling)
    left = jnp.concatenate([vectors, w_rows], axis=1)
    right = jnp.concatenate([w_cols, vec_cols], axis=1)
    return matrix - lax.dot_general(
        left, right, (((1,), (1,)), ((), ())),
        precision=lax.Precision.HIGHEST, preferred_element_type=jnp.float32,
    )


def solution(mesh):
    in_specs = (P("row", "col"), P("row", None), P())
    out_specs = P("row", "col")
    return jax.shard_map(shards, mesh=mesh, in_specs=in_specs, out_specs=out_specs, check_vma=False)
```

time: 339 us -> 271 us (0.80)
  the two profiles are of different devices: /device:TPU:1 before, /device:TPU:64 now
where the time goes in v1:
time: 271 us; the launch traced here: 270 us
  waiting for transfers between devices  203 us (75%)
  starting transfers between devices  50.4 us (19%)
  matrix products  15.9 us (6%)
    ppermute x8, waiting for transfers between devices, to_columns(): block = lax.ppermute(panel_rows, ('row', 'col'), pairs)  142 us
    ppermute x8, waiting for transfers between devices, butterfly_sum(): value = value + lax.ppermute(value, axis, pairs)  61.1 us
    ppermute x8, starting transfers between devices, to_columns(): block = lax.ppermute(panel_rows, ('row', 'col'), pairs)  29.8 us
    ppermute x8, starting transfers between devices, butterfly_sum(): value = value + lax.ppermute(value, axis, pairs)  20.6 us
    dot_general x6, matrix products, product(): jnp.dot(left, right, precision=lax.Precision.HIGHEST, preferred_element_t...  10 us
  transfers between devices with their start and end apart: 16, of which 12 were waited for; matrix products, arithmetic and copies ran while one was open for 0% of the time, Pallas kernels for 0%

profile of v1, /device:TPU:64, one launch (start us, length us, event | category | flops | bytes accessed | tf_op | source)
XLA Modules:
  0.0 270.5 jit_solution(9949228818996716892)
XLA Ops:
  0.0 2.6 collective-permute-start
  2.6 4.3 %collective-permute-start.2 = (f32[512,128]{1,0:T(8,128)}, f32[512,128]{1,0:T(8,128)S(1)}, u32[]{:S(2)}, u32[]{:S(2)}) collective-permute-start(f32[512,128]{1,0:T(8,128)} %param.4), channel_id=1, source_target_pairs={{0,16},{1,48},{2,80},{3,112},{4,144},{5,176},{6,208},{7,240},{8,24... | collective-permute-start | bytes 786440 | tf_op jit(solution)/shard_map/ppermute | solution.py:44
  7.0 4.4 %collective-permute-start.3 = (f32[512,128]{1,0:T(8,128)}, f32[512,128]{1,0:T(8,128)S(1)}, u32[]{:S(2)}, u32[]{:S(2)}) collective-permute-start(f32[512,128]{1,0:T(8,128)} %param.4), channel_id=1, source_target_pairs={{0,24},{1,56},{2,88},{3,120},{4,152},{5,184},{6,216},{7,248},{8,0}... | collective-permute-start | bytes 786440 | tf_op jit(solution)/shard_map/ppermute | solution.py:44
  11.4 51.4 %collective-permute-done = f32[512,128]{1,0:T(8,128)S(1)} collective-permute-done((f32[512,128]{1,0:T(8,128)}, f32[512,128]{1,0:T(8,128)S(1)}, u32[]{:S(2)}, u32[]{:S(2)}) %collective-permute-start) | collective-permute-done | bytes 262176 | tf_op jit(solution)/shard_map/ppermute | solution.py:44
  63.1 13.7 %collective-permute-done.2 = f32[512,128]{1,0:T(8,128)S(1)} collective-permute-done((f32[512,128]{1,0:T(8,128)}, f32[512,128]{1,0:T(8,128)S(1)}, u32[]{:S(2)}, u32[]{:S(2)}) %collective-permute-start.2) | collective-permute-done | bytes 262176 | tf_op jit(solution)/shard_map/ppermute | solution.py:44
  76.9 11.4 %collective-permute-done.1 = f32[512,128]{1,0:T(8,128)S(1)} collective-permute-done((f32[512,128]{1,0:T(8,128)}, f32[512,128]{1,0:T(8,128)S(1)}, u32[]{:S(2)}, u32[]{:S(2)}) %collective-permute-start.1) | collective-permute-done | bytes 262176 | tf_op jit(solution)/shard_map/ppermute | solution.py:44
  88.5 4.3 %collective-permute-done.3 = f32[512,128]{1,0:T(8,128)S(1)} collective-permute-done((f32[512,128]{1,0:T(8,128)}, f32[512,128]{1,0:T(8,128)S(1)}, u32[]{:S(2)}, u32[]{:S(2)}) %collective-permute-start.3) | collective-permute-done | bytes 262176 | tf_op jit(solution)/shard_map/ppermute | solution.py:44
  92.9 6.6 %fusion.12 = f32[128,512]{1,0:T(8,128)S(1)} fusion(f32[2048,128]{0,1:T(8,128)S(1)} %constant_dynamic-update-slice_fusion.4, f32[512,2048]{1,0:T(8,128)} %param.3), kind=kOutput, calls=%fused_computation.28 | convolution fusion | flops 1610612736 | bytes 5505024 | tf_op jit(solution)/shard_map/dot_general | solution.py:8
  100.0 8.9 %collective-permute-done.4 = f32[640,128]{0,1:T(8,128)S(1)} collective-permute-done((f32[640,128]{0,1:T(8,128)S(1)}, f32[640,128]{0,1:T(8,128)S(1)}, u32[]{:S(2)}, u32[]{:S(2)}) %collective-permute-start.4) | collective-permute-done | bytes 327712 | tf_op jit(solution)/shard_map/ppermute | solution.py:25
  109.1 12.1 %collective-permute-done.5 = f32[640,128]{0,1:T(8,128)S(1)} collective-permute-done((f32[640,128]{0,1:T(8,128)S(1)}, f32[640,128]{0,1:T(8,128)S(1)}, u32[]{:S(2)}, u32[]{:S(2)}) %collective-permute-start.5) | collective-permute-done | bytes 327712 | tf_op jit(solution)/shard_map/ppermute | solution.py:25
  121.3 14.1 %collective-permute-start.6 = (f32[640,128]{0,1:T(8,128)S(1)}, f32[640,128]{0,1:T(8,128)S(1)}, u32[]{:S(2)}, u32[]{:S(2)}) collective-permute-start(f32[640,128]{0,1:T(8,128)S(1)} %add.80), channel_id=1, source_target_pairs={{0,4},{1,5},{2,6},{3,7},{4,0},{5,1},{6,2},{7,3},{8,12},{9,13},{10,... | collective-permute-start | bytes 983048 | tf_op jit(solution)/shard_map/ppermute | solution.py:25
  135.4 13.4 %collective-permute-done.6 = f32[640,128]{0,1:T(8,128)S(1)} collective-permute-done((f32[640,128]{0,1:T(8,128)S(1)}, f32[640,128]{0,1:T(8,128)S(1)}, u32[]{:S(2)}, u32[]{:S(2)}) %collective-permute-start.6) | collective-permute-done | bytes 327712 | tf_op jit(solution)/shard_map/ppermute | solution.py:25
  149.0 14.2 %collective-permute-start.13 = (f32[512,128]{0,1:T(8,128)S(1)}, f32[512,128]{0,1:T(8,128)S(1)}, u32[]{:S(2)}, u32[]{:S(2)}) collective-permute-start(f32[512,128]{0,1:T(8,128)S(1)} %slice.8), channel_id=1, source_target_pairs={{0,8},{1,40},{2,72},{3,104},{4,136},{5,168},{6,200},{7,232},{8,16}... | collective-permute-start | bytes 786440 | tf_op jit(solution)/shard_map/ppermute | solution.py:44
  163.2 1.9 collective-permute-start.12
  165.1 1.6 collective-permute-start.8
  166.7 3.4 %collective-permute-done.8 = f32[128,128]{0,1:T(8,128)S(1)} collective-permute-done((f32[128,128]{0,1:T(8,128)S(1)}, f32[128,128]{0,1:T(8,128)S(1)}, u32[]{:S(2)}, u32[]{:S(2)}) %collective-permute-start.8) | collective-permute-done | bytes 65568 | tf_op jit(solution)/shard_map/ppermute | solution.py:25
  170.2 4.5 %collective-permute-start.9 = (f32[128,128]{0,1:T(8,128)S(1)}, f32[128,128]{0,1:T(8,128)S(1)}, u32[]{:S(2)}, u32[]{:S(2)}) collective-permute-start(f32[128,128]{0,1:T(8,128)S(1)} %add.83), channel_id=1, source_target_pairs={{0,32},{8,40},{16,48},{24,56},{32,0},{40,8},{48,16},{56,24},{64,96... | collective-permute-start | bytes 196616 | tf_op jit(solution)/shard_map/ppermute | solution.py:25
  174.9 2.1 collective-permute-start.15
  177.1 50.8 %collective-permute-done.12 = f32[512,128]{0,1:T(8,128)S(1)} collective-permute-done((f32[512,128]{0,1:T(8,128)S(1)}, f32[512,128]{0,1:T(8,128)S(1)}, u32[]{:S(2)}, u32[]{:S(2)}) %collective-permute-start.12) | collective-permute-done | bytes 262176 | tf_op jit(solution)/shard_map/ppermute | solution.py:44
  228.1 10.0 %collective-permute-done.14 = f32[512,128]{0,1:T(8,128)S(1)} collective-permute-done((f32[512,128]{0,1:T(8,128)S(1)}, f32[512,128]{0,1:T(8,128)S(1)}, u32[]{:S(2)}, u32[]{:S(2)}) %collective-permute-start.14) | collective-permute-done | bytes 262176 | tf_op jit(solution)/shard_map/ppermute | solution.py:44
  238.2 17.5 %collective-permute-done.10 = f32[128,128]{0,1:T(8,128)S(1)} collective-permute-done((f32[128,128]{0,1:T(8,128)S(1)}, f32[128,128]{0,1:T(8,128)S(1)}, u32[]{:S(2)}, u32[]{:S(2)}) %collective-permute-start.10) | collective-permute-done | bytes 65568 | tf_op jit(solution)/shard_map/ppermute | solution.py:25
  255.8 5.7 %collective-permute-done.11 = f32[128,128]{0,1:T(8,128)S(1)} collective-permute-done((f32[128,128]{0,1:T(8,128)S(1)}, f32[128,128]{0,1:T(8,128)S(1)}, u32[]{:S(2)}, u32[]{:S(2)}) %collective-permute-start.11) | collective-permute-done | bytes 65568 | tf_op jit(solution)/shard_map/ppermute | solution.py:25
  264.2 1.1 convolution_subtract_fusion.1
  265.3 5.2 %convolution_subtract_fusion = f32[512,2048]{1,0:T(8,128)} fusion(f32[512,2048]{1,0:T(8,128)S(1)} %copy-done.1, f32[2048,128]{0,1:T(8,128)S(1)} %constant_dynamic-update-slice_fusion.4, f32[2048,128]{0,1:T(8,128)S(1)} %convolution_subtract_fusion.1, f32[512,128]{1,0:T(8,128)S(1)} %convolution_subtract_fusion.2, f32[512,128]{1,0:T(8,128)S(1)} %copy-done.2), kind=kOutput, calls=%fused_computation | convolution fusion | flops 3222929408 | bytes 11010048 | tf_op jit(solution)/shard_map/dot_general | solution.py:64
  (47 shorter events, 4.8 us)
Async XLA Ops:
  0.0 261.5 %copy-start = (f32[128,128]{1,0:T(8,128)S(1)}, f32[128,128]{1,0:T(8,128)}, u32[]{:S(2)}) copy-start(f32[128,128]{1,0:T(8,128)} %param.5) | copy-start | bytes 196612
  0.0 62.8 %collective-permute-start = (f32[512,128]{1,0:T(8,128)}, f32[512,128]{1,0:T(8,128)S(1)}, u32[]{:S(2)}, u32[]{:S(2)}) collective-permute-start(f32[512,128]{1,0:T(8,128)} %param.4), channel_id=1, source_target_pairs={{0,0},{1,32},{2,64},{3,96},{4,128},{5,160},{6,192},{7,224},{8,8},{... | collective-permute-start | bytes 786440 | tf_op jit(solution)/shard_map/ppermute | solution.py:44
  2.6 74.1 %collective-permute-start.2 = (f32[512,128]{1,0:T(8,128)}, f32[512,128]{1,0:T(8,128)S(1)}, u32[]{:S(2)}, u32[]{:S(2)}) collective-permute-start(f32[512,128]{1,0:T(8,128)} %param.4), channel_id=1, source_target_pairs={{0,16},{1,48},{2,80},{3,112},{4,144},{5,176},{6,208},{7,240},{8,24... | collective-permute-start | bytes 786440 | tf_op jit(solution)/shard_map/ppermute | solution.py:44
  7.0 81.3 %collective-permute-start.1 = (f32[512,128]{1,0:T(8,128)}, f32[512,128]{1,0:T(8,128)S(1)}, u32[]{:S(2)}, u32[]{:S(2)}) collective-permute-start(f32[512,128]{1,0:T(8,128)} %param.4), channel_id=1, source_target_pairs={{0,8},{1,40},{2,72},{3,104},{4,136},{5,168},{6,200},{7,232},{8,16}... | collective-permute-start | bytes 786440 | tf_op jit(solution)/shard_map/ppermute | solution.py:44
  7.0 85.8 %collective-permute-start.3 = (f32[512,128]{1,0:T(8,128)}, f32[512,128]{1,0:T(8,128)S(1)}, u32[]{:S(2)}, u32[]{:S(2)}) collective-permute-start(f32[512,128]{1,0:T(8,128)} %param.4), channel_id=1, source_target_pairs={{0,24},{1,56},{2,88},{3,120},{4,152},{5,184},{6,216},{7,248},{8,0}... | collective-permute-start | bytes 786440 | tf_op jit(solution)/shard_map/ppermute | solution.py:44
  76.9 22.6 %copy-start.2 = (f32[512,128]{1,0:T(8,128)S(1)}, f32[512,128]{1,0:T(8,128)}, u32[]{:S(2)}) copy-start(f32[512,128]{1,0:T(8,128)} %param.4) | copy-start | bytes 786436
  99.9 9.0 %collective-permute-start.4 = (f32[640,128]{0,1:T(8,128)S(1)}, f32[640,128]{0,1:T(8,128)S(1)}, u32[]{:S(2)}, u32[]{:S(2)}) collective-permute-start(f32[640,128]{0,1:T(8,128)S(1)} %pad_maximum_fusion), channel_id=1, source_target_pairs={{0,1},{1,0},{2,3},{3,2},{4,5},{5,4},{6,7},{7,6},{8,9},{9,8},{10,11... | collective-permute-start | bytes 983048 | tf_op jit(solution)/shard_map/ppermute | solution.py:25
  109.0 12.2 %collective-permute-start.5 = (f32[640,128]{0,1:T(8,128)S(1)}, f32[640,128]{0,1:T(8,128)S(1)}, u32[]{:S(2)}, u32[]{:S(2)}) collective-permute-start(f32[640,128]{0,1:T(8,128)S(1)} %fusion.11), channel_id=1, source_target_pairs={{0,2},{1,3},{2,0},{3,1},{4,6},{5,7},{6,4},{7,5},{8,10},{9,11},{10,... | collective-permute-start | bytes 983048 | tf_op jit(solution)/shard_map/ppermute | solution.py:25
  121.3 27.5 %collective-permute-start.6 = (f32[640,128]{0,1:T(8,128)S(1)}, f32[640,128]{0,1:T(8,128)S(1)}, u32[]{:S(2)}, u32[]{:S(2)}) collective-permute-start(f32[640,128]{0,1:T(8,128)S(1)} %add.80), channel_id=1, source_target_pairs={{0,4},{1,5},{2,6},{3,7},{4,0},{5,1},{6,2},{7,3},{8,12},{9,13},{10,... | collective-permute-start | bytes 983048 | tf_op jit(solution)/shard_map/ppermute | solution.py:25
  148.9 16.3 %collective-permute-start.7 = (f32[128,128]{0,1:T(8,128)S(1)}, f32[128,128]{0,1:T(8,128)S(1)}, u32[]{:S(2)}, u32[]{:S(2)}) collective-permute-start(f32[128,128]{0,1:T(8,128)S(1)} %slice.9), channel_id=1, source_target_pairs={{0,8},{8,0},{16,24},{24,16},{32,40},{40,32},{48,56},{56,48},{64,72... | collective-permute-start | bytes 196616 | tf_op jit(solution)/shard_map/ppermute | solution.py:25
  149.0 79.1 %collective-permute-start.13 = (f32[512,128]{0,1:T(8,128)S(1)}, f32[512,128]{0,1:T(8,128)S(1)}, u32[]{:S(2)}, u32[]{:S(2)}) collective-permute-start(f32[512,128]{0,1:T(8,128)S(1)} %slice.8), channel_id=1, source_target_pairs={{0,8},{1,40},{2,72},{3,104},{4,136},{5,168},{6,200},{7,232},{8,16}... | collective-permute-start | bytes 786440 | tf_op jit(solution)/shard_map/ppermute | solution.py:44
  163.2 64.7 %collective-permute-start.12 = (f32[512,128]{0,1:T(8,128)S(1)}, f32[512,128]{0,1:T(8,128)S(1)}, u32[]{:S(2)}, u32[]{:S(2)}) collective-permute-start(f32[512,128]{0,1:T(8,128)S(1)} %slice.8), channel_id=1, source_target_pairs={{0,0},{1,32},{2,64},{3,96},{4,128},{5,160},{6,192},{7,224},{8,8},{... | collective-permute-start | bytes 786440 | tf_op jit(solution)/shard_map/ppermute | solution.py:44
  165.1 5.0 %collective-permute-start.8 = (f32[128,128]{0,1:T(8,128)S(1)}, f32[128,128]{0,1:T(8,128)S(1)}, u32[]{:S(2)}, u32[]{:S(2)}) collective-permute-start(f32[128,128]{0,1:T(8,128)S(1)} %slice_add_fusion), channel_id=1, source_target_pairs={{0,16},{8,24},{16,0},{24,8},{32,48},{40,56},{48,32},{56,40},{64,80... | collective-permute-start | bytes 196616 | tf_op jit(solution)/shard_map/ppermute | solution.py:25
  170.2 6.8 %collective-permute-start.9 = (f32[128,128]{0,1:T(8,128)S(1)}, f32[128,128]{0,1:T(8,128)S(1)}, u32[]{:S(2)}, u32[]{:S(2)}) collective-permute-start(f32[128,128]{0,1:T(8,128)S(1)} %add.83), channel_id=1, source_target_pairs={{0,32},{8,40},{16,48},{24,56},{32,0},{40,8},{48,16},{56,24},{64,96... | collective-permute-start | bytes 196616 | tf_op jit(solution)/shard_map/ppermute | solution.py:25
  174.6 63.5 %collective-permute-start.14 = (f32[512,128]{0,1:T(8,128)S(1)}, f32[512,128]{0,1:T(8,128)S(1)}, u32[]{:S(2)}, u32[]{:S(2)}) collective-permute-start(f32[512,128]{0,1:T(8,128)S(1)} %slice.8), channel_id=1, source_target_pairs={{0,16},{1,48},{2,80},{3,112},{4,144},{5,176},{6,208},{7,240},{8,24... | collective-permute-start | bytes 786440 | tf_op jit(solution)/shard_map/ppermute | solution.py:44
  174.9 80.9 %collective-permute-start.15 = (f32[512,128]{0,1:T(8,128)S(1)}, f32[512,128]{0,1:T(8,128)S(1)}, u32[]{:S(2)}, u32[]{:S(2)}) collective-permute-start(f32[512,128]{0,1:T(8,128)S(1)} %slice.8), channel_id=1, source_target_pairs={{0,24},{1,56},{2,88},{3,120},{4,152},{5,184},{6,216},{7,248},{8,0}... | collective-permute-start | bytes 786440 | tf_op jit(solution)/shard_map/ppermute | solution.py:44
  177.0 78.7 %collective-permute-start.10 = (f32[128,128]{0,1:T(8,128)S(1)}, f32[128,128]{0,1:T(8,128)S(1)}, u32[]{:S(2)}, u32[]{:S(2)}) collective-permute-start(f32[128,128]{0,1:T(8,128)S(1)} %add.84), channel_id=1, source_target_pairs={{0,64},{8,72},{16,80},{24,88},{32,96},{40,104},{48,112},{56,120},{... | collective-permute-start | bytes 196616 | tf_op jit(solution)/shard_map/ppermute | solution.py:25
  228.1 37.2 %copy-start.1 = (f32[512,2048]{1,0:T(8,128)S(1)}, f32[512,2048]{1,0:T(8,128)}, u32[]{:S(2)}) copy-start(f32[512,2048]{1,0:T(8,128)} %param.3) | copy-start | bytes 12582916
  255.7 5.9 %collective-permute-start.11 = (f32[128,128]{0,1:T(8,128)S(1)}, f32[128,128]{0,1:T(8,128)S(1)}, u32[]{:S(2)}, u32[]{:S(2)}) collective-permute-start(f32[128,128]{0,1:T(8,128)S(1)} %add.85), channel_id=1, source_target_pairs={{0,128},{8,136},{16,144},{24,152},{32,160},{40,168},{48,176},{56,1... | collective-permute-start | bytes 196616 | tf_op jit(solution)/shard_map/ppermute | solution.py:25

commit v2 on v1

v2 whole, which is shorter than its diff:
```python
import jax
import jax.numpy as jnp
from jax import lax
from jax.sharding import PartitionSpec as P


def product(left, right):
    return jnp.dot(left, right, precision=lax.Precision.HIGHEST, preferred_element_type=jnp.float32)


def inner_product(left, right):
    return lax.dot_general(
        left,
        right,
        (((0,), (0,)), ((), ())),
        precision=lax.Precision.HIGHEST,
        preferred_element_type=jnp.float32,
    )


def to_columns(panel_rows):
    rows_here = panel_rows.shape[0]
    row_count = lax.axis_size("row")
    col_count = lax.axis_size("col")
    per = row_count // col_count
    pairs = []
    for src_row in range(row_count):
        for src_col in range(col_count):
            dst_row = per * src_col + src_row % per
            dst_col = src_row // per
            pairs.append((src_row * col_count + src_col, dst_row * col_count + dst_col))
    mine = lax.ppermute(panel_rows, ("row", "col"), pairs)
    low = lax.axis_index("row") % per
    gathered = jnp.zeros((per * rows_here,) + panel_rows.shape[1:], panel_rows.dtype)
    gathered = lax.dynamic_update_slice_in_dim(gathered, mine, low * rows_here, 0)
    for mask in range(1, per):
        block = lax.ppermute(mine, "row", [(i, i ^ mask) for i in range(row_count)])
        gathered = lax.dynamic_update_slice_in_dim(gathered, block, (low ^ mask) * rows_here, 0)
    return gathered


def col_sum_rows(partial):
    count = lax.axis_size("col")
    col = lax.axis_index("col")
    chunk = partial.shape[0] // count
    pieces = partial.reshape((count, chunk) + partial.shape[1:])
    total = lax.dynamic_index_in_dim(pieces, col, 0, keepdims=False)
    for shift in range(1, count):
        pairs = [(i, (i + shift) % count) for i in range(count)]
        sent = lax.dynamic_index_in_dim(pieces, (col + shift) % count, 0, keepdims=False)
        total = total + lax.ppermute(sent, "col", pairs)
    whole = jnp.zeros_like(pieces)
    whole = lax.dynamic_update_index_in_dim(whole, total, col, 0)
    for shift in range(1, count):
        pairs = [(i, (i + shift) % count) for i in range(count)]
        got = lax.ppermute(total, "col", pairs)
        whole = lax.dynamic_update_index_in_dim(whole, got, (col - shift) % count, 0)
    return whole.reshape(partial.shape)


def col_sum(value):
    count = lax.axis_size("col")
    total = value
    for shift in range(1, count):
        pairs = [(i, (i + shift) % count) for i in range(count)]
        total = total + lax.ppermute(value, "col", pairs)
    return total


def shards(matrix, vectors, tfactor):
    vec_cols = to_columns(vectors)
    x_rows = col_sum_rows(product(matrix, vec_cols))
    x_cols = to_columns(x_rows)
    s_full = col_sum(inner_product(vec_cols, x_cols))
    coupling = inner_product(tfactor, product(s_full, tfactor))
    w_rows = product(x_rows, tfactor) - 0.5 * product(vectors, coupling)
    w_cols = product(x_cols, tfactor) - 0.5 * product(vec_cols, coupling)
    left = jnp.concatenate([vectors, w_rows], axis=1)
    right = jnp.concatenate([w_cols, vec_cols], axis=1)
    return matrix - lax.dot_general(
        left, right, (((1,), (1,)), ((), ())),
        precision=lax.Precision.HIGHEST, preferred_element_type=jnp.float32,
    )


def solution(mesh):
    in_specs = (P("row", "col"), P("row", None), P())
    out_specs = P("row", "col")
    return jax.shard_map(shards, mesh=mesh, in_specs=in_specs, out_specs=out_specs, check_vma=False)
```

time: 271 us -> 168 us (0.62)
  the two profiles are of different devices: /device:TPU:64 before, /device:TPU:17 now
where the time goes in v2:
time: 168 us; the launch traced here: 167 us
  waiting for transfers between devices  75.1 us (45%)
  starting transfers between devices  74.4 us (44%)
  matrix products  17 us (10%)
    ppermute x2, waiting for transfers between devices, to_columns(): mine = lax.ppermute(panel_rows, ('row', 'col'), pairs)  34 us
    ppermute x7, starting transfers between devices, col_sum_rows(): total = total + lax.ppermute(sent, 'col', pairs)  25.8 us
    ppermute x7, starting transfers between devices, col_sum(): total = total + lax.ppermute(value, 'col', pairs)  23.7 us
    ppermute x6, waiting for transfers between devices, to_columns(): block = lax.ppermute(mine, 'row', [(i, i ^ mask) for i in range(row_count)])  23.7 us
    ppermute x7, starting transfers between devices, col_sum_rows(): got = lax.ppermute(total, 'col', pairs)  13.6 us
    dot_general x6, matrix products, product(): jnp.dot(left, right, precision=lax.Precision.HIGHEST, preferred_element_t...  9.55 us
    ppermute x7, waiting for transfers between devices, col_sum(): total = total + lax.ppermute(value, 'col', pairs)  9.49 us
    ppermute x6, starting transfers between devices, to_columns(): block = lax.ppermute(mine, 'row', [(i, i ^ mask) for i in range(row_count)])  5.94 us
  transfers between devices with their start and end apart: 29, of which 14 were waited for; matrix products, arithmetic and copies ran while one was open for 0% of the time, Pallas kernels for 0%

profile of v2, /device:TPU:17, one launch (start us, length us, event | category | flops | bytes accessed | tf_op | source)
XLA Modules:
  0.0 167.4 jit_solution(10789008194785328498)
XLA Ops:
  0.0 3.4 %collective-permute-start = (f32[512,128]{1,0:T(8,128)}, f32[512,128]{1,0:T(8,128)S(1)}, u32[]{:S(2)}, u32[]{:S(2)}) collective-permute-start(f32[512,128]{1,0:T(8,128)} %param.4), channel_id=1, source_target_pairs={{0,0},{1,32},{2,64},{3,96},{4,128},{5,160},{6,192},{7,224},{8,8},{... | collective-permute-start | bytes 786440 | tf_op jit(solution)/shard_map/ppermute | solution.py:32
  3.5 18.4 %collective-permute-done = f32[512,128]{1,0:T(8,128)S(1)} collective-permute-done((f32[512,128]{1,0:T(8,128)}, f32[512,128]{1,0:T(8,128)S(1)}, u32[]{:S(2)}, u32[]{:S(2)}) %collective-permute-start) | collective-permute-done | bytes 262176 | tf_op jit(solution)/shard_map/ppermute | solution.py:32
  24.2 6.2 %collective-permute-done.2 = f32[512,128]{1,0:T(8,128)S(1)} collective-permute-done((f32[512,128]{1,0:T(8,128)S(1)}, f32[512,128]{1,0:T(8,128)S(1)}, u32[]{:S(2)}, u32[]{:S(2)}) %collective-permute-start.2) | collective-permute-done | bytes 262176 | tf_op jit(solution)/shard_map/ppermute | solution.py:37
  30.4 5.7 %collective-permute-done.3 = f32[512,128]{1,0:T(8,128)S(1)} collective-permute-done((f32[512,128]{1,0:T(8,128)S(1)}, f32[512,128]{1,0:T(8,128)S(1)}, u32[]{:S(2)}, u32[]{:S(2)}) %collective-permute-start.3) | collective-permute-done | bytes 262176 | tf_op jit(solution)/shard_map/ppermute | solution.py:37
  36.1 6.6 %convolution_bitcast_fusion = f32[512,128]{0,1:T(8,128)S(1)} fusion(f32[2048,128]{1,0:T(8,128)S(1)} %constant_dynamic-update-slice_fusion.4, f32[512,2048]{1,0:T(8,128)} %param.3), kind=kOutput, calls=%fused_computation.9 | convolution fusion | flops 1610612736 | bytes 5505024 | tf_op jit(solution)/shard_map/dot_general | solution.py:8
  43.0 16.2 %collective-permute-start.10 = (f32[64,128]{1,0:T(8,128)S(1)}, f32[64,128]{1,0:T(8,128)S(1)}, u32[]{:S(2)}, u32[]{:S(2)}) collective-permute-start(f32[64,128]{1,0:T(8,128)S(1)} %get-tuple-element.8), channel_id=1, source_target_pairs={{0,7},{1,0},{2,1},{3,2},{4,3},{5,4},{6,5},{7,6},{8,15},{9,8},{10,9... | collective-permute-start | bytes 98312 | tf_op jit(solution)/shard_map/ppermute | solution.py:51
  61.8 4.1 %collective-permute-start.7 = (f32[64,128]{1,0:T(8,128)S(1)}, f32[64,128]{1,0:T(8,128)S(1)}, u32[]{:S(2)}, u32[]{:S(2)}) collective-permute-start(f32[64,128]{1,0:T(8,128)S(1)} %get-tuple-element.11), channel_id=1, source_target_pairs={{0,4},{1,5},{2,6},{3,7},{4,0},{5,1},{6,2},{7,3},{8,12},{9,13},{10,... | collective-permute-start | bytes 98312 | tf_op jit(solution)/shard_map/ppermute | solution.py:51
  66.0 2.7 %collective-permute-start.5 = (f32[64,128]{1,0:T(8,128)S(1)}, f32[64,128]{1,0:T(8,128)S(1)}, u32[]{:S(2)}, u32[]{:S(2)}) collective-permute-start(f32[64,128]{1,0:T(8,128)S(1)} %get-tuple-element.13), channel_id=1, source_target_pairs={{0,2},{1,3},{2,4},{3,5},{4,6},{5,7},{6,0},{7,1},{8,10},{9,11},{10,... | collective-permute-start | bytes 98312 | tf_op jit(solution)/shard_map/ppermute | solution.py:51
  69.0 3.2 %collective-permute-done.6 = f32[64,128]{1,0:T(8,128)S(1)} collective-permute-done((f32[64,128]{1,0:T(8,128)S(1)}, f32[64,128]{1,0:T(8,128)S(1)}, u32[]{:S(2)}, u32[]{:S(2)}) %collective-permute-start.6) | collective-permute-done | bytes 32800 | tf_op jit(solution)/shard_map/ppermute | solution.py:51
  74.4 3.3 %collective-permute-start.15 = (f32[64,128]{1,0:T(8,128)S(1)}, f32[64,128]{1,0:T(8,128)S(1)}, u32[]{:S(2)}, u32[]{:S(2)}) collective-permute-start(f32[64,128]{1,0:T(8,128)S(1)} %get-tuple-element.6), channel_id=1, source_target_pairs={{0,5},{1,6},{2,7},{3,0},{4,1},{5,2},{6,3},{7,4},{8,13},{9,14},{10,... | collective-permute-start | bytes 98312 | tf_op jit(solution)/shard_map/ppermute | solution.py:56
  77.7 3.1 %collective-permute-start.14 = (f32[64,128]{1,0:T(8,128)S(1)}, f32[64,128]{1,0:T(8,128)S(1)}, u32[]{:S(2)}, u32[]{:S(2)}) collective-permute-start(f32[64,128]{1,0:T(8,128)S(1)} %get-tuple-element.6), channel_id=1, source_target_pairs={{0,4},{1,5},{2,6},{3,7},{4,0},{5,1},{6,2},{7,3},{8,12},{9,13},{10,... | collective-permute-start | bytes 98312 | tf_op jit(solution)/shard_map/ppermute | solution.py:56
  80.9 3.0 %collective-permute-start.12 = (f32[64,128]{1,0:T(8,128)S(1)}, f32[64,128]{1,0:T(8,128)S(1)}, u32[]{:S(2)}, u32[]{:S(2)}) collective-permute-start(f32[64,128]{1,0:T(8,128)S(1)} %get-tuple-element.6), channel_id=1, source_target_pairs={{0,2},{1,3},{2,4},{3,5},{4,6},{5,7},{6,0},{7,1},{8,10},{9,11},{10,... | collective-permute-start | bytes 98312 | tf_op jit(solution)/shard_map/ppermute | solution.py:56
  85.7 2.5 %collective-permute-start.17 = (f32[64,128]{1,0:T(8,128)S(1)}, f32[64,128]{1,0:T(8,128)S(1)}, u32[]{:S(2)}, u32[]{:S(2)}) collective-permute-start(f32[64,128]{1,0:T(8,128)S(1)} %get-tuple-element.6), channel_id=1, source_target_pairs={{0,7},{1,0},{2,1},{3,2},{4,3},{5,4},{6,5},{7,6},{8,15},{9,8},{10,9... | collective-permute-start | bytes 98312 | tf_op jit(solution)/shard_map/ppermute | solution.py:56
  92.3 15.6 %collective-permute-done.18 = f32[512,128]{1,0:T(8,128)S(1)} collective-permute-done((f32[512,128]{1,0:T(8,128)S(1)}, f32[512,128]{1,0:T(8,128)S(1)}, u32[]{:S(2)}, u32[]{:S(2)}) %collective-permute-start.18) | collective-permute-done | bytes 262176 | tf_op jit(solution)/shard_map/ppermute | solution.py:32
  111.8 6.2 %collective-permute-done.20 = f32[512,128]{1,0:T(8,128)S(1)} collective-permute-done((f32[512,128]{1,0:T(8,128)S(1)}, f32[512,128]{1,0:T(8,128)S(1)}, u32[]{:S(2)}, u32[]{:S(2)}) %collective-permute-start.20) | collective-permute-done | bytes 262176 | tf_op jit(solution)/shard_map/ppermute | solution.py:37
  118.0 5.7 %collective-permute-done.21 = f32[512,128]{1,0:T(8,128)S(1)} collective-permute-done((f32[512,128]{1,0:T(8,128)S(1)}, f32[512,128]{1,0:T(8,128)S(1)}, u32[]{:S(2)}, u32[]{:S(2)}) %collective-permute-start.21) | collective-permute-done | bytes 262176 | tf_op jit(solution)/shard_map/ppermute | solution.py:37
  125.6 10.9 %collective-permute-start.28 = (f32[128,128]{1,0:T(8,128)S(1)}, f32[128,128]{1,0:T(8,128)S(1)}, u32[]{:S(2)}, u32[]{:S(2)}) collective-permute-start(f32[128,128]{1,0:T(8,128)S(1)} %fusion.23), channel_id=1, source_target_pairs={{0,7},{1,0},{2,1},{3,2},{4,3},{5,4},{6,5},{7,6},{8,15},{9,8},{10,9... | collective-permute-start | bytes 196616 | tf_op jit(solution)/shard_map/ppermute | solution.py:66
  136.4 6.9 %collective-permute-start.26 = (f32[128,128]{1,0:T(8,128)S(1)}, f32[128,128]{1,0:T(8,128)S(1)}, u32[]{:S(2)}, u32[]{:S(2)}) collective-permute-start(f32[128,128]{1,0:T(8,128)S(1)} %fusion.23), channel_id=1, source_target_pairs={{0,5},{1,6},{2,7},{3,0},{4,1},{5,2},{6,3},{7,4},{8,13},{9,14},{10,... | collective-permute-start | bytes 196616 | tf_op jit(solution)/shard_map/ppermute | solution.py:66
  143.4 3.1 %collective-permute-start.24 = (f32[128,128]{1,0:T(8,128)S(1)}, f32[128,128]{1,0:T(8,128)S(1)}, u32[]{:S(2)}, u32[]{:S(2)}) collective-permute-start(f32[128,128]{1,0:T(8,128)S(1)} %fusion.23), channel_id=1, source_target_pairs={{0,3},{1,4},{2,5},{3,6},{4,7},{5,0},{6,1},{7,2},{8,11},{9,12},{10,... | collective-permute-start | bytes 196616 | tf_op jit(solution)/shard_map/ppermute | solution.py:66
  146.4 2.9 %collective-permute-start.22 = (f32[128,128]{1,0:T(8,128)S(1)}, f32[128,128]{1,0:T(8,128)S(1)}, u32[]{:S(2)}, u32[]{:S(2)}) collective-permute-start(f32[128,128]{1,0:T(8,128)S(1)} %fusion.23), channel_id=1, source_target_pairs={{0,1},{1,2},{2,3},{3,4},{4,5},{5,6},{6,7},{7,0},{8,9},{9,10},{10,1... | collective-permute-start | bytes 196616 | tf_op jit(solution)/shard_map/ppermute | solution.py:66
  149.3 2.5 %collective-permute-done.25 = f32[128,128]{1,0:T(8,128)S(1)} collective-permute-done((f32[128,128]{1,0:T(8,128)S(1)}, f32[128,128]{1,0:T(8,128)S(1)}, u32[]{:S(2)}, u32[]{:S(2)}) %collective-permute-start.25) | collective-permute-done | bytes 65568 | tf_op jit(solution)/shard_map/ppermute | solution.py:66
  151.8 2.7 %collective-permute-done.23 = f32[128,128]{1,0:T(8,128)S(1)} collective-permute-done((f32[128,128]{1,0:T(8,128)S(1)}, f32[128,128]{1,0:T(8,128)S(1)}, u32[]{:S(2)}, u32[]{:S(2)}) %collective-permute-start.23) | collective-permute-done | bytes 65568 | tf_op jit(solution)/shard_map/ppermute | solution.py:66
  154.6 4.2 %collective-permute-done.22 = f32[128,128]{1,0:T(8,128)S(1)} collective-permute-done((f32[128,128]{1,0:T(8,128)S(1)}, f32[128,128]{1,0:T(8,128)S(1)}, u32[]{:S(2)}, u32[]{:S(2)}) %collective-permute-start.22) | collective-permute-done | bytes 65568 | tf_op jit(solution)/shard_map/ppermute | solution.py:66
  162.1 5.3 %convolution_subtract_fusion = f32[512,2048]{1,0:T(8,128)} fusion(f32[512,2048]{1,0:T(8,128)S(1)} %copy-done.1, f32[2048,128]{1,0:T(8,128)S(1)} %constant_dynamic-update-slice_fusion.4, f32[2048,128]{1,0:T(8,128)S(1)} %convolution_subtract_fusion.1, f32[512,128]{1,0:T(8,128)S(1)} %convolution_subtract_fusion.2, f32[512,128]{1,0:T(8,128)S(1)} %copy-done.2), kind=kOutput, calls=%fused_computation | convolution fusion | flops 3222929408 | bytes 11010048 | tf_op jit(solution)/shard_map/dot_general | solution.py:80
  (70 shorter events, 22.7 us)
Async XLA Ops:
  0.0 21.8 %collective-permute-start = (f32[512,128]{1,0:T(8,128)}, f32[512,128]{1,0:T(8,128)S(1)}, u32[]{:S(2)}, u32[]{:S(2)}) collective-permute-start(f32[512,128]{1,0:T(8,128)} %param.4), channel_id=1, source_target_pairs={{0,0},{1,32},{2,64},{3,96},{4,128},{5,160},{6,192},{7,224},{8,8},{... | collective-permute-start | bytes 786440 | tf_op jit(solution)/shard_map/ppermute | solution.py:32
  22.4 7.9 %collective-permute-start.2 = (f32[512,128]{1,0:T(8,128)S(1)}, f32[512,128]{1,0:T(8,128)S(1)}, u32[]{:S(2)}, u32[]{:S(2)}) collective-permute-start(f32[512,128]{1,0:T(8,128)S(1)} %collective-permute-done), channel_id=1, source_target_pairs={{0,16},{8,24},{16,0},{24,8},{32,48},{40,56},{48,32},{56,40},{64,80... | collective-permute-start | bytes 786440 | tf_op jit(solution)/shard_map/ppermute | solution.py:37
  23.9 12.2 %collective-permute-start.3 = (f32[512,128]{1,0:T(8,128)S(1)}, f32[512,128]{1,0:T(8,128)S(1)}, u32[]{:S(2)}, u32[]{:S(2)}) collective-permute-start(f32[512,128]{1,0:T(8,128)S(1)} %collective-permute-done), channel_id=1, source_target_pairs={{0,24},{8,16},{16,8},{24,0},{32,56},{40,48},{48,40},{56,32},{64,88... | collective-permute-start | bytes 786440 | tf_op jit(solution)/shard_map/ppermute | solution.py:37
  42.9 23.0 %collective-permute-start.4 = (f32[64,128]{1,0:T(8,128)S(1)}, f32[64,128]{1,0:T(8,128)S(1)}, u32[]{:S(2)}, u32[]{:S(2)}) collective-permute-start(f32[64,128]{1,0:T(8,128)S(1)} %get-tuple-element.7), channel_id=1, source_target_pairs={{0,1},{1,2},{2,3},{3,4},{4,5},{5,6},{6,7},{7,0},{8,9},{9,10},{10,1... | collective-permute-start | bytes 98312 | tf_op jit(solution)/shard_map/ppermute | solution.py:51
  43.0 22.9 %collective-permute-start.10 = (f32[64,128]{1,0:T(8,128)S(1)}, f32[64,128]{1,0:T(8,128)S(1)}, u32[]{:S(2)}, u32[]{:S(2)}) collective-permute-start(f32[64,128]{1,0:T(8,128)S(1)} %get-tuple-element.8), channel_id=1, source_target_pairs={{0,7},{1,0},{2,1},{3,2},{4,3},{5,4},{6,5},{7,6},{8,15},{9,8},{10,9... | collective-permute-start | bytes 98312 | tf_op jit(solution)/shard_map/ppermute | solution.py:51
  59.2 9.5 %collective-permute-start.9 = (f32[64,128]{1,0:T(8,128)S(1)}, f32[64,128]{1,0:T(8,128)S(1)}, u32[]{:S(2)}, u32[]{:S(2)}) collective-permute-start(f32[64,128]{1,0:T(8,128)S(1)} %get-tuple-element.9), channel_id=1, source_target_pairs={{0,6},{1,7},{2,0},{3,1},{4,2},{5,3},{6,4},{7,5},{8,14},{9,15},{10,... | collective-permute-start | bytes 98312 | tf_op jit(solution)/shard_map/ppermute | solution.py:51
  60.3 8.4 %collective-permute-start.8 = (f32[64,128]{1,0:T(8,128)S(1)}, f32[64,128]{1,0:T(8,128)S(1)}, u32[]{:S(2)}, u32[]{:S(2)}) collective-permute-start(f32[64,128]{1,0:T(8,128)S(1)} %get-tuple-element.10), channel_id=1, source_target_pairs={{0,5},{1,6},{2,7},{3,0},{4,1},{5,2},{6,3},{7,4},{8,13},{9,14},{10,... | collective-permute-start | bytes 98312 | tf_op jit(solution)/shard_map/ppermute | solution.py:51
  61.8 7.1 %collective-permute-start.7 = (f32[64,128]{1,0:T(8,128)S(1)}, f32[64,128]{1,0:T(8,128)S(1)}, u32[]{:S(2)}, u32[]{:S(2)}) collective-permute-start(f32[64,128]{1,0:T(8,128)S(1)} %get-tuple-element.11), channel_id=1, source_target_pairs={{0,4},{1,5},{2,6},{3,7},{4,0},{5,1},{6,2},{7,3},{8,12},{9,13},{10,... | collective-permute-start | bytes 98312 | tf_op jit(solution)/shard_map/ppermute | solution.py:51
  66.0 6.7 %collective-permute-start.5 = (f32[64,128]{1,0:T(8,128)S(1)}, f32[64,128]{1,0:T(8,128)S(1)}, u32[]{:S(2)}, u32[]{:S(2)}) collective-permute-start(f32[64,128]{1,0:T(8,128)S(1)} %get-tuple-element.13), channel_id=1, source_target_pairs={{0,2},{1,3},{2,4},{3,5},{4,6},{5,7},{6,0},{7,1},{8,10},{9,11},{10,... | collective-permute-start | bytes 98312 | tf_op jit(solution)/shard_map/ppermute | solution.py:51
  72.7 8.1 %collective-permute-start.11 = (f32[64,128]{1,0:T(8,128)S(1)}, f32[64,128]{1,0:T(8,128)S(1)}, u32[]{:S(2)}, u32[]{:S(2)}) collective-permute-start(f32[64,128]{1,0:T(8,128)S(1)} %get-tuple-element.6), channel_id=1, source_target_pairs={{0,1},{1,2},{2,3},{3,4},{4,5},{5,6},{6,7},{7,0},{8,9},{9,10},{10,1... | collective-permute-start | bytes 98312 | tf_op jit(solution)/shard_map/ppermute | solution.py:56
  73.4 15.0 %collective-permute-start.16 = (f32[64,128]{1,0:T(8,128)S(1)}, f32[64,128]{1,0:T(8,128)S(1)}, u32[]{:S(2)}, u32[]{:S(2)}) collective-permute-start(f32[64,128]{1,0:T(8,128)S(1)} %get-tuple-element.6), channel_id=1, source_target_pairs={{0,6},{1,7},{2,0},{3,1},{4,2},{5,3},{6,4},{7,5},{8,14},{9,15},{10,... | collective-permute-start | bytes 98312 | tf_op jit(solution)/shard_map/ppermute | solution.py:56
  74.4 13.9 %collective-permute-start.15 = (f32[64,128]{1,0:T(8,128)S(1)}, f32[64,128]{1,0:T(8,128)S(1)}, u32[]{:S(2)}, u32[]{:S(2)}) collective-permute-start(f32[64,128]{1,0:T(8,128)S(1)} %get-tuple-element.6), channel_id=1, source_target_pairs={{0,5},{1,6},{2,7},{3,0},{4,1},{5,2},{6,3},{7,4},{8,13},{9,14},{10,... | collective-permute-start | bytes 98312 | tf_op jit(solution)/shard_map/ppermute | solution.py:56
  77.7 10.6 %collective-permute-start.14 = (f32[64,128]{1,0:T(8,128)S(1)}, f32[64,128]{1,0:T(8,128)S(1)}, u32[]{:S(2)}, u32[]{:S(2)}) collective-permute-start(f32[64,128]{1,0:T(8,128)S(1)} %get-tuple-element.6), channel_id=1, source_target_pairs={{0,4},{1,5},{2,6},{3,7},{4,0},{5,1},{6,2},{7,3},{8,12},{9,13},{10,... | collective-permute-start | bytes 98312 | tf_op jit(solution)/shard_map/ppermute | solution.py:56
  80.9 7.4 %collective-permute-start.13 = (f32[64,128]{1,0:T(8,128)S(1)}, f32[64,128]{1,0:T(8,128)S(1)}, u32[]{:S(2)}, u32[]{:S(2)}) collective-permute-start(f32[64,128]{1,0:T(8,128)S(1)} %get-tuple-element.6), channel_id=1, source_target_pairs={{0,3},{1,4},{2,5},{3,6},{4,7},{5,0},{6,1},{7,2},{8,11},{9,12},{10,... | collective-permute-start | bytes 98312 | tf_op jit(solution)/shard_map/ppermute | solution.py:56
  90.4 17.6 %collective-permute-start.18 = (f32[512,128]{1,0:T(8,128)S(1)}, f32[512,128]{1,0:T(8,128)S(1)}, u32[]{:S(2)}, u32[]{:S(2)}) collective-permute-start(f32[512,128]{1,0:T(8,128)S(1)} %bitcast.68), channel_id=1, source_target_pairs={{0,0},{1,32},{2,64},{3,96},{4,128},{5,160},{6,192},{7,224},{8,8},{... | collective-permute-start | bytes 786440 | tf_op jit(solution)/shard_map/ppermute | solution.py:32
  110.1 7.9 %collective-permute-start.20 = (f32[512,128]{1,0:T(8,128)S(1)}, f32[512,128]{1,0:T(8,128)S(1)}, u32[]{:S(2)}, u32[]{:S(2)}) collective-permute-start(f32[512,128]{1,0:T(8,128)S(1)} %collective-permute-done.18), channel_id=1, source_target_pairs={{0,16},{8,24},{16,0},{24,8},{32,48},{40,56},{48,32},{56,40},{64,80... | collective-permute-start | bytes 786440 | tf_op jit(solution)/shard_map/ppermute | solution.py:37
  111.1 12.6 %collective-permute-start.21 = (f32[512,128]{1,0:T(8,128)S(1)}, f32[512,128]{1,0:T(8,128)S(1)}, u32[]{:S(2)}, u32[]{:S(2)}) collective-permute-start(f32[512,128]{1,0:T(8,128)S(1)} %collective-permute-done.18), channel_id=1, source_target_pairs={{0,24},{8,16},{16,8},{24,0},{32,56},{40,48},{48,40},{56,32},{64,88... | collective-permute-start | bytes 786440 | tf_op jit(solution)/shard_map/ppermute | solution.py:37
  125.6 20.9 %collective-permute-start.28 = (f32[128,128]{1,0:T(8,128)S(1)}, f32[128,128]{1,0:T(8,128)S(1)}, u32[]{:S(2)}, u32[]{:S(2)}) collective-permute-start(f32[128,128]{1,0:T(8,128)S(1)} %fusion.23), channel_id=1, source_target_pairs={{0,7},{1,0},{2,1},{3,2},{4,3},{5,4},{6,5},{7,6},{8,15},{9,8},{10,9... | collective-permute-start | bytes 196616 | tf_op jit(solution)/shard_map/ppermute | solution.py:66
  136.4 10.0 %collective-permute-start.27 = (f32[128,128]{1,0:T(8,128)S(1)}, f32[128,128]{1,0:T(8,128)S(1)}, u32[]{:S(2)}, u32[]{:S(2)}) collective-permute-start(f32[128,128]{1,0:T(8,128)S(1)} %fusion.23), channel_id=1, source_target_pairs={{0,6},{1,7},{2,0},{3,1},{4,2},{5,3},{6,4},{7,5},{8,14},{9,15},{10,... | collective-permute-start | bytes 196616 | tf_op jit(solution)/shard_map/ppermute | solution.py:66
  136.4 12.9 %collective-permute-start.26 = (f32[128,128]{1,0:T(8,128)S(1)}, f32[128,128]{1,0:T(8,128)S(1)}, u32[]{:S(2)}, u32[]{:S(2)}) collective-permute-start(f32[128,128]{1,0:T(8,128)S(1)} %fusion.23), channel_id=1, source_target_pairs={{0,5},{1,6},{2,7},{3,0},{4,1},{5,2},{6,3},{7,4},{8,13},{9,14},{10,... | collective-permute-start | bytes 196616 | tf_op jit(solution)/shard_map/ppermute | solution.py:66
  143.4 8.5 %collective-permute-start.25 = (f32[128,128]{1,0:T(8,128)S(1)}, f32[128,128]{1,0:T(8,128)S(1)}, u32[]{:S(2)}, u32[]{:S(2)}) collective-permute-start(f32[128,128]{1,0:T(8,128)S(1)} %fusion.23), channel_id=1, source_target_pairs={{0,4},{1,5},{2,6},{3,7},{4,0},{5,1},{6,2},{7,3},{8,12},{9,13},{10,... | collective-permute-start | bytes 196616 | tf_op jit(solution)/shard_map/ppermute | solution.py:66
  143.4 8.5 %collective-permute-start.24 = (f32[128,128]{1,0:T(8,128)S(1)}, f32[128,128]{1,0:T(8,128)S(1)}, u32[]{:S(2)}, u32[]{:S(2)}) collective-permute-start(f32[128,128]{1,0:T(8,128)S(1)} %fusion.23), channel_id=1, source_target_pairs={{0,3},{1,4},{2,5},{3,6},{4,7},{5,0},{6,1},{7,2},{8,11},{9,12},{10,... | collective-permute-start | bytes 196616 | tf_op jit(solution)/shard_map/ppermute | solution.py:66
  146.4 8.1 %collective-permute-start.23 = (f32[128,128]{1,0:T(8,128)S(1)}, f32[128,128]{1,0:T(8,128)S(1)}, u32[]{:S(2)}, u32[]{:S(2)}) collective-permute-start(f32[128,128]{1,0:T(8,128)S(1)} %fusion.23), channel_id=1, source_target_pairs={{0,2},{1,3},{2,4},{3,5},{4,6},{5,7},{6,0},{7,1},{8,10},{9,11},{10,... | collective-permute-start | bytes 196616 | tf_op jit(solution)/shard_map/ppermute | solution.py:66
  146.4 12.4 %collective-permute-start.22 = (f32[128,128]{1,0:T(8,128)S(1)}, f32[128,128]{1,0:T(8,128)S(1)}, u32[]{:S(2)}, u32[]{:S(2)}) collective-permute-start(f32[128,128]{1,0:T(8,128)S(1)} %fusion.23), channel_id=1, source_target_pairs={{0,1},{1,2},{2,3},{3,4},{4,5},{5,6},{6,7},{7,0},{8,9},{9,10},{10,1... | collective-permute-start | bytes 196616 | tf_op jit(solution)/shard_map/ppermute | solution.py:66
  (8 other events, 333.8 us)

commit v3 on v2

--- a/solution.py
+++ b/solution.py
@@ -26,15 +26,19 @@
     pairs = []
     for src_row in range(row_count):
         for src_col in range(col_count):
-            dst_row = per * src_col + src_row % per
             dst_col = src_row // per
+            low = src_row % per
+            dst_row = per * (src_col ^ dst_col ^ low) + low
             pairs.append((src_row * col_count + src_col, dst_row * col_count + dst_col))
     mine = lax.ppermute(panel_rows, ("row", "col"), pairs)
     low = lax.axis_index("row") % per
     gathered = jnp.zeros((per * rows_here,) + panel_rows.shape[1:], panel_rows.dtype)
     gathered = lax.dynamic_update_slice_in_dim(gathered, mine, low * rows_here, 0)
-    for mask in range(1, per):
-        block = lax.ppermute(mine, "row", [(i, i ^ mask) for i in range(row_count)])
+    core_pairs = [(i, i ^ 1) for i in range(row_count)]
+    other = lax.ppermute(mine, "row", core_pairs)
+    across = lax.ppermute(mine, "row", [(i, i ^ 2) for i in range(row_count)])
+    diagonal = lax.ppermute(across, "row", core_pairs)
+    for mask, block in ((1, other), (2, across), (3, diagonal)):
         gathered = lax.dynamic_update_slice_in_dim(gathered, block, (low ^ mask) * rows_here, 0)
     return gathered
 
@@ -60,11 +64,11 @@
 
 def col_sum(value):
     count = lax.axis_size("col")
-    total = value
-    for shift in range(1, count):
-        pairs = [(i, (i + shift) % count) for i in range(count)]
-        total = total + lax.ppermute(value, "col", pairs)
-    return total
+    step = 1
+    while step < count:
+        value = value + lax.ppermute(value, "col", [(i, i ^ step) for i in range(count)])
+        step *= 2
+    return value
 
 
 def shards(matrix, vectors, tfactor):

time: 168 us -> 155 us (0.923)
  the two profiles are of different devices: /device:TPU:17 before, /device:TPU:6 now
where the time goes in v3:
time: 155 us
  waiting for transfers between devices  92.5 us (60%)
  starting transfers between devices  44.2 us (29%)
  matrix products  17 us (11%)
    ppermute x2, waiting for transfers between devices, to_columns(): mine = lax.ppermute(panel_rows, ('row', 'col'), pairs)  49.6 us
    ppermute x3, waiting for transfers between devices, col_sum(): lax.ppermute(value, 'col', [(i, i ^ step) for i in range(count)])  17.4 us
    ppermute x7, starting transfers between devices, col_sum_rows(): total = total + lax.ppermute(sent, 'col', pairs)  17.2 us
    ppermute x7, starting transfers between devices, col_sum_rows(): got = lax.ppermute(total, 'col', pairs)  14.4 us
    ppermute x2, waiting for transfers between devices, to_columns(): across = lax.ppermute(mine, 'row', [(i, i ^ 2) for i in range(row_count)])  12.7 us
    ppermute x2, starting transfers between devices, to_columns(): mine = lax.ppermute(panel_rows, ('row', 'col'), pairs)  11.6 us
    dot_general x6, matrix products, product(): jnp.dot(left, right, precision=lax.Precision.HIGHEST, preferred_element_t...  9.53 us
    ppermute x7, waiting for transfers between devices, col_sum_rows(): got = lax.ppermute(total, 'col', pairs)  6.63 us
  transfers between devices with their start and end apart: 25, of which 13 were waited for; matrix products, arithmetic and copies ran while one was open for 0% of the time, Pallas kernels for 0%

profile of v3, /device:TPU:6, one launch (start us, length us, event | category | flops | bytes accessed | tf_op | source)
XLA Modules:
  0.0 154.6 jit_solution(4705735532209906890)
XLA Ops:
  0.0 8.3 %collective-permute-start = (f32[512,128]{1,0:T(8,128)}, f32[512,128]{1,0:T(8,128)S(1)}, u32[]{:S(2)}, u32[]{:S(2)}) collective-permute-start(f32[512,128]{1,0:T(8,128)} %param.4), channel_id=1, source_target_pairs={{0,0},{1,32},{2,64},{3,96},{4,128},{5,160},{6,192},{7,224},{8,40},... | collective-permute-start | bytes 786440 | tf_op jit(solution)/shard_map/ppermute | solution.py:33
  8.3 24.9 %collective-permute-done = f32[512,128]{1,0:T(8,128)S(1)} collective-permute-done((f32[512,128]{1,0:T(8,128)}, f32[512,128]{1,0:T(8,128)S(1)}, u32[]{:S(2)}, u32[]{:S(2)}) %collective-permute-start) | collective-permute-done | bytes 262176 | tf_op jit(solution)/shard_map/ppermute | solution.py:33
  33.2 6.4 %collective-permute-done.2 = f32[512,128]{1,0:T(8,128)S(1)} collective-permute-done((f32[512,128]{1,0:T(8,128)S(1)}, f32[512,128]{1,0:T(8,128)S(1)}, u32[]{:S(2)}, u32[]{:S(2)}) %collective-permute-start.2) | collective-permute-done | bytes 262176 | tf_op jit(solution)/shard_map/ppermute | solution.py:39
  41.1 6.6 %convolution_bitcast_fusion = f32[512,128]{0,1:T(8,128)S(1)} fusion(f32[2048,128]{1,0:T(8,128)S(1)} %constant_dynamic-update-slice_fusion.4, f32[512,2048]{1,0:T(8,128)} %param.3), kind=kOutput, calls=%fused_computation.9 | convolution fusion | flops 1610612736 | bytes 5505024 | tf_op jit(solution)/shard_map/dot_general | solution.py:8
  48.0 5.7 %collective-permute-start.10 = (f32[64,128]{1,0:T(8,128)S(1)}, f32[64,128]{1,0:T(8,128)S(1)}, u32[]{:S(2)}, u32[]{:S(2)}) collective-permute-start(f32[64,128]{1,0:T(8,128)S(1)} %get-tuple-element.8), channel_id=1, source_target_pairs={{0,7},{1,0},{2,1},{3,2},{4,3},{5,4},{6,5},{7,6},{8,15},{9,8},{10,9... | collective-permute-start | bytes 98312 | tf_op jit(solution)/shard_map/ppermute | solution.py:55
  53.7 1.4 collective-permute-start.9
  55.1 2.7 %collective-permute-start.8 = (f32[64,128]{1,0:T(8,128)S(1)}, f32[64,128]{1,0:T(8,128)S(1)}, u32[]{:S(2)}, u32[]{:S(2)}) collective-permute-start(f32[64,128]{1,0:T(8,128)S(1)} %get-tuple-element.10), channel_id=1, source_target_pairs={{0,5},{1,6},{2,7},{3,0},{4,1},{5,2},{6,3},{7,4},{8,13},{9,14},{10,... | collective-permute-start | bytes 98312 | tf_op jit(solution)/shard_map/ppermute | solution.py:55
  57.8 3.7 %collective-permute-start.7 = (f32[64,128]{1,0:T(8,128)S(1)}, f32[64,128]{1,0:T(8,128)S(1)}, u32[]{:S(2)}, u32[]{:S(2)}) collective-permute-start(f32[64,128]{1,0:T(8,128)S(1)} %get-tuple-element.11), channel_id=1, source_target_pairs={{0,4},{1,5},{2,6},{3,7},{4,0},{5,1},{6,2},{7,3},{8,12},{9,13},{10,... | collective-permute-start | bytes 98312 | tf_op jit(solution)/shard_map/ppermute | solution.py:55
  61.6 3.6 %collective-permute-start.5 = (f32[64,128]{1,0:T(8,128)S(1)}, f32[64,128]{1,0:T(8,128)S(1)}, u32[]{:S(2)}, u32[]{:S(2)}) collective-permute-start(f32[64,128]{1,0:T(8,128)S(1)} %get-tuple-element.13), channel_id=1, source_target_pairs={{0,2},{1,3},{2,4},{3,5},{4,6},{5,7},{6,0},{7,1},{8,10},{9,11},{10,... | collective-permute-start | bytes 98312 | tf_op jit(solution)/shard_map/ppermute | solution.py:55
  65.8 2.8 %collective-permute-done.6 = f32[64,128]{1,0:T(8,128)S(1)} collective-permute-done((f32[64,128]{1,0:T(8,128)S(1)}, f32[64,128]{1,0:T(8,128)S(1)}, u32[]{:S(2)}, u32[]{:S(2)}) %collective-permute-start.6) | collective-permute-done | bytes 32800 | tf_op jit(solution)/shard_map/ppermute | solution.py:55
  68.6 1.9 %collective-permute-start.11 = (f32[64,128]{1,0:T(8,128)S(1)}, f32[64,128]{1,0:T(8,128)S(1)}, u32[]{:S(2)}, u32[]{:S(2)}) collective-permute-start(f32[64,128]{1,0:T(8,128)S(1)} %get-tuple-element.6), channel_id=1, source_target_pairs={{0,1},{1,2},{2,3},{3,4},{4,5},{5,6},{6,7},{7,0},{8,9},{9,10},{10,1... | collective-permute-start | bytes 98312 | tf_op jit(solution)/shard_map/ppermute | solution.py:60
  71.1 4.3 %collective-permute-start.15 = (f32[64,128]{1,0:T(8,128)S(1)}, f32[64,128]{1,0:T(8,128)S(1)}, u32[]{:S(2)}, u32[]{:S(2)}) collective-permute-start(f32[64,128]{1,0:T(8,128)S(1)} %get-tuple-element.6), channel_id=1, source_target_pairs={{0,5},{1,6},{2,7},{3,0},{4,1},{5,2},{6,3},{7,4},{8,13},{9,14},{10,... | collective-permute-start | bytes 98312 | tf_op jit(solution)/shard_map/ppermute | solution.py:60
  75.3 2.5 %collective-permute-start.14 = (f32[64,128]{1,0:T(8,128)S(1)}, f32[64,128]{1,0:T(8,128)S(1)}, u32[]{:S(2)}, u32[]{:S(2)}) collective-permute-start(f32[64,128]{1,0:T(8,128)S(1)} %get-tuple-element.6), channel_id=1, source_target_pairs={{0,4},{1,5},{2,6},{3,7},{4,0},{5,1},{6,2},{7,3},{8,12},{9,13},{10,... | collective-permute-start | bytes 98312 | tf_op jit(solution)/shard_map/ppermute | solution.py:60
  78.1 4.1 %collective-permute-start.12 = (f32[64,128]{1,0:T(8,128)S(1)}, f32[64,128]{1,0:T(8,128)S(1)}, u32[]{:S(2)}, u32[]{:S(2)}) collective-permute-start(f32[64,128]{1,0:T(8,128)S(1)} %get-tuple-element.6), channel_id=1, source_target_pairs={{0,2},{1,3},{2,4},{3,5},{4,6},{5,7},{6,0},{7,1},{8,10},{9,11},{10,... | collective-permute-start | bytes 98312 | tf_op jit(solution)/shard_map/ppermute | solution.py:60
  82.2 3.1 %collective-permute-done.12 = f32[64,128]{1,0:T(8,128)S(1)} collective-permute-done((f32[64,128]{1,0:T(8,128)S(1)}, f32[64,128]{1,0:T(8,128)S(1)}, u32[]{:S(2)}, u32[]{:S(2)}) %collective-permute-start.12) | collective-permute-done | bytes 32800 | tf_op jit(solution)/shard_map/ppermute | solution.py:60
  86.2 3.5 %collective-permute-done.17 = f32[64,128]{1,0:T(8,128)S(1)} collective-permute-done((f32[64,128]{1,0:T(8,128)S(1)}, f32[64,128]{1,0:T(8,128)S(1)}, u32[]{:S(2)}, u32[]{:S(2)}) %collective-permute-start.17) | collective-permute-done | bytes 32800 | tf_op jit(solution)/shard_map/ppermute | solution.py:60
  89.8 3.3 %collective-permute-start.18 = (f32[512,128]{1,0:T(8,128)S(1)}, f32[512,128]{1,0:T(8,128)S(1)}, u32[]{:S(2)}, u32[]{:S(2)}) collective-permute-start(f32[512,128]{1,0:T(8,128)S(1)} %bitcast.68), channel_id=1, source_target_pairs={{0,0},{1,32},{2,64},{3,96},{4,128},{5,160},{6,192},{7,224},{8,40},... | collective-permute-start | bytes 786440 | tf_op jit(solution)/shard_map/ppermute | solution.py:33
  93.1 24.8 %collective-permute-done.18 = f32[512,128]{1,0:T(8,128)S(1)} collective-permute-done((f32[512,128]{1,0:T(8,128)S(1)}, f32[512,128]{1,0:T(8,128)S(1)}, u32[]{:S(2)}, u32[]{:S(2)}) %collective-permute-start.18) | collective-permute-done | bytes 262176 | tf_op jit(solution)/shard_map/ppermute | solution.py:33
  117.9 6.4 %collective-permute-done.20 = f32[512,128]{1,0:T(8,128)S(1)} collective-permute-done((f32[512,128]{1,0:T(8,128)S(1)}, f32[512,128]{1,0:T(8,128)S(1)}, u32[]{:S(2)}, u32[]{:S(2)}) %collective-permute-start.20) | collective-permute-done | bytes 262176 | tf_op jit(solution)/shard_map/ppermute | solution.py:39
  125.8 1.8 %fusion.17 = f32[128,128]{1,0:T(8,128)S(1)} fusion(f32[2048,128]{1,0:T(8,128)S(1)} %constant_dynamic-update-slice_fusion.4, f32[2048,128]{1,0:T(8,128)S(1)} %constant_dynamic-update-slice_fusion), kind=kOutput, calls=%fused_computation.46 | convolution fusion | flops 402653184 | bytes 2162688 | tf_op jit(solution)/shard_map/dot_general | solution.py:12
  127.7 4.3 %collective-permute-done.22 = f32[128,128]{1,0:T(8,128)S(1)} collective-permute-done((f32[128,128]{1,0:T(8,128)S(1)}, f32[128,128]{1,0:T(8,128)S(1)}, u32[]{:S(2)}, u32[]{:S(2)}) %collective-permute-start.22) | collective-permute-done | bytes 65568 | tf_op jit(solution)/shard_map/ppermute | solution.py:69
  132.1 5.5 %collective-permute-done.23 = f32[128,128]{1,0:T(8,128)S(1)} collective-permute-done((f32[128,128]{1,0:T(8,128)S(1)}, f32[128,128]{1,0:T(8,128)S(1)}, u32[]{:S(2)}, u32[]{:S(2)}) %collective-permute-start.23) | collective-permute-done | bytes 65568 | tf_op jit(solution)/shard_map/ppermute | solution.py:69
  138.3 7.7 %collective-permute-done.24 = f32[128,128]{1,0:T(8,128)S(1)} collective-permute-done((f32[128,128]{1,0:T(8,128)S(1)}, f32[128,128]{1,0:T(8,128)S(1)}, u32[]{:S(2)}, u32[]{:S(2)}) %collective-permute-start.24) | collective-permute-done | bytes 65568 | tf_op jit(solution)/shard_map/ppermute | solution.py:69
  149.3 5.3 %convolution_subtract_fusion = f32[512,2048]{1,0:T(8,128)} fusion(f32[512,2048]{1,0:T(8,128)S(1)} %copy-done.1, f32[2048,128]{1,0:T(8,128)S(1)} %constant_dynamic-update-slice_fusion.4, f32[2048,128]{1,0:T(8,128)S(1)} %convolution_subtract_fusion.1, f32[512,128]{1,0:T(8,128)S(1)} %convolution_subtract_fusion.2, f32[512,128]{1,0:T(8,128)S(1)} %copy-done.2), kind=kOutput, calls=%fused_computation | convolution fusion | flops 3222929408 | bytes 11010048 | tf_op jit(solution)/shard_map/dot_general | solution.py:84
  (64 shorter events, 9.8 us)
Async XLA Ops:
  0.0 33.2 %collective-permute-start = (f32[512,128]{1,0:T(8,128)}, f32[512,128]{1,0:T(8,128)S(1)}, u32[]{:S(2)}, u32[]{:S(2)}) collective-permute-start(f32[512,128]{1,0:T(8,128)} %param.4), channel_id=1, source_target_pairs={{0,0},{1,32},{2,64},{3,96},{4,128},{5,160},{6,192},{7,224},{8,40},... | collective-permute-start | bytes 786440 | tf_op jit(solution)/shard_map/ppermute | solution.py:33
  33.2 6.4 %collective-permute-start.2 = (f32[512,128]{1,0:T(8,128)S(1)}, f32[512,128]{1,0:T(8,128)S(1)}, u32[]{:S(2)}, u32[]{:S(2)}) collective-permute-start(f32[512,128]{1,0:T(8,128)S(1)} %collective-permute-done), channel_id=1, source_target_pairs={{0,16},{8,24},{16,0},{24,8},{32,48},{40,56},{48,32},{56,40},{64,80... | collective-permute-start | bytes 786440 | tf_op jit(solution)/shard_map/ppermute | solution.py:39
  33.2 6.5 %collective-permute-start.1 = (f32[512,128]{1,0:T(8,128)S(1)}, f32[512,128]{1,0:T(8,128)S(1)}, u32[]{:S(2)}, u32[]{:S(2)}) collective-permute-start(f32[512,128]{1,0:T(8,128)S(1)} %collective-permute-done), channel_id=1, source_target_pairs={{0,8},{8,0},{16,24},{24,16},{32,40},{40,32},{48,56},{56,48},{64,72... | collective-permute-start | bytes 786440 | tf_op jit(solution)/shard_map/ppermute | solution.py:38
  48.0 13.6 %collective-permute-start.4 = (f32[64,128]{1,0:T(8,128)S(1)}, f32[64,128]{1,0:T(8,128)S(1)}, u32[]{:S(2)}, u32[]{:S(2)}) collective-permute-start(f32[64,128]{1,0:T(8,128)S(1)} %get-tuple-element.7), channel_id=1, source_target_pairs={{0,1},{1,2},{2,3},{3,4},{4,5},{5,6},{6,7},{7,0},{8,9},{9,10},{10,1... | collective-permute-start | bytes 98312 | tf_op jit(solution)/shard_map/ppermute | solution.py:55
  48.0 13.5 %collective-permute-start.10 = (f32[64,128]{1,0:T(8,128)S(1)}, f32[64,128]{1,0:T(8,128)S(1)}, u32[]{:S(2)}, u32[]{:S(2)}) collective-permute-start(f32[64,128]{1,0:T(8,128)S(1)} %get-tuple-element.8), channel_id=1, source_target_pairs={{0,7},{1,0},{2,1},{3,2},{4,3},{5,4},{6,5},{7,6},{8,15},{9,8},{10,9... | collective-permute-start | bytes 98312 | tf_op jit(solution)/shard_map/ppermute | solution.py:55
  53.7 11.5 %collective-permute-start.9 = (f32[64,128]{1,0:T(8,128)S(1)}, f32[64,128]{1,0:T(8,128)S(1)}, u32[]{:S(2)}, u32[]{:S(2)}) collective-permute-start(f32[64,128]{1,0:T(8,128)S(1)} %get-tuple-element.9), channel_id=1, source_target_pairs={{0,6},{1,7},{2,0},{3,1},{4,2},{5,3},{6,4},{7,5},{8,14},{9,15},{10,... | collective-permute-start | bytes 98312 | tf_op jit(solution)/shard_map/ppermute | solution.py:55
  55.1 10.1 %collective-permute-start.8 = (f32[64,128]{1,0:T(8,128)S(1)}, f32[64,128]{1,0:T(8,128)S(1)}, u32[]{:S(2)}, u32[]{:S(2)}) collective-permute-start(f32[64,128]{1,0:T(8,128)S(1)} %get-tuple-element.10), channel_id=1, source_target_pairs={{0,5},{1,6},{2,7},{3,0},{4,1},{5,2},{6,3},{7,4},{8,13},{9,14},{10,... | collective-permute-start | bytes 98312 | tf_op jit(solution)/shard_map/ppermute | solution.py:55
  57.8 7.9 %collective-permute-start.7 = (f32[64,128]{1,0:T(8,128)S(1)}, f32[64,128]{1,0:T(8,128)S(1)}, u32[]{:S(2)}, u32[]{:S(2)}) collective-permute-start(f32[64,128]{1,0:T(8,128)S(1)} %get-tuple-element.11), channel_id=1, source_target_pairs={{0,4},{1,5},{2,6},{3,7},{4,0},{5,1},{6,2},{7,3},{8,12},{9,13},{10,... | collective-permute-start | bytes 98312 | tf_op jit(solution)/shard_map/ppermute | solution.py:55
  61.6 7.0 %collective-permute-start.6 = (f32[64,128]{1,0:T(8,128)S(1)}, f32[64,128]{1,0:T(8,128)S(1)}, u32[]{:S(2)}, u32[]{:S(2)}) collective-permute-start(f32[64,128]{1,0:T(8,128)S(1)} %get-tuple-element.12), channel_id=1, source_target_pairs={{0,3},{1,4},{2,5},{3,6},{4,7},{5,0},{6,1},{7,2},{8,11},{9,12},{10,... | collective-permute-start | bytes 98312 | tf_op jit(solution)/shard_map/ppermute | solution.py:55
  61.6 7.0 %collective-permute-start.5 = (f32[64,128]{1,0:T(8,128)S(1)}, f32[64,128]{1,0:T(8,128)S(1)}, u32[]{:S(2)}, u32[]{:S(2)}) collective-permute-start(f32[64,128]{1,0:T(8,128)S(1)} %get-tuple-element.13), channel_id=1, source_target_pairs={{0,2},{1,3},{2,4},{3,5},{4,6},{5,7},{6,0},{7,1},{8,10},{9,11},{10,... | collective-permute-start | bytes 98312 | tf_op jit(solution)/shard_map/ppermute | solution.py:55
  68.6 9.5 %collective-permute-start.11 = (f32[64,128]{1,0:T(8,128)S(1)}, f32[64,128]{1,0:T(8,128)S(1)}, u32[]{:S(2)}, u32[]{:S(2)}) collective-permute-start(f32[64,128]{1,0:T(8,128)S(1)} %get-tuple-element.6), channel_id=1, source_target_pairs={{0,1},{1,2},{2,3},{3,4},{4,5},{5,6},{6,7},{7,0},{8,9},{9,10},{10,1... | collective-permute-start | bytes 98312 | tf_op jit(solution)/shard_map/ppermute | solution.py:60
  70.5 15.7 %collective-permute-start.16 = (f32[64,128]{1,0:T(8,128)S(1)}, f32[64,128]{1,0:T(8,128)S(1)}, u32[]{:S(2)}, u32[]{:S(2)}) collective-permute-start(f32[64,128]{1,0:T(8,128)S(1)} %get-tuple-element.6), channel_id=1, source_target_pairs={{0,6},{1,7},{2,0},{3,1},{4,2},{5,3},{6,4},{7,5},{8,14},{9,15},{10,... | collective-permute-start | bytes 98312 | tf_op jit(solution)/shard_map/ppermute | solution.py:60
  71.1 15.1 %collective-permute-start.15 = (f32[64,128]{1,0:T(8,128)S(1)}, f32[64,128]{1,0:T(8,128)S(1)}, u32[]{:S(2)}, u32[]{:S(2)}) collective-permute-start(f32[64,128]{1,0:T(8,128)S(1)} %get-tuple-element.6), channel_id=1, source_target_pairs={{0,5},{1,6},{2,7},{3,0},{4,1},{5,2},{6,3},{7,4},{8,13},{9,14},{10,... | collective-permute-start | bytes 98312 | tf_op jit(solution)/shard_map/ppermute | solution.py:60
  75.3 10.8 %collective-permute-start.14 = (f32[64,128]{1,0:T(8,128)S(1)}, f32[64,128]{1,0:T(8,128)S(1)}, u32[]{:S(2)}, u32[]{:S(2)}) collective-permute-start(f32[64,128]{1,0:T(8,128)S(1)} %get-tuple-element.6), channel_id=1, source_target_pairs={{0,4},{1,5},{2,6},{3,7},{4,0},{5,1},{6,2},{7,3},{8,12},{9,13},{10,... | collective-permute-start | bytes 98312 | tf_op jit(solution)/shard_map/ppermute | solution.py:60
  77.8 8.3 %collective-permute-start.13 = (f32[64,128]{1,0:T(8,128)S(1)}, f32[64,128]{1,0:T(8,128)S(1)}, u32[]{:S(2)}, u32[]{:S(2)}) collective-permute-start(f32[64,128]{1,0:T(8,128)S(1)} %get-tuple-element.6), channel_id=1, source_target_pairs={{0,3},{1,4},{2,5},{3,6},{4,7},{5,0},{6,1},{7,2},{8,11},{9,12},{10,... | collective-permute-start | bytes 98312 | tf_op jit(solution)/shard_map/ppermute | solution.py:60
  78.1 7.2 %collective-permute-start.12 = (f32[64,128]{1,0:T(8,128)S(1)}, f32[64,128]{1,0:T(8,128)S(1)}, u32[]{:S(2)}, u32[]{:S(2)}) collective-permute-start(f32[64,128]{1,0:T(8,128)S(1)} %get-tuple-element.6), channel_id=1, source_target_pairs={{0,2},{1,3},{2,4},{3,5},{4,6},{5,7},{6,0},{7,1},{8,10},{9,11},{10,... | collective-permute-start | bytes 98312 | tf_op jit(solution)/shard_map/ppermute | solution.py:60
  85.3 4.5 %collective-permute-start.17 = (f32[64,128]{1,0:T(8,128)S(1)}, f32[64,128]{1,0:T(8,128)S(1)}, u32[]{:S(2)}, u32[]{:S(2)}) collective-permute-start(f32[64,128]{1,0:T(8,128)S(1)} %get-tuple-element.6), channel_id=1, source_target_pairs={{0,7},{1,0},{2,1},{3,2},{4,3},{5,4},{6,5},{7,6},{8,15},{9,8},{10,9... | collective-permute-start | bytes 98312 | tf_op jit(solution)/shard_map/ppermute | solution.py:60
  89.8 28.1 %collective-permute-start.18 = (f32[512,128]{1,0:T(8,128)S(1)}, f32[512,128]{1,0:T(8,128)S(1)}, u32[]{:S(2)}, u32[]{:S(2)}) collective-permute-start(f32[512,128]{1,0:T(8,128)S(1)} %bitcast.68), channel_id=1, source_target_pairs={{0,0},{1,32},{2,64},{3,96},{4,128},{5,160},{6,192},{7,224},{8,40},... | collective-permute-start | bytes 786440 | tf_op jit(solution)/shard_map/ppermute | solution.py:33
  117.8 6.4 %collective-permute-start.20 = (f32[512,128]{1,0:T(8,128)S(1)}, f32[512,128]{1,0:T(8,128)S(1)}, u32[]{:S(2)}, u32[]{:S(2)}) collective-permute-start(f32[512,128]{1,0:T(8,128)S(1)} %collective-permute-done.18), channel_id=1, source_target_pairs={{0,16},{8,24},{16,0},{24,8},{32,48},{40,56},{48,32},{56,40},{64,80... | collective-permute-start | bytes 786440 | tf_op jit(solution)/shard_map/ppermute | solution.py:39
  117.8 6.5 %collective-permute-start.19 = (f32[512,128]{1,0:T(8,128)S(1)}, f32[512,128]{1,0:T(8,128)S(1)}, u32[]{:S(2)}, u32[]{:S(2)}) collective-permute-start(f32[512,128]{1,0:T(8,128)S(1)} %collective-permute-done.18), channel_id=1, source_target_pairs={{0,8},{8,0},{16,24},{24,16},{32,40},{40,32},{48,56},{56,48},{64,72... | collective-permute-start | bytes 786440 | tf_op jit(solution)/shard_map/ppermute | solution.py:38
  124.2 1.5 collective-permute-start.21
  127.6 4.4 %collective-permute-start.22 = (f32[128,128]{1,0:T(8,128)S(1)}, f32[128,128]{1,0:T(8,128)S(1)}, u32[]{:S(2)}, u32[]{:S(2)}) collective-permute-start(f32[128,128]{1,0:T(8,128)S(1)} %fusion.17), channel_id=1, source_target_pairs={{0,1},{1,0},{2,3},{3,2},{4,5},{5,4},{6,7},{7,6},{8,9},{9,8},{10,11... | collective-permute-start | bytes 196616 | tf_op jit(solution)/shard_map/ppermute | solution.py:69
  132.0 5.6 %collective-permute-start.23 = (f32[128,128]{1,0:T(8,128)S(1)}, f32[128,128]{1,0:T(8,128)S(1)}, u32[]{:S(2)}, u32[]{:S(2)}) collective-permute-start(f32[128,128]{1,0:T(8,128)S(1)} %add.217), channel_id=1, source_target_pairs={{0,2},{1,3},{2,0},{3,1},{4,6},{5,7},{6,4},{7,5},{8,10},{9,11},{10,... | collective-permute-start | bytes 196616 | tf_op jit(solution)/shard_map/ppermute | solution.py:69
  137.6 8.5 %collective-permute-start.24 = (f32[128,128]{1,0:T(8,128)S(1)}, f32[128,128]{1,0:T(8,128)S(1)}, u32[]{:S(2)}, u32[]{:S(2)}) collective-permute-start(f32[128,128]{1,0:T(8,128)S(1)} %add.218), channel_id=1, source_target_pairs={{0,4},{1,5},{2,6},{3,7},{4,0},{5,1},{6,2},{7,3},{8,12},{9,13},{10,... | collective-permute-start | bytes 196616 | tf_op jit(solution)/shard_map/ppermute | solution.py:69
  (4 other events, 268.1 us)

commit v4 on v3

--- a/solution.py
+++ b/solution.py
@@ -2,6 +2,18 @@
 import jax.numpy as jnp
 from jax import lax
 from jax.sharding import PartitionSpec as P
+
+
+SOURCE_COL = (
+    ((2, 0, 6, 1, 3, 5, 4, 7), (6, 2, 1, 4, 0, 7, 3, 5), (6, 7, 2, 1, 0, 3, 5, 4), (0, 5, 1, 3, 7, 4, 2, 6)),
+    ((2, 1, 5, 3, 6, 4, 7, 0), (5, 0, 4, 1, 7, 3, 6, 2), (7, 4, 5, 6, 2, 0, 1, 3), (4, 6, 7, 1, 5, 3, 2, 0)),
+    ((0, 7, 2, 6, 4, 1, 5, 3), (5, 4, 3, 7, 1, 6, 0, 2), (3, 4, 6, 0, 2, 1, 5, 7), (7, 1, 5, 4, 6, 2, 0, 3)),
+    ((0, 7, 1, 4, 3, 6, 2, 5), (3, 6, 7, 4, 5, 2, 1, 0), (5, 1, 3, 0, 6, 4, 7, 2), (0, 3, 1, 2, 4, 7, 5, 6)),
+    ((4, 6, 2, 5, 7, 3, 1, 0), (5, 2, 6, 3, 1, 0, 7, 4), (2, 3, 4, 7, 1, 6, 0, 5), (7, 6, 3, 2, 5, 0, 4, 1)),
+    ((7, 4, 6, 0, 1, 5, 3, 2), (2, 5, 3, 1, 0, 7, 4, 6), (3, 2, 6, 5, 1, 7, 0, 4), (6, 7, 2, 0, 3, 5, 4, 1)),
+    ((2, 5, 3, 0, 6, 4, 7, 1), (4, 1, 7, 2, 3, 0, 5, 6), (2, 0, 4, 6, 1, 7, 3, 5), (1, 3, 7, 5, 4, 2, 6, 0)),
+    ((6, 3, 0, 7, 5, 1, 2, 4), (1, 6, 2, 5, 4, 3, 0, 7), (1, 7, 0, 4, 2, 6, 3, 5), (5, 1, 4, 3, 7, 0, 6, 2)),
+)
 
 
 def product(left, right):
@@ -28,7 +40,11 @@
         for src_col in range(col_count):
             dst_col = src_row // per
             low = src_row % per
-            dst_row = per * (src_col ^ dst_col ^ low) + low
+            if (row_count, col_count) == (32, 8):
+                high = SOURCE_COL[dst_col][low].index(src_col)
+            else:
+                high = src_col ^ dst_col ^ low
+            dst_row = per * high + low
             pairs.append((src_row * col_count + src_col, dst_row * col_count + dst_col))
     mine = lax.ppermute(panel_rows, ("row", "col"), pairs)
     low = lax.axis_index("row") % per
@@ -64,11 +80,16 @@
 
 def col_sum(value):
     count = lax.axis_size("col")
-    step = 1
-    while step < count:
-        value = value + lax.ppermute(value, "col", [(i, i ^ step) for i in range(count)])
-        step *= 2
-    return value
+    if count != 8:
+        step = 1
+        while step < count:
+            value = value + lax.ppermute(value, "col", [(i, i ^ step) for i in range(count)])
+            step *= 2
+        return value
+    total = value
+    for shift in (1, 2, 3):
+        total = total + lax.ppermute(value, "col", [(i, (i + shift) % count) for i in range(count)])
+    return total + lax.ppermute(total, "col", [(i, (i + 4) % count) for i in range(count)])
 
 
 def shards(matrix, vectors, tfactor):

time: 155 us -> 154 us (level)
  the two profiles are of different devices: /device:TPU:6 before, /device:TPU:1 now
where the time goes in v4:
time: 154 us; the launch traced here: 151 us
  starting transfers between devices  81.1 us (53%)
  waiting for transfers between devices  52.3 us (34%)
  matrix products  17 us (11%)
    ppermute x2, waiting for transfers between devices, to_columns(): mine = lax.ppermute(panel_rows, ('row', 'col'), pairs)  26 us
    ppermute x2, starting transfers between devices, to_columns(): other = lax.ppermute(mine, 'row', core_pairs)  24.4 us
    ppermute x7, starting transfers between devices, col_sum_rows(): total = total + lax.ppermute(sent, 'col', pairs)  16.8 us
    ppermute x7, starting transfers between devices, col_sum_rows(): got = lax.ppermute(total, 'col', pairs)  11.8 us
    ppermute x2, starting transfers between devices, to_columns(): mine = lax.ppermute(panel_rows, ('row', 'col'), pairs)  9.62 us
    dot_general x6, matrix products, product(): jnp.dot(left, right, precision=lax.Precision.HIGHEST, preferred_element_t...  9.54 us
    ppermute x3, starting transfers between devices, col_sum(): lax.ppermute(value, 'col', [(i, (i + shift) % count) for i in range(count)])  8.43 us
    ppermute x2, waiting for transfers between devices, to_columns(): across = lax.ppermute(mine, 'row', [(i, i ^ 2) for i in range(row_count)])  6.48 us
  transfers between devices with their start and end apart: 26, of which 13 were waited for; matrix products, arithmetic and copies ran while one was open for 0% of the time, Pallas kernels for 0%

profile of v4, /device:TPU:1, one launch (start us, length us, event | category | flops | bytes accessed | tf_op | source)
XLA Modules:
  0.0 151.2 jit_solution(5732964159008551664)
XLA Ops:
  0.0 5.6 %collective-permute-start = (f32[512,128]{1,0:T(8,128)}, f32[512,128]{1,0:T(8,128)S(1)}, u32[]{:S(2)}, u32[]{:S(2)}) collective-permute-start(f32[512,128]{1,0:T(8,128)} %param.4), channel_id=1, source_target_pairs={{0,32},{1,96},{2,0},{3,128},{4,192},{5,160},{6,64},{7,224},{8,136}... | collective-permute-start | bytes 786440 | tf_op jit(solution)/shard_map/ppermute | solution.py:49
  5.6 20.5 %collective-permute-done = f32[512,128]{1,0:T(8,128)S(1)} collective-permute-done((f32[512,128]{1,0:T(8,128)}, f32[512,128]{1,0:T(8,128)S(1)}, u32[]{:S(2)}, u32[]{:S(2)}) %collective-permute-start) | collective-permute-done | bytes 262176 | tf_op jit(solution)/shard_map/ppermute | solution.py:49
  26.2 3.5 %collective-permute-start.1 = (f32[512,128]{1,0:T(8,128)S(1)}, f32[512,128]{1,0:T(8,128)S(1)}, u32[]{:S(2)}, u32[]{:S(2)}) collective-permute-start(f32[512,128]{1,0:T(8,128)S(1)} %collective-permute-done), channel_id=1, source_target_pairs={{0,8},{8,0},{16,24},{24,16},{32,40},{40,32},{48,56},{56,48},{64,72... | collective-permute-start | bytes 786440 | tf_op jit(solution)/shard_map/ppermute | solution.py:54
  29.6 6.5 %collective-permute-done.2 = f32[512,128]{1,0:T(8,128)S(1)} collective-permute-done((f32[512,128]{1,0:T(8,128)S(1)}, f32[512,128]{1,0:T(8,128)S(1)}, u32[]{:S(2)}, u32[]{:S(2)}) %collective-permute-start.2) | collective-permute-done | bytes 262176 | tf_op jit(solution)/shard_map/ppermute | solution.py:55
  38.7 6.6 %convolution_bitcast_fusion = f32[512,128]{0,1:T(8,128)S(1)} fusion(f32[2048,128]{1,0:T(8,128)S(1)} %constant_dynamic-update-slice_fusion.4, f32[512,2048]{1,0:T(8,128)} %param.3), kind=kOutput, calls=%fused_computation.9 | convolution fusion | flops 1610612736 | bytes 5505024 | tf_op jit(solution)/shard_map/dot_general | solution.py:20
  45.6 4.6 %collective-permute-start.10 = (f32[64,128]{1,0:T(8,128)S(1)}, f32[64,128]{1,0:T(8,128)S(1)}, u32[]{:S(2)}, u32[]{:S(2)}) collective-permute-start(f32[64,128]{1,0:T(8,128)S(1)} %get-tuple-element.8), channel_id=1, source_target_pairs={{0,7},{1,0},{2,1},{3,2},{4,3},{5,4},{6,5},{7,6},{8,15},{9,8},{10,9... | collective-permute-start | bytes 98312 | tf_op jit(solution)/shard_map/ppermute | solution.py:71
  50.3 4.0 %collective-permute-start.9 = (f32[64,128]{1,0:T(8,128)S(1)}, f32[64,128]{1,0:T(8,128)S(1)}, u32[]{:S(2)}, u32[]{:S(2)}) collective-permute-start(f32[64,128]{1,0:T(8,128)S(1)} %get-tuple-element.9), channel_id=1, source_target_pairs={{0,6},{1,7},{2,0},{3,1},{4,2},{5,3},{6,4},{7,5},{8,14},{9,15},{10,... | collective-permute-start | bytes 98312 | tf_op jit(solution)/shard_map/ppermute | solution.py:71
  58.8 3.6 %collective-permute-start.5 = (f32[64,128]{1,0:T(8,128)S(1)}, f32[64,128]{1,0:T(8,128)S(1)}, u32[]{:S(2)}, u32[]{:S(2)}) collective-permute-start(f32[64,128]{1,0:T(8,128)S(1)} %get-tuple-element.13), channel_id=1, source_target_pairs={{0,2},{1,3},{2,4},{3,5},{4,6},{5,7},{6,0},{7,1},{8,10},{9,11},{10,... | collective-permute-start | bytes 98312 | tf_op jit(solution)/shard_map/ppermute | solution.py:71
  63.0 2.3 %collective-permute-done.5 = f32[64,128]{1,0:T(8,128)S(1)} collective-permute-done((f32[64,128]{1,0:T(8,128)S(1)}, f32[64,128]{1,0:T(8,128)S(1)}, u32[]{:S(2)}, u32[]{:S(2)}) %collective-permute-start.5) | collective-permute-done | bytes 32800 | tf_op jit(solution)/shard_map/ppermute | solution.py:71
  65.3 2.0 %collective-permute-start.11 = (f32[64,128]{1,0:T(8,128)S(1)}, f32[64,128]{1,0:T(8,128)S(1)}, u32[]{:S(2)}, u32[]{:S(2)}) collective-permute-start(f32[64,128]{1,0:T(8,128)S(1)} %get-tuple-element.6), channel_id=1, source_target_pairs={{0,1},{1,2},{2,3},{3,4},{4,5},{5,6},{6,7},{7,0},{8,9},{9,10},{10,1... | collective-permute-start | bytes 98312 | tf_op jit(solution)/shard_map/ppermute | solution.py:76
  68.1 2.8 %collective-permute-start.15 = (f32[64,128]{1,0:T(8,128)S(1)}, f32[64,128]{1,0:T(8,128)S(1)}, u32[]{:S(2)}, u32[]{:S(2)}) collective-permute-start(f32[64,128]{1,0:T(8,128)S(1)} %get-tuple-element.6), channel_id=1, source_target_pairs={{0,5},{1,6},{2,7},{3,0},{4,1},{5,2},{6,3},{7,4},{8,13},{9,14},{10,... | collective-permute-start | bytes 98312 | tf_op jit(solution)/shard_map/ppermute | solution.py:76
  70.8 2.6 %collective-permute-start.14 = (f32[64,128]{1,0:T(8,128)S(1)}, f32[64,128]{1,0:T(8,128)S(1)}, u32[]{:S(2)}, u32[]{:S(2)}) collective-permute-start(f32[64,128]{1,0:T(8,128)S(1)} %get-tuple-element.6), channel_id=1, source_target_pairs={{0,4},{1,5},{2,6},{3,7},{4,0},{5,1},{6,2},{7,3},{8,12},{9,13},{10,... | collective-permute-start | bytes 98312 | tf_op jit(solution)/shard_map/ppermute | solution.py:76
  76.4 3.9 %collective-permute-done.12 = f32[64,128]{1,0:T(8,128)S(1)} collective-permute-done((f32[64,128]{1,0:T(8,128)S(1)}, f32[64,128]{1,0:T(8,128)S(1)}, u32[]{:S(2)}, u32[]{:S(2)}) %collective-permute-start.12) | collective-permute-done | bytes 32800 | tf_op jit(solution)/shard_map/ppermute | solution.py:76
  81.1 2.3 %collective-permute-done.17 = f32[64,128]{1,0:T(8,128)S(1)} collective-permute-done((f32[64,128]{1,0:T(8,128)S(1)}, f32[64,128]{1,0:T(8,128)S(1)}, u32[]{:S(2)}, u32[]{:S(2)}) %collective-permute-start.17) | collective-permute-done | bytes 32800 | tf_op jit(solution)/shard_map/ppermute | solution.py:76
  83.4 4.0 %collective-permute-start.18 = (f32[512,128]{1,0:T(8,128)S(1)}, f32[512,128]{1,0:T(8,128)S(1)}, u32[]{:S(2)}, u32[]{:S(2)}) collective-permute-start(f32[512,128]{1,0:T(8,128)S(1)} %bitcast.68), channel_id=1, source_target_pairs={{0,32},{1,96},{2,0},{3,128},{4,192},{5,160},{6,64},{7,224},{8,136}... | collective-permute-start | bytes 786440 | tf_op jit(solution)/shard_map/ppermute | solution.py:49
  87.4 5.5 %collective-permute-done.18 = f32[512,128]{1,0:T(8,128)S(1)} collective-permute-done((f32[512,128]{1,0:T(8,128)S(1)}, f32[512,128]{1,0:T(8,128)S(1)}, u32[]{:S(2)}, u32[]{:S(2)}) %collective-permute-start.18) | collective-permute-done | bytes 262176 | tf_op jit(solution)/shard_map/ppermute | solution.py:49
  92.9 20.9 %collective-permute-start.19 = (f32[512,128]{1,0:T(8,128)S(1)}, f32[512,128]{1,0:T(8,128)S(1)}, u32[]{:S(2)}, u32[]{:S(2)}) collective-permute-start(f32[512,128]{1,0:T(8,128)S(1)} %collective-permute-done.18), channel_id=1, source_target_pairs={{0,8},{8,0},{16,24},{24,16},{32,40},{40,32},{48,56},{56,48},{64,72... | collective-permute-start | bytes 786440 | tf_op jit(solution)/shard_map/ppermute | solution.py:54
  113.8 4.3 %collective-permute-start.21 = (f32[512,128]{1,0:T(8,128)S(1)}, f32[512,128]{1,0:T(8,128)S(1)}, u32[]{:S(2)}, u32[]{:S(2)}) collective-permute-start(f32[512,128]{1,0:T(8,128)S(1)} %collective-permute-done.20), channel_id=1, source_target_pairs={{0,8},{8,0},{16,24},{24,16},{32,40},{40,32},{48,56},{56,48},{64,72... | collective-permute-start | bytes 786440 | tf_op jit(solution)/shard_map/ppermute | solution.py:56
  121.1 6.1 %collective-permute-start.24 = (f32[128,128]{1,0:T(8,128)S(1)}, f32[128,128]{1,0:T(8,128)S(1)}, u32[]{:S(2)}, u32[]{:S(2)}) collective-permute-start(f32[128,128]{1,0:T(8,128)S(1)} %fusion.17), channel_id=1, source_target_pairs={{0,3},{1,4},{2,5},{3,6},{4,7},{5,0},{6,1},{7,2},{8,11},{9,12},{10,... | collective-permute-start | bytes 196616 | tf_op jit(solution)/shard_map/ppermute | solution.py:91
  127.3 2.3 %collective-permute-start.23 = (f32[128,128]{1,0:T(8,128)S(1)}, f32[128,128]{1,0:T(8,128)S(1)}, u32[]{:S(2)}, u32[]{:S(2)}) collective-permute-start(f32[128,128]{1,0:T(8,128)S(1)} %fusion.17), channel_id=1, source_target_pairs={{0,2},{1,3},{2,4},{3,5},{4,6},{5,7},{6,0},{7,1},{8,10},{9,11},{10,... | collective-permute-start | bytes 196616 | tf_op jit(solution)/shard_map/ppermute | solution.py:91
  129.6 4.4 %collective-permute-done.24 = f32[128,128]{1,0:T(8,128)S(1)} collective-permute-done((f32[128,128]{1,0:T(8,128)S(1)}, f32[128,128]{1,0:T(8,128)S(1)}, u32[]{:S(2)}, u32[]{:S(2)}) %collective-permute-start.24) | collective-permute-done | bytes 65568 | tf_op jit(solution)/shard_map/ppermute | solution.py:91
  135.2 4.3 %collective-permute-start.25 = (f32[128,128]{1,0:T(8,128)S(1)}, f32[128,128]{1,0:T(8,128)S(1)}, u32[]{:S(2)}, u32[]{:S(2)}) collective-permute-start(f32[128,128]{1,0:T(8,128)S(1)} %add_add_fusion), channel_id=1, source_target_pairs={{0,4},{1,5},{2,6},{3,7},{4,0},{5,1},{6,2},{7,3},{8,12},{9,13},{10,... | collective-permute-start | bytes 196616 | tf_op jit(solution)/shard_map/ppermute | solution.py:92
  139.5 3.1 %collective-permute-done.25 = f32[128,128]{1,0:T(8,128)S(1)} collective-permute-done((f32[128,128]{1,0:T(8,128)S(1)}, f32[128,128]{1,0:T(8,128)S(1)}, u32[]{:S(2)}, u32[]{:S(2)}) %collective-permute-start.25) | collective-permute-done | bytes 65568 | tf_op jit(solution)/shard_map/ppermute | solution.py:92
  145.9 5.3 %convolution_subtract_fusion = f32[512,2048]{1,0:T(8,128)} fusion(f32[512,2048]{1,0:T(8,128)S(1)} %copy-done.1, f32[2048,128]{1,0:T(8,128)S(1)} %constant_dynamic-update-slice_fusion.4, f32[2048,128]{1,0:T(8,128)S(1)} %convolution_subtract_fusion.1, f32[512,128]{1,0:T(8,128)S(1)} %convolution_subtract_fusion.2, f32[512,128]{1,0:T(8,128)S(1)} %copy-done.2), kind=kOutput, calls=%fused_computation | convolution fusion | flops 3222929408 | bytes 11010048 | tf_op jit(solution)/shard_map/dot_general | solution.py:105
  (65 shorter events, 19.8 us)
Async XLA Ops:
  0.0 26.2 %collective-permute-start = (f32[512,128]{1,0:T(8,128)}, f32[512,128]{1,0:T(8,128)S(1)}, u32[]{:S(2)}, u32[]{:S(2)}) collective-permute-start(f32[512,128]{1,0:T(8,128)} %param.4), channel_id=1, source_target_pairs={{0,32},{1,96},{2,0},{3,128},{4,192},{5,160},{6,64},{7,224},{8,136}... | collective-permute-start | bytes 786440 | tf_op jit(solution)/shard_map/ppermute | solution.py:49
  26.2 10.0 %collective-permute-start.2 = (f32[512,128]{1,0:T(8,128)S(1)}, f32[512,128]{1,0:T(8,128)S(1)}, u32[]{:S(2)}, u32[]{:S(2)}) collective-permute-start(f32[512,128]{1,0:T(8,128)S(1)} %collective-permute-done), channel_id=1, source_target_pairs={{0,16},{8,24},{16,0},{24,8},{32,48},{40,56},{48,32},{56,40},{64,80... | collective-permute-start | bytes 786440 | tf_op jit(solution)/shard_map/ppermute | solution.py:55
  26.2 11.5 %collective-permute-start.1 = (f32[512,128]{1,0:T(8,128)S(1)}, f32[512,128]{1,0:T(8,128)S(1)}, u32[]{:S(2)}, u32[]{:S(2)}) collective-permute-start(f32[512,128]{1,0:T(8,128)S(1)} %collective-permute-done), channel_id=1, source_target_pairs={{0,8},{8,0},{16,24},{24,16},{32,40},{40,32},{48,56},{56,48},{64,72... | collective-permute-start | bytes 786440 | tf_op jit(solution)/shard_map/ppermute | solution.py:54
  45.6 11.5 %collective-permute-start.4 = (f32[64,128]{1,0:T(8,128)S(1)}, f32[64,128]{1,0:T(8,128)S(1)}, u32[]{:S(2)}, u32[]{:S(2)}) collective-permute-start(f32[64,128]{1,0:T(8,128)S(1)} %get-tuple-element.7), channel_id=1, source_target_pairs={{0,1},{1,2},{2,3},{3,4},{4,5},{5,6},{6,7},{7,0},{8,9},{9,10},{10,1... | collective-permute-start | bytes 98312 | tf_op jit(solution)/shard_map/ppermute | solution.py:71
  45.6 13.1 %collective-permute-start.10 = (f32[64,128]{1,0:T(8,128)S(1)}, f32[64,128]{1,0:T(8,128)S(1)}, u32[]{:S(2)}, u32[]{:S(2)}) collective-permute-start(f32[64,128]{1,0:T(8,128)S(1)} %get-tuple-element.8), channel_id=1, source_target_pairs={{0,7},{1,0},{2,1},{3,2},{4,3},{5,4},{6,5},{7,6},{8,15},{9,8},{10,9... | collective-permute-start | bytes 98312 | tf_op jit(solution)/shard_map/ppermute | solution.py:71
  50.3 12.0 %collective-permute-start.9 = (f32[64,128]{1,0:T(8,128)S(1)}, f32[64,128]{1,0:T(8,128)S(1)}, u32[]{:S(2)}, u32[]{:S(2)}) collective-permute-start(f32[64,128]{1,0:T(8,128)S(1)} %get-tuple-element.9), channel_id=1, source_target_pairs={{0,6},{1,7},{2,0},{3,1},{4,2},{5,3},{6,4},{7,5},{8,14},{9,15},{10,... | collective-permute-start | bytes 98312 | tf_op jit(solution)/shard_map/ppermute | solution.py:71
  54.3 8.0 %collective-permute-start.8 = (f32[64,128]{1,0:T(8,128)S(1)}, f32[64,128]{1,0:T(8,128)S(1)}, u32[]{:S(2)}, u32[]{:S(2)}) collective-permute-start(f32[64,128]{1,0:T(8,128)S(1)} %get-tuple-element.10), channel_id=1, source_target_pairs={{0,5},{1,6},{2,7},{3,0},{4,1},{5,2},{6,3},{7,4},{8,13},{9,14},{10,... | collective-permute-start | bytes 98312 | tf_op jit(solution)/shard_map/ppermute | solution.py:71
  55.5 7.1 %collective-permute-start.7 = (f32[64,128]{1,0:T(8,128)S(1)}, f32[64,128]{1,0:T(8,128)S(1)}, u32[]{:S(2)}, u32[]{:S(2)}) collective-permute-start(f32[64,128]{1,0:T(8,128)S(1)} %get-tuple-element.11), channel_id=1, source_target_pairs={{0,4},{1,5},{2,6},{3,7},{4,0},{5,1},{6,2},{7,3},{8,12},{9,13},{10,... | collective-permute-start | bytes 98312 | tf_op jit(solution)/shard_map/ppermute | solution.py:71
  57.1 5.9 %collective-permute-start.6 = (f32[64,128]{1,0:T(8,128)S(1)}, f32[64,128]{1,0:T(8,128)S(1)}, u32[]{:S(2)}, u32[]{:S(2)}) collective-permute-start(f32[64,128]{1,0:T(8,128)S(1)} %get-tuple-element.12), channel_id=1, source_target_pairs={{0,3},{1,4},{2,5},{3,6},{4,7},{5,0},{6,1},{7,2},{8,11},{9,12},{10,... | collective-permute-start | bytes 98312 | tf_op jit(solution)/shard_map/ppermute | solution.py:71
  58.8 6.5 %collective-permute-start.5 = (f32[64,128]{1,0:T(8,128)S(1)}, f32[64,128]{1,0:T(8,128)S(1)}, u32[]{:S(2)}, u32[]{:S(2)}) collective-permute-start(f32[64,128]{1,0:T(8,128)S(1)} %get-tuple-element.13), channel_id=1, source_target_pairs={{0,2},{1,3},{2,4},{3,5},{4,6},{5,7},{6,0},{7,1},{8,10},{9,11},{10,... | collective-permute-start | bytes 98312 | tf_op jit(solution)/shard_map/ppermute | solution.py:71
  65.3 9.3 %collective-permute-start.11 = (f32[64,128]{1,0:T(8,128)S(1)}, f32[64,128]{1,0:T(8,128)S(1)}, u32[]{:S(2)}, u32[]{:S(2)}) collective-permute-start(f32[64,128]{1,0:T(8,128)S(1)} %get-tuple-element.6), channel_id=1, source_target_pairs={{0,1},{1,2},{2,3},{3,4},{4,5},{5,6},{6,7},{7,0},{8,9},{9,10},{10,1... | collective-permute-start | bytes 98312 | tf_op jit(solution)/shard_map/ppermute | solution.py:76
  67.3 13.8 %collective-permute-start.16 = (f32[64,128]{1,0:T(8,128)S(1)}, f32[64,128]{1,0:T(8,128)S(1)}, u32[]{:S(2)}, u32[]{:S(2)}) collective-permute-start(f32[64,128]{1,0:T(8,128)S(1)} %get-tuple-element.6), channel_id=1, source_target_pairs={{0,6},{1,7},{2,0},{3,1},{4,2},{5,3},{6,4},{7,5},{8,14},{9,15},{10,... | collective-permute-start | bytes 98312 | tf_op jit(solution)/shard_map/ppermute | solution.py:76
  68.1 13.0 %collective-permute-start.15 = (f32[64,128]{1,0:T(8,128)S(1)}, f32[64,128]{1,0:T(8,128)S(1)}, u32[]{:S(2)}, u32[]{:S(2)}) collective-permute-start(f32[64,128]{1,0:T(8,128)S(1)} %get-tuple-element.6), channel_id=1, source_target_pairs={{0,5},{1,6},{2,7},{3,0},{4,1},{5,2},{6,3},{7,4},{8,13},{9,14},{10,... | collective-permute-start | bytes 98312 | tf_op jit(solution)/shard_map/ppermute | solution.py:76
  70.8 10.2 %collective-permute-start.14 = (f32[64,128]{1,0:T(8,128)S(1)}, f32[64,128]{1,0:T(8,128)S(1)}, u32[]{:S(2)}, u32[]{:S(2)}) collective-permute-start(f32[64,128]{1,0:T(8,128)S(1)} %get-tuple-element.6), channel_id=1, source_target_pairs={{0,4},{1,5},{2,6},{3,7},{4,0},{5,1},{6,2},{7,3},{8,12},{9,13},{10,... | collective-permute-start | bytes 98312 | tf_op jit(solution)/shard_map/ppermute | solution.py:76
  73.4 7.6 %collective-permute-start.13 = (f32[64,128]{1,0:T(8,128)S(1)}, f32[64,128]{1,0:T(8,128)S(1)}, u32[]{:S(2)}, u32[]{:S(2)}) collective-permute-start(f32[64,128]{1,0:T(8,128)S(1)} %get-tuple-element.6), channel_id=1, source_target_pairs={{0,3},{1,4},{2,5},{3,6},{4,7},{5,0},{6,1},{7,2},{8,11},{9,12},{10,... | collective-permute-start | bytes 98312 | tf_op jit(solution)/shard_map/ppermute | solution.py:76
  74.6 5.7 %collective-permute-start.12 = (f32[64,128]{1,0:T(8,128)S(1)}, f32[64,128]{1,0:T(8,128)S(1)}, u32[]{:S(2)}, u32[]{:S(2)}) collective-permute-start(f32[64,128]{1,0:T(8,128)S(1)} %get-tuple-element.6), channel_id=1, source_target_pairs={{0,2},{1,3},{2,4},{3,5},{4,6},{5,7},{6,0},{7,1},{8,10},{9,11},{10,... | collective-permute-start | bytes 98312 | tf_op jit(solution)/shard_map/ppermute | solution.py:76
  83.4 9.5 %collective-permute-start.18 = (f32[512,128]{1,0:T(8,128)S(1)}, f32[512,128]{1,0:T(8,128)S(1)}, u32[]{:S(2)}, u32[]{:S(2)}) collective-permute-start(f32[512,128]{1,0:T(8,128)S(1)} %bitcast.68), channel_id=1, source_target_pairs={{0,32},{1,96},{2,0},{3,128},{4,192},{5,160},{6,64},{7,224},{8,136}... | collective-permute-start | bytes 786440 | tf_op jit(solution)/shard_map/ppermute | solution.py:49
  92.9 20.9 %collective-permute-start.20 = (f32[512,128]{1,0:T(8,128)S(1)}, f32[512,128]{1,0:T(8,128)S(1)}, u32[]{:S(2)}, u32[]{:S(2)}) collective-permute-start(f32[512,128]{1,0:T(8,128)S(1)} %collective-permute-done.18), channel_id=1, source_target_pairs={{0,16},{8,24},{16,0},{24,8},{32,48},{40,56},{48,32},{56,40},{64,80... | collective-permute-start | bytes 786440 | tf_op jit(solution)/shard_map/ppermute | solution.py:55
  92.9 25.4 %collective-permute-start.19 = (f32[512,128]{1,0:T(8,128)S(1)}, f32[512,128]{1,0:T(8,128)S(1)}, u32[]{:S(2)}, u32[]{:S(2)}) collective-permute-start(f32[512,128]{1,0:T(8,128)S(1)} %collective-permute-done.18), channel_id=1, source_target_pairs={{0,8},{8,0},{16,24},{24,16},{32,40},{40,32},{48,56},{56,48},{64,72... | collective-permute-start | bytes 786440 | tf_op jit(solution)/shard_map/ppermute | solution.py:54
  113.8 5.5 %collective-permute-start.21 = (f32[512,128]{1,0:T(8,128)S(1)}, f32[512,128]{1,0:T(8,128)S(1)}, u32[]{:S(2)}, u32[]{:S(2)}) collective-permute-start(f32[512,128]{1,0:T(8,128)S(1)} %collective-permute-done.20), channel_id=1, source_target_pairs={{0,8},{8,0},{16,24},{24,16},{32,40},{40,32},{48,56},{56,48},{64,72... | collective-permute-start | bytes 786440 | tf_op jit(solution)/shard_map/ppermute | solution.py:56
  121.1 12.9 %collective-permute-start.24 = (f32[128,128]{1,0:T(8,128)S(1)}, f32[128,128]{1,0:T(8,128)S(1)}, u32[]{:S(2)}, u32[]{:S(2)}) collective-permute-start(f32[128,128]{1,0:T(8,128)S(1)} %fusion.17), channel_id=1, source_target_pairs={{0,3},{1,4},{2,5},{3,6},{4,7},{5,0},{6,1},{7,2},{8,11},{9,12},{10,... | collective-permute-start | bytes 196616 | tf_op jit(solution)/shard_map/ppermute | solution.py:91
  127.3 6.7 %collective-permute-start.23 = (f32[128,128]{1,0:T(8,128)S(1)}, f32[128,128]{1,0:T(8,128)S(1)}, u32[]{:S(2)}, u32[]{:S(2)}) collective-permute-start(f32[128,128]{1,0:T(8,128)S(1)} %fusion.17), channel_id=1, source_target_pairs={{0,2},{1,3},{2,4},{3,5},{4,6},{5,7},{6,0},{7,1},{8,10},{9,11},{10,... | collective-permute-start | bytes 196616 | tf_op jit(solution)/shard_map/ppermute | solution.py:91
  129.6 5.6 %collective-permute-start.22 = (f32[128,128]{1,0:T(8,128)S(1)}, f32[128,128]{1,0:T(8,128)S(1)}, u32[]{:S(2)}, u32[]{:S(2)}) collective-permute-start(f32[128,128]{1,0:T(8,128)S(1)} %fusion.17), channel_id=1, source_target_pairs={{0,1},{1,2},{2,3},{3,4},{4,5},{5,6},{6,7},{7,0},{8,9},{9,10},{10,1... | collective-permute-start | bytes 196616 | tf_op jit(solution)/shard_map/ppermute | solution.py:91
  135.2 7.4 %collective-permute-start.25 = (f32[128,128]{1,0:T(8,128)S(1)}, f32[128,128]{1,0:T(8,128)S(1)}, u32[]{:S(2)}, u32[]{:S(2)}) collective-permute-start(f32[128,128]{1,0:T(8,128)S(1)} %add_add_fusion), channel_id=1, source_target_pairs={{0,4},{1,5},{2,6},{3,7},{4,0},{5,1},{6,2},{7,3},{8,12},{9,13},{10,... | collective-permute-start | bytes 196616 | tf_op jit(solution)/shard_map/ppermute | solution.py:92
  (5 other events, 270.8 us)

commit v5 on v4

--- a/solution.py
+++ b/solution.py
@@ -17,7 +17,7 @@
 
 
 def product(left, right):
-    return jnp.dot(left, right, precision=lax.Precision.HIGHEST, preferred_element_type=jnp.float32)
+    return jnp.dot(left, right, precision=lax.Precision.HIGH, preferred_element_type=jnp.float32)
 
 
 def inner_product(left, right):
@@ -25,7 +25,7 @@
         left,
         right,
         (((0,), (0,)), ((), ())),
-        precision=lax.Precision.HIGHEST,
+        precision=lax.Precision.HIGH,
         preferred_element_type=jnp.float32,
     )
 
@@ -104,7 +104,7 @@
     right = jnp.concatenate([w_cols, vec_cols], axis=1)
     return matrix - lax.dot_general(
         left, right, (((1,), (1,)), ((), ())),
-        precision=lax.Precision.HIGHEST, preferred_element_type=jnp.float32,
+        precision=lax.Precision.HIGH, preferred_element_type=jnp.float32,
     )
 
 

time: 154 us -> 149 us (0.968)
  matrix products: 17 us -> 11.7 us
    dot_general x6, matrix products: 9.54 us -> 6.33 us  [product(): jnp.dot(left, right, precision=lax.Precision.HIGH, preferred_element_type...]
where the time goes in v5:
time: 149 us; the launch traced here: 146 us
  starting transfers between devices  80.1 us (54%)
  waiting for transfers between devices  53.7 us (36%)
  matrix products  11.7 us (8%)
    ppermute x2, waiting for transfers between devices, to_columns(): mine = lax.ppermute(panel_rows, ('row', 'col'), pairs)  25.9 us
    ppermute x2, starting transfers between devices, to_columns(): other = lax.ppermute(mine, 'row', core_pairs)  24.5 us
    ppermute x7, starting transfers between devices, col_sum_rows(): total = total + lax.ppermute(sent, 'col', pairs)  16.8 us
    ppermute x7, starting transfers between devices, col_sum_rows(): got = lax.ppermute(total, 'col', pairs)  11 us
    ppermute x2, starting transfers between devices, to_columns(): mine = lax.ppermute(panel_rows, ('row', 'col'), pairs)  9.46 us
    ppermute x3, starting transfers between devices, col_sum(): lax.ppermute(value, 'col', [(i, (i + shift) % count) for i in range(count)])  8.68 us
    ppermute x7, waiting for transfers between devices, col_sum_rows(): got = lax.ppermute(total, 'col', pairs)  7.04 us
    ppermute x2, waiting for transfers between devices, to_columns(): across = lax.ppermute(mine, 'row', [(i, i ^ 2) for i in range(row_count)])  6.48 us
  transfers between devices with their start and end apart: 26, of which 13 were waited for; matrix products, arithmetic and copies ran while one was open for 0% of the time, Pallas kernels for 0%

profile of v5, /device:TPU:1, one launch (start us, length us, event | category | flops | bytes accessed | tf_op | source)
XLA Modules:
  0.0 146.4 jit_solution(14562422953818231832)
XLA Ops:
  0.0 5.6 %collective-permute-start = (f32[512,128]{1,0:T(8,128)}, f32[512,128]{1,0:T(8,128)S(1)}, u32[]{:S(2)}, u32[]{:S(2)}) collective-permute-start(f32[512,128]{1,0:T(8,128)} %param.4), channel_id=1, source_target_pairs={{0,32},{1,96},{2,0},{3,128},{4,192},{5,160},{6,64},{7,224},{8,136}... | collective-permute-start | bytes 786440 | tf_op jit(solution)/shard_map/ppermute | solution.py:49
  5.6 20.5 %collective-permute-done = f32[512,128]{1,0:T(8,128)S(1)} collective-permute-done((f32[512,128]{1,0:T(8,128)}, f32[512,128]{1,0:T(8,128)S(1)}, u32[]{:S(2)}, u32[]{:S(2)}) %collective-permute-start) | collective-permute-done | bytes 262176 | tf_op jit(solution)/shard_map/ppermute | solution.py:49
  26.2 3.5 %collective-permute-start.1 = (f32[512,128]{1,0:T(8,128)S(1)}, f32[512,128]{1,0:T(8,128)S(1)}, u32[]{:S(2)}, u32[]{:S(2)}) collective-permute-start(f32[512,128]{1,0:T(8,128)S(1)} %collective-permute-done), channel_id=1, source_target_pairs={{0,8},{8,0},{16,24},{24,16},{32,40},{40,32},{48,56},{56,48},{64,72... | collective-permute-start | bytes 786440 | tf_op jit(solution)/shard_map/ppermute | solution.py:54
  29.6 6.5 %collective-permute-done.2 = f32[512,128]{1,0:T(8,128)S(1)} collective-permute-done((f32[512,128]{1,0:T(8,128)S(1)}, f32[512,128]{1,0:T(8,128)S(1)}, u32[]{:S(2)}, u32[]{:S(2)}) %collective-permute-start.2) | collective-permute-done | bytes 262176 | tf_op jit(solution)/shard_map/ppermute | solution.py:55
  38.7 4.5 %convolution_bitcast_fusion = f32[512,128]{0,1:T(8,128)S(1)} fusion(f32[2048,128]{1,0:T(8,128)S(1)} %constant_dynamic-update-slice_fusion.4, f32[512,2048]{1,0:T(8,128)} %param.3), kind=kOutput, calls=%fused_computation.9 | convolution fusion | flops 805306368 | bytes 5505024 | tf_op jit(solution)/shard_map/dot_general | solution.py:20
  43.5 4.6 %collective-permute-start.10 = (f32[64,128]{1,0:T(8,128)S(1)}, f32[64,128]{1,0:T(8,128)S(1)}, u32[]{:S(2)}, u32[]{:S(2)}) collective-permute-start(f32[64,128]{1,0:T(8,128)S(1)} %get-tuple-element.8), channel_id=1, source_target_pairs={{0,7},{1,0},{2,1},{3,2},{4,3},{5,4},{6,5},{7,6},{8,15},{9,8},{10,9... | collective-permute-start | bytes 98312 | tf_op jit(solution)/shard_map/ppermute | solution.py:71
  48.1 4.0 %collective-permute-start.9 = (f32[64,128]{1,0:T(8,128)S(1)}, f32[64,128]{1,0:T(8,128)S(1)}, u32[]{:S(2)}, u32[]{:S(2)}) collective-permute-start(f32[64,128]{1,0:T(8,128)S(1)} %get-tuple-element.9), channel_id=1, source_target_pairs={{0,6},{1,7},{2,0},{3,1},{4,2},{5,3},{6,4},{7,5},{8,14},{9,15},{10,... | collective-permute-start | bytes 98312 | tf_op jit(solution)/shard_map/ppermute | solution.py:71
  56.6 3.6 %collective-permute-start.5 = (f32[64,128]{1,0:T(8,128)S(1)}, f32[64,128]{1,0:T(8,128)S(1)}, u32[]{:S(2)}, u32[]{:S(2)}) collective-permute-start(f32[64,128]{1,0:T(8,128)S(1)} %get-tuple-element.13), channel_id=1, source_target_pairs={{0,2},{1,3},{2,4},{3,5},{4,6},{5,7},{6,0},{7,1},{8,10},{9,11},{10,... | collective-permute-start | bytes 98312 | tf_op jit(solution)/shard_map/ppermute | solution.py:71
  60.8 2.3 %collective-permute-done.5 = f32[64,128]{1,0:T(8,128)S(1)} collective-permute-done((f32[64,128]{1,0:T(8,128)S(1)}, f32[64,128]{1,0:T(8,128)S(1)}, u32[]{:S(2)}, u32[]{:S(2)}) %collective-permute-start.5) | collective-permute-done | bytes 32800 | tf_op jit(solution)/shard_map/ppermute | solution.py:71
  63.2 2.0 %collective-permute-start.11 = (f32[64,128]{1,0:T(8,128)S(1)}, f32[64,128]{1,0:T(8,128)S(1)}, u32[]{:S(2)}, u32[]{:S(2)}) collective-permute-start(f32[64,128]{1,0:T(8,128)S(1)} %get-tuple-element.6), channel_id=1, source_target_pairs={{0,1},{1,2},{2,3},{3,4},{4,5},{5,6},{6,7},{7,0},{8,9},{9,10},{10,1... | collective-permute-start | bytes 98312 | tf_op jit(solution)/shard_map/ppermute | solution.py:76
  65.7 2.9 %collective-permute-start.15 = (f32[64,128]{1,0:T(8,128)S(1)}, f32[64,128]{1,0:T(8,128)S(1)}, u32[]{:S(2)}, u32[]{:S(2)}) collective-permute-start(f32[64,128]{1,0:T(8,128)S(1)} %get-tuple-element.6), channel_id=1, source_target_pairs={{0,5},{1,6},{2,7},{3,0},{4,1},{5,2},{6,3},{7,4},{8,13},{9,14},{10,... | collective-permute-start | bytes 98312 | tf_op jit(solution)/shard_map/ppermute | solution.py:76
  68.7 2.6 %collective-permute-start.14 = (f32[64,128]{1,0:T(8,128)S(1)}, f32[64,128]{1,0:T(8,128)S(1)}, u32[]{:S(2)}, u32[]{:S(2)}) collective-permute-start(f32[64,128]{1,0:T(8,128)S(1)} %get-tuple-element.6), channel_id=1, source_target_pairs={{0,4},{1,5},{2,6},{3,7},{4,0},{5,1},{6,2},{7,3},{8,12},{9,13},{10,... | collective-permute-start | bytes 98312 | tf_op jit(solution)/shard_map/ppermute | solution.py:76
  74.2 3.9 %collective-permute-done.12 = f32[64,128]{1,0:T(8,128)S(1)} collective-permute-done((f32[64,128]{1,0:T(8,128)S(1)}, f32[64,128]{1,0:T(8,128)S(1)}, u32[]{:S(2)}, u32[]{:S(2)}) %collective-permute-start.12) | collective-permute-done | bytes 32800 | tf_op jit(solution)/shard_map/ppermute | solution.py:76
  78.2 3.1 %collective-permute-done.17 = f32[64,128]{1,0:T(8,128)S(1)} collective-permute-done((f32[64,128]{1,0:T(8,128)S(1)}, f32[64,128]{1,0:T(8,128)S(1)}, u32[]{:S(2)}, u32[]{:S(2)}) %collective-permute-start.17) | collective-permute-done | bytes 32800 | tf_op jit(solution)/shard_map/ppermute | solution.py:76
  81.4 3.9 %collective-permute-start.18 = (f32[512,128]{1,0:T(8,128)S(1)}, f32[512,128]{1,0:T(8,128)S(1)}, u32[]{:S(2)}, u32[]{:S(2)}) collective-permute-start(f32[512,128]{1,0:T(8,128)S(1)} %bitcast.68), channel_id=1, source_target_pairs={{0,32},{1,96},{2,0},{3,128},{4,192},{5,160},{6,64},{7,224},{8,136}... | collective-permute-start | bytes 786440 | tf_op jit(solution)/shard_map/ppermute | solution.py:49
  85.2 5.4 %collective-permute-done.18 = f32[512,128]{1,0:T(8,128)S(1)} collective-permute-done((f32[512,128]{1,0:T(8,128)S(1)}, f32[512,128]{1,0:T(8,128)S(1)}, u32[]{:S(2)}, u32[]{:S(2)}) %collective-permute-start.18) | collective-permute-done | bytes 262176 | tf_op jit(solution)/shard_map/ppermute | solution.py:49
  90.6 21.0 %collective-permute-start.19 = (f32[512,128]{1,0:T(8,128)S(1)}, f32[512,128]{1,0:T(8,128)S(1)}, u32[]{:S(2)}, u32[]{:S(2)}) collective-permute-start(f32[512,128]{1,0:T(8,128)S(1)} %collective-permute-done.18), channel_id=1, source_target_pairs={{0,8},{8,0},{16,24},{24,16},{32,40},{40,32},{48,56},{56,48},{64,72... | collective-permute-start | bytes 786440 | tf_op jit(solution)/shard_map/ppermute | solution.py:54
  111.6 4.3 %collective-permute-start.21 = (f32[512,128]{1,0:T(8,128)S(1)}, f32[512,128]{1,0:T(8,128)S(1)}, u32[]{:S(2)}, u32[]{:S(2)}) collective-permute-start(f32[512,128]{1,0:T(8,128)S(1)} %collective-permute-done.20), channel_id=1, source_target_pairs={{0,8},{8,0},{16,24},{24,16},{32,40},{40,32},{48,56},{56,48},{64,72... | collective-permute-start | bytes 786440 | tf_op jit(solution)/shard_map/ppermute | solution.py:56
  118.2 5.8 %collective-permute-start.24 = (f32[128,128]{1,0:T(8,128)S(1)}, f32[128,128]{1,0:T(8,128)S(1)}, u32[]{:S(2)}, u32[]{:S(2)}) collective-permute-start(f32[128,128]{1,0:T(8,128)S(1)} %fusion.17), channel_id=1, source_target_pairs={{0,3},{1,4},{2,5},{3,6},{4,7},{5,0},{6,1},{7,2},{8,11},{9,12},{10,... | collective-permute-start | bytes 196616 | tf_op jit(solution)/shard_map/ppermute | solution.py:91
  124.0 2.9 %collective-permute-start.23 = (f32[128,128]{1,0:T(8,128)S(1)}, f32[128,128]{1,0:T(8,128)S(1)}, u32[]{:S(2)}, u32[]{:S(2)}) collective-permute-start(f32[128,128]{1,0:T(8,128)S(1)} %fusion.17), channel_id=1, source_target_pairs={{0,2},{1,3},{2,4},{3,5},{4,6},{5,7},{6,0},{7,1},{8,10},{9,11},{10,... | collective-permute-start | bytes 196616 | tf_op jit(solution)/shard_map/ppermute | solution.py:91
  126.8 4.7 %collective-permute-done.24 = f32[128,128]{1,0:T(8,128)S(1)} collective-permute-done((f32[128,128]{1,0:T(8,128)S(1)}, f32[128,128]{1,0:T(8,128)S(1)}, u32[]{:S(2)}, u32[]{:S(2)}) %collective-permute-start.24) | collective-permute-done | bytes 65568 | tf_op jit(solution)/shard_map/ppermute | solution.py:91
  132.9 3.9 %collective-permute-start.25 = (f32[128,128]{1,0:T(8,128)S(1)}, f32[128,128]{1,0:T(8,128)S(1)}, u32[]{:S(2)}, u32[]{:S(2)}) collective-permute-start(f32[128,128]{1,0:T(8,128)S(1)} %add_add_fusion), channel_id=1, source_target_pairs={{0,4},{1,5},{2,6},{3,7},{4,0},{5,1},{6,2},{7,3},{8,12},{9,13},{10,... | collective-permute-start | bytes 196616 | tf_op jit(solution)/shard_map/ppermute | solution.py:92
  136.8 3.3 %collective-permute-done.25 = f32[128,128]{1,0:T(8,128)S(1)} collective-permute-done((f32[128,128]{1,0:T(8,128)S(1)}, f32[128,128]{1,0:T(8,128)S(1)}, u32[]{:S(2)}, u32[]{:S(2)}) %collective-permute-start.25) | collective-permute-done | bytes 65568 | tf_op jit(solution)/shard_map/ppermute | solution.py:92
  142.3 4.1 %convolution_subtract_fusion = f32[512,2048]{1,0:T(8,128)} fusion(f32[512,2048]{1,0:T(8,128)S(1)} %copy-done.1, f32[2048,128]{1,0:T(8,128)S(1)} %constant_dynamic-update-slice_fusion.4, f32[2048,128]{1,0:T(8,128)S(1)} %convolution_subtract_fusion.1, f32[512,128]{1,0:T(8,128)S(1)} %convolution_subtract_fusion.2, f32[512,128]{1,0:T(8,128)S(1)} %copy-done.2), kind=kOutput, calls=%fused_computation | convolution fusion | flops 1612316672 | bytes 11010048 | tf_op jit(solution)/shard_map/dot_general | solution.py:105
  (65 shorter events, 17.0 us)
Async XLA Ops:
  0.0 26.2 %collective-permute-start = (f32[512,128]{1,0:T(8,128)}, f32[512,128]{1,0:T(8,128)S(1)}, u32[]{:S(2)}, u32[]{:S(2)}) collective-permute-start(f32[512,128]{1,0:T(8,128)} %param.4), channel_id=1, source_target_pairs={{0,32},{1,96},{2,0},{3,128},{4,192},{5,160},{6,64},{7,224},{8,136}... | collective-permute-start | bytes 786440 | tf_op jit(solution)/shard_map/ppermute | solution.py:49
  26.2 10.0 %collective-permute-start.2 = (f32[512,128]{1,0:T(8,128)S(1)}, f32[512,128]{1,0:T(8,128)S(1)}, u32[]{:S(2)}, u32[]{:S(2)}) collective-permute-start(f32[512,128]{1,0:T(8,128)S(1)} %collective-permute-done), channel_id=1, source_target_pairs={{0,16},{8,24},{16,0},{24,8},{32,48},{40,56},{48,32},{56,40},{64,80... | collective-permute-start | bytes 786440 | tf_op jit(solution)/shard_map/ppermute | solution.py:55
  26.2 11.5 %collective-permute-start.1 = (f32[512,128]{1,0:T(8,128)S(1)}, f32[512,128]{1,0:T(8,128)S(1)}, u32[]{:S(2)}, u32[]{:S(2)}) collective-permute-start(f32[512,128]{1,0:T(8,128)S(1)} %collective-permute-done), channel_id=1, source_target_pairs={{0,8},{8,0},{16,24},{24,16},{32,40},{40,32},{48,56},{56,48},{64,72... | collective-permute-start | bytes 786440 | tf_op jit(solution)/shard_map/ppermute | solution.py:54
  43.4 11.5 %collective-permute-start.4 = (f32[64,128]{1,0:T(8,128)S(1)}, f32[64,128]{1,0:T(8,128)S(1)}, u32[]{:S(2)}, u32[]{:S(2)}) collective-permute-start(f32[64,128]{1,0:T(8,128)S(1)} %get-tuple-element.7), channel_id=1, source_target_pairs={{0,1},{1,2},{2,3},{3,4},{4,5},{5,6},{6,7},{7,0},{8,9},{9,10},{10,1... | collective-permute-start | bytes 98312 | tf_op jit(solution)/shard_map/ppermute | solution.py:71
  43.5 13.1 %collective-permute-start.10 = (f32[64,128]{1,0:T(8,128)S(1)}, f32[64,128]{1,0:T(8,128)S(1)}, u32[]{:S(2)}, u32[]{:S(2)}) collective-permute-start(f32[64,128]{1,0:T(8,128)S(1)} %get-tuple-element.8), channel_id=1, source_target_pairs={{0,7},{1,0},{2,1},{3,2},{4,3},{5,4},{6,5},{7,6},{8,15},{9,8},{10,9... | collective-permute-start | bytes 98312 | tf_op jit(solution)/shard_map/ppermute | solution.py:71
  48.1 12.0 %collective-permute-start.9 = (f32[64,128]{1,0:T(8,128)S(1)}, f32[64,128]{1,0:T(8,128)S(1)}, u32[]{:S(2)}, u32[]{:S(2)}) collective-permute-start(f32[64,128]{1,0:T(8,128)S(1)} %get-tuple-element.9), channel_id=1, source_target_pairs={{0,6},{1,7},{2,0},{3,1},{4,2},{5,3},{6,4},{7,5},{8,14},{9,15},{10,... | collective-permute-start | bytes 98312 | tf_op jit(solution)/shard_map/ppermute | solution.py:71
  52.1 8.0 %collective-permute-start.8 = (f32[64,128]{1,0:T(8,128)S(1)}, f32[64,128]{1,0:T(8,128)S(1)}, u32[]{:S(2)}, u32[]{:S(2)}) collective-permute-start(f32[64,128]{1,0:T(8,128)S(1)} %get-tuple-element.10), channel_id=1, source_target_pairs={{0,5},{1,6},{2,7},{3,0},{4,1},{5,2},{6,3},{7,4},{8,13},{9,14},{10,... | collective-permute-start | bytes 98312 | tf_op jit(solution)/shard_map/ppermute | solution.py:71
  53.3 7.1 %collective-permute-start.7 = (f32[64,128]{1,0:T(8,128)S(1)}, f32[64,128]{1,0:T(8,128)S(1)}, u32[]{:S(2)}, u32[]{:S(2)}) collective-permute-start(f32[64,128]{1,0:T(8,128)S(1)} %get-tuple-element.11), channel_id=1, source_target_pairs={{0,4},{1,5},{2,6},{3,7},{4,0},{5,1},{6,2},{7,3},{8,12},{9,13},{10,... | collective-permute-start | bytes 98312 | tf_op jit(solution)/shard_map/ppermute | solution.py:71
  54.9 5.9 %collective-permute-start.6 = (f32[64,128]{1,0:T(8,128)S(1)}, f32[64,128]{1,0:T(8,128)S(1)}, u32[]{:S(2)}, u32[]{:S(2)}) collective-permute-start(f32[64,128]{1,0:T(8,128)S(1)} %get-tuple-element.12), channel_id=1, source_target_pairs={{0,3},{1,4},{2,5},{3,6},{4,7},{5,0},{6,1},{7,2},{8,11},{9,12},{10,... | collective-permute-start | bytes 98312 | tf_op jit(solution)/shard_map/ppermute | solution.py:71
  56.6 6.5 %collective-permute-start.5 = (f32[64,128]{1,0:T(8,128)S(1)}, f32[64,128]{1,0:T(8,128)S(1)}, u32[]{:S(2)}, u32[]{:S(2)}) collective-permute-start(f32[64,128]{1,0:T(8,128)S(1)} %get-tuple-element.13), channel_id=1, source_target_pairs={{0,2},{1,3},{2,4},{3,5},{4,6},{5,7},{6,0},{7,1},{8,10},{9,11},{10,... | collective-permute-start | bytes 98312 | tf_op jit(solution)/shard_map/ppermute | solution.py:71
  63.2 9.3 %collective-permute-start.11 = (f32[64,128]{1,0:T(8,128)S(1)}, f32[64,128]{1,0:T(8,128)S(1)}, u32[]{:S(2)}, u32[]{:S(2)}) collective-permute-start(f32[64,128]{1,0:T(8,128)S(1)} %get-tuple-element.6), channel_id=1, source_target_pairs={{0,1},{1,2},{2,3},{3,4},{4,5},{5,6},{6,7},{7,0},{8,9},{9,10},{10,1... | collective-permute-start | bytes 98312 | tf_op jit(solution)/shard_map/ppermute | solution.py:76
  65.2 13.1 %collective-permute-start.16 = (f32[64,128]{1,0:T(8,128)S(1)}, f32[64,128]{1,0:T(8,128)S(1)}, u32[]{:S(2)}, u32[]{:S(2)}) collective-permute-start(f32[64,128]{1,0:T(8,128)S(1)} %get-tuple-element.6), channel_id=1, source_target_pairs={{0,6},{1,7},{2,0},{3,1},{4,2},{5,3},{6,4},{7,5},{8,14},{9,15},{10,... | collective-permute-start | bytes 98312 | tf_op jit(solution)/shard_map/ppermute | solution.py:76
  65.7 12.5 %collective-permute-start.15 = (f32[64,128]{1,0:T(8,128)S(1)}, f32[64,128]{1,0:T(8,128)S(1)}, u32[]{:S(2)}, u32[]{:S(2)}) collective-permute-start(f32[64,128]{1,0:T(8,128)S(1)} %get-tuple-element.6), channel_id=1, source_target_pairs={{0,5},{1,6},{2,7},{3,0},{4,1},{5,2},{6,3},{7,4},{8,13},{9,14},{10,... | collective-permute-start | bytes 98312 | tf_op jit(solution)/shard_map/ppermute | solution.py:76
  68.7 9.5 %collective-permute-start.14 = (f32[64,128]{1,0:T(8,128)S(1)}, f32[64,128]{1,0:T(8,128)S(1)}, u32[]{:S(2)}, u32[]{:S(2)}) collective-permute-start(f32[64,128]{1,0:T(8,128)S(1)} %get-tuple-element.6), channel_id=1, source_target_pairs={{0,4},{1,5},{2,6},{3,7},{4,0},{5,1},{6,2},{7,3},{8,12},{9,13},{10,... | collective-permute-start | bytes 98312 | tf_op jit(solution)/shard_map/ppermute | solution.py:76
  71.3 6.8 %collective-permute-start.13 = (f32[64,128]{1,0:T(8,128)S(1)}, f32[64,128]{1,0:T(8,128)S(1)}, u32[]{:S(2)}, u32[]{:S(2)}) collective-permute-start(f32[64,128]{1,0:T(8,128)S(1)} %get-tuple-element.6), channel_id=1, source_target_pairs={{0,3},{1,4},{2,5},{3,6},{4,7},{5,0},{6,1},{7,2},{8,11},{9,12},{10,... | collective-permute-start | bytes 98312 | tf_op jit(solution)/shard_map/ppermute | solution.py:76
  72.4 5.7 %collective-permute-start.12 = (f32[64,128]{1,0:T(8,128)S(1)}, f32[64,128]{1,0:T(8,128)S(1)}, u32[]{:S(2)}, u32[]{:S(2)}) collective-permute-start(f32[64,128]{1,0:T(8,128)S(1)} %get-tuple-element.6), channel_id=1, source_target_pairs={{0,2},{1,3},{2,4},{3,5},{4,6},{5,7},{6,0},{7,1},{8,10},{9,11},{10,... | collective-permute-start | bytes 98312 | tf_op jit(solution)/shard_map/ppermute | solution.py:76
  81.4 9.2 %collective-permute-start.18 = (f32[512,128]{1,0:T(8,128)S(1)}, f32[512,128]{1,0:T(8,128)S(1)}, u32[]{:S(2)}, u32[]{:S(2)}) collective-permute-start(f32[512,128]{1,0:T(8,128)S(1)} %bitcast.68), channel_id=1, source_target_pairs={{0,32},{1,96},{2,0},{3,128},{4,192},{5,160},{6,64},{7,224},{8,136}... | collective-permute-start | bytes 786440 | tf_op jit(solution)/shard_map/ppermute | solution.py:49
  90.6 21.0 %collective-permute-start.20 = (f32[512,128]{1,0:T(8,128)S(1)}, f32[512,128]{1,0:T(8,128)S(1)}, u32[]{:S(2)}, u32[]{:S(2)}) collective-permute-start(f32[512,128]{1,0:T(8,128)S(1)} %collective-permute-done.18), channel_id=1, source_target_pairs={{0,16},{8,24},{16,0},{24,8},{32,48},{40,56},{48,32},{56,40},{64,80... | collective-permute-start | bytes 786440 | tf_op jit(solution)/shard_map/ppermute | solution.py:55
  90.6 25.5 %collective-permute-start.19 = (f32[512,128]{1,0:T(8,128)S(1)}, f32[512,128]{1,0:T(8,128)S(1)}, u32[]{:S(2)}, u32[]{:S(2)}) collective-permute-start(f32[512,128]{1,0:T(8,128)S(1)} %collective-permute-done.18), channel_id=1, source_target_pairs={{0,8},{8,0},{16,24},{24,16},{32,40},{40,32},{48,56},{56,48},{64,72... | collective-permute-start | bytes 786440 | tf_op jit(solution)/shard_map/ppermute | solution.py:54
  111.6 5.5 %collective-permute-start.21 = (f32[512,128]{1,0:T(8,128)S(1)}, f32[512,128]{1,0:T(8,128)S(1)}, u32[]{:S(2)}, u32[]{:S(2)}) collective-permute-start(f32[512,128]{1,0:T(8,128)S(1)} %collective-permute-done.20), channel_id=1, source_target_pairs={{0,8},{8,0},{16,24},{24,16},{32,40},{40,32},{48,56},{56,48},{64,72... | collective-permute-start | bytes 786440 | tf_op jit(solution)/shard_map/ppermute | solution.py:56
  118.2 13.4 %collective-permute-start.24 = (f32[128,128]{1,0:T(8,128)S(1)}, f32[128,128]{1,0:T(8,128)S(1)}, u32[]{:S(2)}, u32[]{:S(2)}) collective-permute-start(f32[128,128]{1,0:T(8,128)S(1)} %fusion.17), channel_id=1, source_target_pairs={{0,3},{1,4},{2,5},{3,6},{4,7},{5,0},{6,1},{7,2},{8,11},{9,12},{10,... | collective-permute-start | bytes 196616 | tf_op jit(solution)/shard_map/ppermute | solution.py:91
  124.0 7.6 %collective-permute-start.23 = (f32[128,128]{1,0:T(8,128)S(1)}, f32[128,128]{1,0:T(8,128)S(1)}, u32[]{:S(2)}, u32[]{:S(2)}) collective-permute-start(f32[128,128]{1,0:T(8,128)S(1)} %fusion.17), channel_id=1, source_target_pairs={{0,2},{1,3},{2,4},{3,5},{4,6},{5,7},{6,0},{7,1},{8,10},{9,11},{10,... | collective-permute-start | bytes 196616 | tf_op jit(solution)/shard_map/ppermute | solution.py:91
  126.8 6.0 %collective-permute-start.22 = (f32[128,128]{1,0:T(8,128)S(1)}, f32[128,128]{1,0:T(8,128)S(1)}, u32[]{:S(2)}, u32[]{:S(2)}) collective-permute-start(f32[128,128]{1,0:T(8,128)S(1)} %fusion.17), channel_id=1, source_target_pairs={{0,1},{1,2},{2,3},{3,4},{4,5},{5,6},{6,7},{7,0},{8,9},{9,10},{10,1... | collective-permute-start | bytes 196616 | tf_op jit(solution)/shard_map/ppermute | solution.py:91
  132.9 7.2 %collective-permute-start.25 = (f32[128,128]{1,0:T(8,128)S(1)}, f32[128,128]{1,0:T(8,128)S(1)}, u32[]{:S(2)}, u32[]{:S(2)}) collective-permute-start(f32[128,128]{1,0:T(8,128)S(1)} %add_add_fusion), channel_id=1, source_target_pairs={{0,4},{1,5},{2,6},{3,7},{4,0},{5,1},{6,2},{7,3},{8,12},{9,13},{10,... | collective-permute-start | bytes 196616 | tf_op jit(solution)/shard_map/ppermute | solution.py:92
  (5 other events, 267.3 us)

commit v6 on v5

--- a/solution.py
+++ b/solution.py
@@ -47,49 +47,24 @@
             dst_row = per * high + low
             pairs.append((src_row * col_count + src_col, dst_row * col_count + dst_col))
     mine = lax.ppermute(panel_rows, ("row", "col"), pairs)
-    low = lax.axis_index("row") % per
-    gathered = jnp.zeros((per * rows_here,) + panel_rows.shape[1:], panel_rows.dtype)
-    gathered = lax.dynamic_update_slice_in_dim(gathered, mine, low * rows_here, 0)
-    core_pairs = [(i, i ^ 1) for i in range(row_count)]
-    other = lax.ppermute(mine, "row", core_pairs)
-    across = lax.ppermute(mine, "row", [(i, i ^ 2) for i in range(row_count)])
-    diagonal = lax.ppermute(across, "row", core_pairs)
-    for mask, block in ((1, other), (2, across), (3, diagonal)):
-        gathered = lax.dynamic_update_slice_in_dim(gathered, block, (low ^ mask) * rows_here, 0)
-    return gathered
+    groups = [list(range(per * g, per * g + per)) for g in range(row_count // per)]
+    spread = jnp.broadcast_to(mine[None], (per,) + mine.shape)
+    gathered = lax.all_to_all(spread, "row", 0, 0, axis_index_groups=groups, tiled=True)
+    return gathered.reshape((per * rows_here,) + panel_rows.shape[1:])
 
 
 def col_sum_rows(partial):
     count = lax.axis_size("col")
-    col = lax.axis_index("col")
-    chunk = partial.shape[0] // count
-    pieces = partial.reshape((count, chunk) + partial.shape[1:])
-    total = lax.dynamic_index_in_dim(pieces, col, 0, keepdims=False)
-    for shift in range(1, count):
-        pairs = [(i, (i + shift) % count) for i in range(count)]
-        sent = lax.dynamic_index_in_dim(pieces, (col + shift) % count, 0, keepdims=False)
-        total = total + lax.ppermute(sent, "col", pairs)
-    whole = jnp.zeros_like(pieces)
-    whole = lax.dynamic_update_index_in_dim(whole, total, col, 0)
-    for shift in range(1, count):
-        pairs = [(i, (i + shift) % count) for i in range(count)]
-        got = lax.ppermute(total, "col", pairs)
-        whole = lax.dynamic_update_index_in_dim(whole, got, (col - shift) % count, 0)
-    return whole.reshape(partial.shape)
+    pieces = partial.reshape((count, partial.shape[0] // count) + partial.shape[1:])
+    total = jnp.sum(lax.all_to_all(pieces, "col", 0, 0, tiled=True), axis=0)
+    spread = jnp.broadcast_to(total[None], pieces.shape)
+    return lax.all_to_all(spread, "col", 0, 0, tiled=True).reshape(partial.shape)
 
 
 def col_sum(value):
     count = lax.axis_size("col")
-    if count != 8:
-        step = 1
-        while step < count:
-            value = value + lax.ppermute(value, "col", [(i, i ^ step) for i in range(count)])
-            step *= 2
-        return value
-    total = value
-    for shift in (1, 2, 3):
-        total = total + lax.ppermute(value, "col", [(i, (i + shift) % count) for i in range(count)])
-    return total + lax.ppermute(total, "col", [(i, (i + 4) % count) for i in range(count)])
+    spread = jnp.broadcast_to(value[None], (count,) + value.shape)
+    return jnp.sum(lax.all_to_all(spread, "col", 0, 0, tiled=True), axis=0)
 
 
 def shards(matrix, vectors, tfactor):

time: 149 us -> 160 us (1.074); the launches traced: 146 us -> 160 us
  blocking collectives: 0 us -> 86.1 us
  starting transfers between devices: 80.1 us -> 16.7 us
  waiting for transfers between devices: 53.7 us -> 44.4 us
    all_to_all x0 -> x4, blocking collectives: none -> 86.1 us  [the longest x2 50.9 us: to_columns(): lax.all_to_all(spread, 'row', 0, 0, axis_index_groups=groups, tiled=True)]
    ppermute x24 -> x0, starting transfers between devices: 70.7 us -> none  [the longest x2 24.5 us: to_columns(): other = lax.ppermute(mine, 'row', core_pairs)]
    ppermute x24 -> x0, waiting for transfers between devices: 27.8 us -> none  [the longest x7 7.04 us: col_sum_rows(): got = lax.ppermute(total, 'col', pairs)]
    all_to_all x0 -> x1, waiting for transfers between devices: none -> 16.5 us  [col_sum(): return jnp.sum(lax.all_to_all(spread, 'col', 0, 0, tiled=True), axis=0)]
    all_to_all x0 -> x1, starting transfers between devices: none -> 9.02 us  [col_sum(): return jnp.sum(lax.all_to_all(spread, 'col', 0, 0, tiled=True), axis=0)]
    ppermute x2, waiting for transfers between devices: 25.9 us -> 27.9 us  [to_columns(): mine = lax.ppermute(panel_rows, ('row', 'col'), pairs)]
    ppermute x2, starting transfers between devices: 9.46 us -> 7.64 us  [to_columns(): mine = lax.ppermute(panel_rows, ('row', 'col'), pairs)]
  transfers between devices with their start and end apart: 26 -> 3, of which waited for: 13 -> 3; matrix products, arithmetic and copies ran while one was open for 0% -> 0% of each run, Pallas kernels for 0% -> 0%
where the time goes in v6:
time: 160 us
  blocking collectives  86.1 us (54%)
  waiting for transfers between devices  44.4 us (28%)
  starting transfers between devices  16.7 us (10%)
  matrix products  11.2 us (7%)
    all_to_all x2, blocking collectives, to_columns(): lax.all_to_all(spread, 'row', 0, 0, axis_index_groups=groups, tiled=True)  50.9 us
    ppermute x2, waiting for transfers between devices, to_columns(): mine = lax.ppermute(panel_rows, ('row', 'col'), pairs)  27.9 us
    all_to_all x1, blocking collectives, col_sum_rows(): total = jnp.sum(lax.all_to_all(pieces, 'col', 0, 0, tiled=True), axis=0)  23.2 us
    all_to_all x1, waiting for transfers between devices, col_sum(): return jnp.sum(lax.all_to_all(spread, 'col', 0, 0, tiled=True), axis=0)  16.5 us
    all_to_all x1, blocking collectives, col_sum_rows(): lax.all_to_all(spread, 'col', 0, 0, tiled=True).reshape(partial.shape)  12 us
    all_to_all x1, starting transfers between devices, col_sum(): return jnp.sum(lax.all_to_all(spread, 'col', 0, 0, tiled=True), axis=0)  9.02 us
    ppermute x2, starting transfers between devices, to_columns(): mine = lax.ppermute(panel_rows, ('row', 'col'), pairs)  7.64 us
    dot_general x6, matrix products, product(): jnp.dot(left, right, precision=lax.Precision.HIGH, preferred_element_type...  5.86 us
  transfers between devices with their start and end apart: 3, of which 3 were waited for; matrix products, arithmetic and copies ran while one was open for 0% of the time, Pallas kernels for 0%

profile of v6, /device:TPU:1, one launch (start us, length us, event | category | flops | bytes accessed | tf_op | source)
XLA Modules:
  0.0 159.8 jit_solution(13689378541300852023)
XLA Ops:
  0.0 5.6 %collective-permute-start = (f32[512,128]{1,0:T(8,128)}, f32[512,128]{1,0:T(8,128)S(1)}, u32[]{:S(2)}, u32[]{:S(2)}) collective-permute-start(f32[512,128]{1,0:T(8,128)} %param.4), channel_id=1, source_target_pairs={{0,32},{1,96},{2,0},{3,128},{4,192},{5,160},{6,64},{7,224},{8,136}... | collective-permute-start | bytes 786440 | tf_op jit(solution)/shard_map/ppermute | solution.py:49
  5.6 20.5 %collective-permute-done = f32[512,128]{1,0:T(8,128)S(1)} collective-permute-done((f32[512,128]{1,0:T(8,128)}, f32[512,128]{1,0:T(8,128)S(1)}, u32[]{:S(2)}, u32[]{:S(2)}) %collective-permute-start) | collective-permute-done | bytes 262176 | tf_op jit(solution)/shard_map/ppermute | solution.py:49
  26.2 0.1 broadcast_in_dim.8
  26.2 18.0 %all_to_all.25 = f32[4,512,128]{2,1,0:T(8,128)S(1)} all-to-all(f32[4,512,128]{2,1,0:T(8,128)S(1)} %broadcast_in_dim.8), channel_id=1, replica_groups={{0,8,16,24},{32,40,48,56},{64,72,80,88},{96,104,112,120},{128,136,144,1..., dimensions={0} | all-to-all | bytes 2097152 | tf_op jit(solution)/shard_map/all_to_all | solution.py:52
  44.2 4.0 %fusion.10 = f32[8,64,128]{2,1,0:T(8,128)S(1)} fusion(f32[8,64,2048]{2,1,0:T(8,128)} %bitcast.35, f32[2048,128,1]{1,0,2:T(8,128)S(1)} %bitcast.32), kind=kOutput, calls=%fused_computation.15 | convolution fusion | flops 805306368 | bytes 5505024 | tf_op jit(solution)/shard_map/dot_general | solution.py:20
  48.2 23.2 %all_to_all.26 = f32[8,64,128]{2,1,0:T(8,128)S(1)} all-to-all(f32[8,64,128]{2,1,0:T(8,128)S(1)} %fusion.10), channel_id=1, replica_groups=mesh['row'=32,'col'=8] {'col'}, dimensions={0} | all-to-all | bytes 524288 | tf_op jit(solution)/shard_map/all_to_all | solution.py:59
  71.5 12.0 %all_to_all.27 = f32[8,64,128]{2,1,0:T(8,128)S(1)} all-to-all(f32[8,64,128]{2,1,0:T(8,128)S(1)} %broadcast_in_dim.9), channel_id=1, replica_groups=mesh['row'=32,'col'=8] {'col'}, dimensions={0} | all-to-all | bytes 524288 | tf_op jit(solution)/shard_map/all_to_all | solution.py:61
  83.5 2.0 %collective-permute-start.1 = (f32[512,128]{1,0:T(8,128)S(1)}, f32[512,128]{1,0:T(8,128)S(1)}, u32[]{:S(2)}, u32[]{:S(2)}) collective-permute-start(f32[512,128]{1,0:T(8,128)S(1)} %bitcast.37), channel_id=1, source_target_pairs={{0,32},{1,96},{2,0},{3,128},{4,192},{5,160},{6,64},{7,224},{8,136}... | collective-permute-start | bytes 786440 | tf_op jit(solution)/shard_map/ppermute | solution.py:49
  85.5 7.4 %collective-permute-done.1 = f32[512,128]{1,0:T(8,128)S(1)} collective-permute-done((f32[512,128]{1,0:T(8,128)S(1)}, f32[512,128]{1,0:T(8,128)S(1)}, u32[]{:S(2)}, u32[]{:S(2)}) %collective-permute-start.1) | collective-permute-done | bytes 262176 | tf_op jit(solution)/shard_map/ppermute | solution.py:49
  92.9 0.1 broadcast_in_dim.10
  92.9 32.9 %all_to_all.28 = f32[4,512,128]{2,1,0:T(8,128)S(1)} all-to-all(f32[4,512,128]{2,1,0:T(8,128)S(1)} %broadcast_in_dim.10), channel_id=1, replica_groups={{0,8,16,24},{32,40,48,56},{64,72,80,88},{96,104,112,120},{128,136,144,1..., dimensions={0} | all-to-all | bytes 2097152 | tf_op jit(solution)/shard_map/all_to_all | solution.py:52
  125.9 1.0 convolution_bitcast_fusion
  126.9 0.8 broadcast_in_dim.11
  127.7 9.0 %all-to-all-start.4 = ((f32[8,128,128]{2,1,0:T(8,128)}), f32[8,128,128]{2,1,0:T(8,128)S(1)}, u32[]{:S(2)}, u32[]{:S(2)}) async-start(f32[8,128,128]{2,1,0:T(8,128)} %broadcast_in_dim.11), calls=%async_computation.4 | async-start | bytes 1048576 | tf_op jit(solution)/shard_map/all_to_all | solution.py:67
  136.7 0.3 fusion.11
  137.0 16.5 %all-to-all-done.4 = f32[8,128,128]{2,1,0:T(8,128)S(1)} async-done(((f32[8,128,128]{2,1,0:T(8,128)}), f32[8,128,128]{2,1,0:T(8,128)S(1)}, u32[]{:S(2)}, u32[]{:S(2)}) %all-to-all-start.4) | async-done | bytes 524320 | tf_op jit(solution)/shard_map/all_to_all | solution.py:67
  153.5 0.0 copy-start.1
  153.5 0.2 fusion.12
  153.7 0.2 fusion.13
  153.9 0.3 fusion.5
  154.2 0.6 fusion
  154.8 0.6 convolution_subtract_fusion.1
  155.4 0.3 copy-done.1
  155.7 4.1 %convolution_subtract_fusion = f32[512,2048]{1,0:T(8,128)} fusion(f32[512,2048]{1,0:T(8,128)S(1)} %copy-done.1, f32[2048,128]{1,0:T(8,128)S(1)} %bitcast.34, f32[2048,128]{1,0:T(8,128)S(1)} %convolution_subtract_fusion.1, f32[512,128]{1,0:T(8,128)S(1)} %fusion.5, f32[512,128]{1,0:T(8,128)S(1)} %copy-done.2), kind=kOutput, calls=%fused_computation | convolution fusion | flops 1612316672 | bytes 11010048 | tf_op jit(solution)/shard_map/dot_general | solution.py:80
  (7 shorter events, 0.1 us)
Async XLA Ops:
  0.0 136.7 %copy-start = (f32[128,128]{1,0:T(8,128)S(1)}, f32[128,128]{1,0:T(8,128)}, u32[]{:S(2)}) copy-start(f32[128,128]{1,0:T(8,128)} %param.5) | copy-start | bytes 196612
  0.0 26.2 %collective-permute-start = (f32[512,128]{1,0:T(8,128)}, f32[512,128]{1,0:T(8,128)S(1)}, u32[]{:S(2)}, u32[]{:S(2)}) collective-permute-start(f32[512,128]{1,0:T(8,128)} %param.4), channel_id=1, source_target_pairs={{0,32},{1,96},{2,0},{3,128},{4,192},{5,160},{6,64},{7,224},{8,136}... | collective-permute-start | bytes 786440 | tf_op jit(solution)/shard_map/ppermute | solution.py:49
  83.5 70.5 %copy-start.2 = (f32[512,128]{1,0:T(8,128)S(1)}, f32[512,128]{1,0:T(8,128)}, u32[]{:S(2)}) copy-start(f32[512,128]{1,0:T(8,128)} %param.4) | copy-start | bytes 786436
  83.5 9.4 %collective-permute-start.1 = (f32[512,128]{1,0:T(8,128)S(1)}, f32[512,128]{1,0:T(8,128)S(1)}, u32[]{:S(2)}, u32[]{:S(2)}) collective-permute-start(f32[512,128]{1,0:T(8,128)S(1)} %bitcast.37), channel_id=1, source_target_pairs={{0,32},{1,96},{2,0},{3,128},{4,192},{5,160},{6,64},{7,224},{8,136}... | collective-permute-start | bytes 786440 | tf_op jit(solution)/shard_map/ppermute | solution.py:49
  127.7 25.8 %all-to-all-start.4 = ((f32[8,128,128]{2,1,0:T(8,128)}), f32[8,128,128]{2,1,0:T(8,128)S(1)}, u32[]{:S(2)}, u32[]{:S(2)}) async-start(f32[8,128,128]{2,1,0:T(8,128)} %broadcast_in_dim.11), calls=%async_computation.4 | async-start | bytes 1048576 | tf_op jit(solution)/shard_map/all_to_all | solution.py:67
  153.5 2.2 %copy-start.1 = (f32[512,2048]{1,0:T(8,128)S(1)}, f32[512,2048]{1,0:T(8,128)}, u32[]{:S(2)}) copy-start(f32[512,2048]{1,0:T(8,128)} %param.3) | copy-start | bytes 12582916

commit v7 on v6

--- a/solution.py
+++ b/solution.py
@@ -47,31 +47,45 @@
             dst_row = per * high + low
             pairs.append((src_row * col_count + src_col, dst_row * col_count + dst_col))
     mine = lax.ppermute(panel_rows, ("row", "col"), pairs)
-    groups = [list(range(per * g, per * g + per)) for g in range(row_count // per)]
-    spread = jnp.broadcast_to(mine[None], (per,) + mine.shape)
-    gathered = lax.all_to_all(spread, "row", 0, 0, axis_index_groups=groups, tiled=True)
-    return gathered.reshape((per * rows_here,) + panel_rows.shape[1:])
+    low = lax.axis_index("row") % per
+    gathered = jnp.zeros((per * rows_here,) + panel_rows.shape[1:], panel_rows.dtype)
+    gathered = lax.dynamic_update_slice_in_dim(gathered, mine, low * rows_here, 0)
+    core_pairs = [(i, i ^ 1) for i in range(row_count)]
+    other = lax.ppermute(mine, "row", core_pairs)
+    across = lax.ppermute(mine, "row", [(i, i ^ 2) for i in range(row_count)])
+    diagonal = lax.ppermute(across, "row", core_pairs)
+    for mask, block in ((1, other), (2, across), (3, diagonal)):
+        gathered = lax.dynamic_update_slice_in_dim(gathered, block, (low ^ mask) * rows_here, 0)
+    return gathered
 
 
-def col_sum_rows(partial):
+def col_sum_rows(partial, vectors):
     count = lax.axis_size("col")
-    pieces = partial.reshape((count, partial.shape[0] // count) + partial.shape[1:])
+    chunk = partial.shape[0] // count
+    pieces = partial.reshape((count, chunk) + partial.shape[1:])
     total = jnp.sum(lax.all_to_all(pieces, "col", 0, 0, tiled=True), axis=0)
-    spread = jnp.broadcast_to(total[None], pieces.shape)
-    return lax.all_to_all(spread, "col", 0, 0, tiled=True).reshape(partial.shape)
+    vec_chunk = lax.dynamic_slice_in_dim(vectors, lax.axis_index("col") * chunk, chunk, 0)
+    inner = inner_product(vec_chunk, total)
+    both = jnp.concatenate([total, inner], axis=0)
+    spread = jnp.broadcast_to(both[None], (count,) + both.shape)
+    got = lax.all_to_all(spread, "col", 0, 0, tiled=True)
+    return got[:, :chunk].reshape(partial.shape), jnp.sum(got[:, chunk:], axis=0)
 
 
-def col_sum(value):
-    count = lax.axis_size("col")
-    spread = jnp.broadcast_to(value[None], (count,) + value.shape)
-    return jnp.sum(lax.all_to_all(spread, "col", 0, 0, tiled=True), axis=0)
+def butterfly_sum(value, axis):
+    count = lax.axis_size(axis)
+    step = 1
+    while step < count:
+        value = value + lax.ppermute(value, axis, [(i, i ^ step) for i in range(count)])
+        step *= 2
+    return value
 
 
 def shards(matrix, vectors, tfactor):
     vec_cols = to_columns(vectors)
-    x_rows = col_sum_rows(product(matrix, vec_cols))
+    x_rows, s_rows = col_sum_rows(product(matrix, vec_cols), vectors)
+    s_full = butterfly_sum(s_rows, "row")
     x_cols = to_columns(x_rows)
-    s_full = col_sum(inner_product(vec_cols, x_cols))
     coupling = inner_product(tfactor, product(s_full, tfactor))
     w_rows = product(x_rows, tfactor) - 0.5 * product(vectors, coupling)
     w_cols = product(x_cols, tfactor) - 0.5 * product(vec_cols, coupling)

time: 160 us -> 143 us (0.89)
  blocking collectives: 86.1 us -> 25.4 us
  starting transfers between devices: 16.7 us -> 38.9 us
  waiting for transfers between devices: 44.4 us -> 65.2 us
    all_to_all x4 -> x1, blocking collectives: 86.1 us -> 25.4 us  [col_sum_rows(): got = lax.all_to_all(spread, 'col', 0, 0, tiled=True)]
    ppermute x0 -> x11, starting transfers between devices: none -> 20.7 us  [the longest x2 9.68 us: to_columns(): other = lax.ppermute(mine, 'row', core_pairs)]
    ppermute x0 -> x11, waiting for transfers between devices: none -> 13.6 us  [the longest x2 6.48 us: to_columns(): across = lax.ppermute(mine, 'row', [(i, i ^ 2) for i in range(row_count)])]
    ppermute x2, waiting for transfers between devices: 27.9 us -> 39.4 us  [to_columns(): mine = lax.ppermute(panel_rows, ('row', 'col'), pairs)]
    all_to_all x1, waiting for transfers between devices: 16.5 us -> 12.3 us  [col_sum_rows(): total = jnp.sum(lax.all_to_all(pieces, 'col', 0, 0, tiled=True), axis=0)]
  transfers between devices with their start and end apart: 3 -> 14, of which waited for: 3 -> 9; matrix products, arithmetic and copies ran while one was open for 0% -> 1% of each run, Pallas kernels for 0% -> 0%
where the time goes in v7:
time: 143 us; the launch traced here: 142 us
  waiting for transfers between devices  65.2 us (46%)
  starting transfers between devices  38.9 us (27%)
  blocking collectives  25.4 us (18%)
  matrix products  10.9 us (8%)
    ppermute x2, waiting for transfers between devices, to_columns(): mine = lax.ppermute(panel_rows, ('row', 'col'), pairs)  39.4 us
    all_to_all x1, blocking collectives, col_sum_rows(): got = lax.all_to_all(spread, 'col', 0, 0, tiled=True)  25.4 us
    all_to_all x1, waiting for transfers between devices, col_sum_rows(): total = jnp.sum(lax.all_to_all(pieces, 'col', 0, 0, tiled=True), axis=0)  12.3 us
    ppermute x2, starting transfers between devices, to_columns(): other = lax.ppermute(mine, 'row', core_pairs)  9.68 us
    all_to_all x1, starting transfers between devices, col_sum_rows(): total = jnp.sum(lax.all_to_all(pieces, 'col', 0, 0, tiled=True), axis=0)  9.57 us
    ppermute x5, starting transfers between devices, butterfly_sum(): lax.ppermute(value, axis, [(i, i ^ step) for i in range(count)])  8.72 us
    ppermute x2, starting transfers between devices, to_columns(): mine = lax.ppermute(panel_rows, ('row', 'col'), pairs)  8.6 us
    ppermute x2, waiting for transfers between devices, to_columns(): across = lax.ppermute(mine, 'row', [(i, i ^ 2) for i in range(row_count)])  6.48 us
  transfers between devices with their start and end apart: 14, of which 9 were waited for; matrix products, arithmetic and copies ran while one was open for 1% of the time, Pallas kernels for 0%

profile of v7, /device:TPU:1, one launch (start us, length us, event | category | flops | bytes accessed | tf_op | source)
XLA Modules:
  0.0 142.0 jit_solution(6955531997303687198)
XLA Ops:
  0.0 5.6 %collective-permute-start = (f32[512,128]{1,0:T(8,128)}, f32[512,128]{1,0:T(8,128)S(1)}, u32[]{:S(2)}, u32[]{:S(2)}) collective-permute-start(f32[512,128]{1,0:T(8,128)} %param.4), channel_id=1, source_target_pairs={{0,32},{1,96},{2,0},{3,128},{4,192},{5,160},{6,64},{7,224},{8,136}... | collective-permute-start | bytes 786440 | tf_op jit(solution)/shard_map/ppermute | solution.py:49
  5.6 20.5 %collective-permute-done = f32[512,128]{1,0:T(8,128)S(1)} collective-permute-done((f32[512,128]{1,0:T(8,128)}, f32[512,128]{1,0:T(8,128)S(1)}, u32[]{:S(2)}, u32[]{:S(2)}) %collective-permute-start) | collective-permute-done | bytes 262176 | tf_op jit(solution)/shard_map/ppermute | solution.py:49
  26.2 3.5 %collective-permute-start.1 = (f32[512,128]{1,0:T(8,128)S(1)}, f32[512,128]{1,0:T(8,128)S(1)}, u32[]{:S(2)}, u32[]{:S(2)}) collective-permute-start(f32[512,128]{1,0:T(8,128)S(1)} %collective-permute-done), channel_id=1, source_target_pairs={{0,8},{8,0},{16,24},{24,16},{32,40},{40,32},{48,56},{56,48},{64,72... | collective-permute-start | bytes 786440 | tf_op jit(solution)/shard_map/ppermute | solution.py:54
  29.6 6.5 %collective-permute-done.2 = f32[512,128]{1,0:T(8,128)S(1)} collective-permute-done((f32[512,128]{1,0:T(8,128)S(1)}, f32[512,128]{1,0:T(8,128)S(1)}, u32[]{:S(2)}, u32[]{:S(2)}) %collective-permute-start.2) | collective-permute-done | bytes 262176 | tf_op jit(solution)/shard_map/ppermute | solution.py:55
  36.1 1.4 %collective-permute-start.3 = (f32[512,128]{1,0:T(8,128)S(1)}, f32[512,128]{1,0:T(8,128)S(1)}, u32[]{:S(2)}, u32[]{:S(2)}) collective-permute-start(f32[512,128]{1,0:T(8,128)S(1)} %collective-permute-done.2), channel_id=1, source_target_pairs={{0,8},{8,0},{16,24},{24,16},{32,40},{40,32},{48,56},{56,48},{64,72... | collective-permute-start | bytes 786440 | tf_op jit(solution)/shard_map/ppermute | solution.py:56
  37.7 1.0 collective-permute-done.3
  38.7 4.5 %convolution_bitcast_fusion = f32[512,128]{0,1:T(8,128)S(1)} fusion(f32[2048,128]{1,0:T(8,128)S(1)} %constant_dynamic-update-slice_fusion.4, f32[512,2048]{1,0:T(8,128)} %param.3), kind=kOutput, calls=%fused_computation.9 | convolution fusion | flops 805306368 | bytes 5505024 | tf_op jit(solution)/shard_map/dot_general | solution.py:20
  43.2 0.8 copy.4
  44.0 9.6 %all-to-all-start = ((f32[8,64,128]{2,1,0:T(8,128)}), f32[8,64,128]{2,1,0:T(8,128)S(1)}, u32[]{:S(2)}, u32[]{:S(2)}) async-start(f32[8,64,128]{2,1,0:T(8,128)} %bitcast.1), calls=%async_computation | async-start | bytes 524288 | tf_op jit(solution)/shard_map/all_to_all | solution.py:66
  53.6 12.3 %all-to-all-done = f32[8,64,128]{2,1,0:T(8,128)S(1)} async-done(((f32[8,64,128]{2,1,0:T(8,128)}), f32[8,64,128]{2,1,0:T(8,128)S(1)}, u32[]{:S(2)}, u32[]{:S(2)}) %all-to-all-start) | async-done | bytes 262176 | tf_op jit(solution)/shard_map/all_to_all | solution.py:66
  66.3 25.4 %all_to_all.10 = f32[8,192,128]{2,1,0:T(8,128)S(1)} all-to-all(f32[8,192,128]{2,1,0:T(8,128)S(1)} %broadcast_in_dim.2), channel_id=1, replica_groups=mesh['row'=32,'col'=8] {'col'}, dimensions={0} | all-to-all | bytes 1572864 | tf_op jit(solution)/shard_map/all_to_all | solution.py:71
  91.7 1.2 collective-permute-start.4
  92.8 0.9 collective-permute-done.4
  93.8 1.2 collective-permute-start.5
  94.9 2.0 %collective-permute-done.5 = f32[128,128]{1,0:T(8,128)S(1)} collective-permute-done((f32[128,128]{1,0:T(8,128)S(1)}, f32[128,128]{1,0:T(8,128)S(1)}, u32[]{:S(2)}, u32[]{:S(2)}) %collective-permute-start.5) | collective-permute-done | bytes 65568 | tf_op jit(solution)/shard_map/ppermute | solution.py:79
  97.0 2.4 %collective-permute-start.6 = (f32[128,128]{1,0:T(8,128)S(1)}, f32[128,128]{1,0:T(8,128)S(1)}, u32[]{:S(2)}, u32[]{:S(2)}) collective-permute-start(f32[128,128]{1,0:T(8,128)S(1)} %add.46), channel_id=1, source_target_pairs={{0,32},{8,40},{16,48},{24,56},{32,0},{40,8},{48,16},{56,24},{64,96... | collective-permute-start | bytes 196616 | tf_op jit(solution)/shard_map/ppermute | solution.py:79
  99.4 3.0 %collective-permute-start.9 = (f32[512,128]{1,0:T(8,128)S(1)}, f32[512,128]{1,0:T(8,128)S(1)}, u32[]{:S(2)}, u32[]{:S(2)}) collective-permute-start(f32[512,128]{1,0:T(8,128)S(1)} %bitcast.22), channel_id=1, source_target_pairs={{0,32},{1,96},{2,0},{3,128},{4,192},{5,160},{6,64},{7,224},{8,136}... | collective-permute-start | bytes 786440 | tf_op jit(solution)/shard_map/ppermute | solution.py:49
  102.9 18.8 %collective-permute-done.9 = f32[512,128]{1,0:T(8,128)S(1)} collective-permute-done((f32[512,128]{1,0:T(8,128)S(1)}, f32[512,128]{1,0:T(8,128)S(1)}, u32[]{:S(2)}, u32[]{:S(2)}) %collective-permute-start.9) | collective-permute-done | bytes 262176 | tf_op jit(solution)/shard_map/ppermute | solution.py:49
  121.8 6.2 %collective-permute-start.10 = (f32[512,128]{1,0:T(8,128)S(1)}, f32[512,128]{1,0:T(8,128)S(1)}, u32[]{:S(2)}, u32[]{:S(2)}) collective-permute-start(f32[512,128]{1,0:T(8,128)S(1)} %collective-permute-done.9), channel_id=1, source_target_pairs={{0,8},{8,0},{16,24},{24,16},{32,40},{40,32},{48,56},{56,48},{64,72... | collective-permute-start | bytes 786440 | tf_op jit(solution)/shard_map/ppermute | solution.py:54
  128.0 3.8 %collective-permute-start.8 = (f32[128,128]{1,0:T(8,128)S(1)}, f32[128,128]{1,0:T(8,128)S(1)}, u32[]{:S(2)}, u32[]{:S(2)}) collective-permute-start(f32[128,128]{1,0:T(8,128)S(1)} %add.48), channel_id=1, source_target_pairs={{0,128},{8,136},{16,144},{24,152},{32,160},{40,168},{48,176},{56,1... | collective-permute-start | bytes 196616 | tf_op jit(solution)/shard_map/ppermute | solution.py:79
  131.9 2.4 %collective-permute-done.8 = f32[128,128]{1,0:T(8,128)S(1)} collective-permute-done((f32[128,128]{1,0:T(8,128)S(1)}, f32[128,128]{1,0:T(8,128)S(1)}, u32[]{:S(2)}, u32[]{:S(2)}) %collective-permute-start.8) | collective-permute-done | bytes 65568 | tf_op jit(solution)/shard_map/ppermute | solution.py:79
  135.3 0.8 collective-permute-start.12
  136.5 0.8 collective-permute-done.12
  137.9 4.1 %convolution_subtract_fusion = f32[512,2048]{1,0:T(8,128)} fusion(f32[512,2048]{1,0:T(8,128)S(1)} %copy-done.1, f32[2048,128]{1,0:T(8,128)S(1)} %constant_dynamic-update-slice_fusion.4, f32[2048,128]{1,0:T(8,128)S(1)} %convolution_subtract_fusion.1, f32[512,128]{1,0:T(8,128)S(1)} %fusion.4, f32[512,128]{1,0:T(8,128)S(1)} %copy-done.2), kind=kOutput, calls=%fused_computation | convolution fusion | flops 1612316672 | bytes 11010048 | tf_op jit(solution)/shard_map/dot_general | solution.py:94
  (40 shorter events, 3.2 us)
Async XLA Ops:
  0.0 102.7 %copy-start = (f32[128,128]{1,0:T(8,128)S(1)}, f32[128,128]{1,0:T(8,128)}, u32[]{:S(2)}) copy-start(f32[128,128]{1,0:T(8,128)} %param.5) | copy-start | bytes 196612
  0.0 26.2 %collective-permute-start = (f32[512,128]{1,0:T(8,128)}, f32[512,128]{1,0:T(8,128)S(1)}, u32[]{:S(2)}, u32[]{:S(2)}) collective-permute-start(f32[512,128]{1,0:T(8,128)} %param.4), channel_id=1, source_target_pairs={{0,32},{1,96},{2,0},{3,128},{4,192},{5,160},{6,64},{7,224},{8,136}... | collective-permute-start | bytes 786440 | tf_op jit(solution)/shard_map/ppermute | solution.py:49
  26.2 10.0 %collective-permute-start.2 = (f32[512,128]{1,0:T(8,128)S(1)}, f32[512,128]{1,0:T(8,128)S(1)}, u32[]{:S(2)}, u32[]{:S(2)}) collective-permute-start(f32[512,128]{1,0:T(8,128)S(1)} %collective-permute-done), channel_id=1, source_target_pairs={{0,16},{8,24},{16,0},{24,8},{32,48},{40,56},{48,32},{56,40},{64,80... | collective-permute-start | bytes 786440 | tf_op jit(solution)/shard_map/ppermute | solution.py:55
  26.2 11.5 %collective-permute-start.1 = (f32[512,128]{1,0:T(8,128)S(1)}, f32[512,128]{1,0:T(8,128)S(1)}, u32[]{:S(2)}, u32[]{:S(2)}) collective-permute-start(f32[512,128]{1,0:T(8,128)S(1)} %collective-permute-done), channel_id=1, source_target_pairs={{0,8},{8,0},{16,24},{24,16},{32,40},{40,32},{48,56},{56,48},{64,72... | collective-permute-start | bytes 786440 | tf_op jit(solution)/shard_map/ppermute | solution.py:54
  36.1 2.6 %collective-permute-start.3 = (f32[512,128]{1,0:T(8,128)S(1)}, f32[512,128]{1,0:T(8,128)S(1)}, u32[]{:S(2)}, u32[]{:S(2)}) collective-permute-start(f32[512,128]{1,0:T(8,128)S(1)} %collective-permute-done.2), channel_id=1, source_target_pairs={{0,8},{8,0},{16,24},{24,16},{32,40},{40,32},{48,56},{56,48},{64,72... | collective-permute-start | bytes 786440 | tf_op jit(solution)/shard_map/ppermute | solution.py:56
  37.7 28.3 %copy-start.2 = (f32[512,128]{1,0:T(8,128)S(1)}, f32[512,128]{1,0:T(8,128)}, u32[]{:S(2)}) copy-start(f32[512,128]{1,0:T(8,128)} %param.4) | copy-start | bytes 786436
  44.0 21.8 %all-to-all-start = ((f32[8,64,128]{2,1,0:T(8,128)}), f32[8,64,128]{2,1,0:T(8,128)S(1)}, u32[]{:S(2)}, u32[]{:S(2)}) async-start(f32[8,64,128]{2,1,0:T(8,128)} %bitcast.1), calls=%async_computation | async-start | bytes 524288 | tf_op jit(solution)/shard_map/all_to_all | solution.py:66
  91.7 2.1 %collective-permute-start.4 = (f32[128,128]{1,0:T(8,128)S(1)}, f32[128,128]{1,0:T(8,128)S(1)}, u32[]{:S(2)}, u32[]{:S(2)}) collective-permute-start(f32[128,128]{1,0:T(8,128)S(1)} %slice_reduce_fusion), channel_id=1, source_target_pairs={{0,8},{8,0},{16,24},{24,16},{32,40},{40,32},{48,56},{56,48},{64,72... | collective-permute-start | bytes 196616 | tf_op jit(solution)/shard_map/ppermute | solution.py:79
  93.8 3.2 %collective-permute-start.5 = (f32[128,128]{1,0:T(8,128)S(1)}, f32[128,128]{1,0:T(8,128)S(1)}, u32[]{:S(2)}, u32[]{:S(2)}) collective-permute-start(f32[128,128]{1,0:T(8,128)S(1)} %add.45), channel_id=1, source_target_pairs={{0,16},{8,24},{16,0},{24,8},{32,48},{40,56},{48,32},{56,40},{64,80... | collective-permute-start | bytes 196616 | tf_op jit(solution)/shard_map/ppermute | solution.py:79
  97.0 5.4 %collective-permute-start.6 = (f32[128,128]{1,0:T(8,128)S(1)}, f32[128,128]{1,0:T(8,128)S(1)}, u32[]{:S(2)}, u32[]{:S(2)}) collective-permute-start(f32[128,128]{1,0:T(8,128)S(1)} %add.46), channel_id=1, source_target_pairs={{0,32},{8,40},{16,48},{24,56},{32,0},{40,8},{48,16},{56,24},{64,96... | collective-permute-start | bytes 196616 | tf_op jit(solution)/shard_map/ppermute | solution.py:79
  99.4 22.4 %collective-permute-start.9 = (f32[512,128]{1,0:T(8,128)S(1)}, f32[512,128]{1,0:T(8,128)S(1)}, u32[]{:S(2)}, u32[]{:S(2)}) collective-permute-start(f32[512,128]{1,0:T(8,128)S(1)} %bitcast.22), channel_id=1, source_target_pairs={{0,32},{1,96},{2,0},{3,128},{4,192},{5,160},{6,64},{7,224},{8,136}... | collective-permute-start | bytes 786440 | tf_op jit(solution)/shard_map/ppermute | solution.py:49
  102.4 25.5 %collective-permute-start.7 = (f32[128,128]{1,0:T(8,128)S(1)}, f32[128,128]{1,0:T(8,128)S(1)}, u32[]{:S(2)}, u32[]{:S(2)}) collective-permute-start(f32[128,128]{1,0:T(8,128)S(1)} %add.47), channel_id=1, source_target_pairs={{0,64},{8,72},{16,80},{24,88},{32,96},{40,104},{48,112},{56,120},{... | collective-permute-start | bytes 196616 | tf_op jit(solution)/shard_map/ppermute | solution.py:79
  121.8 13.5 %collective-permute-start.11 = (f32[512,128]{1,0:T(8,128)S(1)}, f32[512,128]{1,0:T(8,128)S(1)}, u32[]{:S(2)}, u32[]{:S(2)}) collective-permute-start(f32[512,128]{1,0:T(8,128)S(1)} %collective-permute-done.9), channel_id=1, source_target_pairs={{0,16},{8,24},{16,0},{24,8},{32,48},{40,56},{48,32},{56,40},{64,80... | collective-permute-start | bytes 786440 | tf_op jit(solution)/shard_map/ppermute | solution.py:55
  121.8 14.7 %collective-permute-start.10 = (f32[512,128]{1,0:T(8,128)S(1)}, f32[512,128]{1,0:T(8,128)S(1)}, u32[]{:S(2)}, u32[]{:S(2)}) collective-permute-start(f32[512,128]{1,0:T(8,128)S(1)} %collective-permute-done.9), channel_id=1, source_target_pairs={{0,8},{8,0},{16,24},{24,16},{32,40},{40,32},{48,56},{56,48},{64,72... | collective-permute-start | bytes 786440 | tf_op jit(solution)/shard_map/ppermute | solution.py:54
  128.0 6.3 %collective-permute-start.8 = (f32[128,128]{1,0:T(8,128)S(1)}, f32[128,128]{1,0:T(8,128)S(1)}, u32[]{:S(2)}, u32[]{:S(2)}) collective-permute-start(f32[128,128]{1,0:T(8,128)S(1)} %add.48), channel_id=1, source_target_pairs={{0,128},{8,136},{16,144},{24,152},{32,160},{40,168},{48,176},{56,1... | collective-permute-start | bytes 196616 | tf_op jit(solution)/shard_map/ppermute | solution.py:79
  131.9 6.0 %copy-start.1 = (f32[512,2048]{1,0:T(8,128)S(1)}, f32[512,2048]{1,0:T(8,128)}, u32[]{:S(2)}) copy-start(f32[512,2048]{1,0:T(8,128)} %param.3) | copy-start | bytes 12582916
  135.3 2.0 %collective-permute-start.12 = (f32[512,128]{1,0:T(8,128)S(1)}, f32[512,128]{1,0:T(8,128)S(1)}, u32[]{:S(2)}, u32[]{:S(2)}) collective-permute-start(f32[512,128]{1,0:T(8,128)S(1)} %collective-permute-done.11), channel_id=1, source_target_pairs={{0,8},{8,0},{16,24},{24,16},{32,40},{40,32},{48,56},{56,48},{64,72... | collective-permute-start | bytes 786440 | tf_op jit(solution)/shard_map/ppermute | solution.py:56

commit v8 on v7

--- a/solution.py
+++ b/solution.py
@@ -59,17 +59,12 @@
     return gathered
 
 
-def col_sum_rows(partial, vectors):
+def col_sum_rows(partial):
     count = lax.axis_size("col")
-    chunk = partial.shape[0] // count
-    pieces = partial.reshape((count, chunk) + partial.shape[1:])
+    pieces = partial.reshape((count, partial.shape[0] // count) + partial.shape[1:])
     total = jnp.sum(lax.all_to_all(pieces, "col", 0, 0, tiled=True), axis=0)
-    vec_chunk = lax.dynamic_slice_in_dim(vectors, lax.axis_index("col") * chunk, chunk, 0)
-    inner = inner_product(vec_chunk, total)
-    both = jnp.concatenate([total, inner], axis=0)
-    spread = jnp.broadcast_to(both[None], (count,) + both.shape)
-    got = lax.all_to_all(spread, "col", 0, 0, tiled=True)
-    return got[:, :chunk].reshape(partial.shape), jnp.sum(got[:, chunk:], axis=0)
+    spread = jnp.broadcast_to(total[None], pieces.shape)
+    return lax.all_to_all(spread, "col", 0, 0, tiled=True).reshape(partial.shape)
 
 
 def butterfly_sum(value, axis):
@@ -83,8 +78,8 @@
 
 def shards(matrix, vectors, tfactor):
     vec_cols = to_columns(vectors)
-    x_rows, s_rows = col_sum_rows(product(matrix, vec_cols), vectors)
-    s_full = butterfly_sum(s_rows, "row")
+    x_rows = col_sum_rows(product(matrix, vec_cols))
+    s_full = butterfly_sum(inner_product(vectors, x_rows), "row")
     x_cols = to_columns(x_rows)
     coupling = inner_product(tfactor, product(s_full, tfactor))
     w_rows = product(x_rows, tfactor) - 0.5 * product(vectors, coupling)

time: 143 us -> 130 us (0.909)
  waiting for transfers between devices: 65.2 us -> 52.9 us
  blocking collectives: 25.4 us -> 35.8 us
  starting transfers between devices: 38.9 us -> 29.3 us
    all_to_all x1 -> x0, waiting for transfers between devices: 12.3 us -> none  [col_sum_rows(): total = jnp.sum(lax.all_to_all(pieces, 'col', 0, 0, tiled=True), axis=0)]
    all_to_all x1 -> x2, blocking collectives: 25.4 us -> 35.8 us  [the longest x1 21.6 us: col_sum_rows(): total = jnp.sum(lax.all_to_all(pieces, 'col', 0, 0, tiled=True), axis=0)]
    all_to_all x1 -> x0, starting transfers between devices: 9.57 us -> none  [col_sum_rows(): total = jnp.sum(lax.all_to_all(pieces, 'col', 0, 0, tiled=True), axis=0)]
  transfers between devices with their start and end apart: 14 -> 13, of which waited for: 9 -> 8; matrix products, arithmetic and copies ran while one was open for 1% -> 1% of each run, Pallas kernels for 0% -> 0%
where the time goes in v8:
time: 130 us
  waiting for transfers between devices  52.9 us (41%)
  blocking collectives  35.8 us (28%)
  starting transfers between devices  29.3 us (23%)
  matrix products  11.1 us (9%)
    ppermute x2, waiting for transfers between devices, to_columns(): mine = lax.ppermute(panel_rows, ('row', 'col'), pairs)  39.4 us
    all_to_all x1, blocking collectives, col_sum_rows(): total = jnp.sum(lax.all_to_all(pieces, 'col', 0, 0, tiled=True), axis=0)  21.6 us
    all_to_all x1, blocking collectives, col_sum_rows(): lax.all_to_all(spread, 'col', 0, 0, tiled=True).reshape(partial.shape)  14.2 us
    ppermute x2, starting transfers between devices, to_columns(): other = lax.ppermute(mine, 'row', core_pairs)  9.71 us
    ppermute x5, starting transfers between devices, butterfly_sum(): lax.ppermute(value, axis, [(i, i ^ step) for i in range(count)])  8.72 us
    ppermute x2, starting transfers between devices, to_columns(): mine = lax.ppermute(panel_rows, ('row', 'col'), pairs)  8.59 us
    ppermute x2, waiting for transfers between devices, to_columns(): across = lax.ppermute(mine, 'row', [(i, i ^ 2) for i in range(row_count)])  6.48 us
    dot_general x6, matrix products, product(): jnp.dot(left, right, precision=lax.Precision.HIGH, preferred_element_type...  6.41 us
  transfers between devices with their start and end apart: 13, of which 8 were waited for; matrix products, arithmetic and copies ran while one was open for 1% of the time, Pallas kernels for 0%

profile of v8, /device:TPU:1, one launch (start us, length us, event | category | flops | bytes accessed | tf_op | source)
XLA Modules:
  0.0 130.0 jit_solution(4509484590252267865)
XLA Ops:
  0.0 5.6 %collective-permute-start = (f32[512,128]{1,0:T(8,128)}, f32[512,128]{1,0:T(8,128)S(1)}, u32[]{:S(2)}, u32[]{:S(2)}) collective-permute-start(f32[512,128]{1,0:T(8,128)} %param.4), channel_id=1, source_target_pairs={{0,32},{1,96},{2,0},{3,128},{4,192},{5,160},{6,64},{7,224},{8,136}... | collective-permute-start | bytes 786440 | tf_op jit(solution)/shard_map/ppermute | solution.py:49
  5.6 20.5 %collective-permute-done = f32[512,128]{1,0:T(8,128)S(1)} collective-permute-done((f32[512,128]{1,0:T(8,128)}, f32[512,128]{1,0:T(8,128)S(1)}, u32[]{:S(2)}, u32[]{:S(2)}) %collective-permute-start) | collective-permute-done | bytes 262176 | tf_op jit(solution)/shard_map/ppermute | solution.py:49
  26.2 3.5 %collective-permute-start.1 = (f32[512,128]{1,0:T(8,128)S(1)}, f32[512,128]{1,0:T(8,128)S(1)}, u32[]{:S(2)}, u32[]{:S(2)}) collective-permute-start(f32[512,128]{1,0:T(8,128)S(1)} %collective-permute-done), channel_id=1, source_target_pairs={{0,8},{8,0},{16,24},{24,16},{32,40},{40,32},{48,56},{56,48},{64,72... | collective-permute-start | bytes 786440 | tf_op jit(solution)/shard_map/ppermute | solution.py:54
  29.6 6.5 %collective-permute-done.2 = f32[512,128]{1,0:T(8,128)S(1)} collective-permute-done((f32[512,128]{1,0:T(8,128)S(1)}, f32[512,128]{1,0:T(8,128)S(1)}, u32[]{:S(2)}, u32[]{:S(2)}) %collective-permute-start.2) | collective-permute-done | bytes 262176 | tf_op jit(solution)/shard_map/ppermute | solution.py:55
  36.1 1.4 %collective-permute-start.3 = (f32[512,128]{1,0:T(8,128)S(1)}, f32[512,128]{1,0:T(8,128)S(1)}, u32[]{:S(2)}, u32[]{:S(2)}) collective-permute-start(f32[512,128]{1,0:T(8,128)S(1)} %collective-permute-done.2), channel_id=1, source_target_pairs={{0,8},{8,0},{16,24},{24,16},{32,40},{40,32},{48,56},{56,48},{64,72... | collective-permute-start | bytes 786440 | tf_op jit(solution)/shard_map/ppermute | solution.py:56
  37.7 1.0 collective-permute-done.3
  38.7 4.5 %convolution_bitcast_fusion = f32[512,128]{0,1:T(8,128)S(1)} fusion(f32[2048,128]{1,0:T(8,128)S(1)} %constant_dynamic-update-slice_fusion.4, f32[512,2048]{1,0:T(8,128)} %param.3), kind=kOutput, calls=%fused_computation.9 | convolution fusion | flops 805306368 | bytes 5505024 | tf_op jit(solution)/shard_map/dot_general | solution.py:20
  43.3 21.6 %all_to_all.11 = f32[8,64,128]{2,1,0:T(8,128)S(1)} all-to-all(f32[8,64,128]{2,1,0:T(8,128)S(1)} %bitcast.28), channel_id=1, replica_groups=mesh['row'=32,'col'=8] {'col'}, dimensions={0} | all-to-all | bytes 524288 | tf_op jit(solution)/shard_map/all_to_all | solution.py:65
  65.0 14.2 %all_to_all.10 = f32[8,64,128]{2,1,0:T(8,128)S(1)} all-to-all(f32[8,64,128]{2,1,0:T(8,128)S(1)} %broadcast_in_dim.2), channel_id=1, replica_groups=mesh['row'=32,'col'=8] {'col'}, dimensions={0} | all-to-all | bytes 524288 | tf_op jit(solution)/shard_map/all_to_all | solution.py:67
  79.6 1.1 collective-permute-start.4
  80.7 0.9 collective-permute-done.4
  81.7 1.2 collective-permute-start.5
  82.8 2.0 %collective-permute-done.5 = f32[128,128]{0,1:T(8,128)S(1)} collective-permute-done((f32[128,128]{0,1:T(8,128)S(1)}, f32[128,128]{0,1:T(8,128)S(1)}, u32[]{:S(2)}, u32[]{:S(2)}) %collective-permute-start.5) | collective-permute-done | bytes 65568 | tf_op jit(solution)/shard_map/ppermute | solution.py:74
  84.9 2.4 %collective-permute-start.6 = (f32[128,128]{0,1:T(8,128)S(1)}, f32[128,128]{0,1:T(8,128)S(1)}, u32[]{:S(2)}, u32[]{:S(2)}) collective-permute-start(f32[128,128]{0,1:T(8,128)S(1)} %add.42), channel_id=1, source_target_pairs={{0,32},{8,40},{16,48},{24,56},{32,0},{40,8},{48,16},{56,24},{64,96... | collective-permute-start | bytes 196616 | tf_op jit(solution)/shard_map/ppermute | solution.py:74
  87.3 3.0 %collective-permute-start.9 = (f32[512,128]{1,0:T(8,128)S(1)}, f32[512,128]{1,0:T(8,128)S(1)}, u32[]{:S(2)}, u32[]{:S(2)}) collective-permute-start(f32[512,128]{1,0:T(8,128)S(1)} %bitcast.26), channel_id=1, source_target_pairs={{0,32},{1,96},{2,0},{3,128},{4,192},{5,160},{6,64},{7,224},{8,136}... | collective-permute-start | bytes 786440 | tf_op jit(solution)/shard_map/ppermute | solution.py:49
  90.8 18.8 %collective-permute-done.9 = f32[512,128]{1,0:T(8,128)S(1)} collective-permute-done((f32[512,128]{1,0:T(8,128)S(1)}, f32[512,128]{1,0:T(8,128)S(1)}, u32[]{:S(2)}, u32[]{:S(2)}) %collective-permute-start.9) | collective-permute-done | bytes 262176 | tf_op jit(solution)/shard_map/ppermute | solution.py:49
  109.6 6.2 %collective-permute-start.10 = (f32[512,128]{1,0:T(8,128)S(1)}, f32[512,128]{1,0:T(8,128)S(1)}, u32[]{:S(2)}, u32[]{:S(2)}) collective-permute-start(f32[512,128]{1,0:T(8,128)S(1)} %collective-permute-done.9), channel_id=1, source_target_pairs={{0,8},{8,0},{16,24},{24,16},{32,40},{40,32},{48,56},{56,48},{64,72... | collective-permute-start | bytes 786440 | tf_op jit(solution)/shard_map/ppermute | solution.py:54
  115.9 3.8 %collective-permute-start.8 = (f32[128,128]{0,1:T(8,128)S(1)}, f32[128,128]{0,1:T(8,128)S(1)}, u32[]{:S(2)}, u32[]{:S(2)}) collective-permute-start(f32[128,128]{0,1:T(8,128)S(1)} %add.44), channel_id=1, source_target_pairs={{0,128},{8,136},{16,144},{24,152},{32,160},{40,168},{48,176},{56,1... | collective-permute-start | bytes 196616 | tf_op jit(solution)/shard_map/ppermute | solution.py:74
  119.8 2.4 %collective-permute-done.8 = f32[128,128]{0,1:T(8,128)S(1)} collective-permute-done((f32[128,128]{0,1:T(8,128)S(1)}, f32[128,128]{0,1:T(8,128)S(1)}, u32[]{:S(2)}, u32[]{:S(2)}) %collective-permute-start.8) | collective-permute-done | bytes 65568 | tf_op jit(solution)/shard_map/ppermute | solution.py:74
  122.6 0.6 convolution_multiply_fusion
  123.2 0.8 collective-permute-start.12
  124.5 0.8 collective-permute-done.12
  125.3 0.6 convolution_subtract_fusion.1
  125.9 4.1 %convolution_subtract_fusion = f32[512,2048]{1,0:T(8,128)} fusion(f32[512,2048]{1,0:T(8,128)S(1)} %copy-done.1, f32[2048,128]{1,0:T(8,128)S(1)} %constant_dynamic-update-slice_fusion.4, f32[2048,128]{1,0:T(8,128)S(1)} %convolution_subtract_fusion.1, f32[512,128]{1,0:T(8,128)S(1)} %fusion.4, f32[512,128]{1,0:T(8,128)S(1)} %copy-done.2), kind=kOutput, calls=%fused_computation | convolution fusion | flops 1612316672 | bytes 11010048 | tf_op jit(solution)/shard_map/dot_general | solution.py:89
  (36 shorter events, 2.2 us)
Async XLA Ops:
  0.0 90.5 %copy-start = (f32[128,128]{1,0:T(8,128)S(1)}, f32[128,128]{1,0:T(8,128)}, u32[]{:S(2)}) copy-start(f32[128,128]{1,0:T(8,128)} %param.5) | copy-start | bytes 196612
  0.0 26.2 %collective-permute-start = (f32[512,128]{1,0:T(8,128)}, f32[512,128]{1,0:T(8,128)S(1)}, u32[]{:S(2)}, u32[]{:S(2)}) collective-permute-start(f32[512,128]{1,0:T(8,128)} %param.4), channel_id=1, source_target_pairs={{0,32},{1,96},{2,0},{3,128},{4,192},{5,160},{6,64},{7,224},{8,136}... | collective-permute-start | bytes 786440 | tf_op jit(solution)/shard_map/ppermute | solution.py:49
  26.2 10.0 %collective-permute-start.2 = (f32[512,128]{1,0:T(8,128)S(1)}, f32[512,128]{1,0:T(8,128)S(1)}, u32[]{:S(2)}, u32[]{:S(2)}) collective-permute-start(f32[512,128]{1,0:T(8,128)S(1)} %collective-permute-done), channel_id=1, source_target_pairs={{0,16},{8,24},{16,0},{24,8},{32,48},{40,56},{48,32},{56,40},{64,80... | collective-permute-start | bytes 786440 | tf_op jit(solution)/shard_map/ppermute | solution.py:55
  26.2 11.5 %collective-permute-start.1 = (f32[512,128]{1,0:T(8,128)S(1)}, f32[512,128]{1,0:T(8,128)S(1)}, u32[]{:S(2)}, u32[]{:S(2)}) collective-permute-start(f32[512,128]{1,0:T(8,128)S(1)} %collective-permute-done), channel_id=1, source_target_pairs={{0,8},{8,0},{16,24},{24,16},{32,40},{40,32},{48,56},{56,48},{64,72... | collective-permute-start | bytes 786440 | tf_op jit(solution)/shard_map/ppermute | solution.py:54
  36.1 2.6 %collective-permute-start.3 = (f32[512,128]{1,0:T(8,128)S(1)}, f32[512,128]{1,0:T(8,128)S(1)}, u32[]{:S(2)}, u32[]{:S(2)}) collective-permute-start(f32[512,128]{1,0:T(8,128)S(1)} %collective-permute-done.2), channel_id=1, source_target_pairs={{0,8},{8,0},{16,24},{24,16},{32,40},{40,32},{48,56},{56,48},{64,72... | collective-permute-start | bytes 786440 | tf_op jit(solution)/shard_map/ppermute | solution.py:56
  37.7 41.5 %copy-start.2 = (f32[512,128]{1,0:T(8,128)S(1)}, f32[512,128]{1,0:T(8,128)}, u32[]{:S(2)}) copy-start(f32[512,128]{1,0:T(8,128)} %param.4) | copy-start | bytes 786436
  79.6 2.0 %collective-permute-start.4 = (f32[128,128]{0,1:T(8,128)S(1)}, f32[128,128]{0,1:T(8,128)S(1)}, u32[]{:S(2)}, u32[]{:S(2)}) collective-permute-start(f32[128,128]{0,1:T(8,128)S(1)} %convolution_bitcast_fusion.1), channel_id=1, source_target_pairs={{0,8},{8,0},{16,24},{24,16},{32,40},{40,32},{48,56},{56,48},{64,72... | collective-permute-start | bytes 196616 | tf_op jit(solution)/shard_map/ppermute | solution.py:74
  81.7 3.2 %collective-permute-start.5 = (f32[128,128]{0,1:T(8,128)S(1)}, f32[128,128]{0,1:T(8,128)S(1)}, u32[]{:S(2)}, u32[]{:S(2)}) collective-permute-start(f32[128,128]{0,1:T(8,128)S(1)} %add.41), channel_id=1, source_target_pairs={{0,16},{8,24},{16,0},{24,8},{32,48},{40,56},{48,32},{56,40},{64,80... | collective-permute-start | bytes 196616 | tf_op jit(solution)/shard_map/ppermute | solution.py:74
  84.9 5.4 %collective-permute-start.6 = (f32[128,128]{0,1:T(8,128)S(1)}, f32[128,128]{0,1:T(8,128)S(1)}, u32[]{:S(2)}, u32[]{:S(2)}) collective-permute-start(f32[128,128]{0,1:T(8,128)S(1)} %add.42), channel_id=1, source_target_pairs={{0,32},{8,40},{16,48},{24,56},{32,0},{40,8},{48,16},{56,24},{64,96... | collective-permute-start | bytes 196616 | tf_op jit(solution)/shard_map/ppermute | solution.py:74
  87.3 22.4 %collective-permute-start.9 = (f32[512,128]{1,0:T(8,128)S(1)}, f32[512,128]{1,0:T(8,128)S(1)}, u32[]{:S(2)}, u32[]{:S(2)}) collective-permute-start(f32[512,128]{1,0:T(8,128)S(1)} %bitcast.26), channel_id=1, source_target_pairs={{0,32},{1,96},{2,0},{3,128},{4,192},{5,160},{6,64},{7,224},{8,136}... | collective-permute-start | bytes 786440 | tf_op jit(solution)/shard_map/ppermute | solution.py:49
  90.3 25.6 %collective-permute-start.7 = (f32[128,128]{0,1:T(8,128)S(1)}, f32[128,128]{0,1:T(8,128)S(1)}, u32[]{:S(2)}, u32[]{:S(2)}) collective-permute-start(f32[128,128]{0,1:T(8,128)S(1)} %add.43), channel_id=1, source_target_pairs={{0,64},{8,72},{16,80},{24,88},{32,96},{40,104},{48,112},{56,120},{... | collective-permute-start | bytes 196616 | tf_op jit(solution)/shard_map/ppermute | solution.py:74
  109.6 13.6 %collective-permute-start.11 = (f32[512,128]{1,0:T(8,128)S(1)}, f32[512,128]{1,0:T(8,128)S(1)}, u32[]{:S(2)}, u32[]{:S(2)}) collective-permute-start(f32[512,128]{1,0:T(8,128)S(1)} %collective-permute-done.9), channel_id=1, source_target_pairs={{0,16},{8,24},{16,0},{24,8},{32,48},{40,56},{48,32},{56,40},{64,80... | collective-permute-start | bytes 786440 | tf_op jit(solution)/shard_map/ppermute | solution.py:55
  109.6 14.8 %collective-permute-start.10 = (f32[512,128]{1,0:T(8,128)S(1)}, f32[512,128]{1,0:T(8,128)S(1)}, u32[]{:S(2)}, u32[]{:S(2)}) collective-permute-start(f32[512,128]{1,0:T(8,128)S(1)} %collective-permute-done.9), channel_id=1, source_target_pairs={{0,8},{8,0},{16,24},{24,16},{32,40},{40,32},{48,56},{56,48},{64,72... | collective-permute-start | bytes 786440 | tf_op jit(solution)/shard_map/ppermute | solution.py:54
  115.9 6.3 %collective-permute-start.8 = (f32[128,128]{0,1:T(8,128)S(1)}, f32[128,128]{0,1:T(8,128)S(1)}, u32[]{:S(2)}, u32[]{:S(2)}) collective-permute-start(f32[128,128]{0,1:T(8,128)S(1)} %add.44), channel_id=1, source_target_pairs={{0,128},{8,136},{16,144},{24,152},{32,160},{40,168},{48,176},{56,1... | collective-permute-start | bytes 196616 | tf_op jit(solution)/shard_map/ppermute | solution.py:74
  119.8 6.1 %copy-start.1 = (f32[512,2048]{1,0:T(8,128)S(1)}, f32[512,2048]{1,0:T(8,128)}, u32[]{:S(2)}) copy-start(f32[512,2048]{1,0:T(8,128)} %param.3) | copy-start | bytes 12582916
  123.2 2.0 %collective-permute-start.12 = (f32[512,128]{1,0:T(8,128)S(1)}, f32[512,128]{1,0:T(8,128)S(1)}, u32[]{:S(2)}, u32[]{:S(2)}) collective-permute-start(f32[512,128]{1,0:T(8,128)S(1)} %collective-permute-done.11), channel_id=1, source_target_pairs={{0,8},{8,0},{16,24},{24,16},{32,40},{40,32},{48,56},{56,48},{64,72... | collective-permute-start | bytes 786440 | tf_op jit(solution)/shard_map/ppermute | solution.py:56

commit v9 on v8

--- a/solution.py
+++ b/solution.py
@@ -2,18 +2,6 @@
 import jax.numpy as jnp
 from jax import lax
 from jax.sharding import PartitionSpec as P
-
-
-SOURCE_COL = (
-    ((2, 0, 6, 1, 3, 5, 4, 7), (6, 2, 1, 4, 0, 7, 3, 5), (6, 7, 2, 1, 0, 3, 5, 4), (0, 5, 1, 3, 7, 4, 2, 6)),
-    ((2, 1, 5, 3, 6, 4, 7, 0), (5, 0, 4, 1, 7, 3, 6, 2), (7, 4, 5, 6, 2, 0, 1, 3), (4, 6, 7, 1, 5, 3, 2, 0)),
-    ((0, 7, 2, 6, 4, 1, 5, 3), (5, 4, 3, 7, 1, 6, 0, 2), (3, 4, 6, 0, 2, 1, 5, 7), (7, 1, 5, 4, 6, 2, 0, 3)),
-    ((0, 7, 1, 4, 3, 6, 2, 5), (3, 6, 7, 4, 5, 2, 1, 0), (5, 1, 3, 0, 6, 4, 7, 2), (0, 3, 1, 2, 4, 7, 5, 6)),
-    ((4, 6, 2, 5, 7, 3, 1, 0), (5, 2, 6, 3, 1, 0, 7, 4), (2, 3, 4, 7, 1, 6, 0, 5), (7, 6, 3, 2, 5, 0, 4, 1)),
-    ((7, 4, 6, 0, 1, 5, 3, 2), (2, 5, 3, 1, 0, 7, 4, 6), (3, 2, 6, 5, 1, 7, 0, 4), (6, 7, 2, 0, 3, 5, 4, 1)),
-    ((2, 5, 3, 0, 6, 4, 7, 1), (4, 1, 7, 2, 3, 0, 5, 6), (2, 0, 4, 6, 1, 7, 3, 5), (1, 3, 7, 5, 4, 2, 6, 0)),
-    ((6, 3, 0, 7, 5, 1, 2, 4), (1, 6, 2, 5, 4, 3, 0, 7), (1, 7, 0, 4, 2, 6, 3, 5), (5, 1, 4, 3, 7, 0, 6, 2)),
-)
 
 
 def product(left, right):
@@ -35,19 +23,22 @@
     row_count = lax.axis_size("row")
     col_count = lax.axis_size("col")
     per = row_count // col_count
-    pairs = []
-    for src_row in range(row_count):
-        for src_col in range(col_count):
-            dst_col = src_row // per
-            low = src_row % per
-            if (row_count, col_count) == (32, 8):
-                high = SOURCE_COL[dst_col][low].index(src_col)
-            else:
-                high = src_col ^ dst_col ^ low
-            dst_row = per * high + low
-            pairs.append((src_row * col_count + src_col, dst_row * col_count + dst_col))
-    mine = lax.ppermute(panel_rows, ("row", "col"), pairs)
+    high = lax.axis_index("row") // per
     low = lax.axis_index("row") % per
+    col = lax.axis_index("col")
+    mine = jnp.where(high == col, panel_rows, jnp.zeros_like(panel_rows))
+    step = 1
+    while step < col_count:
+        pairs = []
+        for src_high in range(col_count):
+            for src_low in range(per):
+                for src_col in range(col_count):
+                    if (src_high ^ src_col) < step:
+                        src = (per * src_high + src_low) * col_count + src_col
+                        dst = (per * (src_high ^ step) + src_low) * col_count + src_col
+                        pairs.append((src, dst))
+        mine = mine + lax.ppermute(mine, ("row", "col"), pairs)
+        step *= 2
     gathered = jnp.zeros((per * rows_here,) + panel_rows.shape[1:], panel_rows.dtype)
     gathered = lax.dynamic_update_slice_in_dim(gathered, mine, low * rows_here, 0)
     core_pairs = [(i, i ^ 1) for i in range(row_count)]

time: 130 us -> 125 us (0.962); the launches traced: 130 us -> 123 us
  waiting for transfers between devices: 52.9 us -> 39.7 us
  starting transfers between devices: 29.3 us -> 33.7 us
  other arithmetic: 0.06 us -> 2.24 us
    ppermute x2 -> x6, waiting for transfers between devices: 39.4 us -> 20.2 us  [to_columns(): mine = mine + lax.ppermute(mine, ('row', 'col'), pairs)]
    ppermute x2 -> x6, starting transfers between devices: 8.59 us -> 17 us  [to_columns(): mine = mine + lax.ppermute(mine, ('row', 'col'), pairs)]
    ppermute x5, starting transfers between devices: 8.72 us -> 4.29 us  [butterfly_sum(): lax.ppermute(value, axis, [(i, i ^ step) for i in range(count)])]
    ppermute x5, waiting for transfers between devices: 5.3 us -> 9.23 us  [butterfly_sum(): lax.ppermute(value, axis, [(i, i ^ step) for i in range(count)])]
    ppermute x2, starting transfers between devices: 9.71 us -> 6.4 us  [to_columns(): other = lax.ppermute(mine, 'row', core_pairs)]
    ppermute x2, starting transfers between devices: 2.27 us -> 4.85 us  [to_columns(): diagonal = lax.ppermute(across, 'row', core_pairs)]
    all_to_all x1, blocking collectives: 14.2 us -> 12.1 us  [col_sum_rows(): lax.all_to_all(spread, 'col', 0, 0, tiled=True).reshape(partial.shape)]
    all_to_all x1, blocking collectives: 21.6 us -> 23.7 us  [col_sum_rows(): total = jnp.sum(lax.all_to_all(pieces, 'col', 0, 0, tiled=True), axis=0)]
  transfers between devices with their start and end apart: 13 -> 17, of which waited for: 8 -> 12; matrix products, arithmetic and copies ran while one was open for 1% -> 2% of each run, Pallas kernels for 0% -> 0%
where the time goes in v9:
time: 125 us; the launch traced here: 123 us
  waiting for transfers between devices  39.7 us (32%)
  blocking collectives  35.8 us (29%)
  starting transfers between devices  33.7 us (27%)
  matrix products  11.2 us (9%)
  other arithmetic  2.24 us (2%)
    all_to_all x1, blocking collectives, col_sum_rows(): total = jnp.sum(lax.all_to_all(pieces, 'col', 0, 0, tiled=True), axis=0)  23.7 us
    ppermute x6, waiting for transfers between devices, to_columns(): mine = mine + lax.ppermute(mine, ('row', 'col'), pairs)  20.2 us
    ppermute x6, starting transfers between devices, to_columns(): mine = mine + lax.ppermute(mine, ('row', 'col'), pairs)  17 us
    all_to_all x1, blocking collectives, col_sum_rows(): lax.all_to_all(spread, 'col', 0, 0, tiled=True).reshape(partial.shape)  12.1 us
    ppermute x5, waiting for transfers between devices, butterfly_sum(): lax.ppermute(value, axis, [(i, i ^ step) for i in range(count)])  9.23 us
    ppermute x2, waiting for transfers between devices, to_columns(): across = lax.ppermute(mine, 'row', [(i, i ^ 2) for i in range(row_count)])  8.33 us
    dot_general x6, matrix products, product(): jnp.dot(left, right, precision=lax.Precision.HIGH, preferred_element_type...  6.44 us
    ppermute x2, starting transfers between devices, to_columns(): other = lax.ppermute(mine, 'row', core_pairs)  6.4 us
  transfers between devices with their start and end apart: 17, of which 12 were waited for; matrix products, arithmetic and copies ran while one was open for 2% of the time, Pallas kernels for 0%

profile of v9, /device:TPU:1, one launch (start us, length us, event | category | flops | bytes accessed | tf_op | source)
XLA Modules:
  0.0 123.3 jit_solution(3152875196444038801)
XLA Ops:
  1.0 4.7 %collective-permute-start = (f32[512,128]{1,0:T(8,128)S(1)}, f32[512,128]{1,0:T(8,128)S(1)}, u32[]{:S(2)}, u32[]{:S(2)}) collective-permute-start(f32[512,128]{1,0:T(8,128)S(1)} %broadcast_select_fusion.1), channel_id=1, source_target_pairs={{0,32},{8,40},{16,48},{24,56},{33,1},{41,9},{49,17},{57,25},{66,98... | collective-permute-start | bytes 786440 | tf_op jit(solution)/shard_map/ppermute | solution.py:40
  5.7 4.9 %collective-permute-done = f32[512,128]{1,0:T(8,128)S(1)} collective-permute-done((f32[512,128]{1,0:T(8,128)S(1)}, f32[512,128]{1,0:T(8,128)S(1)}, u32[]{:S(2)}, u32[]{:S(2)}) %collective-permute-start) | collective-permute-done | bytes 262176 | tf_op jit(solution)/shard_map/ppermute | solution.py:40
  11.6 1.3 %collective-permute-start.1 = (f32[512,128]{1,0:T(8,128)S(1)}, f32[512,128]{1,0:T(8,128)S(1)}, u32[]{:S(2)}, u32[]{:S(2)}) collective-permute-start(f32[512,128]{1,0:T(8,128)S(1)} %fusion.29), channel_id=1, source_target_pairs={{0,64},{1,65},{8,72},{9,73},{16,80},{17,81},{24,88},{25,89},{32,96... | collective-permute-start | bytes 786440 | tf_op jit(solution)/shard_map/ppermute | solution.py:40
  12.9 4.3 %collective-permute-done.1 = f32[512,128]{1,0:T(8,128)S(1)} collective-permute-done((f32[512,128]{1,0:T(8,128)S(1)}, f32[512,128]{1,0:T(8,128)S(1)}, u32[]{:S(2)}, u32[]{:S(2)}) %collective-permute-start.1) | collective-permute-done | bytes 262176 | tf_op jit(solution)/shard_map/ppermute | solution.py:40
  17.3 1.3 %collective-permute-start.2 = (f32[512,128]{1,0:T(8,128)S(1)}, f32[512,128]{1,0:T(8,128)S(1)}, u32[]{:S(2)}, u32[]{:S(2)}) collective-permute-start(f32[512,128]{1,0:T(8,128)S(1)} %add.56), channel_id=1, source_target_pairs={{0,128},{1,129},{2,130},{3,131},{8,136},{9,137},{10,138},{11,139},... | collective-permute-start | bytes 786440 | tf_op jit(solution)/shard_map/ppermute | solution.py:40
  18.6 3.6 %collective-permute-done.2 = f32[512,128]{1,0:T(8,128)S(1)} collective-permute-done((f32[512,128]{1,0:T(8,128)S(1)}, f32[512,128]{1,0:T(8,128)S(1)}, u32[]{:S(2)}, u32[]{:S(2)}) %collective-permute-start.2) | collective-permute-done | bytes 262176 | tf_op jit(solution)/shard_map/ppermute | solution.py:40
  22.9 3.1 %collective-permute-start.3 = (f32[512,128]{1,0:T(8,128)S(1)}, f32[512,128]{1,0:T(8,128)S(1)}, u32[]{:S(2)}, u32[]{:S(2)}) collective-permute-start(f32[512,128]{1,0:T(8,128)S(1)} %get-tuple-element.8), channel_id=1, source_target_pairs={{0,8},{8,0},{16,24},{24,16},{32,40},{40,32},{48,56},{56,48},{64,72... | collective-permute-start | bytes 786440 | tf_op jit(solution)/shard_map/ppermute | solution.py:45
  26.0 1.7 %collective-permute-done.4 = f32[512,128]{1,0:T(8,128)S(1)} collective-permute-done((f32[512,128]{1,0:T(8,128)S(1)}, f32[512,128]{1,0:T(8,128)S(1)}, u32[]{:S(2)}, u32[]{:S(2)}) %collective-permute-start.4) | collective-permute-done | bytes 262176 | tf_op jit(solution)/shard_map/ppermute | solution.py:46
  27.7 4.0 %collective-permute-start.5 = (f32[512,128]{1,0:T(8,128)S(1)}, f32[512,128]{1,0:T(8,128)S(1)}, u32[]{:S(2)}, u32[]{:S(2)}) collective-permute-start(f32[512,128]{1,0:T(8,128)S(1)} %collective-permute-done.4), channel_id=1, source_target_pairs={{0,8},{8,0},{16,24},{24,16},{32,40},{40,32},{48,56},{56,48},{64,72... | collective-permute-start | bytes 786440 | tf_op jit(solution)/shard_map/ppermute | solution.py:47
  31.7 1.1 collective-permute-done.5
  32.9 4.5 %convolution_bitcast_fusion = f32[512,128]{0,1:T(8,128)S(1)} fusion(f32[2048,128]{1,0:T(8,128)S(1)} %constant_dynamic-update-slice_fusion.4, f32[512,2048]{1,0:T(8,128)} %param.3), kind=kOutput, calls=%fused_computation.9 | convolution fusion | flops 805306368 | bytes 5505024 | tf_op jit(solution)/shard_map/dot_general | solution.py:8
  37.5 23.7 %all_to_all.11 = f32[8,64,128]{2,1,0:T(8,128)S(1)} all-to-all(f32[8,64,128]{2,1,0:T(8,128)S(1)} %bitcast.30), channel_id=1, replica_groups=mesh['row'=32,'col'=8] {'col'}, dimensions={0} | all-to-all | bytes 524288 | tf_op jit(solution)/shard_map/all_to_all | solution.py:56
  61.2 12.1 %all_to_all.10 = f32[8,64,128]{2,1,0:T(8,128)S(1)} all-to-all(f32[8,64,128]{2,1,0:T(8,128)S(1)} %broadcast_in_dim.2), channel_id=1, replica_groups=mesh['row'=32,'col'=8] {'col'}, dimensions={0} | all-to-all | bytes 524288 | tf_op jit(solution)/shard_map/all_to_all | solution.py:58
  73.3 4.3 %collective-permute-start.11 = (f32[512,128]{1,0:T(8,128)S(1)}, f32[512,128]{1,0:T(8,128)S(1)}, u32[]{:S(2)}, u32[]{:S(2)}) collective-permute-start(f32[512,128]{1,0:T(8,128)S(1)} %broadcast_select_fusion), channel_id=1, source_target_pairs={{0,32},{8,40},{16,48},{24,56},{33,1},{41,9},{49,17},{57,25},{66,98... | collective-permute-start | bytes 786440 | tf_op jit(solution)/shard_map/ppermute | solution.py:40
  78.0 3.5 %collective-permute-start.6 = (f32[128,128]{0,1:T(8,128)S(1)}, f32[128,128]{0,1:T(8,128)S(1)}, u32[]{:S(2)}, u32[]{:S(2)}) collective-permute-start(f32[128,128]{0,1:T(8,128)S(1)} %convolution_bitcast_fusion.1), channel_id=1, source_target_pairs={{0,8},{8,0},{16,24},{24,16},{32,40},{40,32},{48,56},{56,48},{64,72... | collective-permute-start | bytes 196616 | tf_op jit(solution)/shard_map/ppermute | solution.py:65
  83.0 3.7 %collective-permute-done.7 = f32[128,128]{0,1:T(8,128)S(1)} collective-permute-done((f32[128,128]{0,1:T(8,128)S(1)}, f32[128,128]{0,1:T(8,128)S(1)}, u32[]{:S(2)}, u32[]{:S(2)}) %collective-permute-start.7) | collective-permute-done | bytes 65568 | tf_op jit(solution)/shard_map/ppermute | solution.py:65
  86.8 4.6 %collective-permute-done.8 = f32[128,128]{0,1:T(8,128)S(1)} collective-permute-done((f32[128,128]{0,1:T(8,128)S(1)}, f32[128,128]{0,1:T(8,128)S(1)}, u32[]{:S(2)}, u32[]{:S(2)}) %collective-permute-start.8) | collective-permute-done | bytes 65568 | tf_op jit(solution)/shard_map/ppermute | solution.py:65
  91.6 3.4 %collective-permute-start.12 = (f32[512,128]{1,0:T(8,128)S(1)}, f32[512,128]{1,0:T(8,128)S(1)}, u32[]{:S(2)}, u32[]{:S(2)}) collective-permute-start(f32[512,128]{1,0:T(8,128)S(1)} %fusion.28), channel_id=1, source_target_pairs={{0,64},{1,65},{8,72},{9,73},{16,80},{17,81},{24,88},{25,89},{32,96... | collective-permute-start | bytes 786440 | tf_op jit(solution)/shard_map/ppermute | solution.py:40
  95.3 2.9 %collective-permute-done.12 = f32[512,128]{1,0:T(8,128)S(1)} collective-permute-done((f32[512,128]{1,0:T(8,128)S(1)}, f32[512,128]{1,0:T(8,128)S(1)}, u32[]{:S(2)}, u32[]{:S(2)}) %collective-permute-start.12) | collective-permute-done | bytes 262176 | tf_op jit(solution)/shard_map/ppermute | solution.py:40
  98.3 2.0 %collective-permute-start.13 = (f32[512,128]{1,0:T(8,128)S(1)}, f32[512,128]{1,0:T(8,128)S(1)}, u32[]{:S(2)}, u32[]{:S(2)}) collective-permute-start(f32[512,128]{1,0:T(8,128)S(1)} %add.69), channel_id=1, source_target_pairs={{0,128},{1,129},{2,130},{3,131},{8,136},{9,137},{10,138},{11,139},... | collective-permute-start | bytes 786440 | tf_op jit(solution)/shard_map/ppermute | solution.py:40
  100.8 4.5 %collective-permute-done.13 = f32[512,128]{1,0:T(8,128)S(1)} collective-permute-done((f32[512,128]{1,0:T(8,128)S(1)}, f32[512,128]{1,0:T(8,128)S(1)}, u32[]{:S(2)}, u32[]{:S(2)}) %collective-permute-start.13) | collective-permute-done | bytes 262176 | tf_op jit(solution)/shard_map/ppermute | solution.py:40
  105.4 3.3 %collective-permute-start.14 = (f32[512,128]{1,0:T(8,128)S(1)}, f32[512,128]{1,0:T(8,128)S(1)}, u32[]{:S(2)}, u32[]{:S(2)}) collective-permute-start(f32[512,128]{1,0:T(8,128)S(1)} %get-tuple-element.6), channel_id=1, source_target_pairs={{0,8},{8,0},{16,24},{24,16},{32,40},{40,32},{48,56},{56,48},{64,72... | collective-permute-start | bytes 786440 | tf_op jit(solution)/shard_map/ppermute | solution.py:45
  109.9 6.6 %collective-permute-done.15 = f32[512,128]{1,0:T(8,128)S(1)} collective-permute-done((f32[512,128]{1,0:T(8,128)S(1)}, f32[512,128]{1,0:T(8,128)S(1)}, u32[]{:S(2)}, u32[]{:S(2)}) %collective-permute-start.15) | collective-permute-done | bytes 262176 | tf_op jit(solution)/shard_map/ppermute | solution.py:46
  119.2 4.1 %convolution_subtract_fusion = f32[512,2048]{1,0:T(8,128)} fusion(f32[512,2048]{1,0:T(8,128)S(1)} %copy-done.1, f32[2048,128]{1,0:T(8,128)S(1)} %constant_dynamic-update-slice_fusion.4, f32[2048,128]{1,0:T(8,128)S(1)} %convolution_subtract_fusion.1, f32[512,128]{1,0:T(8,128)S(1)} %fusion.4, f32[512,128]{1,0:T(8,128)S(1)} %copy-done.2), kind=kOutput, calls=%fused_computation | convolution fusion | flops 1612316672 | bytes 11010048 | tf_op jit(solution)/shard_map/dot_general | solution.py:80
  (50 shorter events, 9.8 us)
Async XLA Ops:
  0.0 95.1 %copy-start = (f32[128,128]{1,0:T(8,128)S(1)}, f32[128,128]{1,0:T(8,128)}, u32[]{:S(2)}) copy-start(f32[128,128]{1,0:T(8,128)} %param.5) | copy-start | bytes 196612
  1.0 9.6 %collective-permute-start = (f32[512,128]{1,0:T(8,128)S(1)}, f32[512,128]{1,0:T(8,128)S(1)}, u32[]{:S(2)}, u32[]{:S(2)}) collective-permute-start(f32[512,128]{1,0:T(8,128)S(1)} %broadcast_select_fusion.1), channel_id=1, source_target_pairs={{0,32},{8,40},{16,48},{24,56},{33,1},{41,9},{49,17},{57,25},{66,98... | collective-permute-start | bytes 786440 | tf_op jit(solution)/shard_map/ppermute | solution.py:40
  11.6 5.6 %collective-permute-start.1 = (f32[512,128]{1,0:T(8,128)S(1)}, f32[512,128]{1,0:T(8,128)S(1)}, u32[]{:S(2)}, u32[]{:S(2)}) collective-permute-start(f32[512,128]{1,0:T(8,128)S(1)} %fusion.29), channel_id=1, source_target_pairs={{0,64},{1,65},{8,72},{9,73},{16,80},{17,81},{24,88},{25,89},{32,96... | collective-permute-start | bytes 786440 | tf_op jit(solution)/shard_map/ppermute | solution.py:40
  17.3 5.0 %collective-permute-start.2 = (f32[512,128]{1,0:T(8,128)S(1)}, f32[512,128]{1,0:T(8,128)S(1)}, u32[]{:S(2)}, u32[]{:S(2)}) collective-permute-start(f32[512,128]{1,0:T(8,128)S(1)} %add.56), channel_id=1, source_target_pairs={{0,128},{1,129},{2,130},{3,131},{8,136},{9,137},{10,138},{11,139},... | collective-permute-start | bytes 786440 | tf_op jit(solution)/shard_map/ppermute | solution.py:40
  22.4 5.3 %collective-permute-start.4 = (f32[512,128]{1,0:T(8,128)S(1)}, f32[512,128]{1,0:T(8,128)S(1)}, u32[]{:S(2)}, u32[]{:S(2)}) collective-permute-start(f32[512,128]{1,0:T(8,128)S(1)} %get-tuple-element.8), channel_id=1, source_target_pairs={{0,16},{8,24},{16,0},{24,8},{32,48},{40,56},{48,32},{56,40},{64,80... | collective-permute-start | bytes 786440 | tf_op jit(solution)/shard_map/ppermute | solution.py:46
  22.9 8.8 %collective-permute-start.3 = (f32[512,128]{1,0:T(8,128)S(1)}, f32[512,128]{1,0:T(8,128)S(1)}, u32[]{:S(2)}, u32[]{:S(2)}) collective-permute-start(f32[512,128]{1,0:T(8,128)S(1)} %get-tuple-element.8), channel_id=1, source_target_pairs={{0,8},{8,0},{16,24},{24,16},{32,40},{40,32},{48,56},{56,48},{64,72... | collective-permute-start | bytes 786440 | tf_op jit(solution)/shard_map/ppermute | solution.py:45
  27.7 5.1 %collective-permute-start.5 = (f32[512,128]{1,0:T(8,128)S(1)}, f32[512,128]{1,0:T(8,128)S(1)}, u32[]{:S(2)}, u32[]{:S(2)}) collective-permute-start(f32[512,128]{1,0:T(8,128)S(1)} %collective-permute-done.4), channel_id=1, source_target_pairs={{0,8},{8,0},{16,24},{24,16},{32,40},{40,32},{48,56},{56,48},{64,72... | collective-permute-start | bytes 786440 | tf_op jit(solution)/shard_map/ppermute | solution.py:47
  32.8 44.8 %copy-start.2 = (f32[512,128]{1,0:T(8,128)S(1)}, f32[512,128]{1,0:T(8,128)}, u32[]{:S(2)}) copy-start(f32[512,128]{1,0:T(8,128)} %param.4) | copy-start | bytes 786436
  73.3 18.2 %collective-permute-start.11 = (f32[512,128]{1,0:T(8,128)S(1)}, f32[512,128]{1,0:T(8,128)S(1)}, u32[]{:S(2)}, u32[]{:S(2)}) collective-permute-start(f32[512,128]{1,0:T(8,128)S(1)} %broadcast_select_fusion), channel_id=1, source_target_pairs={{0,32},{8,40},{16,48},{24,56},{33,1},{41,9},{49,17},{57,25},{66,98... | collective-permute-start | bytes 786440 | tf_op jit(solution)/shard_map/ppermute | solution.py:40
  78.0 4.4 %collective-permute-start.6 = (f32[128,128]{0,1:T(8,128)S(1)}, f32[128,128]{0,1:T(8,128)S(1)}, u32[]{:S(2)}, u32[]{:S(2)}) collective-permute-start(f32[128,128]{0,1:T(8,128)S(1)} %convolution_bitcast_fusion.1), channel_id=1, source_target_pairs={{0,8},{8,0},{16,24},{24,16},{32,40},{40,32},{48,56},{56,48},{64,72... | collective-permute-start | bytes 196616 | tf_op jit(solution)/shard_map/ppermute | solution.py:65
  82.5 4.2 %collective-permute-start.7 = (f32[128,128]{0,1:T(8,128)S(1)}, f32[128,128]{0,1:T(8,128)S(1)}, u32[]{:S(2)}, u32[]{:S(2)}) collective-permute-start(f32[128,128]{0,1:T(8,128)S(1)} %add.63), channel_id=1, source_target_pairs={{0,16},{8,24},{16,0},{24,8},{32,48},{40,56},{48,32},{56,40},{64,80... | collective-permute-start | bytes 196616 | tf_op jit(solution)/shard_map/ppermute | solution.py:65
  86.7 4.7 %collective-permute-start.8 = (f32[128,128]{0,1:T(8,128)S(1)}, f32[128,128]{0,1:T(8,128)S(1)}, u32[]{:S(2)}, u32[]{:S(2)}) collective-permute-start(f32[128,128]{0,1:T(8,128)S(1)} %add.64), channel_id=1, source_target_pairs={{0,32},{8,40},{16,48},{24,56},{32,0},{40,8},{48,16},{56,24},{64,96... | collective-permute-start | bytes 196616 | tf_op jit(solution)/shard_map/ppermute | solution.py:65
  91.4 3.5 %collective-permute-start.9 = (f32[128,128]{0,1:T(8,128)S(1)}, f32[128,128]{0,1:T(8,128)S(1)}, u32[]{:S(2)}, u32[]{:S(2)}) collective-permute-start(f32[128,128]{0,1:T(8,128)S(1)} %add.65), channel_id=1, source_target_pairs={{0,64},{8,72},{16,80},{24,88},{32,96},{40,104},{48,112},{56,120},{... | collective-permute-start | bytes 196616 | tf_op jit(solution)/shard_map/ppermute | solution.py:65
  91.6 6.7 %collective-permute-start.12 = (f32[512,128]{1,0:T(8,128)S(1)}, f32[512,128]{1,0:T(8,128)S(1)}, u32[]{:S(2)}, u32[]{:S(2)}) collective-permute-start(f32[512,128]{1,0:T(8,128)S(1)} %fusion.28), channel_id=1, source_target_pairs={{0,64},{1,65},{8,72},{9,73},{16,80},{17,81},{24,88},{25,89},{32,96... | collective-permute-start | bytes 786440 | tf_op jit(solution)/shard_map/ppermute | solution.py:40
  95.0 5.3 %collective-permute-start.10 = (f32[128,128]{0,1:T(8,128)S(1)}, f32[128,128]{0,1:T(8,128)S(1)}, u32[]{:S(2)}, u32[]{:S(2)}) collective-permute-start(f32[128,128]{0,1:T(8,128)S(1)} %add.66), channel_id=1, source_target_pairs={{0,128},{8,136},{16,144},{24,152},{32,160},{40,168},{48,176},{56,1... | collective-permute-start | bytes 196616 | tf_op jit(solution)/shard_map/ppermute | solution.py:65
  98.3 7.0 %collective-permute-start.13 = (f32[512,128]{1,0:T(8,128)S(1)}, f32[512,128]{1,0:T(8,128)S(1)}, u32[]{:S(2)}, u32[]{:S(2)}) collective-permute-start(f32[512,128]{1,0:T(8,128)S(1)} %add.69), channel_id=1, source_target_pairs={{0,128},{1,129},{2,130},{3,131},{8,136},{9,137},{10,138},{11,139},... | collective-permute-start | bytes 786440 | tf_op jit(solution)/shard_map/ppermute | solution.py:40
  105.3 13.9 %copy-start.1 = (f32[512,2048]{1,0:T(8,128)S(1)}, f32[512,2048]{1,0:T(8,128)}, u32[]{:S(2)}) copy-start(f32[512,2048]{1,0:T(8,128)} %param.3) | copy-start | bytes 12582916
  105.4 12.3 %collective-permute-start.14 = (f32[512,128]{1,0:T(8,128)S(1)}, f32[512,128]{1,0:T(8,128)S(1)}, u32[]{:S(2)}, u32[]{:S(2)}) collective-permute-start(f32[512,128]{1,0:T(8,128)S(1)} %get-tuple-element.6), channel_id=1, source_target_pairs={{0,8},{8,0},{16,24},{24,16},{32,40},{40,32},{48,56},{56,48},{64,72... | collective-permute-start | bytes 786440 | tf_op jit(solution)/shard_map/ppermute | solution.py:45
  108.7 7.9 %collective-permute-start.15 = (f32[512,128]{1,0:T(8,128)S(1)}, f32[512,128]{1,0:T(8,128)S(1)}, u32[]{:S(2)}, u32[]{:S(2)}) collective-permute-start(f32[512,128]{1,0:T(8,128)S(1)} %get-tuple-element.6), channel_id=1, source_target_pairs={{0,16},{8,24},{16,0},{24,8},{32,48},{40,56},{48,32},{56,40},{64,80... | collective-permute-start | bytes 786440 | tf_op jit(solution)/shard_map/ppermute | solution.py:46
  116.5 2.0 %collective-permute-start.16 = (f32[512,128]{1,0:T(8,128)S(1)}, f32[512,128]{1,0:T(8,128)S(1)}, u32[]{:S(2)}, u32[]{:S(2)}) collective-permute-start(f32[512,128]{1,0:T(8,128)S(1)} %collective-permute-done.15), channel_id=1, source_target_pairs={{0,8},{8,0},{16,24},{24,16},{32,40},{40,32},{48,56},{56,48},{64,72... | collective-permute-start | bytes 786440 | tf_op jit(solution)/shard_map/ppermute | solution.py:47

commit v10 on v9

--- a/solution.py
+++ b/solution.py
@@ -18,7 +18,7 @@
     )
 
 
-def to_columns(panel_rows):
+def to_columns(panel_rows, held=None):
     rows_here = panel_rows.shape[0]
     row_count = lax.axis_size("row")
     col_count = lax.axis_size("col")
@@ -39,6 +39,7 @@
                         pairs.append((src, dst))
         mine = mine + lax.ppermute(mine, ("row", "col"), pairs)
         step *= 2
+    mine, held = lax.optimization_barrier((mine, held))
     gathered = jnp.zeros((per * rows_here,) + panel_rows.shape[1:], panel_rows.dtype)
     gathered = lax.dynamic_update_slice_in_dim(gathered, mine, low * rows_here, 0)
     core_pairs = [(i, i ^ 1) for i in range(row_count)]
@@ -47,7 +48,7 @@
     diagonal = lax.ppermute(across, "row", core_pairs)
     for mask, block in ((1, other), (2, across), (3, diagonal)):
         gathered = lax.dynamic_update_slice_in_dim(gathered, block, (low ^ mask) * rows_here, 0)
-    return gathered
+    return gathered, held
 
 
 def col_sum_rows(partial):
@@ -68,10 +69,10 @@
 
 
 def shards(matrix, vectors, tfactor):
-    vec_cols = to_columns(vectors)
+    vec_cols, _ = to_columns(vectors)
     x_rows = col_sum_rows(product(matrix, vec_cols))
-    s_full = butterfly_sum(inner_product(vectors, x_rows), "row")
-    x_cols = to_columns(x_rows)
+    x_cols, s_part = to_columns(x_rows, inner_product(vectors, x_rows))
+    s_full = butterfly_sum(s_part, "row")
     coupling = inner_product(tfactor, product(s_full, tfactor))
     w_rows = product(x_rows, tfactor) - 0.5 * product(vectors, coupling)
     w_cols = product(x_cols, tfactor) - 0.5 * product(vec_cols, coupling)

time: 125 us -> 132 us (1.056)
  the two profiles are of different devices: /device:TPU:1 before, /device:TPU:6 now
where the time goes in v10:
time: 132 us
  waiting for transfers between devices  74.2 us (56%)
  blocking collectives  32.7 us (25%)
  starting transfers between devices  12.9 us (10%)
  matrix products  11.2 us (8%)
    ppermute x6, waiting for transfers between devices, to_columns(): mine = mine + lax.ppermute(mine, ('row', 'col'), pairs)  47.6 us
    ppermute x5, waiting for transfers between devices, butterfly_sum(): lax.ppermute(value, axis, [(i, i ^ step) for i in range(count)])  19.5 us
    all_to_all x1, blocking collectives, col_sum_rows(): total = jnp.sum(lax.all_to_all(pieces, 'col', 0, 0, tiled=True), axis=0)  19.2 us
    all_to_all x1, blocking collectives, col_sum_rows(): lax.all_to_all(spread, 'col', 0, 0, tiled=True).reshape(partial.shape)  13.5 us
    dot_general x6, matrix products, product(): jnp.dot(left, right, precision=lax.Precision.HIGH, preferred_element_type...  6.45 us
    ppermute x2, waiting for transfers between devices, to_columns(): across = lax.ppermute(mine, 'row', [(i, i ^ 2) for i in range(row_count)])  5.69 us
    ppermute x6, starting transfers between devices, to_columns(): mine = mine + lax.ppermute(mine, ('row', 'col'), pairs)  5.29 us
    ppermute x5, starting transfers between devices, butterfly_sum(): lax.ppermute(value, axis, [(i, i ^ step) for i in range(count)])  5.21 us
  transfers between devices with their start and end apart: 17, of which 9 were waited for; matrix products, arithmetic and copies ran while one was open for 2% of the time, Pallas kernels for 0%

profile of v10, /device:TPU:6, one launch (start us, length us, event | category | flops | bytes accessed | tf_op | source)
XLA Modules:
  0.0 132.1 jit_solution(18396235401819314168)
XLA Ops:
  0.0 0.7 collective-permute-start
  0.8 0.7 collective-permute-start.1
  1.5 1.3 collective-permute-start.2
  2.8 23.6 %collective-permute-done.2 = f32[512,128]{1,0:T(8,128)S(1)} collective-permute-done((f32[512,128]{1,0:T(8,128)S(1)}, f32[512,128]{1,0:T(8,128)S(1)}, u32[]{:S(2)}, u32[]{:S(2)}) %collective-permute-start.2) | collective-permute-done | bytes 262176 | tf_op jit(solution)/shard_map/ppermute | solution.py:40
  26.5 0.8 collective-permute-start.4
  27.2 5.7 %collective-permute-done.4 = f32[512,128]{1,0:T(8,128)S(1)} collective-permute-done((f32[512,128]{1,0:T(8,128)S(1)}, f32[512,128]{1,0:T(8,128)S(1)}, u32[]{:S(2)}, u32[]{:S(2)}) %collective-permute-start.4) | collective-permute-done | bytes 262176 | tf_op jit(solution)/shard_map/ppermute | solution.py:47
  33.1 1.4 %collective-permute-done.5 = f32[512,128]{1,0:T(8,128)S(1)} collective-permute-done((f32[512,128]{1,0:T(8,128)S(1)}, f32[512,128]{1,0:T(8,128)S(1)}, u32[]{:S(2)}, u32[]{:S(2)}) %collective-permute-start.5) | collective-permute-done | bytes 262176 | tf_op jit(solution)/shard_map/ppermute | solution.py:48
  34.5 4.5 %convolution_bitcast_fusion = f32[512,128]{0,1:T(8,128)S(1)} fusion(f32[2048,128]{1,0:T(8,128)S(1)} %constant_dynamic-update-slice_fusion.4, f32[512,2048]{1,0:T(8,128)} %param.3), kind=kOutput, calls=%fused_computation.9 | convolution fusion | flops 805306368 | bytes 5505024 | tf_op jit(solution)/shard_map/dot_general | solution.py:8
  39.1 19.2 %all_to_all.11 = f32[8,64,128]{2,1,0:T(8,128)S(1)} all-to-all(f32[8,64,128]{2,1,0:T(8,128)S(1)} %bitcast.30), channel_id=1, replica_groups=mesh['row'=32,'col'=8] {'col'}, dimensions={0} | all-to-all | bytes 524288 | tf_op jit(solution)/shard_map/all_to_all | solution.py:57
  58.4 13.5 %all_to_all.10 = f32[8,64,128]{2,1,0:T(8,128)S(1)} all-to-all(f32[8,64,128]{2,1,0:T(8,128)S(1)} %broadcast_in_dim.2), channel_id=1, replica_groups=mesh['row'=32,'col'=8] {'col'}, dimensions={0} | all-to-all | bytes 524288 | tf_op jit(solution)/shard_map/all_to_all | solution.py:59
  71.9 0.7 collective-permute-start.6
  72.7 0.7 collective-permute-start.7
  73.4 1.3 collective-permute-start.8
  75.1 24.0 %collective-permute-done.8 = f32[512,128]{1,0:T(8,128)S(1)} collective-permute-done((f32[512,128]{1,0:T(8,128)S(1)}, f32[512,128]{1,0:T(8,128)S(1)}, u32[]{:S(2)}, u32[]{:S(2)}) %collective-permute-start.8) | collective-permute-done | bytes 262176 | tf_op jit(solution)/shard_map/ppermute | solution.py:40
  99.2 1.2 collective-permute-done.9
  100.5 0.8 collective-permute-start.10
  101.2 1.3 %collective-permute-start.15 = (f32[512,128]{1,0:T(8,128)S(1)}, f32[512,128]{1,0:T(8,128)S(1)}, u32[]{:S(2)}, u32[]{:S(2)}) collective-permute-start(f32[512,128]{1,0:T(8,128)S(1)} %add.65), channel_id=1, source_target_pairs={{0,16},{8,24},{16,0},{24,8},{32,48},{40,56},{48,32},{56,40},{64,80... | collective-permute-start | bytes 786440 | tf_op jit(solution)/shard_map/ppermute | solution.py:47
  102.6 2.9 %collective-permute-done.10 = f32[128,128]{0,1:T(8,128)S(1)} collective-permute-done((f32[128,128]{0,1:T(8,128)S(1)}, f32[128,128]{0,1:T(8,128)S(1)}, u32[]{:S(2)}, u32[]{:S(2)}) %collective-permute-start.10) | collective-permute-done | bytes 65568 | tf_op jit(solution)/shard_map/ppermute | solution.py:66
  105.5 4.2 %collective-permute-start.11 = (f32[128,128]{0,1:T(8,128)S(1)}, f32[128,128]{0,1:T(8,128)S(1)}, u32[]{:S(2)}, u32[]{:S(2)}) collective-permute-start(f32[128,128]{0,1:T(8,128)S(1)} %add.67), channel_id=1, source_target_pairs={{0,32},{8,40},{16,48},{24,56},{32,0},{40,8},{48,16},{56,24},{64,96... | collective-permute-start | bytes 196616 | tf_op jit(solution)/shard_map/ppermute | solution.py:66
  109.9 5.3 %collective-permute-done.11 = f32[128,128]{0,1:T(8,128)S(1)} collective-permute-done((f32[128,128]{0,1:T(8,128)S(1)}, f32[128,128]{0,1:T(8,128)S(1)}, u32[]{:S(2)}, u32[]{:S(2)}) %collective-permute-start.11) | collective-permute-done | bytes 65568 | tf_op jit(solution)/shard_map/ppermute | solution.py:66
  115.5 4.7 %collective-permute-done.12 = f32[128,128]{0,1:T(8,128)S(1)} collective-permute-done((f32[128,128]{0,1:T(8,128)S(1)}, f32[128,128]{0,1:T(8,128)S(1)}, u32[]{:S(2)}, u32[]{:S(2)}) %collective-permute-start.12) | collective-permute-done | bytes 65568 | tf_op jit(solution)/shard_map/ppermute | solution.py:66
  120.6 5.4 %collective-permute-done.13 = f32[128,128]{0,1:T(8,128)S(1)} collective-permute-done((f32[128,128]{0,1:T(8,128)S(1)}, f32[128,128]{0,1:T(8,128)S(1)}, u32[]{:S(2)}, u32[]{:S(2)}) %collective-permute-start.13) | collective-permute-done | bytes 65568 | tf_op jit(solution)/shard_map/ppermute | solution.py:66
  126.5 0.6 convolution_multiply_fusion
  128.0 4.1 %convolution_subtract_fusion = f32[512,2048]{1,0:T(8,128)} fusion(f32[512,2048]{1,0:T(8,128)S(1)} %copy-done.1, f32[2048,128]{1,0:T(8,128)S(1)} %constant_dynamic-update-slice_fusion.4, f32[2048,128]{1,0:T(8,128)S(1)} %convolution_subtract_fusion.1, f32[512,128]{1,0:T(8,128)S(1)} %fusion.4, f32[512,128]{1,0:T(8,128)S(1)} %copy-done.2), kind=kOutput, calls=%fused_computation | convolution fusion | flops 1612316672 | bytes 11010048 | tf_op jit(solution)/shard_map/dot_general | solution.py:81
  (52 shorter events, 3.4 us)
Async XLA Ops:
  0.0 109.7 %copy-start = (f32[128,128]{1,0:T(8,128)S(1)}, f32[128,128]{1,0:T(8,128)}, u32[]{:S(2)}) copy-start(f32[128,128]{1,0:T(8,128)} %param.5) | copy-start | bytes 196612
  0.0 0.7 collective-permute-start
  0.8 0.7 collective-permute-start.1
  1.5 24.9 %collective-permute-start.2 = (f32[512,128]{1,0:T(8,128)S(1)}, f32[512,128]{1,0:T(8,128)S(1)}, u32[]{:S(2)}, u32[]{:S(2)}) collective-permute-start(f32[512,128]{1,0:T(8,128)S(1)} %add.56), channel_id=1, source_target_pairs={{0,128},{1,129},{2,130},{3,131},{8,136},{9,137},{10,138},{11,139},... | collective-permute-start | bytes 786440 | tf_op jit(solution)/shard_map/ppermute | solution.py:40
  26.5 6.5 %collective-permute-start.4 = (f32[512,128]{1,0:T(8,128)S(1)}, f32[512,128]{1,0:T(8,128)S(1)}, u32[]{:S(2)}, u32[]{:S(2)}) collective-permute-start(f32[512,128]{1,0:T(8,128)S(1)} %add.57), channel_id=1, source_target_pairs={{0,16},{8,24},{16,0},{24,8},{32,48},{40,56},{48,32},{56,40},{64,80... | collective-permute-start | bytes 786440 | tf_op jit(solution)/shard_map/ppermute | solution.py:47
  27.2 5.8 %collective-permute-start.3 = (f32[512,128]{1,0:T(8,128)S(1)}, f32[512,128]{1,0:T(8,128)S(1)}, u32[]{:S(2)}, u32[]{:S(2)}) collective-permute-start(f32[512,128]{1,0:T(8,128)S(1)} %add.57), channel_id=1, source_target_pairs={{0,8},{8,0},{16,24},{24,16},{32,40},{40,32},{48,56},{56,48},{64,72... | collective-permute-start | bytes 786440 | tf_op jit(solution)/shard_map/ppermute | solution.py:46
  32.9 1.5 %collective-permute-start.5 = (f32[512,128]{1,0:T(8,128)S(1)}, f32[512,128]{1,0:T(8,128)S(1)}, u32[]{:S(2)}, u32[]{:S(2)}) collective-permute-start(f32[512,128]{1,0:T(8,128)S(1)} %collective-permute-done.4), channel_id=1, source_target_pairs={{0,8},{8,0},{16,24},{24,16},{32,40},{40,32},{48,56},{56,48},{64,72... | collective-permute-start | bytes 786440 | tf_op jit(solution)/shard_map/ppermute | solution.py:48
  34.5 40.2 %copy-start.2 = (f32[512,128]{1,0:T(8,128)S(1)}, f32[512,128]{1,0:T(8,128)}, u32[]{:S(2)}) copy-start(f32[512,128]{1,0:T(8,128)} %param.4) | copy-start | bytes 786436
  71.9 0.7 collective-permute-start.6
  72.7 0.7 collective-permute-start.7
  73.4 25.7 %collective-permute-start.8 = (f32[512,128]{1,0:T(8,128)S(1)}, f32[512,128]{1,0:T(8,128)S(1)}, u32[]{:S(2)}, u32[]{:S(2)}) collective-permute-start(f32[512,128]{1,0:T(8,128)S(1)} %add.64), channel_id=1, source_target_pairs={{0,128},{1,129},{2,130},{3,131},{8,136},{9,137},{10,138},{11,139},... | collective-permute-start | bytes 786440 | tf_op jit(solution)/shard_map/ppermute | solution.py:40
  99.1 1.3 %collective-permute-start.9 = (f32[128,128]{0,1:T(8,128)S(1)}, f32[128,128]{0,1:T(8,128)S(1)}, u32[]{:S(2)}, u32[]{:S(2)}) collective-permute-start(f32[128,128]{0,1:T(8,128)S(1)} %convolution_bitcast_fusion.1), channel_id=1, source_target_pairs={{0,8},{8,0},{16,24},{24,16},{32,40},{40,32},{48,56},{56,48},{64,72... | collective-permute-start | bytes 196616 | tf_op jit(solution)/shard_map/ppermute | solution.py:66
  100.5 5.0 %collective-permute-start.10 = (f32[128,128]{0,1:T(8,128)S(1)}, f32[128,128]{0,1:T(8,128)S(1)}, u32[]{:S(2)}, u32[]{:S(2)}) collective-permute-start(f32[128,128]{0,1:T(8,128)S(1)} %add.66), channel_id=1, source_target_pairs={{0,16},{8,24},{16,0},{24,8},{32,48},{40,56},{48,32},{56,40},{64,80... | collective-permute-start | bytes 196616 | tf_op jit(solution)/shard_map/ppermute | solution.py:66
  101.2 19.0 %collective-permute-start.15 = (f32[512,128]{1,0:T(8,128)S(1)}, f32[512,128]{1,0:T(8,128)S(1)}, u32[]{:S(2)}, u32[]{:S(2)}) collective-permute-start(f32[512,128]{1,0:T(8,128)S(1)} %add.65), channel_id=1, source_target_pairs={{0,16},{8,24},{16,0},{24,8},{32,48},{40,56},{48,32},{56,40},{64,80... | collective-permute-start | bytes 786440 | tf_op jit(solution)/shard_map/ppermute | solution.py:47
  102.6 18.0 %collective-permute-start.14 = (f32[512,128]{1,0:T(8,128)S(1)}, f32[512,128]{1,0:T(8,128)S(1)}, u32[]{:S(2)}, u32[]{:S(2)}) collective-permute-start(f32[512,128]{1,0:T(8,128)S(1)} %add.65), channel_id=1, source_target_pairs={{0,8},{8,0},{16,24},{24,16},{32,40},{40,32},{48,56},{56,48},{64,72... | collective-permute-start | bytes 786440 | tf_op jit(solution)/shard_map/ppermute | solution.py:46
  105.5 9.7 %collective-permute-start.11 = (f32[128,128]{0,1:T(8,128)S(1)}, f32[128,128]{0,1:T(8,128)S(1)}, u32[]{:S(2)}, u32[]{:S(2)}) collective-permute-start(f32[128,128]{0,1:T(8,128)S(1)} %add.67), channel_id=1, source_target_pairs={{0,32},{8,40},{16,48},{24,56},{32,0},{40,8},{48,16},{56,24},{64,96... | collective-permute-start | bytes 196616 | tf_op jit(solution)/shard_map/ppermute | solution.py:66
  115.2 4.9 %collective-permute-start.12 = (f32[128,128]{0,1:T(8,128)S(1)}, f32[128,128]{0,1:T(8,128)S(1)}, u32[]{:S(2)}, u32[]{:S(2)}) collective-permute-start(f32[128,128]{0,1:T(8,128)S(1)} %add.68), channel_id=1, source_target_pairs={{0,64},{8,72},{16,80},{24,88},{32,96},{40,104},{48,112},{56,120},{... | collective-permute-start | bytes 196616 | tf_op jit(solution)/shard_map/ppermute | solution.py:66
  115.5 12.6 %copy-start.1 = (f32[512,2048]{1,0:T(8,128)S(1)}, f32[512,2048]{1,0:T(8,128)}, u32[]{:S(2)}) copy-start(f32[512,2048]{1,0:T(8,128)} %param.3) | copy-start | bytes 12582916
  120.1 5.9 %collective-permute-start.13 = (f32[128,128]{0,1:T(8,128)S(1)}, f32[128,128]{0,1:T(8,128)S(1)}, u32[]{:S(2)}, u32[]{:S(2)}) collective-permute-start(f32[128,128]{0,1:T(8,128)S(1)} %add.69), channel_id=1, source_target_pairs={{0,128},{8,136},{16,144},{24,152},{32,160},{40,168},{48,176},{56,1... | collective-permute-start | bytes 196616 | tf_op jit(solution)/shard_map/ppermute | solution.py:66
  120.3 7.1 %collective-permute-start.16 = (f32[512,128]{1,0:T(8,128)S(1)}, f32[512,128]{1,0:T(8,128)S(1)}, u32[]{:S(2)}, u32[]{:S(2)}) collective-permute-start(f32[512,128]{1,0:T(8,128)S(1)} %collective-permute-done.15), channel_id=1, source_target_pairs={{0,8},{8,0},{16,24},{24,16},{32,40},{40,32},{48,56},{56,48},{64,72... | collective-permute-start | bytes 786440 | tf_op jit(solution)/shard_map/ppermute | solution.py:48

commit v11 on v10

--- a/solution.py
+++ b/solution.py
@@ -18,7 +18,7 @@
     )
 
 
-def to_columns(panel_rows, held=None):
+def to_columns(panel_rows, extra=None):
     rows_here = panel_rows.shape[0]
     row_count = lax.axis_size("row")
     col_count = lax.axis_size("col")
@@ -33,22 +33,30 @@
         for src_high in range(col_count):
             for src_low in range(per):
                 for src_col in range(col_count):
-                    if (src_high ^ src_col) < step:
+                    if extra is not None or (src_high ^ src_col) < step:
                         src = (per * src_high + src_low) * col_count + src_col
                         dst = (per * (src_high ^ step) + src_low) * col_count + src_col
                         pairs.append((src, dst))
-        mine = mine + lax.ppermute(mine, ("row", "col"), pairs)
+        if extra is None:
+            mine = mine + lax.ppermute(mine, ("row", "col"), pairs)
+        else:
+            got = lax.ppermute(jnp.concatenate([mine, extra], axis=0), ("row", "col"), pairs)
+            mine = mine + got[:rows_here]
+            extra = extra + got[rows_here:]
         step *= 2
-    mine, held = lax.optimization_barrier((mine, held))
     gathered = jnp.zeros((per * rows_here,) + panel_rows.shape[1:], panel_rows.dtype)
     gathered = lax.dynamic_update_slice_in_dim(gathered, mine, low * rows_here, 0)
     core_pairs = [(i, i ^ 1) for i in range(row_count)]
-    other = lax.ppermute(mine, "row", core_pairs)
-    across = lax.ppermute(mine, "row", [(i, i ^ 2) for i in range(row_count)])
+    sent = mine if extra is None else jnp.concatenate([mine, extra], axis=0)
+    other = lax.ppermute(sent, "row", core_pairs)
+    across = lax.ppermute(sent, "row", [(i, i ^ 2) for i in range(row_count)])
     diagonal = lax.ppermute(across, "row", core_pairs)
     for mask, block in ((1, other), (2, across), (3, diagonal)):
-        gathered = lax.dynamic_update_slice_in_dim(gathered, block, (low ^ mask) * rows_here, 0)
-    return gathered, held
+        gathered = lax.dynamic_update_slice_in_dim(gathered, block[:rows_here], (low ^ mask) * rows_here, 0)
+    if extra is None:
+        return gathered, None
+    total = extra + other[rows_here:] + across[rows_here:] + diagonal[rows_here:]
+    return gathered, total
 
 
 def col_sum_rows(partial):
@@ -59,20 +67,10 @@
     return lax.all_to_all(spread, "col", 0, 0, tiled=True).reshape(partial.shape)
 
 
-def butterfly_sum(value, axis):
-    count = lax.axis_size(axis)
-    step = 1
-    while step < count:
-        value = value + lax.ppermute(value, axis, [(i, i ^ step) for i in range(count)])
-        step *= 2
-    return value
-
-
 def shards(matrix, vectors, tfactor):
     vec_cols, _ = to_columns(vectors)
     x_rows = col_sum_rows(product(matrix, vec_cols))
-    x_cols, s_part = to_columns(x_rows, inner_product(vectors, x_rows))
-    s_full = butterfly_sum(s_part, "row")
+    x_cols, s_full = to_columns(x_rows, inner_product(vectors, x_rows))
     coupling = inner_product(tfactor, product(s_full, tfactor))
     w_rows = product(x_rows, tfactor) - 0.5 * product(vectors, coupling)
     w_cols = product(x_cols, tfactor) - 0.5 * product(vec_cols, coupling)

time: 132 us -> 119 us (0.902)
  the two profiles are of different devices: /device:TPU:6 before, /device:TPU:1 now
where the time goes in v11:
time: 119 us
  blocking collectives  35.8 us (30%)
  waiting for transfers between devices  34.6 us (29%)
  starting transfers between devices  34.5 us (29%)
  matrix products  11.1 us (9%)
  other arithmetic  2.33 us (2%)
    all_to_all x1, blocking collectives, col_sum_rows(): total = jnp.sum(lax.all_to_all(pieces, 'col', 0, 0, tiled=True), axis=0)  23.7 us
    ppermute x3, waiting for transfers between devices, to_columns(): lax.ppermute(jnp.concatenate([mine, extra], axis=0), ('row', 'col'), pairs)  17.7 us
    ppermute x2, starting transfers between devices, to_columns(): other = lax.ppermute(sent, 'row', core_pairs)  13 us
    ppermute x3, waiting for transfers between devices, to_columns(): mine = mine + lax.ppermute(mine, ('row', 'col'), pairs)  12.9 us
    all_to_all x1, blocking collectives, col_sum_rows(): lax.all_to_all(spread, 'col', 0, 0, tiled=True).reshape(partial.shape)  12.1 us
    ppermute x2, starting transfers between devices, to_columns(): diagonal = lax.ppermute(across, 'row', core_pairs)  10 us
    ppermute x3, starting transfers between devices, to_columns(): mine = mine + lax.ppermute(mine, ('row', 'col'), pairs)  7.3 us
    dot_general x6, matrix products, product(): jnp.dot(left, right, precision=lax.Precision.HIGH, preferred_element_type...  6.33 us
  transfers between devices with their start and end apart: 12, of which 9 were waited for; matrix products, arithmetic and copies ran while one was open for 0% of the time, Pallas kernels for 0%

profile of v11, /device:TPU:1, one launch (start us, length us, event | category | flops | bytes accessed | tf_op | source)
XLA Modules:
  0.0 119.0 jit_solution(13005823209630723464)
XLA Ops:
  0.0 1.0 broadcast_select_fusion.1
  1.0 4.7 %collective-permute-start = (f32[512,128]{1,0:T(8,128)S(1)}, f32[512,128]{1,0:T(8,128)S(1)}, u32[]{:S(2)}, u32[]{:S(2)}) collective-permute-start(f32[512,128]{1,0:T(8,128)S(1)} %broadcast_select_fusion.1), channel_id=1, source_target_pairs={{0,32},{8,40},{16,48},{24,56},{33,1},{41,9},{49,17},{57,25},{66,98... | collective-permute-start | bytes 786440 | tf_op jit(solution)/shard_map/ppermute | solution.py:41
  5.7 4.9 %collective-permute-done = f32[512,128]{1,0:T(8,128)S(1)} collective-permute-done((f32[512,128]{1,0:T(8,128)S(1)}, f32[512,128]{1,0:T(8,128)S(1)}, u32[]{:S(2)}, u32[]{:S(2)}) %collective-permute-start) | collective-permute-done | bytes 262176 | tf_op jit(solution)/shard_map/ppermute | solution.py:41
  10.6 1.0 fusion.27
  11.6 1.3 %collective-permute-start.1 = (f32[512,128]{1,0:T(8,128)S(1)}, f32[512,128]{1,0:T(8,128)S(1)}, u32[]{:S(2)}, u32[]{:S(2)}) collective-permute-start(f32[512,128]{1,0:T(8,128)S(1)} %fusion.27), channel_id=1, source_target_pairs={{0,64},{1,65},{8,72},{9,73},{16,80},{17,81},{24,88},{25,89},{32,96... | collective-permute-start | bytes 786440 | tf_op jit(solution)/shard_map/ppermute | solution.py:41
  12.9 4.3 %collective-permute-done.1 = f32[512,128]{1,0:T(8,128)S(1)} collective-permute-done((f32[512,128]{1,0:T(8,128)S(1)}, f32[512,128]{1,0:T(8,128)S(1)}, u32[]{:S(2)}, u32[]{:S(2)}) %collective-permute-start.1) | collective-permute-done | bytes 262176 | tf_op jit(solution)/shard_map/ppermute | solution.py:41
  17.3 1.3 %collective-permute-start.2 = (f32[512,128]{1,0:T(8,128)S(1)}, f32[512,128]{1,0:T(8,128)S(1)}, u32[]{:S(2)}, u32[]{:S(2)}) collective-permute-start(f32[512,128]{1,0:T(8,128)S(1)} %add.59), channel_id=1, source_target_pairs={{0,128},{1,129},{2,130},{3,131},{8,136},{9,137},{10,138},{11,139},... | collective-permute-start | bytes 786440 | tf_op jit(solution)/shard_map/ppermute | solution.py:41
  18.6 3.6 %collective-permute-done.2 = f32[512,128]{1,0:T(8,128)S(1)} collective-permute-done((f32[512,128]{1,0:T(8,128)S(1)}, f32[512,128]{1,0:T(8,128)S(1)}, u32[]{:S(2)}, u32[]{:S(2)}) %collective-permute-start.2) | collective-permute-done | bytes 262176 | tf_op jit(solution)/shard_map/ppermute | solution.py:41
  22.9 3.1 %collective-permute-start.3 = (f32[512,128]{1,0:T(8,128)S(1)}, f32[512,128]{1,0:T(8,128)S(1)}, u32[]{:S(2)}, u32[]{:S(2)}) collective-permute-start(f32[512,128]{1,0:T(8,128)S(1)} %get-tuple-element.8), channel_id=1, source_target_pairs={{0,8},{8,0},{16,24},{24,16},{32,40},{40,32},{48,56},{56,48},{64,72... | collective-permute-start | bytes 786440 | tf_op jit(solution)/shard_map/ppermute | solution.py:51
  26.0 1.7 %collective-permute-done.4 = f32[512,128]{1,0:T(8,128)S(1)} collective-permute-done((f32[512,128]{1,0:T(8,128)S(1)}, f32[512,128]{1,0:T(8,128)S(1)}, u32[]{:S(2)}, u32[]{:S(2)}) %collective-permute-start.4) | collective-permute-done | bytes 262176 | tf_op jit(solution)/shard_map/ppermute | solution.py:52
  27.7 4.0 %collective-permute-start.5 = (f32[512,128]{1,0:T(8,128)S(1)}, f32[512,128]{1,0:T(8,128)S(1)}, u32[]{:S(2)}, u32[]{:S(2)}) collective-permute-start(f32[512,128]{1,0:T(8,128)S(1)} %collective-permute-done.4), channel_id=1, source_target_pairs={{0,8},{8,0},{16,24},{24,16},{32,40},{40,32},{48,56},{56,48},{64,72... | collective-permute-start | bytes 786440 | tf_op jit(solution)/shard_map/ppermute | solution.py:53
  31.7 1.1 collective-permute-done.5
  32.8 4.5 %convolution_bitcast_fusion = f32[512,128]{0,1:T(8,128)S(1)} fusion(f32[2048,128]{1,0:T(8,128)S(1)} %constant_dynamic-update-slice_fusion.1, f32[512,2048]{1,0:T(8,128)} %param.3), kind=kOutput, calls=%fused_computation.9 | convolution fusion | flops 805306368 | bytes 5505024 | tf_op jit(solution)/shard_map/dot_general | solution.py:8
  37.4 23.7 %all_to_all.11 = f32[8,64,128]{2,1,0:T(8,128)S(1)} all-to-all(f32[8,64,128]{2,1,0:T(8,128)S(1)} %bitcast.30), channel_id=1, replica_groups=mesh['row'=32,'col'=8] {'col'}, dimensions={0} | all-to-all | bytes 524288 | tf_op jit(solution)/shard_map/all_to_all | solution.py:65
  61.2 12.1 %all_to_all.10 = f32[8,64,128]{2,1,0:T(8,128)S(1)} all-to-all(f32[8,64,128]{2,1,0:T(8,128)S(1)} %broadcast_in_dim.2), channel_id=1, replica_groups=mesh['row'=32,'col'=8] {'col'}, dimensions={0} | all-to-all | bytes 524288 | tf_op jit(solution)/shard_map/all_to_all | solution.py:67
  73.7 2.3 %collective-permute-start.6 = (f32[640,128]{1,0:T(8,128)S(1)}, f32[640,128]{1,0:T(8,128)S(1)}, u32[]{:S(2)}, u32[]{:S(2)}) collective-permute-start(f32[640,128]{1,0:T(8,128)S(1)} %pad_maximum_fusion), channel_id=1, source_target_pairs={{0,32},{1,33},{2,34},{3,35},{4,36},{5,37},{6,38},{7,39},{8,40},{9,... | collective-permute-start | bytes 983048 | tf_op jit(solution)/shard_map/ppermute | solution.py:43
  76.0 5.2 %collective-permute-done.6 = f32[640,128]{1,0:T(8,128)S(1)} collective-permute-done((f32[640,128]{1,0:T(8,128)S(1)}, f32[640,128]{1,0:T(8,128)S(1)}, u32[]{:S(2)}, u32[]{:S(2)}) %collective-permute-start.6) | collective-permute-done | bytes 327712 | tf_op jit(solution)/shard_map/ppermute | solution.py:43
  81.3 0.9 collective-permute-start.7
  82.2 5.1 %collective-permute-done.7 = f32[640,128]{1,0:T(8,128)S(1)} collective-permute-done((f32[640,128]{1,0:T(8,128)S(1)}, f32[640,128]{1,0:T(8,128)S(1)}, u32[]{:S(2)}, u32[]{:S(2)}) %collective-permute-start.7) | collective-permute-done | bytes 327712 | tf_op jit(solution)/shard_map/ppermute | solution.py:43
  87.5 7.4 %collective-permute-done.8 = f32[640,128]{1,0:T(8,128)S(1)} collective-permute-done((f32[640,128]{1,0:T(8,128)S(1)}, f32[640,128]{1,0:T(8,128)S(1)}, u32[]{:S(2)}, u32[]{:S(2)}) %collective-permute-start.8) | collective-permute-done | bytes 327712 | tf_op jit(solution)/shard_map/ppermute | solution.py:43
  95.5 9.9 %collective-permute-start.9 = (f32[640,128]{1,0:T(8,128)S(1)}, f32[640,128]{1,0:T(8,128)S(1)}, u32[]{:S(2)}, u32[]{:S(2)}) collective-permute-start(f32[640,128]{1,0:T(8,128)S(1)} %pad_maximum_fusion.3), channel_id=1, source_target_pairs={{0,8},{8,0},{16,24},{24,16},{32,40},{40,32},{48,56},{56,48},{64,72... | collective-permute-start | bytes 983048 | tf_op jit(solution)/shard_map/ppermute | solution.py:51
  105.6 6.1 %collective-permute-start.11 = (f32[640,128]{1,0:T(8,128)S(1)}, f32[640,128]{1,0:T(8,128)S(1)}, u32[]{:S(2)}, u32[]{:S(2)}) collective-permute-start(f32[640,128]{1,0:T(8,128)S(1)} %collective-permute-done.10), channel_id=1, source_target_pairs={{0,8},{8,0},{16,24},{24,16},{32,40},{40,32},{48,56},{56,48},{64,72... | collective-permute-start | bytes 983048 | tf_op jit(solution)/shard_map/ppermute | solution.py:53
  111.8 1.2 %collective-permute-done.11 = f32[640,128]{1,0:T(8,128)S(1)} collective-permute-done((f32[640,128]{1,0:T(8,128)S(1)}, f32[640,128]{1,0:T(8,128)S(1)}, u32[]{:S(2)}, u32[]{:S(2)}) %collective-permute-start.11) | collective-permute-done | bytes 327712 | tf_op jit(solution)/shard_map/ppermute | solution.py:53
  114.9 4.1 %convolution_subtract_fusion = f32[512,2048]{1,0:T(8,128)} fusion(f32[512,2048]{1,0:T(8,128)S(1)} %copy-done.1, f32[2048,128]{1,0:T(8,128)S(1)} %constant_dynamic-update-slice_fusion.1, f32[2048,128]{1,0:T(8,128)S(1)} %convolution_subtract_fusion.1, f32[512,128]{1,0:T(8,128)S(1)} %fusion.4, f32[512,128]{1,0:T(8,128)S(1)} %copy-done.2), kind=kOutput, calls=%fused_computation | convolution fusion | flops 1612316672 | bytes 11010048 | tf_op jit(solution)/shard_map/dot_general | solution.py:79
  (43 shorter events, 4.3 us)
Async XLA Ops:
  0.0 105.4 %copy-start = (f32[128,128]{1,0:T(8,128)S(1)}, f32[128,128]{1,0:T(8,128)}, u32[]{:S(2)}) copy-start(f32[128,128]{1,0:T(8,128)} %param.5) | copy-start | bytes 196612
  1.0 9.6 %collective-permute-start = (f32[512,128]{1,0:T(8,128)S(1)}, f32[512,128]{1,0:T(8,128)S(1)}, u32[]{:S(2)}, u32[]{:S(2)}) collective-permute-start(f32[512,128]{1,0:T(8,128)S(1)} %broadcast_select_fusion.1), channel_id=1, source_target_pairs={{0,32},{8,40},{16,48},{24,56},{33,1},{41,9},{49,17},{57,25},{66,98... | collective-permute-start | bytes 786440 | tf_op jit(solution)/shard_map/ppermute | solution.py:41
  11.6 5.6 %collective-permute-start.1 = (f32[512,128]{1,0:T(8,128)S(1)}, f32[512,128]{1,0:T(8,128)S(1)}, u32[]{:S(2)}, u32[]{:S(2)}) collective-permute-start(f32[512,128]{1,0:T(8,128)S(1)} %fusion.27), channel_id=1, source_target_pairs={{0,64},{1,65},{8,72},{9,73},{16,80},{17,81},{24,88},{25,89},{32,96... | collective-permute-start | bytes 786440 | tf_op jit(solution)/shard_map/ppermute | solution.py:41
  17.3 5.0 %collective-permute-start.2 = (f32[512,128]{1,0:T(8,128)S(1)}, f32[512,128]{1,0:T(8,128)S(1)}, u32[]{:S(2)}, u32[]{:S(2)}) collective-permute-start(f32[512,128]{1,0:T(8,128)S(1)} %add.59), channel_id=1, source_target_pairs={{0,128},{1,129},{2,130},{3,131},{8,136},{9,137},{10,138},{11,139},... | collective-permute-start | bytes 786440 | tf_op jit(solution)/shard_map/ppermute | solution.py:41
  22.4 5.3 %collective-permute-start.4 = (f32[512,128]{1,0:T(8,128)S(1)}, f32[512,128]{1,0:T(8,128)S(1)}, u32[]{:S(2)}, u32[]{:S(2)}) collective-permute-start(f32[512,128]{1,0:T(8,128)S(1)} %get-tuple-element.8), channel_id=1, source_target_pairs={{0,16},{8,24},{16,0},{24,8},{32,48},{40,56},{48,32},{56,40},{64,80... | collective-permute-start | bytes 786440 | tf_op jit(solution)/shard_map/ppermute | solution.py:52
  22.9 8.8 %collective-permute-start.3 = (f32[512,128]{1,0:T(8,128)S(1)}, f32[512,128]{1,0:T(8,128)S(1)}, u32[]{:S(2)}, u32[]{:S(2)}) collective-permute-start(f32[512,128]{1,0:T(8,128)S(1)} %get-tuple-element.8), channel_id=1, source_target_pairs={{0,8},{8,0},{16,24},{24,16},{32,40},{40,32},{48,56},{56,48},{64,72... | collective-permute-start | bytes 786440 | tf_op jit(solution)/shard_map/ppermute | solution.py:51
  27.7 5.1 %collective-permute-start.5 = (f32[512,128]{1,0:T(8,128)S(1)}, f32[512,128]{1,0:T(8,128)S(1)}, u32[]{:S(2)}, u32[]{:S(2)}) collective-permute-start(f32[512,128]{1,0:T(8,128)S(1)} %collective-permute-done.4), channel_id=1, source_target_pairs={{0,8},{8,0},{16,24},{24,16},{32,40},{40,32},{48,56},{56,48},{64,72... | collective-permute-start | bytes 786440 | tf_op jit(solution)/shard_map/ppermute | solution.py:53
  31.7 41.5 %copy-start.2 = (f32[512,128]{1,0:T(8,128)S(1)}, f32[512,128]{1,0:T(8,128)}, u32[]{:S(2)}) copy-start(f32[512,128]{1,0:T(8,128)} %param.4) | copy-start | bytes 786436
  73.7 7.5 %collective-permute-start.6 = (f32[640,128]{1,0:T(8,128)S(1)}, f32[640,128]{1,0:T(8,128)S(1)}, u32[]{:S(2)}, u32[]{:S(2)}) collective-permute-start(f32[640,128]{1,0:T(8,128)S(1)} %pad_maximum_fusion), channel_id=1, source_target_pairs={{0,32},{1,33},{2,34},{3,35},{4,36},{5,37},{6,38},{7,39},{8,40},{9,... | collective-permute-start | bytes 983048 | tf_op jit(solution)/shard_map/ppermute | solution.py:43
  81.3 6.0 %collective-permute-start.7 = (f32[640,128]{1,0:T(8,128)S(1)}, f32[640,128]{1,0:T(8,128)S(1)}, u32[]{:S(2)}, u32[]{:S(2)}) collective-permute-start(f32[640,128]{1,0:T(8,128)S(1)} %pad_maximum_fusion.1), channel_id=1, source_target_pairs={{0,64},{1,65},{2,66},{3,67},{4,68},{5,69},{6,70},{7,71},{8,72},{9,... | collective-permute-start | bytes 983048 | tf_op jit(solution)/shard_map/ppermute | solution.py:43
  87.4 7.5 %collective-permute-start.8 = (f32[640,128]{1,0:T(8,128)S(1)}, f32[640,128]{1,0:T(8,128)S(1)}, u32[]{:S(2)}, u32[]{:S(2)}) collective-permute-start(f32[640,128]{1,0:T(8,128)S(1)} %pad_maximum_fusion.2), channel_id=1, source_target_pairs={{0,128},{1,129},{2,130},{3,131},{4,132},{5,133},{6,134},{7,135},{8... | collective-permute-start | bytes 983048 | tf_op jit(solution)/shard_map/ppermute | solution.py:43
  95.1 10.6 %collective-permute-start.10 = (f32[640,128]{1,0:T(8,128)S(1)}, f32[640,128]{1,0:T(8,128)S(1)}, u32[]{:S(2)}, u32[]{:S(2)}) collective-permute-start(f32[640,128]{1,0:T(8,128)S(1)} %pad_maximum_fusion.3), channel_id=1, source_target_pairs={{0,16},{8,24},{16,0},{24,8},{32,48},{40,56},{48,32},{56,40},{64,80... | collective-permute-start | bytes 983048 | tf_op jit(solution)/shard_map/ppermute | solution.py:52
  95.5 16.2 %collective-permute-start.9 = (f32[640,128]{1,0:T(8,128)S(1)}, f32[640,128]{1,0:T(8,128)S(1)}, u32[]{:S(2)}, u32[]{:S(2)}) collective-permute-start(f32[640,128]{1,0:T(8,128)S(1)} %pad_maximum_fusion.3), channel_id=1, source_target_pairs={{0,8},{8,0},{16,24},{24,16},{32,40},{40,32},{48,56},{56,48},{64,72... | collective-permute-start | bytes 983048 | tf_op jit(solution)/shard_map/ppermute | solution.py:51
  105.6 7.3 %collective-permute-start.11 = (f32[640,128]{1,0:T(8,128)S(1)}, f32[640,128]{1,0:T(8,128)S(1)}, u32[]{:S(2)}, u32[]{:S(2)}) collective-permute-start(f32[640,128]{1,0:T(8,128)S(1)} %collective-permute-done.10), channel_id=1, source_target_pairs={{0,8},{8,0},{16,24},{24,16},{32,40},{40,32},{48,56},{56,48},{64,72... | collective-permute-start | bytes 983048 | tf_op jit(solution)/shard_map/ppermute | solution.py:53
  111.7 3.2 %copy-start.1 = (f32[512,2048]{1,0:T(8,128)S(1)}, f32[512,2048]{1,0:T(8,128)}, u32[]{:S(2)}) copy-start(f32[512,2048]{1,0:T(8,128)} %param.3) | copy-start | bytes 12582916

commit v12 on v11

--- a/solution.py
+++ b/solution.py
@@ -51,10 +51,12 @@
     other = lax.ppermute(sent, "row", core_pairs)
     across = lax.ppermute(sent, "row", [(i, i ^ 2) for i in range(row_count)])
     diagonal = lax.ppermute(across, "row", core_pairs)
+    pieces = [(low, mine)]
     for mask, block in ((1, other), (2, across), (3, diagonal)):
         gathered = lax.dynamic_update_slice_in_dim(gathered, block[:rows_here], (low ^ mask) * rows_here, 0)
+        pieces.append((low ^ mask, block[:rows_here]))
     if extra is None:
-        return gathered, None
+        return gathered, pieces
     total = extra + other[rows_here:] + across[rows_here:] + diagonal[rows_here:]
     return gathered, total
 
@@ -68,8 +70,14 @@
 
 
 def shards(matrix, vectors, tfactor):
-    vec_cols, _ = to_columns(vectors)
-    x_rows = col_sum_rows(product(matrix, vec_cols))
+    vec_cols, vec_pieces = to_columns(vectors)
+    per = len(vec_pieces)
+    column_blocks = matrix.reshape(matrix.shape[0], per, matrix.shape[1] // per)
+    x_part = None
+    for slot, block in vec_pieces:
+        term = product(lax.dynamic_index_in_dim(column_blocks, slot, 1, keepdims=False), block)
+        x_part = term if x_part is None else x_part + term
+    x_rows = col_sum_rows(x_part)
     x_cols, s_full = to_columns(x_rows, inner_product(vectors, x_rows))
     coupling = inner_product(tfactor, product(s_full, tfactor))
     w_rows = product(x_rows, tfactor) - 0.5 * product(vectors, coupling)

time: 119 us -> 120 us (level)
  local copies, waits for them, and re-layouts: 0.43 us -> 16.7 us
  waiting for transfers between devices: 34.6 us -> 27.6 us
  starting transfers between devices: 34.5 us -> 29.5 us
  matrix products: 11.1 us -> 8.97 us
  blocking collectives: 35.8 us -> 33.9 us
    dynamic_slice x0 -> x1, local copies, waits for them, and re-layouts: none -> 10.3 us  [shards(): lax.dynamic_index_in_dim(column_blocks, slot, 1, keepdims=False)]
    reshape x0 -> x1, local copies, waits for them, and re-layouts: none -> 6.02 us  [shards(): column_blocks = matrix.reshape(matrix.shape[0], per, matrix.shape[1] // per)]
    ppermute x2, starting transfers between devices: 10 us -> 5 us  [to_columns(): diagonal = lax.ppermute(across, 'row', core_pairs)]
    ppermute x3, waiting for transfers between devices: 12.9 us -> 9.24 us  [to_columns(): mine = mine + lax.ppermute(mine, ('row', 'col'), pairs)]
    ppermute x2, starting transfers between devices: 13 us -> 9.87 us  [to_columns(): other = lax.ppermute(sent, 'row', core_pairs)]
    ppermute x3, starting transfers between devices: 3.29 us -> 5.96 us  [to_columns(): lax.ppermute(jnp.concatenate([mine, extra], axis=0), ('row', 'col'), pairs)]
    dot_general x6 -> x9, matrix products: 6.33 us -> 4.24 us  [product(): jnp.dot(left, right, precision=lax.Precision.HIGH, preferred_element_type...]
    all_to_all x1, blocking collectives: 23.7 us -> 21.9 us  [col_sum_rows(): total = jnp.sum(lax.all_to_all(pieces, 'col', 0, 0, tiled=True), axis=0)]
  transfers between devices with their start and end apart: 12 -> 12, of which waited for: 9 -> 7; matrix products, arithmetic and copies ran while one was open for 0% -> 16% of each run, Pallas kernels for 0% -> 0%
where the time goes in v12:
time: 120 us; the launch traced here: 119 us
  blocking collectives  33.9 us (28%)
  starting transfers between devices  29.5 us (25%)
  waiting for transfers between devices  27.6 us (23%)
  local copies, waits for them, and re-layouts  16.7 us (14%)
  matrix products  8.97 us (7%)
  other arithmetic  2.34 us (2%)
    all_to_all x1, blocking collectives, col_sum_rows(): total = jnp.sum(lax.all_to_all(pieces, 'col', 0, 0, tiled=True), axis=0)  21.9 us
    ppermute x3, waiting for transfers between devices, to_columns(): lax.ppermute(jnp.concatenate([mine, extra], axis=0), ('row', 'col'), pairs)  16.7 us
    all_to_all x1, blocking collectives, col_sum_rows(): lax.all_to_all(spread, 'col', 0, 0, tiled=True).reshape(partial.shape)  12.1 us
    dynamic_slice x1, local copies, waits for them, and re-layouts, shards(): lax.dynamic_index_in_dim(column_blocks, slot, 1, keepdims=False)  10.3 us
    ppermute x2, starting transfers between devices, to_columns(): other = lax.ppermute(sent, 'row', core_pairs)  9.87 us
    ppermute x3, waiting for transfers between devices, to_columns(): mine = mine + lax.ppermute(mine, ('row', 'col'), pairs)  9.24 us
    ppermute x3, starting transfers between devices, to_columns(): mine = mine + lax.ppermute(mine, ('row', 'col'), pairs)  7.3 us
    reshape x1, local copies, waits for them, and re-layouts, shards(): column_blocks = matrix.reshape(matrix.shape[0], per, matrix.shape[1] // per)  6.02 us
  transfers between devices with their start and end apart: 12, of which 7 were waited for; matrix products, arithmetic and copies ran while one was open for 16% of the time, Pallas kernels for 0%

profile of v12, /device:TPU:1, one launch (start us, length us, event | category | flops | bytes accessed | tf_op | source)
XLA Modules:
  0.0 119.3 jit_solution(6326190788259804332)
XLA Ops:
  0.0 1.0 broadcast_select_fusion.1
  1.0 4.7 %collective-permute-start = (f32[512,128]{1,0:T(8,128)S(1)}, f32[512,128]{1,0:T(8,128)S(1)}, u32[]{:S(2)}, u32[]{:S(2)}) collective-permute-start(f32[512,128]{1,0:T(8,128)S(1)} %broadcast_select_fusion.1), channel_id=1, source_target_pairs={{0,32},{8,40},{16,48},{24,56},{33,1},{41,9},{49,17},{57,25},{66,98... | collective-permute-start | bytes 786440 | tf_op jit(solution)/shard_map/ppermute | solution.py:41
  5.7 4.9 %collective-permute-done = f32[512,128]{1,0:T(8,128)S(1)} collective-permute-done((f32[512,128]{1,0:T(8,128)S(1)}, f32[512,128]{1,0:T(8,128)S(1)}, u32[]{:S(2)}, u32[]{:S(2)}) %collective-permute-start) | collective-permute-done | bytes 262176 | tf_op jit(solution)/shard_map/ppermute | solution.py:41
  10.6 1.0 fusion.40
  11.6 1.3 %collective-permute-start.1 = (f32[512,128]{1,0:T(8,128)S(1)}, f32[512,128]{1,0:T(8,128)S(1)}, u32[]{:S(2)}, u32[]{:S(2)}) collective-permute-start(f32[512,128]{1,0:T(8,128)S(1)} %fusion.40), channel_id=1, source_target_pairs={{0,64},{1,65},{8,72},{9,73},{16,80},{17,81},{24,88},{25,89},{32,96... | collective-permute-start | bytes 786440 | tf_op jit(solution)/shard_map/ppermute | solution.py:41
  12.9 4.3 %collective-permute-done.1 = f32[512,128]{1,0:T(8,128)S(1)} collective-permute-done((f32[512,128]{1,0:T(8,128)S(1)}, f32[512,128]{1,0:T(8,128)S(1)}, u32[]{:S(2)}, u32[]{:S(2)}) %collective-permute-start.1) | collective-permute-done | bytes 262176 | tf_op jit(solution)/shard_map/ppermute | solution.py:41
  17.3 1.3 %collective-permute-start.2 = (f32[512,128]{1,0:T(8,128)S(1)}, f32[512,128]{1,0:T(8,128)S(1)}, u32[]{:S(2)}, u32[]{:S(2)}) collective-permute-start(f32[512,128]{1,0:T(8,128)S(1)} %add.83), channel_id=1, source_target_pairs={{0,128},{1,129},{2,130},{3,131},{8,136},{9,137},{10,138},{11,139},... | collective-permute-start | bytes 786440 | tf_op jit(solution)/shard_map/ppermute | solution.py:41
  18.6 6.0 %reshape.10 = f32[512,4,512]{2,1,0:T(4,128)} reshape(f32[512,2048]{1,0:T(8,128)} %param.3) | data formatting | bytes 8388608 | tf_op jit(solution)/shard_map/reshape | solution.py:75
  25.2 10.3 %constant_dynamic-slice_fusion = (f32[512,1,512]{2,1,0:T(1,128)S(1)}, f32[512,1,512]{2,1,0:T(1,128)S(1)}, f32[512,1,512]{2,1,0:T(1,128)S(1)}, f32[512,1,512]{2,1,0:T(1,128)S(1)}) fusion(f32[512,4,512]{2,1,0:T(4,128)} %reshape.10, s32[]{:T(128)S(6)} %select_n.62, s32[]{:T(128)S(6)} %select_n.61, s32[]{:T(128)S(6)} %select_n.60, s32[]{:T(128)S(6)} %select_n.56), kind=kLoop, calls=%fused_computation.50 | loop fusion | bytes 8388624 | tf_op jit(solution)/shard_map/jit(dynamic_index_in_dim)/dynamic_slice | solution.py:78
  35.6 2.6 %collective-permute-start.3 = (f32[512,128]{1,0:T(8,128)S(1)}, f32[512,128]{1,0:T(8,128)S(1)}, u32[]{:S(2)}, u32[]{:S(2)}) collective-permute-start(f32[512,128]{1,0:T(8,128)S(1)} %get-tuple-element.8), channel_id=1, source_target_pairs={{0,8},{8,0},{16,24},{24,16},{32,40},{40,32},{48,56},{56,48},{64,72... | collective-permute-start | bytes 786440 | tf_op jit(solution)/shard_map/ppermute | solution.py:51
  39.3 0.6 fusion.11
  41.1 21.9 %all_to_all.11 = f32[8,64,128]{2,1,0:T(8,128)S(1)} all-to-all(f32[8,64,128]{2,1,0:T(8,128)S(1)} %bitcast.42), channel_id=1, replica_groups=mesh['row'=32,'col'=8] {'col'}, dimensions={0} | all-to-all | bytes 524288 | tf_op jit(solution)/shard_map/all_to_all | solution.py:67
  63.0 12.1 %all_to_all.10 = f32[8,64,128]{2,1,0:T(8,128)S(1)} all-to-all(f32[8,64,128]{2,1,0:T(8,128)S(1)} %broadcast_in_dim.2), channel_id=1, replica_groups=mesh['row'=32,'col'=8] {'col'}, dimensions={0} | all-to-all | bytes 524288 | tf_op jit(solution)/shard_map/all_to_all | solution.py:69
  75.6 3.2 %collective-permute-start.6 = (f32[640,128]{1,0:T(8,128)S(1)}, f32[640,128]{1,0:T(8,128)S(1)}, u32[]{:S(2)}, u32[]{:S(2)}) collective-permute-start(f32[640,128]{1,0:T(8,128)S(1)} %pad_maximum_fusion), channel_id=1, source_target_pairs={{0,32},{1,33},{2,34},{3,35},{4,36},{5,37},{6,38},{7,39},{8,40},{9,... | collective-permute-start | bytes 983048 | tf_op jit(solution)/shard_map/ppermute | solution.py:43
  78.7 4.5 %collective-permute-done.6 = f32[640,128]{1,0:T(8,128)S(1)} collective-permute-done((f32[640,128]{1,0:T(8,128)S(1)}, f32[640,128]{1,0:T(8,128)S(1)}, u32[]{:S(2)}, u32[]{:S(2)}) %collective-permute-start.6) | collective-permute-done | bytes 327712 | tf_op jit(solution)/shard_map/ppermute | solution.py:43
  83.3 1.2 %collective-permute-start.7 = (f32[640,128]{1,0:T(8,128)S(1)}, f32[640,128]{1,0:T(8,128)S(1)}, u32[]{:S(2)}, u32[]{:S(2)}) collective-permute-start(f32[640,128]{1,0:T(8,128)S(1)} %pad_maximum_fusion.1), channel_id=1, source_target_pairs={{0,64},{1,65},{2,66},{3,67},{4,68},{5,69},{6,70},{7,71},{8,72},{9,... | collective-permute-start | bytes 983048 | tf_op jit(solution)/shard_map/ppermute | solution.py:43
  84.5 4.8 %collective-permute-done.7 = f32[640,128]{1,0:T(8,128)S(1)} collective-permute-done((f32[640,128]{1,0:T(8,128)S(1)}, f32[640,128]{1,0:T(8,128)S(1)}, u32[]{:S(2)}, u32[]{:S(2)}) %collective-permute-start.7) | collective-permute-done | bytes 327712 | tf_op jit(solution)/shard_map/ppermute | solution.py:43
  89.4 1.6 %collective-permute-start.8 = (f32[640,128]{1,0:T(8,128)S(1)}, f32[640,128]{1,0:T(8,128)S(1)}, u32[]{:S(2)}, u32[]{:S(2)}) collective-permute-start(f32[640,128]{1,0:T(8,128)S(1)} %pad_maximum_fusion.2), channel_id=1, source_target_pairs={{0,128},{1,129},{2,130},{3,131},{4,132},{5,133},{6,134},{7,135},{8... | collective-permute-start | bytes 983048 | tf_op jit(solution)/shard_map/ppermute | solution.py:43
  91.0 7.5 %collective-permute-done.8 = f32[640,128]{1,0:T(8,128)S(1)} collective-permute-done((f32[640,128]{1,0:T(8,128)S(1)}, f32[640,128]{1,0:T(8,128)S(1)}, u32[]{:S(2)}, u32[]{:S(2)}) %collective-permute-start.8) | collective-permute-done | bytes 327712 | tf_op jit(solution)/shard_map/ppermute | solution.py:43
  98.6 0.9 collective-permute-start.10
  99.5 7.3 %collective-permute-start.9 = (f32[640,128]{1,0:T(8,128)S(1)}, f32[640,128]{1,0:T(8,128)S(1)}, u32[]{:S(2)}, u32[]{:S(2)}) collective-permute-start(f32[640,128]{1,0:T(8,128)S(1)} %pad_maximum_fusion.3), channel_id=1, source_target_pairs={{0,8},{8,0},{16,24},{24,16},{32,40},{40,32},{48,56},{56,48},{64,72... | collective-permute-start | bytes 983048 | tf_op jit(solution)/shard_map/ppermute | solution.py:51
  107.2 4.9 %collective-permute-start.11 = (f32[640,128]{1,0:T(8,128)S(1)}, f32[640,128]{1,0:T(8,128)S(1)}, u32[]{:S(2)}, u32[]{:S(2)}) collective-permute-start(f32[640,128]{1,0:T(8,128)S(1)} %collective-permute-done.10), channel_id=1, source_target_pairs={{0,8},{8,0},{16,24},{24,16},{32,40},{40,32},{48,56},{56,48},{64,72... | collective-permute-start | bytes 983048 | tf_op jit(solution)/shard_map/ppermute | solution.py:53
  112.1 1.2 collective-permute-done.11
  115.2 4.1 %convolution_subtract_fusion = f32[512,2048]{1,0:T(8,128)} fusion(f32[512,2048]{1,0:T(8,128)S(1)} %copy-done.1, f32[2048,128]{1,0:T(8,128)S(1)} %constant_dynamic-update-slice_fusion, f32[2048,128]{1,0:T(8,128)S(1)} %convolution_subtract_fusion.1, f32[512,128]{1,0:T(8,128)S(1)} %fusion.4, f32[512,128]{1,0:T(8,128)S(1)} %copy-done.2), kind=kOutput, calls=%fused_computation | convolution fusion | flops 1612316672 | bytes 11010048 | tf_op jit(solution)/shard_map/dot_general | solution.py:87
  (47 shorter events, 6.0 us)
Async XLA Ops:
  0.0 106.9 %copy-start = (f32[128,128]{1,0:T(8,128)S(1)}, f32[128,128]{1,0:T(8,128)}, u32[]{:S(2)}) copy-start(f32[128,128]{1,0:T(8,128)} %param.5) | copy-start | bytes 196612
  1.0 9.6 %collective-permute-start = (f32[512,128]{1,0:T(8,128)S(1)}, f32[512,128]{1,0:T(8,128)S(1)}, u32[]{:S(2)}, u32[]{:S(2)}) collective-permute-start(f32[512,128]{1,0:T(8,128)S(1)} %broadcast_select_fusion.1), channel_id=1, source_target_pairs={{0,32},{8,40},{16,48},{24,56},{33,1},{41,9},{49,17},{57,25},{66,98... | collective-permute-start | bytes 786440 | tf_op jit(solution)/shard_map/ppermute | solution.py:41
  11.6 5.6 %collective-permute-start.1 = (f32[512,128]{1,0:T(8,128)S(1)}, f32[512,128]{1,0:T(8,128)S(1)}, u32[]{:S(2)}, u32[]{:S(2)}) collective-permute-start(f32[512,128]{1,0:T(8,128)S(1)} %fusion.40), channel_id=1, source_target_pairs={{0,64},{1,65},{8,72},{9,73},{16,80},{17,81},{24,88},{25,89},{32,96... | collective-permute-start | bytes 786440 | tf_op jit(solution)/shard_map/ppermute | solution.py:41
  17.3 7.4 %collective-permute-start.2 = (f32[512,128]{1,0:T(8,128)S(1)}, f32[512,128]{1,0:T(8,128)S(1)}, u32[]{:S(2)}, u32[]{:S(2)}) collective-permute-start(f32[512,128]{1,0:T(8,128)S(1)} %add.83), channel_id=1, source_target_pairs={{0,128},{1,129},{2,130},{3,131},{8,136},{9,137},{10,138},{11,139},... | collective-permute-start | bytes 786440 | tf_op jit(solution)/shard_map/ppermute | solution.py:41
  24.8 13.4 %collective-permute-start.4 = (f32[512,128]{1,0:T(8,128)S(1)}, f32[512,128]{1,0:T(8,128)S(1)}, u32[]{:S(2)}, u32[]{:S(2)}) collective-permute-start(f32[512,128]{1,0:T(8,128)S(1)} %get-tuple-element.8), channel_id=1, source_target_pairs={{0,16},{8,24},{16,0},{24,8},{32,48},{40,56},{48,32},{56,40},{64,80... | collective-permute-start | bytes 786440 | tf_op jit(solution)/shard_map/ppermute | solution.py:52
  35.6 3.7 %collective-permute-start.3 = (f32[512,128]{1,0:T(8,128)S(1)}, f32[512,128]{1,0:T(8,128)S(1)}, u32[]{:S(2)}, u32[]{:S(2)}) collective-permute-start(f32[512,128]{1,0:T(8,128)S(1)} %get-tuple-element.8), channel_id=1, source_target_pairs={{0,8},{8,0},{16,24},{24,16},{32,40},{40,32},{48,56},{56,48},{64,72... | collective-permute-start | bytes 786440 | tf_op jit(solution)/shard_map/ppermute | solution.py:51
  38.1 2.4 %collective-permute-start.5 = (f32[512,128]{1,0:T(8,128)S(1)}, f32[512,128]{1,0:T(8,128)S(1)}, u32[]{:S(2)}, u32[]{:S(2)}) collective-permute-start(f32[512,128]{1,0:T(8,128)S(1)} %collective-permute-done.4), channel_id=1, source_target_pairs={{0,8},{8,0},{16,24},{24,16},{32,40},{40,32},{48,56},{56,48},{64,72... | collective-permute-start | bytes 786440 | tf_op jit(solution)/shard_map/ppermute | solution.py:53
  38.3 36.8 %copy-start.2 = (f32[512,128]{1,0:T(8,128)S(1)}, f32[512,128]{1,0:T(8,128)}, u32[]{:S(2)}) copy-start(f32[512,128]{1,0:T(8,128)} %param.4) | copy-start | bytes 786436
  75.6 7.6 %collective-permute-start.6 = (f32[640,128]{1,0:T(8,128)S(1)}, f32[640,128]{1,0:T(8,128)S(1)}, u32[]{:S(2)}, u32[]{:S(2)}) collective-permute-start(f32[640,128]{1,0:T(8,128)S(1)} %pad_maximum_fusion), channel_id=1, source_target_pairs={{0,32},{1,33},{2,34},{3,35},{4,36},{5,37},{6,38},{7,39},{8,40},{9,... | collective-permute-start | bytes 983048 | tf_op jit(solution)/shard_map/ppermute | solution.py:43
  83.3 6.0 %collective-permute-start.7 = (f32[640,128]{1,0:T(8,128)S(1)}, f32[640,128]{1,0:T(8,128)S(1)}, u32[]{:S(2)}, u32[]{:S(2)}) collective-permute-start(f32[640,128]{1,0:T(8,128)S(1)} %pad_maximum_fusion.1), channel_id=1, source_target_pairs={{0,64},{1,65},{2,66},{3,67},{4,68},{5,69},{6,70},{7,71},{8,72},{9,... | collective-permute-start | bytes 983048 | tf_op jit(solution)/shard_map/ppermute | solution.py:43
  89.4 9.1 %collective-permute-start.8 = (f32[640,128]{1,0:T(8,128)S(1)}, f32[640,128]{1,0:T(8,128)S(1)}, u32[]{:S(2)}, u32[]{:S(2)}) collective-permute-start(f32[640,128]{1,0:T(8,128)S(1)} %pad_maximum_fusion.2), channel_id=1, source_target_pairs={{0,128},{1,129},{2,130},{3,131},{4,132},{5,133},{6,134},{7,135},{8... | collective-permute-start | bytes 983048 | tf_op jit(solution)/shard_map/ppermute | solution.py:43
  98.6 8.5 %collective-permute-start.10 = (f32[640,128]{1,0:T(8,128)S(1)}, f32[640,128]{1,0:T(8,128)S(1)}, u32[]{:S(2)}, u32[]{:S(2)}) collective-permute-start(f32[640,128]{1,0:T(8,128)S(1)} %pad_maximum_fusion.3), channel_id=1, source_target_pairs={{0,16},{8,24},{16,0},{24,8},{32,48},{40,56},{48,32},{56,40},{64,80... | collective-permute-start | bytes 983048 | tf_op jit(solution)/shard_map/ppermute | solution.py:52
  99.5 12.5 %collective-permute-start.9 = (f32[640,128]{1,0:T(8,128)S(1)}, f32[640,128]{1,0:T(8,128)S(1)}, u32[]{:S(2)}, u32[]{:S(2)}) collective-permute-start(f32[640,128]{1,0:T(8,128)S(1)} %pad_maximum_fusion.3), channel_id=1, source_target_pairs={{0,8},{8,0},{16,24},{24,16},{32,40},{40,32},{48,56},{56,48},{64,72... | collective-permute-start | bytes 983048 | tf_op jit(solution)/shard_map/ppermute | solution.py:51
  107.2 6.1 %collective-permute-start.11 = (f32[640,128]{1,0:T(8,128)S(1)}, f32[640,128]{1,0:T(8,128)S(1)}, u32[]{:S(2)}, u32[]{:S(2)}) collective-permute-start(f32[640,128]{1,0:T(8,128)S(1)} %collective-permute-done.10), channel_id=1, source_target_pairs={{0,8},{8,0},{16,24},{24,16},{32,40},{40,32},{48,56},{56,48},{64,72... | collective-permute-start | bytes 983048 | tf_op jit(solution)/shard_map/ppermute | solution.py:53
  112.0 3.2 %copy-start.1 = (f32[512,2048]{1,0:T(8,128)S(1)}, f32[512,2048]{1,0:T(8,128)}, u32[]{:S(2)}) copy-start(f32[512,2048]{1,0:T(8,128)} %param.3) | copy-start | bytes 12582916

commit v13 on v12

--- a/solution.py
+++ b/solution.py
@@ -72,10 +72,10 @@
 def shards(matrix, vectors, tfactor):
     vec_cols, vec_pieces = to_columns(vectors)
     per = len(vec_pieces)
-    column_blocks = matrix.reshape(matrix.shape[0], per, matrix.shape[1] // per)
+    width = matrix.shape[1] // per
     x_part = None
     for slot, block in vec_pieces:
-        term = product(lax.dynamic_index_in_dim(column_blocks, slot, 1, keepdims=False), block)
+        term = product(lax.dynamic_slice_in_dim(matrix, slot * width, width, 1), block)
         x_part = term if x_part is None else x_part + term
     x_rows = col_sum_rows(x_part)
     x_cols, s_full = to_columns(x_rows, inner_product(vectors, x_rows))

time: 120 us -> 124 us (1.033)
  local copies, waits for them, and re-layouts: 16.7 us -> 0.31 us
  waiting for transfers between devices: 27.6 us -> 40.5 us
  blocking collectives: 33.9 us -> 39.6 us
  matrix products: 8.97 us -> 13.9 us
  starting transfers between devices: 29.5 us -> 26.8 us
    dynamic_slice x1 -> x0, local copies, waits for them, and re-layouts: 10.3 us -> none  [shards(): lax.dynamic_index_in_dim(column_blocks, slot, 1, keepdims=False)]
    ppermute x3, waiting for transfers between devices: 16.7 us -> 23 us  [to_columns(): lax.ppermute(jnp.concatenate([mine, extra], axis=0), ('row', 'col'), pairs)]
    reshape x1 -> x0, local copies, waits for them, and re-layouts: 6.02 us -> none  [shards(): column_blocks = matrix.reshape(matrix.shape[0], per, matrix.shape[1] // per)]
    dot_general x9, matrix products: 4.24 us -> 9.12 us  [product(): jnp.dot(left, right, precision=lax.Precision.HIGH, preferred_element_type...]
    ppermute x3, waiting for transfers between devices: 9.24 us -> 12.9 us  [to_columns(): mine = mine + lax.ppermute(mine, ('row', 'col'), pairs)]
    ppermute x2, waiting for transfers between devices: 0.01 us -> 3.44 us  [to_columns(): across = lax.ppermute(sent, 'row', [(i, i ^ 2) for i in range(row_count)])]
    ppermute x2, starting transfers between devices: 5 us -> 8.4 us  [to_columns(): diagonal = lax.ppermute(across, 'row', core_pairs)]
    ppermute x2, starting transfers between devices: 9.87 us -> 6.67 us  [to_columns(): other = lax.ppermute(sent, 'row', core_pairs)]
  transfers between devices with their start and end apart: 12 -> 12, of which waited for: 7 -> 9; matrix products, arithmetic and copies ran while one was open for 16% -> 5% of each run, Pallas kernels for 0% -> 0%
where the time goes in v13:
time: 124 us
  waiting for transfers between devices  40.5 us (33%)
  blocking collectives  39.6 us (32%)
  starting transfers between devices  26.8 us (22%)
  matrix products  13.9 us (11%)
  other arithmetic  2.33 us (2%)
    all_to_all x1, blocking collectives, col_sum_rows(): total = jnp.sum(lax.all_to_all(pieces, 'col', 0, 0, tiled=True), axis=0)  24.9 us
    ppermute x3, waiting for transfers between devices, to_columns(): lax.ppermute(jnp.concatenate([mine, extra], axis=0), ('row', 'col'), pairs)  23 us
    all_to_all x1, blocking collectives, col_sum_rows(): lax.all_to_all(spread, 'col', 0, 0, tiled=True).reshape(partial.shape)  14.7 us
    ppermute x3, waiting for transfers between devices, to_columns(): mine = mine + lax.ppermute(mine, ('row', 'col'), pairs)  12.9 us
    dot_general x9, matrix products, product(): jnp.dot(left, right, precision=lax.Precision.HIGH, preferred_element_type...  9.12 us
    ppermute x2, starting transfers between devices, to_columns(): diagonal = lax.ppermute(across, 'row', core_pairs)  8.4 us
    ppermute x3, starting transfers between devices, to_columns(): mine = mine + lax.ppermute(mine, ('row', 'col'), pairs)  7.3 us
    ppermute x2, starting transfers between devices, to_columns(): other = lax.ppermute(sent, 'row', core_pairs)  6.67 us
  transfers between devices with their start and end apart: 12, of which 9 were waited for; matrix products, arithmetic and copies ran while one was open for 5% of the time, Pallas kernels for 0%

profile of v13, /device:TPU:1, one launch (start us, length us, event | category | flops | bytes accessed | tf_op | source)
XLA Modules:
  0.0 123.7 jit_solution(10449304909984205013)
XLA Ops:
  1.0 4.7 %collective-permute-start = (f32[512,128]{1,0:T(8,128)S(1)}, f32[512,128]{1,0:T(8,128)S(1)}, u32[]{:S(2)}, u32[]{:S(2)}) collective-permute-start(f32[512,128]{1,0:T(8,128)S(1)} %broadcast_select_fusion.1), channel_id=1, source_target_pairs={{0,32},{8,40},{16,48},{24,56},{33,1},{41,9},{49,17},{57,25},{66,98... | collective-permute-start | bytes 786440 | tf_op jit(solution)/shard_map/ppermute | solution.py:41
  5.7 4.9 %collective-permute-done = f32[512,128]{1,0:T(8,128)S(1)} collective-permute-done((f32[512,128]{1,0:T(8,128)S(1)}, f32[512,128]{1,0:T(8,128)S(1)}, u32[]{:S(2)}, u32[]{:S(2)}) %collective-permute-start) | collective-permute-done | bytes 262176 | tf_op jit(solution)/shard_map/ppermute | solution.py:41
  11.6 1.3 %collective-permute-start.1 = (f32[512,128]{1,0:T(8,128)S(1)}, f32[512,128]{1,0:T(8,128)S(1)}, u32[]{:S(2)}, u32[]{:S(2)}) collective-permute-start(f32[512,128]{1,0:T(8,128)S(1)} %fusion.40), channel_id=1, source_target_pairs={{0,64},{1,65},{8,72},{9,73},{16,80},{17,81},{24,88},{25,89},{32,96... | collective-permute-start | bytes 786440 | tf_op jit(solution)/shard_map/ppermute | solution.py:41
  12.9 4.3 %collective-permute-done.1 = f32[512,128]{1,0:T(8,128)S(1)} collective-permute-done((f32[512,128]{1,0:T(8,128)S(1)}, f32[512,128]{1,0:T(8,128)S(1)}, u32[]{:S(2)}, u32[]{:S(2)}) %collective-permute-start.1) | collective-permute-done | bytes 262176 | tf_op jit(solution)/shard_map/ppermute | solution.py:41
  17.3 1.3 %collective-permute-start.2 = (f32[512,128]{1,0:T(8,128)S(1)}, f32[512,128]{1,0:T(8,128)S(1)}, u32[]{:S(2)}, u32[]{:S(2)}) collective-permute-start(f32[512,128]{1,0:T(8,128)S(1)} %add.74), channel_id=1, source_target_pairs={{0,128},{1,129},{2,130},{3,131},{8,136},{9,137},{10,138},{11,139},... | collective-permute-start | bytes 786440 | tf_op jit(solution)/shard_map/ppermute | solution.py:41
  18.6 3.6 %collective-permute-done.2 = f32[512,128]{1,0:T(8,128)S(1)} collective-permute-done((f32[512,128]{1,0:T(8,128)S(1)}, f32[512,128]{1,0:T(8,128)S(1)}, u32[]{:S(2)}, u32[]{:S(2)}) %collective-permute-start.2) | collective-permute-done | bytes 262176 | tf_op jit(solution)/shard_map/ppermute | solution.py:41
  22.9 3.1 %collective-permute-start.3 = (f32[512,128]{1,0:T(8,128)S(1)}, f32[512,128]{1,0:T(8,128)S(1)}, u32[]{:S(2)}, u32[]{:S(2)}) collective-permute-start(f32[512,128]{1,0:T(8,128)S(1)} %get-tuple-element.8), channel_id=1, source_target_pairs={{0,8},{8,0},{16,24},{24,16},{32,40},{40,32},{48,56},{56,48},{64,72... | collective-permute-start | bytes 786440 | tf_op jit(solution)/shard_map/ppermute | solution.py:51
  26.0 1.7 %collective-permute-done.4 = f32[512,128]{1,0:T(8,128)S(1)} collective-permute-done((f32[512,128]{1,0:T(8,128)S(1)}, f32[512,128]{1,0:T(8,128)S(1)}, u32[]{:S(2)}, u32[]{:S(2)}) %collective-permute-start.4) | collective-permute-done | bytes 262176 | tf_op jit(solution)/shard_map/ppermute | solution.py:52
  27.7 4.0 %collective-permute-start.5 = (f32[512,128]{1,0:T(8,128)S(1)}, f32[512,128]{1,0:T(8,128)S(1)}, u32[]{:S(2)}, u32[]{:S(2)}) collective-permute-start(f32[512,128]{1,0:T(8,128)S(1)} %collective-permute-done.4), channel_id=1, source_target_pairs={{0,8},{8,0},{16,24},{24,16},{32,40},{40,32},{48,56},{56,48},{64,72... | collective-permute-start | bytes 786440 | tf_op jit(solution)/shard_map/ppermute | solution.py:53
  31.7 1.8 %fusion.7 = f32[512,128]{1,0:T(8,128)S(1)} fusion(f32[512,128]{1,0:T(8,128)S(1)} %collective-permute-done.4, f32[512,2048]{1,0:T(8,128)} %param.3, s32[]{:T(128)S(6)} %select_n.52), kind=kOutput, calls=%fused_computation.14 | convolution fusion | flops 201326592 | bytes 1572868 | tf_op jit(solution)/shard_map/dot_general | solution.py:8
  33.5 1.8 %fusion.9 = f32[512,128]{1,0:T(8,128)S(1)} fusion(f32[512,128]{1,0:T(8,128)S(1)} %collective-permute-done.3, f32[512,2048]{1,0:T(8,128)} %param.3, s32[]{:T(128)S(6)} %select_n.51), kind=kOutput, calls=%fused_computation.16 | convolution fusion | flops 201326592 | bytes 1572868 | tf_op jit(solution)/shard_map/dot_general | solution.py:8
  35.3 1.8 %fusion.5 = f32[512,128]{1,0:T(8,128)S(1)} fusion(f32[512,128]{1,0:T(8,128)S(1)} %fusion.7, f32[512,128]{1,0:T(8,128)S(1)} %fusion.9, f32[512,128]{1,0:T(8,128)S(1)} %get-tuple-element.8, f32[512,2048]{1,0:T(8,128)} %param.3, s32[]{:T(128)S(6)} %select_n.47), kind=kOutput, calls=%fused_computation.11 | convolution fusion | flops 201457664 | bytes 2097156 | tf_op jit(solution)/shard_map/dot_general | solution.py:8
  37.1 1.8 %convolution_add_fusion = f32[512,128]{1,0:T(8,128)S(1)} fusion(f32[512,128]{1,0:T(8,128)S(1)} %fusion.5, f32[512,128]{1,0:T(8,128)S(1)} %collective-permute-done.5, f32[512,2048]{1,0:T(8,128)} %param.3, s32[]{:T(128)S(6)} %select_n.53), kind=kOutput, calls=%fused_computation.9 | convolution fusion | flops 201392128 | bytes 1835012 | tf_op jit(solution)/shard_map/dot_general | solution.py:8
  39.0 24.9 %all_to_all.11 = f32[8,64,128]{2,1,0:T(8,128)S(1)} all-to-all(f32[8,64,128]{2,1,0:T(8,128)S(1)} %bitcast.30), channel_id=1, replica_groups=mesh['row'=32,'col'=8] {'col'}, dimensions={0} | all-to-all | bytes 524288 | tf_op jit(solution)/shard_map/all_to_all | solution.py:67
  63.9 14.7 %all_to_all.10 = f32[8,64,128]{2,1,0:T(8,128)S(1)} all-to-all(f32[8,64,128]{2,1,0:T(8,128)S(1)} %broadcast_in_dim.2), channel_id=1, replica_groups=mesh['row'=32,'col'=8] {'col'}, dimensions={0} | all-to-all | bytes 524288 | tf_op jit(solution)/shard_map/all_to_all | solution.py:69
  79.1 2.5 %collective-permute-start.6 = (f32[640,128]{1,0:T(8,128)S(1)}, f32[640,128]{1,0:T(8,128)S(1)}, u32[]{:S(2)}, u32[]{:S(2)}) collective-permute-start(f32[640,128]{1,0:T(8,128)S(1)} %pad_maximum_fusion), channel_id=1, source_target_pairs={{0,32},{1,33},{2,34},{3,35},{4,36},{5,37},{6,38},{7,39},{8,40},{9,... | collective-permute-start | bytes 983048 | tf_op jit(solution)/shard_map/ppermute | solution.py:43
  81.6 7.8 %collective-permute-done.6 = f32[640,128]{1,0:T(8,128)S(1)} collective-permute-done((f32[640,128]{1,0:T(8,128)S(1)}, f32[640,128]{1,0:T(8,128)S(1)}, u32[]{:S(2)}, u32[]{:S(2)}) %collective-permute-start.6) | collective-permute-done | bytes 327712 | tf_op jit(solution)/shard_map/ppermute | solution.py:43
  90.4 6.9 %collective-permute-done.7 = f32[640,128]{1,0:T(8,128)S(1)} collective-permute-done((f32[640,128]{1,0:T(8,128)S(1)}, f32[640,128]{1,0:T(8,128)S(1)}, u32[]{:S(2)}, u32[]{:S(2)}) %collective-permute-start.7) | collective-permute-done | bytes 327712 | tf_op jit(solution)/shard_map/ppermute | solution.py:43
  97.5 8.3 %collective-permute-done.8 = f32[640,128]{1,0:T(8,128)S(1)} collective-permute-done((f32[640,128]{1,0:T(8,128)S(1)}, f32[640,128]{1,0:T(8,128)S(1)}, u32[]{:S(2)}, u32[]{:S(2)}) %collective-permute-start.8) | collective-permute-done | bytes 327712 | tf_op jit(solution)/shard_map/ppermute | solution.py:43
  106.4 3.6 %collective-permute-start.9 = (f32[640,128]{1,0:T(8,128)S(1)}, f32[640,128]{1,0:T(8,128)S(1)}, u32[]{:S(2)}, u32[]{:S(2)}) collective-permute-start(f32[640,128]{1,0:T(8,128)S(1)} %pad_maximum_fusion.3), channel_id=1, source_target_pairs={{0,8},{8,0},{16,24},{24,16},{32,40},{40,32},{48,56},{56,48},{64,72... | collective-permute-start | bytes 983048 | tf_op jit(solution)/shard_map/ppermute | solution.py:51
  110.3 1.7 %collective-permute-done.10 = f32[640,128]{1,0:T(8,128)S(1)} collective-permute-done((f32[640,128]{1,0:T(8,128)S(1)}, f32[640,128]{1,0:T(8,128)S(1)}, u32[]{:S(2)}, u32[]{:S(2)}) %collective-permute-start.10) | collective-permute-done | bytes 327712 | tf_op jit(solution)/shard_map/ppermute | solution.py:52
  112.0 4.4 %collective-permute-start.11 = (f32[640,128]{1,0:T(8,128)S(1)}, f32[640,128]{1,0:T(8,128)S(1)}, u32[]{:S(2)}, u32[]{:S(2)}) collective-permute-start(f32[640,128]{1,0:T(8,128)S(1)} %collective-permute-done.10), channel_id=1, source_target_pairs={{0,8},{8,0},{16,24},{24,16},{32,40},{40,32},{48,56},{56,48},{64,72... | collective-permute-start | bytes 983048 | tf_op jit(solution)/shard_map/ppermute | solution.py:53
  116.5 1.2 collective-permute-done.11
  119.6 4.1 %convolution_subtract_fusion = f32[512,2048]{1,0:T(8,128)} fusion(f32[512,2048]{1,0:T(8,128)S(1)} %copy-done.1, f32[2048,128]{1,0:T(8,128)S(1)} %constant_dynamic-update-slice_fusion, f32[2048,128]{1,0:T(8,128)S(1)} %convolution_subtract_fusion.1, f32[512,128]{1,0:T(8,128)S(1)} %fusion.4, f32[512,128]{1,0:T(8,128)S(1)} %copy-done.2), kind=kOutput, calls=%fused_computation | convolution fusion | flops 1612316672 | bytes 11010048 | tf_op jit(solution)/shard_map/dot_general | solution.py:87
  (45 shorter events, 7.1 us)
Async XLA Ops:
  0.0 110.0 %copy-start = (f32[128,128]{1,0:T(8,128)S(1)}, f32[128,128]{1,0:T(8,128)}, u32[]{:S(2)}) copy-start(f32[128,128]{1,0:T(8,128)} %param.5) | copy-start | bytes 196612
  1.0 9.6 %collective-permute-start = (f32[512,128]{1,0:T(8,128)S(1)}, f32[512,128]{1,0:T(8,128)S(1)}, u32[]{:S(2)}, u32[]{:S(2)}) collective-permute-start(f32[512,128]{1,0:T(8,128)S(1)} %broadcast_select_fusion.1), channel_id=1, source_target_pairs={{0,32},{8,40},{16,48},{24,56},{33,1},{41,9},{49,17},{57,25},{66,98... | collective-permute-start | bytes 786440 | tf_op jit(solution)/shard_map/ppermute | solution.py:41
  11.6 5.6 %collective-permute-start.1 = (f32[512,128]{1,0:T(8,128)S(1)}, f32[512,128]{1,0:T(8,128)S(1)}, u32[]{:S(2)}, u32[]{:S(2)}) collective-permute-start(f32[512,128]{1,0:T(8,128)S(1)} %fusion.40), channel_id=1, source_target_pairs={{0,64},{1,65},{8,72},{9,73},{16,80},{17,81},{24,88},{25,89},{32,96... | collective-permute-start | bytes 786440 | tf_op jit(solution)/shard_map/ppermute | solution.py:41
  17.3 5.0 %collective-permute-start.2 = (f32[512,128]{1,0:T(8,128)S(1)}, f32[512,128]{1,0:T(8,128)S(1)}, u32[]{:S(2)}, u32[]{:S(2)}) collective-permute-start(f32[512,128]{1,0:T(8,128)S(1)} %add.74), channel_id=1, source_target_pairs={{0,128},{1,129},{2,130},{3,131},{8,136},{9,137},{10,138},{11,139},... | collective-permute-start | bytes 786440 | tf_op jit(solution)/shard_map/ppermute | solution.py:41
  22.4 5.3 %collective-permute-start.4 = (f32[512,128]{1,0:T(8,128)S(1)}, f32[512,128]{1,0:T(8,128)S(1)}, u32[]{:S(2)}, u32[]{:S(2)}) collective-permute-start(f32[512,128]{1,0:T(8,128)S(1)} %get-tuple-element.8), channel_id=1, source_target_pairs={{0,16},{8,24},{16,0},{24,8},{32,48},{40,56},{48,32},{56,40},{64,80... | collective-permute-start | bytes 786440 | tf_op jit(solution)/shard_map/ppermute | solution.py:52
  22.9 10.6 %collective-permute-start.3 = (f32[512,128]{1,0:T(8,128)S(1)}, f32[512,128]{1,0:T(8,128)S(1)}, u32[]{:S(2)}, u32[]{:S(2)}) collective-permute-start(f32[512,128]{1,0:T(8,128)S(1)} %get-tuple-element.8), channel_id=1, source_target_pairs={{0,8},{8,0},{16,24},{24,16},{32,40},{40,32},{48,56},{56,48},{64,72... | collective-permute-start | bytes 786440 | tf_op jit(solution)/shard_map/ppermute | solution.py:51
  26.0 52.6 %copy-start.2 = (f32[512,128]{1,0:T(8,128)S(1)}, f32[512,128]{1,0:T(8,128)}, u32[]{:S(2)}) copy-start(f32[512,128]{1,0:T(8,128)} %param.4) | copy-start | bytes 786436
  27.7 9.4 %collective-permute-start.5 = (f32[512,128]{1,0:T(8,128)S(1)}, f32[512,128]{1,0:T(8,128)S(1)}, u32[]{:S(2)}, u32[]{:S(2)}) collective-permute-start(f32[512,128]{1,0:T(8,128)S(1)} %collective-permute-done.4), channel_id=1, source_target_pairs={{0,8},{8,0},{16,24},{24,16},{32,40},{40,32},{48,56},{56,48},{64,72... | collective-permute-start | bytes 786440 | tf_op jit(solution)/shard_map/ppermute | solution.py:53
  79.1 10.3 %collective-permute-start.6 = (f32[640,128]{1,0:T(8,128)S(1)}, f32[640,128]{1,0:T(8,128)S(1)}, u32[]{:S(2)}, u32[]{:S(2)}) collective-permute-start(f32[640,128]{1,0:T(8,128)S(1)} %pad_maximum_fusion), channel_id=1, source_target_pairs={{0,32},{1,33},{2,34},{3,35},{4,36},{5,37},{6,38},{7,39},{8,40},{9,... | collective-permute-start | bytes 983048 | tf_op jit(solution)/shard_map/ppermute | solution.py:43
  89.4 7.9 %collective-permute-start.7 = (f32[640,128]{1,0:T(8,128)S(1)}, f32[640,128]{1,0:T(8,128)S(1)}, u32[]{:S(2)}, u32[]{:S(2)}) collective-permute-start(f32[640,128]{1,0:T(8,128)S(1)} %pad_maximum_fusion.1), channel_id=1, source_target_pairs={{0,64},{1,65},{2,66},{3,67},{4,68},{5,69},{6,70},{7,71},{8,72},{9,... | collective-permute-start | bytes 983048 | tf_op jit(solution)/shard_map/ppermute | solution.py:43
  97.4 8.4 %collective-permute-start.8 = (f32[640,128]{1,0:T(8,128)S(1)}, f32[640,128]{1,0:T(8,128)S(1)}, u32[]{:S(2)}, u32[]{:S(2)}) collective-permute-start(f32[640,128]{1,0:T(8,128)S(1)} %pad_maximum_fusion.2), channel_id=1, source_target_pairs={{0,128},{1,129},{2,130},{3,131},{4,132},{5,133},{6,134},{7,135},{8... | collective-permute-start | bytes 983048 | tf_op jit(solution)/shard_map/ppermute | solution.py:43
  106.0 6.0 %collective-permute-start.10 = (f32[640,128]{1,0:T(8,128)S(1)}, f32[640,128]{1,0:T(8,128)S(1)}, u32[]{:S(2)}, u32[]{:S(2)}) collective-permute-start(f32[640,128]{1,0:T(8,128)S(1)} %pad_maximum_fusion.3), channel_id=1, source_target_pairs={{0,16},{8,24},{16,0},{24,8},{32,48},{40,56},{48,32},{56,40},{64,80... | collective-permute-start | bytes 983048 | tf_op jit(solution)/shard_map/ppermute | solution.py:52
  106.4 10.0 %collective-permute-start.9 = (f32[640,128]{1,0:T(8,128)S(1)}, f32[640,128]{1,0:T(8,128)S(1)}, u32[]{:S(2)}, u32[]{:S(2)}) collective-permute-start(f32[640,128]{1,0:T(8,128)S(1)} %pad_maximum_fusion.3), channel_id=1, source_target_pairs={{0,8},{8,0},{16,24},{24,16},{32,40},{40,32},{48,56},{56,48},{64,72... | collective-permute-start | bytes 983048 | tf_op jit(solution)/shard_map/ppermute | solution.py:51
  112.0 5.7 %collective-permute-start.11 = (f32[640,128]{1,0:T(8,128)S(1)}, f32[640,128]{1,0:T(8,128)S(1)}, u32[]{:S(2)}, u32[]{:S(2)}) collective-permute-start(f32[640,128]{1,0:T(8,128)S(1)} %collective-permute-done.10), channel_id=1, source_target_pairs={{0,8},{8,0},{16,24},{24,16},{32,40},{40,32},{48,56},{56,48},{64,72... | collective-permute-start | bytes 983048 | tf_op jit(solution)/shard_map/ppermute | solution.py:53
  116.4 3.2 %copy-start.1 = (f32[512,2048]{1,0:T(8,128)S(1)}, f32[512,2048]{1,0:T(8,128)}, u32[]{:S(2)}) copy-start(f32[512,2048]{1,0:T(8,128)} %param.3) | copy-start | bytes 12582916

commit v14 on v11

--- a/solution.py
+++ b/solution.py
@@ -27,23 +27,27 @@
     low = lax.axis_index("row") % per
     col = lax.axis_index("col")
     mine = jnp.where(high == col, panel_rows, jnp.zeros_like(panel_rows))
-    step = 1
-    while step < col_count:
-        pairs = []
-        for src_high in range(col_count):
-            for src_low in range(per):
-                for src_col in range(col_count):
-                    if extra is not None or (src_high ^ src_col) < step:
-                        src = (per * src_high + src_low) * col_count + src_col
-                        dst = (per * (src_high ^ step) + src_low) * col_count + src_col
-                        pairs.append((src, dst))
-        if extra is None:
-            mine = mine + lax.ppermute(mine, ("row", "col"), pairs)
-        else:
-            got = lax.ppermute(jnp.concatenate([mine, extra], axis=0), ("row", "col"), pairs)
+    known = 1
+    while known < col_count:
+        width = 4 if col_count % (known * 4) == 0 else 2
+        sent = mine if extra is None else jnp.concatenate([mine, extra], axis=0)
+        arrived = []
+        for digit in range(1, width):
+            mask = digit * known
+            pairs = []
+            for src_high in range(col_count):
+                for src_low in range(per):
+                    for src_col in range(col_count):
+                        if extra is not None or (src_high ^ src_col) < known:
+                            src = (per * src_high + src_low) * col_count + src_col
+                            dst = (per * (src_high ^ mask) + src_low) * col_count + src_col
+                            pairs.append((src, dst))
+            arrived.append(lax.ppermute(sent, ("row", "col"), pairs))
+        for got in arrived:
             mine = mine + got[:rows_here]
-            extra = extra + got[rows_here:]
-        step *= 2
+            if extra is not None:
+                extra = extra + got[rows_here:]
+        known *= width
     gathered = jnp.zeros((per * rows_here,) + panel_rows.shape[1:], panel_rows.dtype)
     gathered = lax.dynamic_update_slice_in_dim(gathered, mine, low * rows_here, 0)
     core_pairs = [(i, i ^ 1) for i in range(row_count)]

time: 119 us -> 118 us (level)
  starting transfers between devices: 34.5 us -> 27.5 us
  waiting for transfers between devices: 34.6 us -> 39.7 us
    ppermute x2, starting transfers between devices: 13 us -> 5.22 us  [to_columns(): other = lax.ppermute(sent, 'row', core_pairs)]
    ppermute x2, waiting for transfers between devices: 1.72 us -> 5.63 us  [to_columns(): across = lax.ppermute(sent, 'row', [(i, i ^ 2) for i in range(row_count)])]
    ppermute x2, starting transfers between devices: 10 us -> 6.26 us  [to_columns(): diagonal = lax.ppermute(across, 'row', core_pairs)]
    ppermute x6 -> x8, starting transfers between devices: 10.6 us -> 13.2 us  [to_columns(): arrived.append(lax.ppermute(sent, ('row', 'col'), pairs))]
    ppermute x2, starting transfers between devices: 0.91 us -> 2.8 us  [to_columns(): across = lax.ppermute(sent, 'row', [(i, i ^ 2) for i in range(row_count)])]
    ppermute x6 -> x8, waiting for transfers between devices: 30.6 us -> 31.8 us  [to_columns(): arrived.append(lax.ppermute(sent, ('row', 'col'), pairs))]
  transfers between devices with their start and end apart: 12 -> 14, of which waited for: 9 -> 10; matrix products, arithmetic and copies ran while one was open for 0% -> 0% of each run, Pallas kernels for 0% -> 0%
where the time goes in v14:
time: 118 us; the launch traced here: 117 us
  waiting for transfers between devices  39.7 us (34%)
  blocking collectives  36 us (31%)
  starting transfers between devices  27.5 us (23%)
  matrix products  11.1 us (9%)
  other arithmetic  2.27 us (2%)
    ppermute x8, waiting for transfers between devices, to_columns(): arrived.append(lax.ppermute(sent, ('row', 'col'), pairs))  31.8 us
    all_to_all x1, blocking collectives, col_sum_rows(): total = jnp.sum(lax.all_to_all(pieces, 'col', 0, 0, tiled=True), axis=0)  24 us
    ppermute x8, starting transfers between devices, to_columns(): arrived.append(lax.ppermute(sent, ('row', 'col'), pairs))  13.2 us
    all_to_all x1, blocking collectives, col_sum_rows(): lax.all_to_all(spread, 'col', 0, 0, tiled=True).reshape(partial.shape)  12 us
    dot_general x6, matrix products, product(): jnp.dot(left, right, precision=lax.Precision.HIGH, preferred_element_type...  6.33 us
    ppermute x2, starting transfers between devices, to_columns(): diagonal = lax.ppermute(across, 'row', core_pairs)  6.26 us
    ppermute x2, waiting for transfers between devices, to_columns(): across = lax.ppermute(sent, 'row', [(i, i ^ 2) for i in range(row_count)])  5.63 us
    ppermute x2, starting transfers between devices, to_columns(): other = lax.ppermute(sent, 'row', core_pairs)  5.22 us
  transfers between devices with their start and end apart: 14, of which 10 were waited for; matrix products, arithmetic and copies ran while one was open for 0% of the time, Pallas kernels for 0%

profile of v14, /device:TPU:1, one launch (start us, length us, event | category | flops | bytes accessed | tf_op | source)
XLA Modules:
  0.0 117.3 jit_solution(16060320123666290087)
XLA Ops:
  1.0 3.0 %collective-permute-start.1 = (f32[512,128]{1,0:T(8,128)S(1)}, f32[512,128]{1,0:T(8,128)S(1)}, u32[]{:S(2)}, u32[]{:S(2)}) collective-permute-start(f32[512,128]{1,0:T(8,128)S(1)} %broadcast_select_fusion.1), channel_id=1, source_target_pairs={{0,64},{8,72},{16,80},{24,88},{33,97},{41,105},{49,113},{57,121},{... | collective-permute-start | bytes 786440 | tf_op jit(solution)/shard_map/ppermute | solution.py:45
  4.0 3.3 %collective-permute-start.2 = (f32[512,128]{1,0:T(8,128)S(1)}, f32[512,128]{1,0:T(8,128)S(1)}, u32[]{:S(2)}, u32[]{:S(2)}) collective-permute-start(f32[512,128]{1,0:T(8,128)S(1)} %broadcast_select_fusion.1), channel_id=1, source_target_pairs={{0,96},{8,104},{16,112},{24,120},{33,65},{41,73},{49,81},{57,89},{... | collective-permute-start | bytes 786440 | tf_op jit(solution)/shard_map/ppermute | solution.py:45
  7.3 1.3 %collective-permute-start = (f32[512,128]{1,0:T(8,128)S(1)}, f32[512,128]{1,0:T(8,128)S(1)}, u32[]{:S(2)}, u32[]{:S(2)}) collective-permute-start(f32[512,128]{1,0:T(8,128)S(1)} %broadcast_select_fusion.1), channel_id=1, source_target_pairs={{0,32},{8,40},{16,48},{24,56},{33,1},{41,9},{49,17},{57,25},{66,98... | collective-permute-start | bytes 786440 | tf_op jit(solution)/shard_map/ppermute | solution.py:45
  8.6 5.3 %collective-permute-done.2 = f32[512,128]{1,0:T(8,128)S(1)} collective-permute-done((f32[512,128]{1,0:T(8,128)S(1)}, f32[512,128]{1,0:T(8,128)S(1)}, u32[]{:S(2)}, u32[]{:S(2)}) %collective-permute-start.2) | collective-permute-done | bytes 262176 | tf_op jit(solution)/shard_map/ppermute | solution.py:45
  14.9 1.3 %collective-permute-start.3 = (f32[512,128]{1,0:T(8,128)S(1)}, f32[512,128]{1,0:T(8,128)S(1)}, u32[]{:S(2)}, u32[]{:S(2)}) collective-permute-start(f32[512,128]{1,0:T(8,128)S(1)} %add_add_fusion), channel_id=1, source_target_pairs={{0,128},{1,129},{2,130},{3,131},{8,136},{9,137},{10,138},{11,139},... | collective-permute-start | bytes 786440 | tf_op jit(solution)/shard_map/ppermute | solution.py:45
  16.2 3.6 %collective-permute-done.3 = f32[512,128]{1,0:T(8,128)S(1)} collective-permute-done((f32[512,128]{1,0:T(8,128)S(1)}, f32[512,128]{1,0:T(8,128)S(1)}, u32[]{:S(2)}, u32[]{:S(2)}) %collective-permute-start.3) | collective-permute-done | bytes 262176 | tf_op jit(solution)/shard_map/ppermute | solution.py:45
  20.0 2.7 %collective-permute-start.5 = (f32[512,128]{1,0:T(8,128)S(1)}, f32[512,128]{1,0:T(8,128)S(1)}, u32[]{:S(2)}, u32[]{:S(2)}) collective-permute-start(f32[512,128]{1,0:T(8,128)S(1)} %get-tuple-element.8), channel_id=1, source_target_pairs={{0,16},{8,24},{16,0},{24,8},{32,48},{40,56},{48,32},{56,40},{64,80... | collective-permute-start | bytes 786440 | tf_op jit(solution)/shard_map/ppermute | solution.py:56
  22.7 2.5 %collective-permute-start.4 = (f32[512,128]{1,0:T(8,128)S(1)}, f32[512,128]{1,0:T(8,128)S(1)}, u32[]{:S(2)}, u32[]{:S(2)}) collective-permute-start(f32[512,128]{1,0:T(8,128)S(1)} %get-tuple-element.8), channel_id=1, source_target_pairs={{0,8},{8,0},{16,24},{24,16},{32,40},{40,32},{48,56},{56,48},{64,72... | collective-permute-start | bytes 786440 | tf_op jit(solution)/shard_map/ppermute | solution.py:55
  25.1 2.0 %collective-permute-done.5 = f32[512,128]{1,0:T(8,128)S(1)} collective-permute-done((f32[512,128]{1,0:T(8,128)S(1)}, f32[512,128]{1,0:T(8,128)S(1)}, u32[]{:S(2)}, u32[]{:S(2)}) %collective-permute-start.5) | collective-permute-done | bytes 262176 | tf_op jit(solution)/shard_map/ppermute | solution.py:56
  27.1 2.8 %collective-permute-start.6 = (f32[512,128]{1,0:T(8,128)S(1)}, f32[512,128]{1,0:T(8,128)S(1)}, u32[]{:S(2)}, u32[]{:S(2)}) collective-permute-start(f32[512,128]{1,0:T(8,128)S(1)} %collective-permute-done.5), channel_id=1, source_target_pairs={{0,8},{8,0},{16,24},{24,16},{32,40},{40,32},{48,56},{56,48},{64,72... | collective-permute-start | bytes 786440 | tf_op jit(solution)/shard_map/ppermute | solution.py:57
  31.1 4.5 %convolution_bitcast_fusion = f32[512,128]{0,1:T(8,128)S(1)} fusion(f32[2048,128]{1,0:T(8,128)S(1)} %constant_dynamic-update-slice_fusion.1, f32[512,2048]{1,0:T(8,128)} %param.3), kind=kOutput, calls=%fused_computation.9 | convolution fusion | flops 805306368 | bytes 5505024 | tf_op jit(solution)/shard_map/dot_general | solution.py:8
  35.7 24.0 %all_to_all.11 = f32[8,64,128]{2,1,0:T(8,128)S(1)} all-to-all(f32[8,64,128]{2,1,0:T(8,128)S(1)} %bitcast.30), channel_id=1, replica_groups=mesh['row'=32,'col'=8] {'col'}, dimensions={0} | all-to-all | bytes 524288 | tf_op jit(solution)/shard_map/all_to_all | solution.py:69
  59.8 12.0 %all_to_all.10 = f32[8,64,128]{2,1,0:T(8,128)S(1)} all-to-all(f32[8,64,128]{2,1,0:T(8,128)S(1)} %broadcast_in_dim.2), channel_id=1, replica_groups=mesh['row'=32,'col'=8] {'col'}, dimensions={0} | all-to-all | bytes 524288 | tf_op jit(solution)/shard_map/all_to_all | solution.py:71
  72.3 2.0 %collective-permute-start.9 = (f32[640,128]{1,0:T(8,128)S(1)}, f32[640,128]{1,0:T(8,128)S(1)}, u32[]{:S(2)}, u32[]{:S(2)}) collective-permute-start(f32[640,128]{1,0:T(8,128)S(1)} %pad_maximum_fusion), channel_id=1, source_target_pairs={{0,96},{1,97},{2,98},{3,99},{4,100},{5,101},{6,102},{7,103},{8,104... | collective-permute-start | bytes 983048 | tf_op jit(solution)/shard_map/ppermute | solution.py:45
  74.6 1.9 %collective-permute-start.7 = (f32[640,128]{1,0:T(8,128)S(1)}, f32[640,128]{1,0:T(8,128)S(1)}, u32[]{:S(2)}, u32[]{:S(2)}) collective-permute-start(f32[640,128]{1,0:T(8,128)S(1)} %pad_maximum_fusion), channel_id=1, source_target_pairs={{0,32},{1,33},{2,34},{3,35},{4,36},{5,37},{6,38},{7,39},{8,40},{9,... | collective-permute-start | bytes 983048 | tf_op jit(solution)/shard_map/ppermute | solution.py:45
  76.5 4.3 %collective-permute-done.9 = f32[640,128]{1,0:T(8,128)S(1)} collective-permute-done((f32[640,128]{1,0:T(8,128)S(1)}, f32[640,128]{1,0:T(8,128)S(1)}, u32[]{:S(2)}, u32[]{:S(2)}) %collective-permute-start.9) | collective-permute-done | bytes 327712 | tf_op jit(solution)/shard_map/ppermute | solution.py:45
  80.8 5.4 %collective-permute-done.8 = f32[640,128]{1,0:T(8,128)S(1)} collective-permute-done((f32[640,128]{1,0:T(8,128)S(1)}, f32[640,128]{1,0:T(8,128)S(1)}, u32[]{:S(2)}, u32[]{:S(2)}) %collective-permute-start.8) | collective-permute-done | bytes 327712 | tf_op jit(solution)/shard_map/ppermute | solution.py:45
  86.2 4.2 %collective-permute-done.7 = f32[640,128]{1,0:T(8,128)S(1)} collective-permute-done((f32[640,128]{1,0:T(8,128)S(1)}, f32[640,128]{1,0:T(8,128)S(1)}, u32[]{:S(2)}, u32[]{:S(2)}) %collective-permute-start.7) | collective-permute-done | bytes 327712 | tf_op jit(solution)/shard_map/ppermute | solution.py:45
  90.5 9.1 %collective-permute-done.10 = f32[640,128]{1,0:T(8,128)S(1)} collective-permute-done((f32[640,128]{1,0:T(8,128)S(1)}, f32[640,128]{1,0:T(8,128)S(1)}, u32[]{:S(2)}, u32[]{:S(2)}) %collective-permute-start.10) | collective-permute-done | bytes 327712 | tf_op jit(solution)/shard_map/ppermute | solution.py:45
  99.9 2.7 %collective-permute-start.11 = (f32[640,128]{1,0:T(8,128)S(1)}, f32[640,128]{1,0:T(8,128)S(1)}, u32[]{:S(2)}, u32[]{:S(2)}) collective-permute-start(f32[640,128]{1,0:T(8,128)S(1)} %pad_maximum_fusion.2), channel_id=1, source_target_pairs={{0,8},{8,0},{16,24},{24,16},{32,40},{40,32},{48,56},{56,48},{64,72... | collective-permute-start | bytes 983048 | tf_op jit(solution)/shard_map/ppermute | solution.py:55
  102.9 3.7 %collective-permute-done.12 = f32[640,128]{1,0:T(8,128)S(1)} collective-permute-done((f32[640,128]{1,0:T(8,128)S(1)}, f32[640,128]{1,0:T(8,128)S(1)}, u32[]{:S(2)}, u32[]{:S(2)}) %collective-permute-start.12) | collective-permute-done | bytes 327712 | tf_op jit(solution)/shard_map/ppermute | solution.py:56
  106.6 3.4 %collective-permute-start.13 = (f32[640,128]{1,0:T(8,128)S(1)}, f32[640,128]{1,0:T(8,128)S(1)}, u32[]{:S(2)}, u32[]{:S(2)}) collective-permute-start(f32[640,128]{1,0:T(8,128)S(1)} %collective-permute-done.12), channel_id=1, source_target_pairs={{0,8},{8,0},{16,24},{24,16},{32,40},{40,32},{48,56},{56,48},{64,72... | collective-permute-start | bytes 983048 | tf_op jit(solution)/shard_map/ppermute | solution.py:57
  110.1 1.2 %collective-permute-done.13 = f32[640,128]{1,0:T(8,128)S(1)} collective-permute-done((f32[640,128]{1,0:T(8,128)S(1)}, f32[640,128]{1,0:T(8,128)S(1)}, u32[]{:S(2)}, u32[]{:S(2)}) %collective-permute-start.13) | collective-permute-done | bytes 327712 | tf_op jit(solution)/shard_map/ppermute | solution.py:57
  113.2 4.1 %convolution_subtract_fusion = f32[512,2048]{1,0:T(8,128)} fusion(f32[512,2048]{1,0:T(8,128)S(1)} %copy-done.1, f32[2048,128]{1,0:T(8,128)S(1)} %constant_dynamic-update-slice_fusion.1, f32[2048,128]{1,0:T(8,128)S(1)} %convolution_subtract_fusion.1, f32[512,128]{1,0:T(8,128)S(1)} %fusion.4, f32[512,128]{1,0:T(8,128)S(1)} %copy-done.2), kind=kOutput, calls=%fused_computation | convolution fusion | flops 1612316672 | bytes 11010048 | tf_op jit(solution)/shard_map/dot_general | solution.py:83
  (43 shorter events, 6.8 us)
Async XLA Ops:
  0.0 102.6 %copy-start = (f32[128,128]{1,0:T(8,128)S(1)}, f32[128,128]{1,0:T(8,128)}, u32[]{:S(2)}) copy-start(f32[128,128]{1,0:T(8,128)} %param.5) | copy-start | bytes 196612
  1.0 7.6 %collective-permute-start.1 = (f32[512,128]{1,0:T(8,128)S(1)}, f32[512,128]{1,0:T(8,128)S(1)}, u32[]{:S(2)}, u32[]{:S(2)}) collective-permute-start(f32[512,128]{1,0:T(8,128)S(1)} %broadcast_select_fusion.1), channel_id=1, source_target_pairs={{0,64},{8,72},{16,80},{24,88},{33,97},{41,105},{49,113},{57,121},{... | collective-permute-start | bytes 786440 | tf_op jit(solution)/shard_map/ppermute | solution.py:45
  4.0 9.9 %collective-permute-start.2 = (f32[512,128]{1,0:T(8,128)S(1)}, f32[512,128]{1,0:T(8,128)S(1)}, u32[]{:S(2)}, u32[]{:S(2)}) collective-permute-start(f32[512,128]{1,0:T(8,128)S(1)} %broadcast_select_fusion.1), channel_id=1, source_target_pairs={{0,96},{8,104},{16,112},{24,120},{33,65},{41,73},{49,81},{57,89},{... | collective-permute-start | bytes 786440 | tf_op jit(solution)/shard_map/ppermute | solution.py:45
  7.3 6.6 %collective-permute-start = (f32[512,128]{1,0:T(8,128)S(1)}, f32[512,128]{1,0:T(8,128)S(1)}, u32[]{:S(2)}, u32[]{:S(2)}) collective-permute-start(f32[512,128]{1,0:T(8,128)S(1)} %broadcast_select_fusion.1), channel_id=1, source_target_pairs={{0,32},{8,40},{16,48},{24,56},{33,1},{41,9},{49,17},{57,25},{66,98... | collective-permute-start | bytes 786440 | tf_op jit(solution)/shard_map/ppermute | solution.py:45
  14.9 4.9 %collective-permute-start.3 = (f32[512,128]{1,0:T(8,128)S(1)}, f32[512,128]{1,0:T(8,128)S(1)}, u32[]{:S(2)}, u32[]{:S(2)}) collective-permute-start(f32[512,128]{1,0:T(8,128)S(1)} %add_add_fusion), channel_id=1, source_target_pairs={{0,128},{1,129},{2,130},{3,131},{8,136},{9,137},{10,138},{11,139},... | collective-permute-start | bytes 786440 | tf_op jit(solution)/shard_map/ppermute | solution.py:45
  20.0 7.1 %collective-permute-start.5 = (f32[512,128]{1,0:T(8,128)S(1)}, f32[512,128]{1,0:T(8,128)S(1)}, u32[]{:S(2)}, u32[]{:S(2)}) collective-permute-start(f32[512,128]{1,0:T(8,128)S(1)} %get-tuple-element.8), channel_id=1, source_target_pairs={{0,16},{8,24},{16,0},{24,8},{32,48},{40,56},{48,32},{56,40},{64,80... | collective-permute-start | bytes 786440 | tf_op jit(solution)/shard_map/ppermute | solution.py:56
  22.7 7.3 %collective-permute-start.4 = (f32[512,128]{1,0:T(8,128)S(1)}, f32[512,128]{1,0:T(8,128)S(1)}, u32[]{:S(2)}, u32[]{:S(2)}) collective-permute-start(f32[512,128]{1,0:T(8,128)S(1)} %get-tuple-element.8), channel_id=1, source_target_pairs={{0,8},{8,0},{16,24},{24,16},{32,40},{40,32},{48,56},{56,48},{64,72... | collective-permute-start | bytes 786440 | tf_op jit(solution)/shard_map/ppermute | solution.py:55
  27.1 4.0 %collective-permute-start.6 = (f32[512,128]{1,0:T(8,128)S(1)}, f32[512,128]{1,0:T(8,128)S(1)}, u32[]{:S(2)}, u32[]{:S(2)}) collective-permute-start(f32[512,128]{1,0:T(8,128)S(1)} %collective-permute-done.5), channel_id=1, source_target_pairs={{0,8},{8,0},{16,24},{24,16},{32,40},{40,32},{48,56},{56,48},{64,72... | collective-permute-start | bytes 786440 | tf_op jit(solution)/shard_map/ppermute | solution.py:57
  30.0 41.8 %copy-start.2 = (f32[512,128]{1,0:T(8,128)S(1)}, f32[512,128]{1,0:T(8,128)}, u32[]{:S(2)}) copy-start(f32[512,128]{1,0:T(8,128)} %param.4) | copy-start | bytes 786436
  72.3 8.5 %collective-permute-start.9 = (f32[640,128]{1,0:T(8,128)S(1)}, f32[640,128]{1,0:T(8,128)S(1)}, u32[]{:S(2)}, u32[]{:S(2)}) collective-permute-start(f32[640,128]{1,0:T(8,128)S(1)} %pad_maximum_fusion), channel_id=1, source_target_pairs={{0,96},{1,97},{2,98},{3,99},{4,100},{5,101},{6,102},{7,103},{8,104... | collective-permute-start | bytes 983048 | tf_op jit(solution)/shard_map/ppermute | solution.py:45
  74.3 11.9 %collective-permute-start.8 = (f32[640,128]{1,0:T(8,128)S(1)}, f32[640,128]{1,0:T(8,128)S(1)}, u32[]{:S(2)}, u32[]{:S(2)}) collective-permute-start(f32[640,128]{1,0:T(8,128)S(1)} %pad_maximum_fusion), channel_id=1, source_target_pairs={{0,64},{1,65},{2,66},{3,67},{4,68},{5,69},{6,70},{7,71},{8,72},{9,... | collective-permute-start | bytes 983048 | tf_op jit(solution)/shard_map/ppermute | solution.py:45
  74.6 15.8 %collective-permute-start.7 = (f32[640,128]{1,0:T(8,128)S(1)}, f32[640,128]{1,0:T(8,128)S(1)}, u32[]{:S(2)}, u32[]{:S(2)}) collective-permute-start(f32[640,128]{1,0:T(8,128)S(1)} %pad_maximum_fusion), channel_id=1, source_target_pairs={{0,32},{1,33},{2,34},{3,35},{4,36},{5,37},{6,38},{7,39},{8,40},{9,... | collective-permute-start | bytes 983048 | tf_op jit(solution)/shard_map/ppermute | solution.py:45
  90.4 9.2 %collective-permute-start.10 = (f32[640,128]{1,0:T(8,128)S(1)}, f32[640,128]{1,0:T(8,128)S(1)}, u32[]{:S(2)}, u32[]{:S(2)}) collective-permute-start(f32[640,128]{1,0:T(8,128)S(1)} %pad_maximum_fusion.1), channel_id=1, source_target_pairs={{0,128},{1,129},{2,130},{3,131},{4,132},{5,133},{6,134},{7,135},{8... | collective-permute-start | bytes 983048 | tf_op jit(solution)/shard_map/ppermute | solution.py:45
  99.8 6.8 %collective-permute-start.12 = (f32[640,128]{1,0:T(8,128)S(1)}, f32[640,128]{1,0:T(8,128)S(1)}, u32[]{:S(2)}, u32[]{:S(2)}) collective-permute-start(f32[640,128]{1,0:T(8,128)S(1)} %pad_maximum_fusion.2), channel_id=1, source_target_pairs={{0,16},{8,24},{16,0},{24,8},{32,48},{40,56},{48,32},{56,40},{64,80... | collective-permute-start | bytes 983048 | tf_op jit(solution)/shard_map/ppermute | solution.py:56
  99.9 10.1 %collective-permute-start.11 = (f32[640,128]{1,0:T(8,128)S(1)}, f32[640,128]{1,0:T(8,128)S(1)}, u32[]{:S(2)}, u32[]{:S(2)}) collective-permute-start(f32[640,128]{1,0:T(8,128)S(1)} %pad_maximum_fusion.2), channel_id=1, source_target_pairs={{0,8},{8,0},{16,24},{24,16},{32,40},{40,32},{48,56},{56,48},{64,72... | collective-permute-start | bytes 983048 | tf_op jit(solution)/shard_map/ppermute | solution.py:55
  106.6 4.7 %collective-permute-start.13 = (f32[640,128]{1,0:T(8,128)S(1)}, f32[640,128]{1,0:T(8,128)S(1)}, u32[]{:S(2)}, u32[]{:S(2)}) collective-permute-start(f32[640,128]{1,0:T(8,128)S(1)} %collective-permute-done.12), channel_id=1, source_target_pairs={{0,8},{8,0},{16,24},{24,16},{32,40},{40,32},{48,56},{56,48},{64,72... | collective-permute-start | bytes 983048 | tf_op jit(solution)/shard_map/ppermute | solution.py:57
  110.0 3.2 %copy-start.1 = (f32[512,2048]{1,0:T(8,128)S(1)}, f32[512,2048]{1,0:T(8,128)}, u32[]{:S(2)}) copy-start(f32[512,2048]{1,0:T(8,128)} %param.3) | copy-start | bytes 12582916

commit v15 on v14

--- a/solution.py
+++ b/solution.py
@@ -71,19 +71,23 @@
     return lax.all_to_all(spread, "col", 0, 0, tiled=True).reshape(partial.shape)
 
 
+def outer_product(left, right):
+    return lax.dot_general(
+        left, right, (((1,), (1,)), ((), ())),
+        precision=lax.Precision.HIGH, preferred_element_type=jnp.float32,
+    )
+
+
 def shards(matrix, vectors, tfactor):
     vec_cols, _ = to_columns(vectors)
     x_rows = col_sum_rows(product(matrix, vec_cols))
+    y_rows = product(x_rows, tfactor)
+    partly = lax.optimization_barrier(matrix - outer_product(y_rows, vec_cols))
     x_cols, s_full = to_columns(x_rows, inner_product(vectors, x_rows))
     coupling = inner_product(tfactor, product(s_full, tfactor))
-    w_rows = product(x_rows, tfactor) - 0.5 * product(vectors, coupling)
-    w_cols = product(x_cols, tfactor) - 0.5 * product(vec_cols, coupling)
-    left = jnp.concatenate([vectors, w_rows], axis=1)
-    right = jnp.concatenate([w_cols, vec_cols], axis=1)
-    return matrix - lax.dot_general(
-        left, right, (((1,), (1,)), ((), ())),
-        precision=lax.Precision.HIGH, preferred_element_type=jnp.float32,
-    )
+    sym = 0.5 * (coupling + coupling.T)
+    w_cols = product(x_cols, tfactor) - product(vec_cols, sym)
+    return partly - outer_product(vectors, w_cols)
 
 
 def solution(mesh):

time: 118 us -> 118 us (level)
  waiting for transfers between devices: 39.7 us -> 35.8 us
  other arithmetic: 2.27 us -> 5.06 us
  matrix products: 11.1 us -> 12.5 us
    ppermute x2, waiting for transfers between devices: 5.63 us -> 1.96 us  [to_columns(): across = lax.ppermute(sent, 'row', [(i, i ^ 2) for i in range(row_count)])]
    sub x0 -> x1, other arithmetic: none -> 2.77 us  [shards(): return partly - outer_product(vectors, w_cols)]
    dot_general x1 -> x2, matrix products: 4.1 us -> 5.8 us  [outer_product(): lax.dot_general(left, right, (((1,), (1,)), ((), ())), precision=lax.Prec...]
    dot_general x6 -> x5, matrix products: 6.33 us -> 6.04 us  [product(): jnp.dot(left, right, precision=lax.Precision.HIGH, preferred_element_type...]
  transfers between devices with their start and end apart: 14 -> 14, of which waited for: 10 -> 9; matrix products, arithmetic and copies ran while one was open for 0% -> 4% of each run, Pallas kernels for 0% -> 0%
where the time goes in v15:
time: 118 us
  blocking collectives  36.3 us (31%)
  waiting for transfers between devices  35.8 us (30%)
  starting transfers between devices  27.5 us (23%)
  matrix products  12.5 us (11%)
  other arithmetic  5.06 us (4%)
    ppermute x8, waiting for transfers between devices, to_columns(): arrived.append(lax.ppermute(sent, ('row', 'col'), pairs))  31.5 us
    all_to_all x1, blocking collectives, col_sum_rows(): total = jnp.sum(lax.all_to_all(pieces, 'col', 0, 0, tiled=True), axis=0)  24 us
    ppermute x8, starting transfers between devices, to_columns(): arrived.append(lax.ppermute(sent, ('row', 'col'), pairs))  13.2 us
    all_to_all x1, blocking collectives, col_sum_rows(): lax.all_to_all(spread, 'col', 0, 0, tiled=True).reshape(partial.shape)  12.3 us
    ppermute x2, starting transfers between devices, to_columns(): diagonal = lax.ppermute(across, 'row', core_pairs)  6.21 us
    dot_general x5, matrix products, product(): jnp.dot(left, right, precision=lax.Precision.HIGH, preferred_element_type...  6.04 us
    dot_general x2, matrix products, outer_product(): lax.dot_general(left, right, (((1,), (1,)), ((), ())), precision=lax.Prec...  5.8 us
    ppermute x2, starting transfers between devices, to_columns(): other = lax.ppermute(sent, 'row', core_pairs)  5.22 us
  transfers between devices with their start and end apart: 14, of which 9 were waited for; matrix products, arithmetic and copies ran while one was open for 4% of the time, Pallas kernels for 0%

profile of v15, /device:TPU:1, one launch (start us, length us, event | category | flops | bytes accessed | tf_op | source)
XLA Modules:
  0.0 117.9 jit_solution(6161327181088766649)
XLA Ops:
  1.0 3.0 %collective-permute-start.1 = (f32[512,128]{1,0:T(8,128)S(1)}, f32[512,128]{1,0:T(8,128)S(1)}, u32[]{:S(2)}, u32[]{:S(2)}) collective-permute-start(f32[512,128]{1,0:T(8,128)S(1)} %broadcast_select_fusion.1), channel_id=1, source_target_pairs={{0,64},{8,72},{16,80},{24,88},{33,97},{41,105},{49,113},{57,121},{... | collective-permute-start | bytes 786440 | tf_op jit(solution)/shard_map/ppermute | solution.py:45
  4.0 3.3 %collective-permute-start.2 = (f32[512,128]{1,0:T(8,128)S(1)}, f32[512,128]{1,0:T(8,128)S(1)}, u32[]{:S(2)}, u32[]{:S(2)}) collective-permute-start(f32[512,128]{1,0:T(8,128)S(1)} %broadcast_select_fusion.1), channel_id=1, source_target_pairs={{0,96},{8,104},{16,112},{24,120},{33,65},{41,73},{49,81},{57,89},{... | collective-permute-start | bytes 786440 | tf_op jit(solution)/shard_map/ppermute | solution.py:45
  7.3 1.3 %collective-permute-start = (f32[512,128]{1,0:T(8,128)S(1)}, f32[512,128]{1,0:T(8,128)S(1)}, u32[]{:S(2)}, u32[]{:S(2)}) collective-permute-start(f32[512,128]{1,0:T(8,128)S(1)} %broadcast_select_fusion.1), channel_id=1, source_target_pairs={{0,32},{8,40},{16,48},{24,56},{33,1},{41,9},{49,17},{57,25},{66,98... | collective-permute-start | bytes 786440 | tf_op jit(solution)/shard_map/ppermute | solution.py:45
  8.6 5.3 %collective-permute-done.2 = f32[512,128]{1,0:T(8,128)S(1)} collective-permute-done((f32[512,128]{1,0:T(8,128)S(1)}, f32[512,128]{1,0:T(8,128)S(1)}, u32[]{:S(2)}, u32[]{:S(2)}) %collective-permute-start.2) | collective-permute-done | bytes 262176 | tf_op jit(solution)/shard_map/ppermute | solution.py:45
  14.9 1.3 %collective-permute-start.3 = (f32[512,128]{1,0:T(8,128)S(1)}, f32[512,128]{1,0:T(8,128)S(1)}, u32[]{:S(2)}, u32[]{:S(2)}) collective-permute-start(f32[512,128]{1,0:T(8,128)S(1)} %add_add_fusion), channel_id=1, source_target_pairs={{0,128},{1,129},{2,130},{3,131},{8,136},{9,137},{10,138},{11,139},... | collective-permute-start | bytes 786440 | tf_op jit(solution)/shard_map/ppermute | solution.py:45
  16.2 3.6 %collective-permute-done.3 = f32[512,128]{1,0:T(8,128)S(1)} collective-permute-done((f32[512,128]{1,0:T(8,128)S(1)}, f32[512,128]{1,0:T(8,128)S(1)}, u32[]{:S(2)}, u32[]{:S(2)}) %collective-permute-start.3) | collective-permute-done | bytes 262176 | tf_op jit(solution)/shard_map/ppermute | solution.py:45
  20.0 2.7 %collective-permute-start.5 = (f32[512,128]{1,0:T(8,128)S(1)}, f32[512,128]{1,0:T(8,128)S(1)}, u32[]{:S(2)}, u32[]{:S(2)}) collective-permute-start(f32[512,128]{1,0:T(8,128)S(1)} %get-tuple-element.8), channel_id=1, source_target_pairs={{0,16},{8,24},{16,0},{24,8},{32,48},{40,56},{48,32},{56,40},{64,80... | collective-permute-start | bytes 786440 | tf_op jit(solution)/shard_map/ppermute | solution.py:56
  22.7 2.5 %collective-permute-start.4 = (f32[512,128]{1,0:T(8,128)S(1)}, f32[512,128]{1,0:T(8,128)S(1)}, u32[]{:S(2)}, u32[]{:S(2)}) collective-permute-start(f32[512,128]{1,0:T(8,128)S(1)} %get-tuple-element.8), channel_id=1, source_target_pairs={{0,8},{8,0},{16,24},{24,16},{32,40},{40,32},{48,56},{56,48},{64,72... | collective-permute-start | bytes 786440 | tf_op jit(solution)/shard_map/ppermute | solution.py:55
  25.1 2.0 %collective-permute-done.5 = f32[512,128]{1,0:T(8,128)S(1)} collective-permute-done((f32[512,128]{1,0:T(8,128)S(1)}, f32[512,128]{1,0:T(8,128)S(1)}, u32[]{:S(2)}, u32[]{:S(2)}) %collective-permute-start.5) | collective-permute-done | bytes 262176 | tf_op jit(solution)/shard_map/ppermute | solution.py:56
  27.1 2.8 %collective-permute-start.6 = (f32[512,128]{1,0:T(8,128)S(1)}, f32[512,128]{1,0:T(8,128)S(1)}, u32[]{:S(2)}, u32[]{:S(2)}) collective-permute-start(f32[512,128]{1,0:T(8,128)S(1)} %collective-permute-done.5), channel_id=1, source_target_pairs={{0,8},{8,0},{16,24},{24,16},{32,40},{40,32},{48,56},{56,48},{64,72... | collective-permute-start | bytes 786440 | tf_op jit(solution)/shard_map/ppermute | solution.py:57
  31.1 4.5 %convolution_bitcast_fusion = f32[512,128]{0,1:T(8,128)S(1)} fusion(f32[2048,128]{1,0:T(8,128)S(1)} %constant_dynamic-update-slice_fusion.1, f32[512,2048]{1,0:T(8,128)} %param.3), kind=kOutput, calls=%fused_computation.3 | convolution fusion | flops 805306368 | bytes 5505024 | tf_op jit(solution)/shard_map/dot_general | solution.py:8
  35.7 24.0 %all_to_all.11 = f32[8,64,128]{2,1,0:T(8,128)S(1)} all-to-all(f32[8,64,128]{2,1,0:T(8,128)S(1)} %bitcast.34), channel_id=1, replica_groups=mesh['row'=32,'col'=8] {'col'}, dimensions={0} | all-to-all | bytes 524288 | tf_op jit(solution)/shard_map/all_to_all | solution.py:69
  59.8 12.3 %all_to_all.10 = f32[8,64,128]{2,1,0:T(8,128)S(1)} all-to-all(f32[8,64,128]{2,1,0:T(8,128)S(1)} %broadcast_in_dim.2), channel_id=1, replica_groups=mesh['row'=32,'col'=8] {'col'}, dimensions={0} | all-to-all | bytes 524288 | tf_op jit(solution)/shard_map/all_to_all | solution.py:71
  72.5 2.0 %collective-permute-start.9 = (f32[640,128]{1,0:T(8,128)S(1)}, f32[640,128]{1,0:T(8,128)S(1)}, u32[]{:S(2)}, u32[]{:S(2)}) collective-permute-start(f32[640,128]{1,0:T(8,128)S(1)} %pad_maximum_fusion), channel_id=1, source_target_pairs={{0,96},{1,97},{2,98},{3,99},{4,100},{5,101},{6,102},{7,103},{8,104... | collective-permute-start | bytes 983048 | tf_op jit(solution)/shard_map/ppermute | solution.py:45
  74.8 1.9 %collective-permute-start.7 = (f32[640,128]{1,0:T(8,128)S(1)}, f32[640,128]{1,0:T(8,128)S(1)}, u32[]{:S(2)}, u32[]{:S(2)}) collective-permute-start(f32[640,128]{1,0:T(8,128)S(1)} %pad_maximum_fusion), channel_id=1, source_target_pairs={{0,32},{1,33},{2,34},{3,35},{4,36},{5,37},{6,38},{7,39},{8,40},{9,... | collective-permute-start | bytes 983048 | tf_op jit(solution)/shard_map/ppermute | solution.py:45
  76.8 4.3 %collective-permute-done.9 = f32[640,128]{1,0:T(8,128)S(1)} collective-permute-done((f32[640,128]{1,0:T(8,128)S(1)}, f32[640,128]{1,0:T(8,128)S(1)}, u32[]{:S(2)}, u32[]{:S(2)}) %collective-permute-start.9) | collective-permute-done | bytes 327712 | tf_op jit(solution)/shard_map/ppermute | solution.py:45
  81.0 5.4 %collective-permute-done.8 = f32[640,128]{1,0:T(8,128)S(1)} collective-permute-done((f32[640,128]{1,0:T(8,128)S(1)}, f32[640,128]{1,0:T(8,128)S(1)}, u32[]{:S(2)}, u32[]{:S(2)}) %collective-permute-start.8) | collective-permute-done | bytes 327712 | tf_op jit(solution)/shard_map/ppermute | solution.py:45
  86.4 4.2 %collective-permute-done.7 = f32[640,128]{1,0:T(8,128)S(1)} collective-permute-done((f32[640,128]{1,0:T(8,128)S(1)}, f32[640,128]{1,0:T(8,128)S(1)}, u32[]{:S(2)}, u32[]{:S(2)}) %collective-permute-start.7) | collective-permute-done | bytes 327712 | tf_op jit(solution)/shard_map/ppermute | solution.py:45
  91.1 8.8 %collective-permute-done.10 = f32[640,128]{1,0:T(8,128)S(1)} collective-permute-done((f32[640,128]{1,0:T(8,128)S(1)}, f32[640,128]{1,0:T(8,128)S(1)}, u32[]{:S(2)}, u32[]{:S(2)}) %collective-permute-start.10) | collective-permute-done | bytes 327712 | tf_op jit(solution)/shard_map/ppermute | solution.py:45
  100.2 2.7 %collective-permute-start.11 = (f32[640,128]{1,0:T(8,128)S(1)}, f32[640,128]{1,0:T(8,128)S(1)}, u32[]{:S(2)}, u32[]{:S(2)}) collective-permute-start(f32[640,128]{1,0:T(8,128)S(1)} %pad_maximum_fusion.2), channel_id=1, source_target_pairs={{0,8},{8,0},{16,24},{24,16},{32,40},{40,32},{48,56},{56,48},{64,72... | collective-permute-start | bytes 983048 | tf_op jit(solution)/shard_map/ppermute | solution.py:55
  102.9 4.0 %convolution_subtract_fusion = f32[512,2048]{1,0:T(8,128)} fusion(f32[512,2048]{1,0:T(8,128)S(1)} %copy-done.2, f32[512,128]{1,0:T(8,128)S(1)} %fusion.6, f32[2048,128]{1,0:T(8,128)S(1)} %constant_dynamic-update-slice_fusion.1), kind=kOutput, calls=%fused_computation.1 | convolution fusion | flops 806354944 | bytes 9699328 | tf_op jit(solution)/shard_map/dot_general | solution.py:75
  106.9 3.4 %collective-permute-start.13 = (f32[640,128]{1,0:T(8,128)S(1)}, f32[640,128]{1,0:T(8,128)S(1)}, u32[]{:S(2)}, u32[]{:S(2)}) collective-permute-start(f32[640,128]{1,0:T(8,128)S(1)} %collective-permute-done.12), channel_id=1, source_target_pairs={{0,8},{8,0},{16,24},{24,16},{32,40},{40,32},{48,56},{56,48},{64,72... | collective-permute-start | bytes 983048 | tf_op jit(solution)/shard_map/ppermute | solution.py:57
  113.3 1.8 %fusion.8 = f32[2048,512]{0,1:T(8,128)S(1)} fusion(f32[2048,128]{1,0:T(8,128)S(1)} %convolution_subtract_fusion.1, f32[512,128]{1,0:T(8,128)S(1)} %copy-done.3), kind=kOutput, calls=%fused_computation.38 | convolution fusion | flops 805306368 | bytes 5505024 | tf_op jit(solution)/shard_map/dot_general | solution.py:75
  115.2 2.8 %bitcast_subtract_fusion = f32[512,2048]{1,0:T(8,128)} fusion(f32[512,2048]{1,0:T(8,128)S(1)} %copy-done.1, f32[2048,512]{0,1:T(8,128)S(1)} %fusion.8), kind=kLoop, calls=%fused_computation | loop fusion | flops 1048576 | bytes 12582912 | tf_op jit(solution)/shard_map/sub | solution.py:90
  (47 shorter events, 7.8 us)
Async XLA Ops:
  0.0 90.8 %copy-start = (f32[128,128]{1,0:T(8,128)S(1)}, f32[128,128]{1,0:T(8,128)}, u32[]{:S(2)}) copy-start(f32[128,128]{1,0:T(8,128)} %param.5) | copy-start | bytes 196612
  1.0 7.6 %collective-permute-start.1 = (f32[512,128]{1,0:T(8,128)S(1)}, f32[512,128]{1,0:T(8,128)S(1)}, u32[]{:S(2)}, u32[]{:S(2)}) collective-permute-start(f32[512,128]{1,0:T(8,128)S(1)} %broadcast_select_fusion.1), channel_id=1, source_target_pairs={{0,64},{8,72},{16,80},{24,88},{33,97},{41,105},{49,113},{57,121},{... | collective-permute-start | bytes 786440 | tf_op jit(solution)/shard_map/ppermute | solution.py:45
  4.0 9.9 %collective-permute-start.2 = (f32[512,128]{1,0:T(8,128)S(1)}, f32[512,128]{1,0:T(8,128)S(1)}, u32[]{:S(2)}, u32[]{:S(2)}) collective-permute-start(f32[512,128]{1,0:T(8,128)S(1)} %broadcast_select_fusion.1), channel_id=1, source_target_pairs={{0,96},{8,104},{16,112},{24,120},{33,65},{41,73},{49,81},{57,89},{... | collective-permute-start | bytes 786440 | tf_op jit(solution)/shard_map/ppermute | solution.py:45
  7.3 6.6 %collective-permute-start = (f32[512,128]{1,0:T(8,128)S(1)}, f32[512,128]{1,0:T(8,128)S(1)}, u32[]{:S(2)}, u32[]{:S(2)}) collective-permute-start(f32[512,128]{1,0:T(8,128)S(1)} %broadcast_select_fusion.1), channel_id=1, source_target_pairs={{0,32},{8,40},{16,48},{24,56},{33,1},{41,9},{49,17},{57,25},{66,98... | collective-permute-start | bytes 786440 | tf_op jit(solution)/shard_map/ppermute | solution.py:45
  14.9 4.9 %collective-permute-start.3 = (f32[512,128]{1,0:T(8,128)S(1)}, f32[512,128]{1,0:T(8,128)S(1)}, u32[]{:S(2)}, u32[]{:S(2)}) collective-permute-start(f32[512,128]{1,0:T(8,128)S(1)} %add_add_fusion), channel_id=1, source_target_pairs={{0,128},{1,129},{2,130},{3,131},{8,136},{9,137},{10,138},{11,139},... | collective-permute-start | bytes 786440 | tf_op jit(solution)/shard_map/ppermute | solution.py:45
  20.0 7.1 %collective-permute-start.5 = (f32[512,128]{1,0:T(8,128)S(1)}, f32[512,128]{1,0:T(8,128)S(1)}, u32[]{:S(2)}, u32[]{:S(2)}) collective-permute-start(f32[512,128]{1,0:T(8,128)S(1)} %get-tuple-element.8), channel_id=1, source_target_pairs={{0,16},{8,24},{16,0},{24,8},{32,48},{40,56},{48,32},{56,40},{64,80... | collective-permute-start | bytes 786440 | tf_op jit(solution)/shard_map/ppermute | solution.py:56
  22.7 7.3 %collective-permute-start.4 = (f32[512,128]{1,0:T(8,128)S(1)}, f32[512,128]{1,0:T(8,128)S(1)}, u32[]{:S(2)}, u32[]{:S(2)}) collective-permute-start(f32[512,128]{1,0:T(8,128)S(1)} %get-tuple-element.8), channel_id=1, source_target_pairs={{0,8},{8,0},{16,24},{24,16},{32,40},{40,32},{48,56},{56,48},{64,72... | collective-permute-start | bytes 786440 | tf_op jit(solution)/shard_map/ppermute | solution.py:55
  27.1 4.0 %collective-permute-start.6 = (f32[512,128]{1,0:T(8,128)S(1)}, f32[512,128]{1,0:T(8,128)S(1)}, u32[]{:S(2)}, u32[]{:S(2)}) collective-permute-start(f32[512,128]{1,0:T(8,128)S(1)} %collective-permute-done.5), channel_id=1, source_target_pairs={{0,8},{8,0},{16,24},{24,16},{32,40},{40,32},{48,56},{56,48},{64,72... | collective-permute-start | bytes 786440 | tf_op jit(solution)/shard_map/ppermute | solution.py:57
  30.0 42.1 %copy-start.3 = (f32[512,128]{1,0:T(8,128)S(1)}, f32[512,128]{1,0:T(8,128)}, u32[]{:S(2)}) copy-start(f32[512,128]{1,0:T(8,128)} %param.4) | copy-start | bytes 786436
  59.8 43.2 %copy-start.2 = (f32[512,2048]{1,0:T(8,128)S(1)}, f32[512,2048]{1,0:T(8,128)}, u32[]{:S(2)}) copy-start(f32[512,2048]{1,0:T(8,128)} %param.3) | copy-start | bytes 12582916
  72.5 8.5 %collective-permute-start.9 = (f32[640,128]{1,0:T(8,128)S(1)}, f32[640,128]{1,0:T(8,128)S(1)}, u32[]{:S(2)}, u32[]{:S(2)}) collective-permute-start(f32[640,128]{1,0:T(8,128)S(1)} %pad_maximum_fusion), channel_id=1, source_target_pairs={{0,96},{1,97},{2,98},{3,99},{4,100},{5,101},{6,102},{7,103},{8,104... | collective-permute-start | bytes 983048 | tf_op jit(solution)/shard_map/ppermute | solution.py:45
  74.6 11.9 %collective-permute-start.8 = (f32[640,128]{1,0:T(8,128)S(1)}, f32[640,128]{1,0:T(8,128)S(1)}, u32[]{:S(2)}, u32[]{:S(2)}) collective-permute-start(f32[640,128]{1,0:T(8,128)S(1)} %pad_maximum_fusion), channel_id=1, source_target_pairs={{0,64},{1,65},{2,66},{3,67},{4,68},{5,69},{6,70},{7,71},{8,72},{9,... | collective-permute-start | bytes 983048 | tf_op jit(solution)/shard_map/ppermute | solution.py:45
  74.8 15.8 %collective-permute-start.7 = (f32[640,128]{1,0:T(8,128)S(1)}, f32[640,128]{1,0:T(8,128)S(1)}, u32[]{:S(2)}, u32[]{:S(2)}) collective-permute-start(f32[640,128]{1,0:T(8,128)S(1)} %pad_maximum_fusion), channel_id=1, source_target_pairs={{0,32},{1,33},{2,34},{3,35},{4,36},{5,37},{6,38},{7,39},{8,40},{9,... | collective-permute-start | bytes 983048 | tf_op jit(solution)/shard_map/ppermute | solution.py:45
  90.7 9.2 %collective-permute-start.10 = (f32[640,128]{1,0:T(8,128)S(1)}, f32[640,128]{1,0:T(8,128)S(1)}, u32[]{:S(2)}, u32[]{:S(2)}) collective-permute-start(f32[640,128]{1,0:T(8,128)S(1)} %pad_maximum_fusion.1), channel_id=1, source_target_pairs={{0,128},{1,129},{2,130},{3,131},{4,132},{5,133},{6,134},{7,135},{8... | collective-permute-start | bytes 983048 | tf_op jit(solution)/shard_map/ppermute | solution.py:45
  100.1 6.8 %collective-permute-start.12 = (f32[640,128]{1,0:T(8,128)S(1)}, f32[640,128]{1,0:T(8,128)S(1)}, u32[]{:S(2)}, u32[]{:S(2)}) collective-permute-start(f32[640,128]{1,0:T(8,128)S(1)} %pad_maximum_fusion.2), channel_id=1, source_target_pairs={{0,16},{8,24},{16,0},{24,8},{32,48},{40,56},{48,32},{56,40},{64,80... | collective-permute-start | bytes 983048 | tf_op jit(solution)/shard_map/ppermute | solution.py:56
  100.2 10.1 %collective-permute-start.11 = (f32[640,128]{1,0:T(8,128)S(1)}, f32[640,128]{1,0:T(8,128)S(1)}, u32[]{:S(2)}, u32[]{:S(2)}) collective-permute-start(f32[640,128]{1,0:T(8,128)S(1)} %pad_maximum_fusion.2), channel_id=1, source_target_pairs={{0,8},{8,0},{16,24},{24,16},{32,40},{40,32},{48,56},{56,48},{64,72... | collective-permute-start | bytes 983048 | tf_op jit(solution)/shard_map/ppermute | solution.py:55
  106.9 4.6 %collective-permute-start.13 = (f32[640,128]{1,0:T(8,128)S(1)}, f32[640,128]{1,0:T(8,128)S(1)}, u32[]{:S(2)}, u32[]{:S(2)}) collective-permute-start(f32[640,128]{1,0:T(8,128)S(1)} %collective-permute-done.12), channel_id=1, source_target_pairs={{0,8},{8,0},{16,24},{24,16},{32,40},{40,32},{48,56},{56,48},{64,72... | collective-permute-start | bytes 983048 | tf_op jit(solution)/shard_map/ppermute | solution.py:57
  112.7 2.4 %copy-start.1 = (f32[512,2048]{1,0:T(8,128)S(1)}, f32[512,2048]{1,0:T(8,128)}, u32[]{:S(2)}) copy-start(f32[512,2048]{1,0:T(8,128)} %convolution_subtract_fusion) | copy-start | bytes 12582916

commit v16 on v14

--- a/solution.py
+++ b/solution.py
@@ -5,7 +5,7 @@
 
 
 def product(left, right):
-    return jnp.dot(left, right, precision=lax.Precision.HIGH, preferred_element_type=jnp.float32)
+    return jnp.dot(left, right, precision=lax.Precision.HIGHEST, preferred_element_type=jnp.float32)
 
 
 def inner_product(left, right):
@@ -13,7 +13,7 @@
         left,
         right,
         (((0,), (0,)), ((), ())),
-        precision=lax.Precision.HIGH,
+        precision=lax.Precision.HIGHEST,
         preferred_element_type=jnp.float32,
     )
 
@@ -82,7 +82,7 @@
     right = jnp.concatenate([w_cols, vec_cols], axis=1)
     return matrix - lax.dot_general(
         left, right, (((1,), (1,)), ((), ())),
-        precision=lax.Precision.HIGH, preferred_element_type=jnp.float32,
+        precision=lax.Precision.HIGHEST, preferred_element_type=jnp.float32,
     )
 
 

time: 118 us -> 122 us (1.034)
  matrix products: 11.1 us -> 15.8 us
    dot_general x6, matrix products: 6.33 us -> 9.54 us  [product(): jnp.dot(left, right, precision=lax.Precision.HIGHEST, preferred_element_t...]
    dot_general x1, matrix products: 4.1 us -> 5.35 us  [shards(): lax.dot_general(left, right, (((1,), (1,)), ((), ())), precision=lax.Prec...]
where the time goes in v16:
time: 122 us
  waiting for transfers between devices  38.5 us (32%)
  blocking collectives  35.9 us (29%)
  starting transfers between devices  28.4 us (23%)
  matrix products  15.8 us (13%)
  other arithmetic  2.27 us (2%)
    ppermute x8, waiting for transfers between devices, to_columns(): arrived.append(lax.ppermute(sent, ('row', 'col'), pairs))  31.6 us
    all_to_all x1, blocking collectives, col_sum_rows(): total = jnp.sum(lax.all_to_all(pieces, 'col', 0, 0, tiled=True), axis=0)  24 us
    ppermute x8, starting transfers between devices, to_columns(): arrived.append(lax.ppermute(sent, ('row', 'col'), pairs))  13.2 us
    all_to_all x1, blocking collectives, col_sum_rows(): lax.all_to_all(spread, 'col', 0, 0, tiled=True).reshape(partial.shape)  11.9 us
    dot_general x6, matrix products, product(): jnp.dot(left, right, precision=lax.Precision.HIGHEST, preferred_element_t...  9.54 us
    ppermute x2, starting transfers between devices, to_columns(): diagonal = lax.ppermute(across, 'row', core_pairs)  6.37 us
    ppermute x2, starting transfers between devices, to_columns(): other = lax.ppermute(sent, 'row', core_pairs)  5.39 us
    dot_general x1, matrix products, shards(): lax.dot_general(left, right, (((1,), (1,)), ((), ())), precision=lax.Prec...  5.35 us
  transfers between devices with their start and end apart: 14, of which 10 were waited for; matrix products, arithmetic and copies ran while one was open for 0% of the time, Pallas kernels for 0%

profile of v16, /device:TPU:1, one launch (start us, length us, event | category | flops | bytes accessed | tf_op | source)
XLA Modules:
  0.0 121.6 jit_solution(755732940324969862)
XLA Ops:
  1.0 3.0 %collective-permute-start.1 = (f32[512,128]{1,0:T(8,128)S(1)}, f32[512,128]{1,0:T(8,128)S(1)}, u32[]{:S(2)}, u32[]{:S(2)}) collective-permute-start(f32[512,128]{1,0:T(8,128)S(1)} %broadcast_select_fusion.1), channel_id=1, source_target_pairs={{0,64},{8,72},{16,80},{24,88},{33,97},{41,105},{49,113},{57,121},{... | collective-permute-start | bytes 786440 | tf_op jit(solution)/shard_map/ppermute | solution.py:45
  4.0 3.3 %collective-permute-start.2 = (f32[512,128]{1,0:T(8,128)S(1)}, f32[512,128]{1,0:T(8,128)S(1)}, u32[]{:S(2)}, u32[]{:S(2)}) collective-permute-start(f32[512,128]{1,0:T(8,128)S(1)} %broadcast_select_fusion.1), channel_id=1, source_target_pairs={{0,96},{8,104},{16,112},{24,120},{33,65},{41,73},{49,81},{57,89},{... | collective-permute-start | bytes 786440 | tf_op jit(solution)/shard_map/ppermute | solution.py:45
  7.3 1.3 %collective-permute-start = (f32[512,128]{1,0:T(8,128)S(1)}, f32[512,128]{1,0:T(8,128)S(1)}, u32[]{:S(2)}, u32[]{:S(2)}) collective-permute-start(f32[512,128]{1,0:T(8,128)S(1)} %broadcast_select_fusion.1), channel_id=1, source_target_pairs={{0,32},{8,40},{16,48},{24,56},{33,1},{41,9},{49,17},{57,25},{66,98... | collective-permute-start | bytes 786440 | tf_op jit(solution)/shard_map/ppermute | solution.py:45
  8.6 5.3 %collective-permute-done.2 = f32[512,128]{1,0:T(8,128)S(1)} collective-permute-done((f32[512,128]{1,0:T(8,128)S(1)}, f32[512,128]{1,0:T(8,128)S(1)}, u32[]{:S(2)}, u32[]{:S(2)}) %collective-permute-start.2) | collective-permute-done | bytes 262176 | tf_op jit(solution)/shard_map/ppermute | solution.py:45
  14.9 1.3 %collective-permute-start.3 = (f32[512,128]{1,0:T(8,128)S(1)}, f32[512,128]{1,0:T(8,128)S(1)}, u32[]{:S(2)}, u32[]{:S(2)}) collective-permute-start(f32[512,128]{1,0:T(8,128)S(1)} %add_add_fusion), channel_id=1, source_target_pairs={{0,128},{1,129},{2,130},{3,131},{8,136},{9,137},{10,138},{11,139},... | collective-permute-start | bytes 786440 | tf_op jit(solution)/shard_map/ppermute | solution.py:45
  16.2 3.6 %collective-permute-done.3 = f32[512,128]{1,0:T(8,128)S(1)} collective-permute-done((f32[512,128]{1,0:T(8,128)S(1)}, f32[512,128]{1,0:T(8,128)S(1)}, u32[]{:S(2)}, u32[]{:S(2)}) %collective-permute-start.3) | collective-permute-done | bytes 262176 | tf_op jit(solution)/shard_map/ppermute | solution.py:45
  20.0 2.7 %collective-permute-start.5 = (f32[512,128]{1,0:T(8,128)S(1)}, f32[512,128]{1,0:T(8,128)S(1)}, u32[]{:S(2)}, u32[]{:S(2)}) collective-permute-start(f32[512,128]{1,0:T(8,128)S(1)} %get-tuple-element.8), channel_id=1, source_target_pairs={{0,16},{8,24},{16,0},{24,8},{32,48},{40,56},{48,32},{56,40},{64,80... | collective-permute-start | bytes 786440 | tf_op jit(solution)/shard_map/ppermute | solution.py:56
  22.7 2.5 %collective-permute-start.4 = (f32[512,128]{1,0:T(8,128)S(1)}, f32[512,128]{1,0:T(8,128)S(1)}, u32[]{:S(2)}, u32[]{:S(2)}) collective-permute-start(f32[512,128]{1,0:T(8,128)S(1)} %get-tuple-element.8), channel_id=1, source_target_pairs={{0,8},{8,0},{16,24},{24,16},{32,40},{40,32},{48,56},{56,48},{64,72... | collective-permute-start | bytes 786440 | tf_op jit(solution)/shard_map/ppermute | solution.py:55
  25.1 2.0 %collective-permute-done.5 = f32[512,128]{1,0:T(8,128)S(1)} collective-permute-done((f32[512,128]{1,0:T(8,128)S(1)}, f32[512,128]{1,0:T(8,128)S(1)}, u32[]{:S(2)}, u32[]{:S(2)}) %collective-permute-start.5) | collective-permute-done | bytes 262176 | tf_op jit(solution)/shard_map/ppermute | solution.py:56
  27.1 2.8 %collective-permute-start.6 = (f32[512,128]{1,0:T(8,128)S(1)}, f32[512,128]{1,0:T(8,128)S(1)}, u32[]{:S(2)}, u32[]{:S(2)}) collective-permute-start(f32[512,128]{1,0:T(8,128)S(1)} %collective-permute-done.5), channel_id=1, source_target_pairs={{0,8},{8,0},{16,24},{24,16},{32,40},{40,32},{48,56},{56,48},{64,72... | collective-permute-start | bytes 786440 | tf_op jit(solution)/shard_map/ppermute | solution.py:57
  31.1 6.6 %convolution_bitcast_fusion = f32[512,128]{0,1:T(8,128)S(1)} fusion(f32[2048,128]{1,0:T(8,128)S(1)} %constant_dynamic-update-slice_fusion.1, f32[512,2048]{1,0:T(8,128)} %param.3), kind=kOutput, calls=%fused_computation.9 | convolution fusion | flops 1610612736 | bytes 5505024 | tf_op jit(solution)/shard_map/dot_general | solution.py:8
  37.9 24.0 %all_to_all.11 = f32[8,64,128]{2,1,0:T(8,128)S(1)} all-to-all(f32[8,64,128]{2,1,0:T(8,128)S(1)} %bitcast.30), channel_id=1, replica_groups=mesh['row'=32,'col'=8] {'col'}, dimensions={0} | all-to-all | bytes 524288 | tf_op jit(solution)/shard_map/all_to_all | solution.py:69
  61.9 11.9 %all_to_all.10 = f32[8,64,128]{2,1,0:T(8,128)S(1)} all-to-all(f32[8,64,128]{2,1,0:T(8,128)S(1)} %broadcast_in_dim.2), channel_id=1, replica_groups=mesh['row'=32,'col'=8] {'col'}, dimensions={0} | all-to-all | bytes 524288 | tf_op jit(solution)/shard_map/all_to_all | solution.py:71
  74.5 1.9 %collective-permute-start.9 = (f32[640,128]{1,0:T(8,128)S(1)}, f32[640,128]{1,0:T(8,128)S(1)}, u32[]{:S(2)}, u32[]{:S(2)}) collective-permute-start(f32[640,128]{1,0:T(8,128)S(1)} %pad_maximum_fusion), channel_id=1, source_target_pairs={{0,96},{1,97},{2,98},{3,99},{4,100},{5,101},{6,102},{7,103},{8,104... | collective-permute-start | bytes 983048 | tf_op jit(solution)/shard_map/ppermute | solution.py:45
  77.0 1.7 %collective-permute-start.7 = (f32[640,128]{1,0:T(8,128)S(1)}, f32[640,128]{1,0:T(8,128)S(1)}, u32[]{:S(2)}, u32[]{:S(2)}) collective-permute-start(f32[640,128]{1,0:T(8,128)S(1)} %pad_maximum_fusion), channel_id=1, source_target_pairs={{0,32},{1,33},{2,34},{3,35},{4,36},{5,37},{6,38},{7,39},{8,40},{9,... | collective-permute-start | bytes 983048 | tf_op jit(solution)/shard_map/ppermute | solution.py:45
  78.8 4.3 %collective-permute-done.9 = f32[640,128]{1,0:T(8,128)S(1)} collective-permute-done((f32[640,128]{1,0:T(8,128)S(1)}, f32[640,128]{1,0:T(8,128)S(1)}, u32[]{:S(2)}, u32[]{:S(2)}) %collective-permute-start.9) | collective-permute-done | bytes 327712 | tf_op jit(solution)/shard_map/ppermute | solution.py:45
  83.0 5.6 %collective-permute-done.8 = f32[640,128]{1,0:T(8,128)S(1)} collective-permute-done((f32[640,128]{1,0:T(8,128)S(1)}, f32[640,128]{1,0:T(8,128)S(1)}, u32[]{:S(2)}, u32[]{:S(2)}) %collective-permute-start.8) | collective-permute-done | bytes 327712 | tf_op jit(solution)/shard_map/ppermute | solution.py:45
  88.7 3.8 %collective-permute-done.7 = f32[640,128]{1,0:T(8,128)S(1)} collective-permute-done((f32[640,128]{1,0:T(8,128)S(1)}, f32[640,128]{1,0:T(8,128)S(1)}, u32[]{:S(2)}, u32[]{:S(2)}) %collective-permute-start.7) | collective-permute-done | bytes 327712 | tf_op jit(solution)/shard_map/ppermute | solution.py:45
  92.7 9.0 %collective-permute-done.10 = f32[640,128]{1,0:T(8,128)S(1)} collective-permute-done((f32[640,128]{1,0:T(8,128)S(1)}, f32[640,128]{1,0:T(8,128)S(1)}, u32[]{:S(2)}, u32[]{:S(2)}) %collective-permute-start.10) | collective-permute-done | bytes 327712 | tf_op jit(solution)/shard_map/ppermute | solution.py:45
  102.5 2.9 %collective-permute-start.11 = (f32[640,128]{1,0:T(8,128)S(1)}, f32[640,128]{1,0:T(8,128)S(1)}, u32[]{:S(2)}, u32[]{:S(2)}) collective-permute-start(f32[640,128]{1,0:T(8,128)S(1)} %pad_maximum_fusion.2), channel_id=1, source_target_pairs={{0,8},{8,0},{16,24},{24,16},{32,40},{40,32},{48,56},{56,48},{64,72... | collective-permute-start | bytes 983048 | tf_op jit(solution)/shard_map/ppermute | solution.py:55
  105.8 2.7 %collective-permute-done.12 = f32[640,128]{1,0:T(8,128)S(1)} collective-permute-done((f32[640,128]{1,0:T(8,128)S(1)}, f32[640,128]{1,0:T(8,128)S(1)}, u32[]{:S(2)}, u32[]{:S(2)}) %collective-permute-start.12) | collective-permute-done | bytes 327712 | tf_op jit(solution)/shard_map/ppermute | solution.py:56
  108.5 3.5 %collective-permute-start.13 = (f32[640,128]{1,0:T(8,128)S(1)}, f32[640,128]{1,0:T(8,128)S(1)}, u32[]{:S(2)}, u32[]{:S(2)}) collective-permute-start(f32[640,128]{1,0:T(8,128)S(1)} %collective-permute-done.12), channel_id=1, source_target_pairs={{0,8},{8,0},{16,24},{24,16},{32,40},{40,32},{48,56},{56,48},{64,72... | collective-permute-start | bytes 983048 | tf_op jit(solution)/shard_map/ppermute | solution.py:57
  112.1 1.2 collective-permute-done.13
  116.2 5.3 %convolution_subtract_fusion = f32[512,2048]{1,0:T(8,128)} fusion(f32[512,2048]{1,0:T(8,128)S(1)} %copy-done.1, f32[2048,128]{1,0:T(8,128)S(1)} %constant_dynamic-update-slice_fusion.1, f32[2048,128]{1,0:T(8,128)S(1)} %convolution_subtract_fusion.1, f32[512,128]{1,0:T(8,128)S(1)} %fusion.4, f32[512,128]{1,0:T(8,128)S(1)} %copy-done.2), kind=kOutput, calls=%fused_computation | convolution fusion | flops 3222929408 | bytes 11010048 | tf_op jit(solution)/shard_map/dot_general | solution.py:83
  (43 shorter events, 8.9 us)
Async XLA Ops:
  0.0 105.4 %copy-start = (f32[128,128]{1,0:T(8,128)S(1)}, f32[128,128]{1,0:T(8,128)}, u32[]{:S(2)}) copy-start(f32[128,128]{1,0:T(8,128)} %param.5) | copy-start | bytes 196612
  1.0 7.6 %collective-permute-start.1 = (f32[512,128]{1,0:T(8,128)S(1)}, f32[512,128]{1,0:T(8,128)S(1)}, u32[]{:S(2)}, u32[]{:S(2)}) collective-permute-start(f32[512,128]{1,0:T(8,128)S(1)} %broadcast_select_fusion.1), channel_id=1, source_target_pairs={{0,64},{8,72},{16,80},{24,88},{33,97},{41,105},{49,113},{57,121},{... | collective-permute-start | bytes 786440 | tf_op jit(solution)/shard_map/ppermute | solution.py:45
  4.0 9.9 %collective-permute-start.2 = (f32[512,128]{1,0:T(8,128)S(1)}, f32[512,128]{1,0:T(8,128)S(1)}, u32[]{:S(2)}, u32[]{:S(2)}) collective-permute-start(f32[512,128]{1,0:T(8,128)S(1)} %broadcast_select_fusion.1), channel_id=1, source_target_pairs={{0,96},{8,104},{16,112},{24,120},{33,65},{41,73},{49,81},{57,89},{... | collective-permute-start | bytes 786440 | tf_op jit(solution)/shard_map/ppermute | solution.py:45
  7.3 6.6 %collective-permute-start = (f32[512,128]{1,0:T(8,128)S(1)}, f32[512,128]{1,0:T(8,128)S(1)}, u32[]{:S(2)}, u32[]{:S(2)}) collective-permute-start(f32[512,128]{1,0:T(8,128)S(1)} %broadcast_select_fusion.1), channel_id=1, source_target_pairs={{0,32},{8,40},{16,48},{24,56},{33,1},{41,9},{49,17},{57,25},{66,98... | collective-permute-start | bytes 786440 | tf_op jit(solution)/shard_map/ppermute | solution.py:45
  14.9 4.9 %collective-permute-start.3 = (f32[512,128]{1,0:T(8,128)S(1)}, f32[512,128]{1,0:T(8,128)S(1)}, u32[]{:S(2)}, u32[]{:S(2)}) collective-permute-start(f32[512,128]{1,0:T(8,128)S(1)} %add_add_fusion), channel_id=1, source_target_pairs={{0,128},{1,129},{2,130},{3,131},{8,136},{9,137},{10,138},{11,139},... | collective-permute-start | bytes 786440 | tf_op jit(solution)/shard_map/ppermute | solution.py:45
  20.0 7.1 %collective-permute-start.5 = (f32[512,128]{1,0:T(8,128)S(1)}, f32[512,128]{1,0:T(8,128)S(1)}, u32[]{:S(2)}, u32[]{:S(2)}) collective-permute-start(f32[512,128]{1,0:T(8,128)S(1)} %get-tuple-element.8), channel_id=1, source_target_pairs={{0,16},{8,24},{16,0},{24,8},{32,48},{40,56},{48,32},{56,40},{64,80... | collective-permute-start | bytes 786440 | tf_op jit(solution)/shard_map/ppermute | solution.py:56
  22.7 7.3 %collective-permute-start.4 = (f32[512,128]{1,0:T(8,128)S(1)}, f32[512,128]{1,0:T(8,128)S(1)}, u32[]{:S(2)}, u32[]{:S(2)}) collective-permute-start(f32[512,128]{1,0:T(8,128)S(1)} %get-tuple-element.8), channel_id=1, source_target_pairs={{0,8},{8,0},{16,24},{24,16},{32,40},{40,32},{48,56},{56,48},{64,72... | collective-permute-start | bytes 786440 | tf_op jit(solution)/shard_map/ppermute | solution.py:55
  27.1 4.0 %collective-permute-start.6 = (f32[512,128]{1,0:T(8,128)S(1)}, f32[512,128]{1,0:T(8,128)S(1)}, u32[]{:S(2)}, u32[]{:S(2)}) collective-permute-start(f32[512,128]{1,0:T(8,128)S(1)} %collective-permute-done.5), channel_id=1, source_target_pairs={{0,8},{8,0},{16,24},{24,16},{32,40},{40,32},{48,56},{56,48},{64,72... | collective-permute-start | bytes 786440 | tf_op jit(solution)/shard_map/ppermute | solution.py:57
  30.0 43.9 %copy-start.2 = (f32[512,128]{1,0:T(8,128)S(1)}, f32[512,128]{1,0:T(8,128)}, u32[]{:S(2)}) copy-start(f32[512,128]{1,0:T(8,128)} %param.4) | copy-start | bytes 786436
  74.5 8.5 %collective-permute-start.9 = (f32[640,128]{1,0:T(8,128)S(1)}, f32[640,128]{1,0:T(8,128)S(1)}, u32[]{:S(2)}, u32[]{:S(2)}) collective-permute-start(f32[640,128]{1,0:T(8,128)S(1)} %pad_maximum_fusion), channel_id=1, source_target_pairs={{0,96},{1,97},{2,98},{3,99},{4,100},{5,101},{6,102},{7,103},{8,104... | collective-permute-start | bytes 983048 | tf_op jit(solution)/shard_map/ppermute | solution.py:45
  76.5 12.2 %collective-permute-start.8 = (f32[640,128]{1,0:T(8,128)S(1)}, f32[640,128]{1,0:T(8,128)S(1)}, u32[]{:S(2)}, u32[]{:S(2)}) collective-permute-start(f32[640,128]{1,0:T(8,128)S(1)} %pad_maximum_fusion), channel_id=1, source_target_pairs={{0,64},{1,65},{2,66},{3,67},{4,68},{5,69},{6,70},{7,71},{8,72},{9,... | collective-permute-start | bytes 983048 | tf_op jit(solution)/shard_map/ppermute | solution.py:45
  77.0 15.4 %collective-permute-start.7 = (f32[640,128]{1,0:T(8,128)S(1)}, f32[640,128]{1,0:T(8,128)S(1)}, u32[]{:S(2)}, u32[]{:S(2)}) collective-permute-start(f32[640,128]{1,0:T(8,128)S(1)} %pad_maximum_fusion), channel_id=1, source_target_pairs={{0,32},{1,33},{2,34},{3,35},{4,36},{5,37},{6,38},{7,39},{8,40},{9,... | collective-permute-start | bytes 983048 | tf_op jit(solution)/shard_map/ppermute | solution.py:45
  92.6 9.1 %collective-permute-start.10 = (f32[640,128]{1,0:T(8,128)S(1)}, f32[640,128]{1,0:T(8,128)S(1)}, u32[]{:S(2)}, u32[]{:S(2)}) collective-permute-start(f32[640,128]{1,0:T(8,128)S(1)} %pad_maximum_fusion.1), channel_id=1, source_target_pairs={{0,128},{1,129},{2,130},{3,131},{4,132},{5,133},{6,134},{7,135},{8... | collective-permute-start | bytes 983048 | tf_op jit(solution)/shard_map/ppermute | solution.py:45
  101.8 6.7 %collective-permute-start.12 = (f32[640,128]{1,0:T(8,128)S(1)}, f32[640,128]{1,0:T(8,128)S(1)}, u32[]{:S(2)}, u32[]{:S(2)}) collective-permute-start(f32[640,128]{1,0:T(8,128)S(1)} %pad_maximum_fusion.2), channel_id=1, source_target_pairs={{0,16},{8,24},{16,0},{24,8},{32,48},{40,56},{48,32},{56,40},{64,80... | collective-permute-start | bytes 983048 | tf_op jit(solution)/shard_map/ppermute | solution.py:56
  102.5 9.6 %collective-permute-start.11 = (f32[640,128]{1,0:T(8,128)S(1)}, f32[640,128]{1,0:T(8,128)S(1)}, u32[]{:S(2)}, u32[]{:S(2)}) collective-permute-start(f32[640,128]{1,0:T(8,128)S(1)} %pad_maximum_fusion.2), channel_id=1, source_target_pairs={{0,8},{8,0},{16,24},{24,16},{32,40},{40,32},{48,56},{56,48},{64,72... | collective-permute-start | bytes 983048 | tf_op jit(solution)/shard_map/ppermute | solution.py:55
  108.5 4.8 %collective-permute-start.13 = (f32[640,128]{1,0:T(8,128)S(1)}, f32[640,128]{1,0:T(8,128)S(1)}, u32[]{:S(2)}, u32[]{:S(2)}) collective-permute-start(f32[640,128]{1,0:T(8,128)S(1)} %collective-permute-done.12), channel_id=1, source_target_pairs={{0,8},{8,0},{16,24},{24,16},{32,40},{40,32},{48,56},{56,48},{64,72... | collective-permute-start | bytes 983048 | tf_op jit(solution)/shard_map/ppermute | solution.py:57
  112.1 4.2 %copy-start.1 = (f32[512,2048]{1,0:T(8,128)S(1)}, f32[512,2048]{1,0:T(8,128)}, u32[]{:S(2)}) copy-start(f32[512,2048]{1,0:T(8,128)} %param.3) | copy-start | bytes 12582916

commit v17 on v14

--- a/solution.py
+++ b/solution.py
@@ -29,7 +29,10 @@
     mine = jnp.where(high == col, panel_rows, jnp.zeros_like(panel_rows))
     known = 1
     while known < col_count:
-        width = 4 if col_count % (known * 4) == 0 else 2
+        if extra is None:
+            width = col_count // known
+        else:
+            width = 4 if col_count % (known * 4) == 0 else 2
         sent = mine if extra is None else jnp.concatenate([mine, extra], axis=0)
         arrived = []
         for digit in range(1, width):

time: 118 us -> 123 us (1.042)
  blocking collectives: 36 us -> 27.1 us
  waiting for transfers between devices: 39.7 us -> 46.9 us
  starting transfers between devices: 27.5 us -> 34.1 us
    ppermute x8 -> x11, starting transfers between devices: 13.2 us -> 24.5 us  [to_columns(): arrived.append(lax.ppermute(sent, ('row', 'col'), pairs))]
    all_to_all x1, blocking collectives: 24 us -> 15.2 us  [col_sum_rows(): total = jnp.sum(lax.all_to_all(pieces, 'col', 0, 0, tiled=True), axis=0)]
    ppermute x8 -> x11, waiting for transfers between devices: 31.8 us -> 35.4 us  [to_columns(): arrived.append(lax.ppermute(sent, ('row', 'col'), pairs))]
    ppermute x2, waiting for transfers between devices: 5.63 us -> 9.19 us  [to_columns(): across = lax.ppermute(sent, 'row', [(i, i ^ 2) for i in range(row_count)])]
    ppermute x2, starting transfers between devices: 2.8 us -> 0.58 us  [to_columns(): across = lax.ppermute(sent, 'row', [(i, i ^ 2) for i in range(row_count)])]
    ppermute x2, starting transfers between devices: 5.22 us -> 3.83 us  [to_columns(): other = lax.ppermute(sent, 'row', core_pairs)]
  transfers between devices with their start and end apart: 14 -> 17, of which waited for: 10 -> 11; matrix products, arithmetic and copies ran while one was open for 0% -> 0% of each run, Pallas kernels for 0% -> 0%
where the time goes in v17:
time: 123 us; the launch traced here: 122 us
  waiting for transfers between devices  46.9 us (38%)
  starting transfers between devices  34.1 us (28%)
  blocking collectives  27.1 us (22%)
  matrix products  11.1 us (9%)
  other arithmetic  2.29 us (2%)
    ppermute x11, waiting for transfers between devices, to_columns(): arrived.append(lax.ppermute(sent, ('row', 'col'), pairs))  35.4 us
    ppermute x11, starting transfers between devices, to_columns(): arrived.append(lax.ppermute(sent, ('row', 'col'), pairs))  24.5 us
    all_to_all x1, blocking collectives, col_sum_rows(): total = jnp.sum(lax.all_to_all(pieces, 'col', 0, 0, tiled=True), axis=0)  15.2 us
    all_to_all x1, blocking collectives, col_sum_rows(): lax.all_to_all(spread, 'col', 0, 0, tiled=True).reshape(partial.shape)  11.9 us
    ppermute x2, waiting for transfers between devices, to_columns(): across = lax.ppermute(sent, 'row', [(i, i ^ 2) for i in range(row_count)])  9.19 us
    dot_general x6, matrix products, product(): jnp.dot(left, right, precision=lax.Precision.HIGH, preferred_element_type...  6.33 us
    ppermute x2, starting transfers between devices, to_columns(): diagonal = lax.ppermute(across, 'row', core_pairs)  5.16 us
    dot_general x1, matrix products, shards(): lax.dot_general(left, right, (((1,), (1,)), ((), ())), precision=lax.Prec...  4.1 us
  transfers between devices with their start and end apart: 17, of which 11 were waited for; matrix products, arithmetic and copies ran while one was open for 0% of the time, Pallas kernels for 0%

profile of v17, /device:TPU:1, one launch (start us, length us, event | category | flops | bytes accessed | tf_op | source)
XLA Modules:
  0.0 122.1 jit_solution(12861012582261970225)
XLA Ops:
  1.0 4.2 %collective-permute-start.5 = (f32[512,128]{1,0:T(8,128)S(1)}, f32[512,128]{1,0:T(8,128)S(1)}, u32[]{:S(2)}, u32[]{:S(2)}) collective-permute-start(f32[512,128]{1,0:T(8,128)S(1)} %broadcast_select_fusion.1), channel_id=1, source_target_pairs={{0,192},{8,200},{16,208},{24,216},{33,225},{41,233},{49,241},{57,2... | collective-permute-start | bytes 786440 | tf_op jit(solution)/shard_map/ppermute | solution.py:48
  5.3 3.6 %collective-permute-start.4 = (f32[512,128]{1,0:T(8,128)S(1)}, f32[512,128]{1,0:T(8,128)S(1)}, u32[]{:S(2)}, u32[]{:S(2)}) collective-permute-start(f32[512,128]{1,0:T(8,128)S(1)} %broadcast_select_fusion.1), channel_id=1, source_target_pairs={{0,160},{8,168},{16,176},{24,184},{33,129},{41,137},{49,145},{57,1... | collective-permute-start | bytes 786440 | tf_op jit(solution)/shard_map/ppermute | solution.py:48
  10.2 1.3 %collective-permute-start.2 = (f32[512,128]{1,0:T(8,128)S(1)}, f32[512,128]{1,0:T(8,128)S(1)}, u32[]{:S(2)}, u32[]{:S(2)}) collective-permute-start(f32[512,128]{1,0:T(8,128)S(1)} %broadcast_select_fusion.1), channel_id=1, source_target_pairs={{0,96},{8,104},{16,112},{24,120},{33,65},{41,73},{49,81},{57,89},{... | collective-permute-start | bytes 786440 | tf_op jit(solution)/shard_map/ppermute | solution.py:48
  11.5 1.3 %collective-permute-start.1 = (f32[512,128]{1,0:T(8,128)S(1)}, f32[512,128]{1,0:T(8,128)S(1)}, u32[]{:S(2)}, u32[]{:S(2)}) collective-permute-start(f32[512,128]{1,0:T(8,128)S(1)} %broadcast_select_fusion.1), channel_id=1, source_target_pairs={{0,64},{8,72},{16,80},{24,88},{33,97},{41,105},{49,113},{57,121},{... | collective-permute-start | bytes 786440 | tf_op jit(solution)/shard_map/ppermute | solution.py:48
  14.1 1.3 %collective-permute-start = (f32[512,128]{1,0:T(8,128)S(1)}, f32[512,128]{1,0:T(8,128)S(1)}, u32[]{:S(2)}, u32[]{:S(2)}) collective-permute-start(f32[512,128]{1,0:T(8,128)S(1)} %broadcast_select_fusion.1), channel_id=1, source_target_pairs={{0,32},{8,40},{16,48},{24,56},{33,1},{41,9},{49,17},{57,25},{66,98... | collective-permute-start | bytes 786440 | tf_op jit(solution)/shard_map/ppermute | solution.py:48
  15.5 4.0 %collective-permute-done.3 = f32[512,128]{1,0:T(8,128)S(1)} collective-permute-done((f32[512,128]{1,0:T(8,128)S(1)}, f32[512,128]{1,0:T(8,128)S(1)}, u32[]{:S(2)}, u32[]{:S(2)}) %collective-permute-start.3) | collective-permute-done | bytes 262176 | tf_op jit(solution)/shard_map/ppermute | solution.py:48
  19.4 5.6 %collective-permute-done.2 = f32[512,128]{1,0:T(8,128)S(1)} collective-permute-done((f32[512,128]{1,0:T(8,128)S(1)}, f32[512,128]{1,0:T(8,128)S(1)}, u32[]{:S(2)}, u32[]{:S(2)}) %collective-permute-start.2) | collective-permute-done | bytes 262176 | tf_op jit(solution)/shard_map/ppermute | solution.py:48
  25.0 5.6 %collective-permute-done.1 = f32[512,128]{1,0:T(8,128)S(1)} collective-permute-done((f32[512,128]{1,0:T(8,128)S(1)}, f32[512,128]{1,0:T(8,128)S(1)}, u32[]{:S(2)}, u32[]{:S(2)}) %collective-permute-start.1) | collective-permute-done | bytes 262176 | tf_op jit(solution)/shard_map/ppermute | solution.py:48
  32.3 1.8 %collective-permute-start.7 = (f32[512,128]{1,0:T(8,128)S(1)}, f32[512,128]{1,0:T(8,128)S(1)}, u32[]{:S(2)}, u32[]{:S(2)}) collective-permute-start(f32[512,128]{1,0:T(8,128)S(1)} %get-tuple-element.8), channel_id=1, source_target_pairs={{0,8},{8,0},{16,24},{24,16},{32,40},{40,32},{48,56},{56,48},{64,72... | collective-permute-start | bytes 786440 | tf_op jit(solution)/shard_map/ppermute | solution.py:58
  34.1 4.0 %collective-permute-done.8 = f32[512,128]{1,0:T(8,128)S(1)} collective-permute-done((f32[512,128]{1,0:T(8,128)S(1)}, f32[512,128]{1,0:T(8,128)S(1)}, u32[]{:S(2)}, u32[]{:S(2)}) %collective-permute-start.8) | collective-permute-done | bytes 262176 | tf_op jit(solution)/shard_map/ppermute | solution.py:59
  38.1 2.5 %collective-permute-start.9 = (f32[512,128]{1,0:T(8,128)S(1)}, f32[512,128]{1,0:T(8,128)S(1)}, u32[]{:S(2)}, u32[]{:S(2)}) collective-permute-start(f32[512,128]{1,0:T(8,128)S(1)} %collective-permute-done.8), channel_id=1, source_target_pairs={{0,8},{8,0},{16,24},{24,16},{32,40},{40,32},{48,56},{56,48},{64,72... | collective-permute-start | bytes 786440 | tf_op jit(solution)/shard_map/ppermute | solution.py:60
  41.8 4.5 %convolution_bitcast_fusion = f32[512,128]{0,1:T(8,128)S(1)} fusion(f32[2048,128]{1,0:T(8,128)S(1)} %constant_dynamic-update-slice_fusion.1, f32[512,2048]{1,0:T(8,128)} %param.3), kind=kOutput, calls=%fused_computation.9 | convolution fusion | flops 805306368 | bytes 5505024 | tf_op jit(solution)/shard_map/dot_general | solution.py:8
  46.4 15.2 %all_to_all.11 = f32[8,64,128]{2,1,0:T(8,128)S(1)} all-to-all(f32[8,64,128]{2,1,0:T(8,128)S(1)} %bitcast.30), channel_id=1, replica_groups=mesh['row'=32,'col'=8] {'col'}, dimensions={0} | all-to-all | bytes 524288 | tf_op jit(solution)/shard_map/all_to_all | solution.py:72
  61.6 11.9 %all_to_all.10 = f32[8,64,128]{2,1,0:T(8,128)S(1)} all-to-all(f32[8,64,128]{2,1,0:T(8,128)S(1)} %broadcast_in_dim.2), channel_id=1, replica_groups=mesh['row'=32,'col'=8] {'col'}, dimensions={0} | all-to-all | bytes 524288 | tf_op jit(solution)/shard_map/all_to_all | solution.py:74
  74.0 2.0 %collective-permute-start.12 = (f32[640,128]{1,0:T(8,128)S(1)}, f32[640,128]{1,0:T(8,128)S(1)}, u32[]{:S(2)}, u32[]{:S(2)}) collective-permute-start(f32[640,128]{1,0:T(8,128)S(1)} %pad_maximum_fusion), channel_id=1, source_target_pairs={{0,96},{1,97},{2,98},{3,99},{4,100},{5,101},{6,102},{7,103},{8,104... | collective-permute-start | bytes 983048 | tf_op jit(solution)/shard_map/ppermute | solution.py:48
  78.2 4.3 %collective-permute-done.12 = f32[640,128]{1,0:T(8,128)S(1)} collective-permute-done((f32[640,128]{1,0:T(8,128)S(1)}, f32[640,128]{1,0:T(8,128)S(1)}, u32[]{:S(2)}, u32[]{:S(2)}) %collective-permute-start.12) | collective-permute-done | bytes 327712 | tf_op jit(solution)/shard_map/ppermute | solution.py:48
  82.5 6.1 %collective-permute-done.11 = f32[640,128]{1,0:T(8,128)S(1)} collective-permute-done((f32[640,128]{1,0:T(8,128)S(1)}, f32[640,128]{1,0:T(8,128)S(1)}, u32[]{:S(2)}, u32[]{:S(2)}) %collective-permute-start.11) | collective-permute-done | bytes 327712 | tf_op jit(solution)/shard_map/ppermute | solution.py:48
  88.7 2.9 %collective-permute-done.10 = f32[640,128]{1,0:T(8,128)S(1)} collective-permute-done((f32[640,128]{1,0:T(8,128)S(1)}, f32[640,128]{1,0:T(8,128)S(1)}, u32[]{:S(2)}, u32[]{:S(2)}) %collective-permute-start.10) | collective-permute-done | bytes 327712 | tf_op jit(solution)/shard_map/ppermute | solution.py:48
  91.6 5.9 %collective-permute-start.13 = (f32[640,128]{1,0:T(8,128)S(1)}, f32[640,128]{1,0:T(8,128)S(1)}, u32[]{:S(2)}, u32[]{:S(2)}) collective-permute-start(f32[640,128]{1,0:T(8,128)S(1)} %pad_maximum_fusion.1), channel_id=1, source_target_pairs={{0,128},{1,129},{2,130},{3,131},{4,132},{5,133},{6,134},{7,135},{8... | collective-permute-start | bytes 983048 | tf_op jit(solution)/shard_map/ppermute | solution.py:48
  97.6 6.9 %collective-permute-done.13 = f32[640,128]{1,0:T(8,128)S(1)} collective-permute-done((f32[640,128]{1,0:T(8,128)S(1)}, f32[640,128]{1,0:T(8,128)S(1)}, u32[]{:S(2)}, u32[]{:S(2)}) %collective-permute-start.13) | collective-permute-done | bytes 327712 | tf_op jit(solution)/shard_map/ppermute | solution.py:48
  104.7 2.0 %collective-permute-start.14 = (f32[640,128]{1,0:T(8,128)S(1)}, f32[640,128]{1,0:T(8,128)S(1)}, u32[]{:S(2)}, u32[]{:S(2)}) collective-permute-start(f32[640,128]{1,0:T(8,128)S(1)} %pad_maximum_fusion.2), channel_id=1, source_target_pairs={{0,8},{8,0},{16,24},{24,16},{32,40},{40,32},{48,56},{56,48},{64,72... | collective-permute-start | bytes 983048 | tf_op jit(solution)/shard_map/ppermute | solution.py:58
  107.0 5.2 %collective-permute-done.15 = f32[640,128]{1,0:T(8,128)S(1)} collective-permute-done((f32[640,128]{1,0:T(8,128)S(1)}, f32[640,128]{1,0:T(8,128)S(1)}, u32[]{:S(2)}, u32[]{:S(2)}) %collective-permute-start.15) | collective-permute-done | bytes 327712 | tf_op jit(solution)/shard_map/ppermute | solution.py:59
  112.2 2.7 %collective-permute-start.16 = (f32[640,128]{1,0:T(8,128)S(1)}, f32[640,128]{1,0:T(8,128)S(1)}, u32[]{:S(2)}, u32[]{:S(2)}) collective-permute-start(f32[640,128]{1,0:T(8,128)S(1)} %collective-permute-done.15), channel_id=1, source_target_pairs={{0,8},{8,0},{16,24},{24,16},{32,40},{40,32},{48,56},{56,48},{64,72... | collective-permute-start | bytes 983048 | tf_op jit(solution)/shard_map/ppermute | solution.py:60
  118.0 4.1 %convolution_subtract_fusion = f32[512,2048]{1,0:T(8,128)} fusion(f32[512,2048]{1,0:T(8,128)S(1)} %copy-done.1, f32[2048,128]{1,0:T(8,128)S(1)} %constant_dynamic-update-slice_fusion.1, f32[2048,128]{1,0:T(8,128)S(1)} %convolution_subtract_fusion.1, f32[512,128]{1,0:T(8,128)S(1)} %fusion.4, f32[512,128]{1,0:T(8,128)S(1)} %copy-done.2), kind=kOutput, calls=%fused_computation | convolution fusion | flops 1612316672 | bytes 11010048 | tf_op jit(solution)/shard_map/dot_general | solution.py:86
  (48 shorter events, 13.0 us)
Async XLA Ops:
  0.0 106.7 %copy-start = (f32[128,128]{1,0:T(8,128)S(1)}, f32[128,128]{1,0:T(8,128)}, u32[]{:S(2)}) copy-start(f32[128,128]{1,0:T(8,128)} %param.5) | copy-start | bytes 196612
  1.0 11.8 %collective-permute-start.5 = (f32[512,128]{1,0:T(8,128)S(1)}, f32[512,128]{1,0:T(8,128)S(1)}, u32[]{:S(2)}, u32[]{:S(2)}) collective-permute-start(f32[512,128]{1,0:T(8,128)S(1)} %broadcast_select_fusion.1), channel_id=1, source_target_pairs={{0,192},{8,200},{16,208},{24,216},{33,225},{41,233},{49,241},{57,2... | collective-permute-start | bytes 786440 | tf_op jit(solution)/shard_map/ppermute | solution.py:48
  5.3 8.8 %collective-permute-start.4 = (f32[512,128]{1,0:T(8,128)S(1)}, f32[512,128]{1,0:T(8,128)S(1)}, u32[]{:S(2)}, u32[]{:S(2)}) collective-permute-start(f32[512,128]{1,0:T(8,128)S(1)} %broadcast_select_fusion.1), channel_id=1, source_target_pairs={{0,160},{8,168},{16,176},{24,184},{33,129},{41,137},{49,145},{57,1... | collective-permute-start | bytes 786440 | tf_op jit(solution)/shard_map/ppermute | solution.py:48
  8.8 10.6 %collective-permute-start.3 = (f32[512,128]{1,0:T(8,128)S(1)}, f32[512,128]{1,0:T(8,128)S(1)}, u32[]{:S(2)}, u32[]{:S(2)}) collective-permute-start(f32[512,128]{1,0:T(8,128)S(1)} %broadcast_select_fusion.1), channel_id=1, source_target_pairs={{0,128},{8,136},{16,144},{24,152},{33,161},{41,169},{49,177},{57,1... | collective-permute-start | bytes 786440 | tf_op jit(solution)/shard_map/ppermute | solution.py:48
  10.2 14.9 %collective-permute-start.2 = (f32[512,128]{1,0:T(8,128)S(1)}, f32[512,128]{1,0:T(8,128)S(1)}, u32[]{:S(2)}, u32[]{:S(2)}) collective-permute-start(f32[512,128]{1,0:T(8,128)S(1)} %broadcast_select_fusion.1), channel_id=1, source_target_pairs={{0,96},{8,104},{16,112},{24,120},{33,65},{41,73},{49,81},{57,89},{... | collective-permute-start | bytes 786440 | tf_op jit(solution)/shard_map/ppermute | solution.py:48
  11.5 19.2 %collective-permute-start.1 = (f32[512,128]{1,0:T(8,128)S(1)}, f32[512,128]{1,0:T(8,128)S(1)}, u32[]{:S(2)}, u32[]{:S(2)}) collective-permute-start(f32[512,128]{1,0:T(8,128)S(1)} %broadcast_select_fusion.1), channel_id=1, source_target_pairs={{0,64},{8,72},{16,80},{24,88},{33,97},{41,105},{49,113},{57,121},{... | collective-permute-start | bytes 786440 | tf_op jit(solution)/shard_map/ppermute | solution.py:48
  12.8 17.8 %collective-permute-start.6 = (f32[512,128]{1,0:T(8,128)S(1)}, f32[512,128]{1,0:T(8,128)S(1)}, u32[]{:S(2)}, u32[]{:S(2)}) collective-permute-start(f32[512,128]{1,0:T(8,128)S(1)} %broadcast_select_fusion.1), channel_id=1, source_target_pairs={{0,224},{8,232},{16,240},{24,248},{33,193},{41,201},{49,209},{57,2... | collective-permute-start | bytes 786440 | tf_op jit(solution)/shard_map/ppermute | solution.py:48
  14.1 16.5 %collective-permute-start = (f32[512,128]{1,0:T(8,128)S(1)}, f32[512,128]{1,0:T(8,128)S(1)}, u32[]{:S(2)}, u32[]{:S(2)}) collective-permute-start(f32[512,128]{1,0:T(8,128)S(1)} %broadcast_select_fusion.1), channel_id=1, source_target_pairs={{0,32},{8,40},{16,48},{24,56},{33,1},{41,9},{49,17},{57,25},{66,98... | collective-permute-start | bytes 786440 | tf_op jit(solution)/shard_map/ppermute | solution.py:48
  31.8 6.3 %collective-permute-start.8 = (f32[512,128]{1,0:T(8,128)S(1)}, f32[512,128]{1,0:T(8,128)S(1)}, u32[]{:S(2)}, u32[]{:S(2)}) collective-permute-start(f32[512,128]{1,0:T(8,128)S(1)} %get-tuple-element.8), channel_id=1, source_target_pairs={{0,16},{8,24},{16,0},{24,8},{32,48},{40,56},{48,32},{56,40},{64,80... | collective-permute-start | bytes 786440 | tf_op jit(solution)/shard_map/ppermute | solution.py:59
  32.3 8.3 %collective-permute-start.7 = (f32[512,128]{1,0:T(8,128)S(1)}, f32[512,128]{1,0:T(8,128)S(1)}, u32[]{:S(2)}, u32[]{:S(2)}) collective-permute-start(f32[512,128]{1,0:T(8,128)S(1)} %get-tuple-element.8), channel_id=1, source_target_pairs={{0,8},{8,0},{16,24},{24,16},{32,40},{40,32},{48,56},{56,48},{64,72... | collective-permute-start | bytes 786440 | tf_op jit(solution)/shard_map/ppermute | solution.py:58
  38.1 3.6 %collective-permute-start.9 = (f32[512,128]{1,0:T(8,128)S(1)}, f32[512,128]{1,0:T(8,128)S(1)}, u32[]{:S(2)}, u32[]{:S(2)}) collective-permute-start(f32[512,128]{1,0:T(8,128)S(1)} %collective-permute-done.8), channel_id=1, source_target_pairs={{0,8},{8,0},{16,24},{24,16},{32,40},{40,32},{48,56},{56,48},{64,72... | collective-permute-start | bytes 786440 | tf_op jit(solution)/shard_map/ppermute | solution.py:60
  40.7 32.9 %copy-start.2 = (f32[512,128]{1,0:T(8,128)S(1)}, f32[512,128]{1,0:T(8,128)}, u32[]{:S(2)}) copy-start(f32[512,128]{1,0:T(8,128)} %param.4) | copy-start | bytes 786436
  74.0 8.5 %collective-permute-start.12 = (f32[640,128]{1,0:T(8,128)S(1)}, f32[640,128]{1,0:T(8,128)S(1)}, u32[]{:S(2)}, u32[]{:S(2)}) collective-permute-start(f32[640,128]{1,0:T(8,128)S(1)} %pad_maximum_fusion), channel_id=1, source_target_pairs={{0,96},{1,97},{2,98},{3,99},{4,100},{5,101},{6,102},{7,103},{8,104... | collective-permute-start | bytes 983048 | tf_op jit(solution)/shard_map/ppermute | solution.py:48
  76.0 12.7 %collective-permute-start.11 = (f32[640,128]{1,0:T(8,128)S(1)}, f32[640,128]{1,0:T(8,128)S(1)}, u32[]{:S(2)}, u32[]{:S(2)}) collective-permute-start(f32[640,128]{1,0:T(8,128)S(1)} %pad_maximum_fusion), channel_id=1, source_target_pairs={{0,64},{1,65},{2,66},{3,67},{4,68},{5,69},{6,70},{7,71},{8,72},{9,... | collective-permute-start | bytes 983048 | tf_op jit(solution)/shard_map/ppermute | solution.py:48
  77.1 14.4 %collective-permute-start.10 = (f32[640,128]{1,0:T(8,128)S(1)}, f32[640,128]{1,0:T(8,128)S(1)}, u32[]{:S(2)}, u32[]{:S(2)}) collective-permute-start(f32[640,128]{1,0:T(8,128)S(1)} %pad_maximum_fusion), channel_id=1, source_target_pairs={{0,32},{1,33},{2,34},{3,35},{4,36},{5,37},{6,38},{7,39},{8,40},{9,... | collective-permute-start | bytes 983048 | tf_op jit(solution)/shard_map/ppermute | solution.py:48
  91.6 12.8 %collective-permute-start.13 = (f32[640,128]{1,0:T(8,128)S(1)}, f32[640,128]{1,0:T(8,128)S(1)}, u32[]{:S(2)}, u32[]{:S(2)}) collective-permute-start(f32[640,128]{1,0:T(8,128)S(1)} %pad_maximum_fusion.1), channel_id=1, source_target_pairs={{0,128},{1,129},{2,130},{3,131},{4,132},{5,133},{6,134},{7,135},{8... | collective-permute-start | bytes 983048 | tf_op jit(solution)/shard_map/ppermute | solution.py:48
  104.6 7.5 %collective-permute-start.15 = (f32[640,128]{1,0:T(8,128)S(1)}, f32[640,128]{1,0:T(8,128)S(1)}, u32[]{:S(2)}, u32[]{:S(2)}) collective-permute-start(f32[640,128]{1,0:T(8,128)S(1)} %pad_maximum_fusion.2), channel_id=1, source_target_pairs={{0,16},{8,24},{16,0},{24,8},{32,48},{40,56},{48,32},{56,40},{64,80... | collective-permute-start | bytes 983048 | tf_op jit(solution)/shard_map/ppermute | solution.py:59
  104.7 10.1 %collective-permute-start.14 = (f32[640,128]{1,0:T(8,128)S(1)}, f32[640,128]{1,0:T(8,128)S(1)}, u32[]{:S(2)}, u32[]{:S(2)}) collective-permute-start(f32[640,128]{1,0:T(8,128)S(1)} %pad_maximum_fusion.2), channel_id=1, source_target_pairs={{0,8},{8,0},{16,24},{24,16},{32,40},{40,32},{48,56},{56,48},{64,72... | collective-permute-start | bytes 983048 | tf_op jit(solution)/shard_map/ppermute | solution.py:58
  112.2 3.9 %collective-permute-start.16 = (f32[640,128]{1,0:T(8,128)S(1)}, f32[640,128]{1,0:T(8,128)S(1)}, u32[]{:S(2)}, u32[]{:S(2)}) collective-permute-start(f32[640,128]{1,0:T(8,128)S(1)} %collective-permute-done.15), channel_id=1, source_target_pairs={{0,8},{8,0},{16,24},{24,16},{32,40},{40,32},{48,56},{56,48},{64,72... | collective-permute-start | bytes 983048 | tf_op jit(solution)/shard_map/ppermute | solution.py:60
  114.8 3.2 %copy-start.1 = (f32[512,2048]{1,0:T(8,128)S(1)}, f32[512,2048]{1,0:T(8,128)}, u32[]{:S(2)}) copy-start(f32[512,2048]{1,0:T(8,128)} %param.3) | copy-start | bytes 12582916

commit v18 on v14

--- a/solution.py
+++ b/solution.py
@@ -29,7 +29,7 @@
     mine = jnp.where(high == col, panel_rows, jnp.zeros_like(panel_rows))
     known = 1
     while known < col_count:
-        width = 4 if col_count % (known * 4) == 0 else 2
+        width = 4 if extra is None and col_count % (known * 4) == 0 else 2
         sent = mine if extra is None else jnp.concatenate([mine, extra], axis=0)
         arrived = []
         for digit in range(1, width):

time: 118 us -> 118 us (level)
  starting transfers between devices: 27.5 us -> 35.2 us
  waiting for transfers between devices: 39.7 us -> 32 us
    ppermute x2, starting transfers between devices: 5.22 us -> 11.5 us  [to_columns(): other = lax.ppermute(sent, 'row', core_pairs)]
    ppermute x8 -> x7, waiting for transfers between devices: 31.8 us -> 27.7 us  [to_columns(): arrived.append(lax.ppermute(sent, ('row', 'col'), pairs))]
    ppermute x2, waiting for transfers between devices: 5.63 us -> 1.96 us  [to_columns(): across = lax.ppermute(sent, 'row', [(i, i ^ 2) for i in range(row_count)])]
    ppermute x2, starting transfers between devices: 6.26 us -> 9.01 us  [to_columns(): diagonal = lax.ppermute(across, 'row', core_pairs)]
    ppermute x8 -> x7, starting transfers between devices: 13.2 us -> 11.5 us  [to_columns(): arrived.append(lax.ppermute(sent, ('row', 'col'), pairs))]
  transfers between devices with their start and end apart: 14 -> 13, of which waited for: 10 -> 8; matrix products, arithmetic and copies ran while one was open for 0% -> 0% of each run, Pallas kernels for 0% -> 0%
where the time goes in v18:
time: 118 us; the launch traced here: 117 us
  blocking collectives  36 us (31%)
  starting transfers between devices  35.2 us (30%)
  waiting for transfers between devices  32 us (27%)
  matrix products  11.1 us (9%)
  other arithmetic  2.31 us (2%)
    ppermute x7, waiting for transfers between devices, to_columns(): arrived.append(lax.ppermute(sent, ('row', 'col'), pairs))  27.7 us
    all_to_all x1, blocking collectives, col_sum_rows(): total = jnp.sum(lax.all_to_all(pieces, 'col', 0, 0, tiled=True), axis=0)  24 us
    all_to_all x1, blocking collectives, col_sum_rows(): lax.all_to_all(spread, 'col', 0, 0, tiled=True).reshape(partial.shape)  12 us
    ppermute x2, starting transfers between devices, to_columns(): other = lax.ppermute(sent, 'row', core_pairs)  11.5 us
    ppermute x7, starting transfers between devices, to_columns(): arrived.append(lax.ppermute(sent, ('row', 'col'), pairs))  11.5 us
    ppermute x2, starting transfers between devices, to_columns(): diagonal = lax.ppermute(across, 'row', core_pairs)  9.01 us
    dot_general x6, matrix products, product(): jnp.dot(left, right, precision=lax.Precision.HIGH, preferred_element_type...  6.33 us
    dot_general x1, matrix products, shards(): lax.dot_general(left, right, (((1,), (1,)), ((), ())), precision=lax.Prec...  4.1 us
  transfers between devices with their start and end apart: 13, of which 8 were waited for; matrix products, arithmetic and copies ran while one was open for 0% of the time, Pallas kernels for 0%

profile of v18, /device:TPU:1, one launch (start us, length us, event | category | flops | bytes accessed | tf_op | source)
XLA Modules:
  0.0 117.3 jit_solution(8441260688787474885)
XLA Ops:
  0.0 1.0 broadcast_select_fusion.1
  1.0 3.0 %collective-permute-start.1 = (f32[512,128]{1,0:T(8,128)S(1)}, f32[512,128]{1,0:T(8,128)S(1)}, u32[]{:S(2)}, u32[]{:S(2)}) collective-permute-start(f32[512,128]{1,0:T(8,128)S(1)} %broadcast_select_fusion.1), channel_id=1, source_target_pairs={{0,64},{8,72},{16,80},{24,88},{33,97},{41,105},{49,113},{57,121},{... | collective-permute-start | bytes 786440 | tf_op jit(solution)/shard_map/ppermute | solution.py:45
  4.0 3.3 %collective-permute-start.2 = (f32[512,128]{1,0:T(8,128)S(1)}, f32[512,128]{1,0:T(8,128)S(1)}, u32[]{:S(2)}, u32[]{:S(2)}) collective-permute-start(f32[512,128]{1,0:T(8,128)S(1)} %broadcast_select_fusion.1), channel_id=1, source_target_pairs={{0,96},{8,104},{16,112},{24,120},{33,65},{41,73},{49,81},{57,89},{... | collective-permute-start | bytes 786440 | tf_op jit(solution)/shard_map/ppermute | solution.py:45
  7.3 1.3 %collective-permute-start = (f32[512,128]{1,0:T(8,128)S(1)}, f32[512,128]{1,0:T(8,128)S(1)}, u32[]{:S(2)}, u32[]{:S(2)}) collective-permute-start(f32[512,128]{1,0:T(8,128)S(1)} %broadcast_select_fusion.1), channel_id=1, source_target_pairs={{0,32},{8,40},{16,48},{24,56},{33,1},{41,9},{49,17},{57,25},{66,98... | collective-permute-start | bytes 786440 | tf_op jit(solution)/shard_map/ppermute | solution.py:45
  8.6 5.3 %collective-permute-done.2 = f32[512,128]{1,0:T(8,128)S(1)} collective-permute-done((f32[512,128]{1,0:T(8,128)S(1)}, f32[512,128]{1,0:T(8,128)S(1)}, u32[]{:S(2)}, u32[]{:S(2)}) %collective-permute-start.2) | collective-permute-done | bytes 262176 | tf_op jit(solution)/shard_map/ppermute | solution.py:45
  14.9 1.3 %collective-permute-start.3 = (f32[512,128]{1,0:T(8,128)S(1)}, f32[512,128]{1,0:T(8,128)S(1)}, u32[]{:S(2)}, u32[]{:S(2)}) collective-permute-start(f32[512,128]{1,0:T(8,128)S(1)} %add_add_fusion), channel_id=1, source_target_pairs={{0,128},{1,129},{2,130},{3,131},{8,136},{9,137},{10,138},{11,139},... | collective-permute-start | bytes 786440 | tf_op jit(solution)/shard_map/ppermute | solution.py:45
  16.2 3.6 %collective-permute-done.3 = f32[512,128]{1,0:T(8,128)S(1)} collective-permute-done((f32[512,128]{1,0:T(8,128)S(1)}, f32[512,128]{1,0:T(8,128)S(1)}, u32[]{:S(2)}, u32[]{:S(2)}) %collective-permute-start.3) | collective-permute-done | bytes 262176 | tf_op jit(solution)/shard_map/ppermute | solution.py:45
  20.0 2.7 %collective-permute-start.5 = (f32[512,128]{1,0:T(8,128)S(1)}, f32[512,128]{1,0:T(8,128)S(1)}, u32[]{:S(2)}, u32[]{:S(2)}) collective-permute-start(f32[512,128]{1,0:T(8,128)S(1)} %get-tuple-element.8), channel_id=1, source_target_pairs={{0,16},{8,24},{16,0},{24,8},{32,48},{40,56},{48,32},{56,40},{64,80... | collective-permute-start | bytes 786440 | tf_op jit(solution)/shard_map/ppermute | solution.py:56
  22.7 2.5 %collective-permute-start.4 = (f32[512,128]{1,0:T(8,128)S(1)}, f32[512,128]{1,0:T(8,128)S(1)}, u32[]{:S(2)}, u32[]{:S(2)}) collective-permute-start(f32[512,128]{1,0:T(8,128)S(1)} %get-tuple-element.8), channel_id=1, source_target_pairs={{0,8},{8,0},{16,24},{24,16},{32,40},{40,32},{48,56},{56,48},{64,72... | collective-permute-start | bytes 786440 | tf_op jit(solution)/shard_map/ppermute | solution.py:55
  25.1 2.0 %collective-permute-done.5 = f32[512,128]{1,0:T(8,128)S(1)} collective-permute-done((f32[512,128]{1,0:T(8,128)S(1)}, f32[512,128]{1,0:T(8,128)S(1)}, u32[]{:S(2)}, u32[]{:S(2)}) %collective-permute-start.5) | collective-permute-done | bytes 262176 | tf_op jit(solution)/shard_map/ppermute | solution.py:56
  27.1 2.8 %collective-permute-start.6 = (f32[512,128]{1,0:T(8,128)S(1)}, f32[512,128]{1,0:T(8,128)S(1)}, u32[]{:S(2)}, u32[]{:S(2)}) collective-permute-start(f32[512,128]{1,0:T(8,128)S(1)} %collective-permute-done.5), channel_id=1, source_target_pairs={{0,8},{8,0},{16,24},{24,16},{32,40},{40,32},{48,56},{56,48},{64,72... | collective-permute-start | bytes 786440 | tf_op jit(solution)/shard_map/ppermute | solution.py:57
  30.0 1.1 collective-permute-done.6
  31.1 4.5 %convolution_bitcast_fusion = f32[512,128]{0,1:T(8,128)S(1)} fusion(f32[2048,128]{1,0:T(8,128)S(1)} %constant_dynamic-update-slice_fusion.1, f32[512,2048]{1,0:T(8,128)} %param.3), kind=kOutput, calls=%fused_computation.9 | convolution fusion | flops 805306368 | bytes 5505024 | tf_op jit(solution)/shard_map/dot_general | solution.py:8
  35.7 24.0 %all_to_all.11 = f32[8,64,128]{2,1,0:T(8,128)S(1)} all-to-all(f32[8,64,128]{2,1,0:T(8,128)S(1)} %bitcast.30), channel_id=1, replica_groups=mesh['row'=32,'col'=8] {'col'}, dimensions={0} | all-to-all | bytes 524288 | tf_op jit(solution)/shard_map/all_to_all | solution.py:69
  59.8 12.0 %all_to_all.10 = f32[8,64,128]{2,1,0:T(8,128)S(1)} all-to-all(f32[8,64,128]{2,1,0:T(8,128)S(1)} %broadcast_in_dim.2), channel_id=1, replica_groups=mesh['row'=32,'col'=8] {'col'}, dimensions={0} | all-to-all | bytes 524288 | tf_op jit(solution)/shard_map/all_to_all | solution.py:71
  72.3 1.1 collective-permute-start.7
  73.4 6.4 %collective-permute-done.7 = f32[640,128]{1,0:T(8,128)S(1)} collective-permute-done((f32[640,128]{1,0:T(8,128)S(1)}, f32[640,128]{1,0:T(8,128)S(1)}, u32[]{:S(2)}, u32[]{:S(2)}) %collective-permute-start.7) | collective-permute-done | bytes 327712 | tf_op jit(solution)/shard_map/ppermute | solution.py:45
  79.9 1.4 %collective-permute-start.8 = (f32[640,128]{1,0:T(8,128)S(1)}, f32[640,128]{1,0:T(8,128)S(1)}, u32[]{:S(2)}, u32[]{:S(2)}) collective-permute-start(f32[640,128]{1,0:T(8,128)S(1)} %pad_maximum_fusion.1), channel_id=1, source_target_pairs={{0,64},{1,65},{2,66},{3,67},{4,68},{5,69},{6,70},{7,71},{8,72},{9,... | collective-permute-start | bytes 983048 | tf_op jit(solution)/shard_map/ppermute | solution.py:45
  81.2 4.6 %collective-permute-done.8 = f32[640,128]{1,0:T(8,128)S(1)} collective-permute-done((f32[640,128]{1,0:T(8,128)S(1)}, f32[640,128]{1,0:T(8,128)S(1)}, u32[]{:S(2)}, u32[]{:S(2)}) %collective-permute-start.8) | collective-permute-done | bytes 327712 | tf_op jit(solution)/shard_map/ppermute | solution.py:45
  86.1 7.8 %collective-permute-done.9 = f32[640,128]{1,0:T(8,128)S(1)} collective-permute-done((f32[640,128]{1,0:T(8,128)S(1)}, f32[640,128]{1,0:T(8,128)S(1)}, u32[]{:S(2)}, u32[]{:S(2)}) %collective-permute-start.9) | collective-permute-done | bytes 327712 | tf_op jit(solution)/shard_map/ppermute | solution.py:45
  94.5 9.1 %collective-permute-start.10 = (f32[640,128]{1,0:T(8,128)S(1)}, f32[640,128]{1,0:T(8,128)S(1)}, u32[]{:S(2)}, u32[]{:S(2)}) collective-permute-start(f32[640,128]{1,0:T(8,128)S(1)} %pad_maximum_fusion.3), channel_id=1, source_target_pairs={{0,8},{8,0},{16,24},{24,16},{32,40},{40,32},{48,56},{56,48},{64,72... | collective-permute-start | bytes 983048 | tf_op jit(solution)/shard_map/ppermute | solution.py:55
  103.8 6.2 %collective-permute-start.12 = (f32[640,128]{1,0:T(8,128)S(1)}, f32[640,128]{1,0:T(8,128)S(1)}, u32[]{:S(2)}, u32[]{:S(2)}) collective-permute-start(f32[640,128]{1,0:T(8,128)S(1)} %collective-permute-done.11), channel_id=1, source_target_pairs={{0,8},{8,0},{16,24},{24,16},{32,40},{40,32},{48,56},{56,48},{64,72... | collective-permute-start | bytes 983048 | tf_op jit(solution)/shard_map/ppermute | solution.py:57
  110.1 1.2 %collective-permute-done.12 = f32[640,128]{1,0:T(8,128)S(1)} collective-permute-done((f32[640,128]{1,0:T(8,128)S(1)}, f32[640,128]{1,0:T(8,128)S(1)}, u32[]{:S(2)}, u32[]{:S(2)}) %collective-permute-start.12) | collective-permute-done | bytes 327712 | tf_op jit(solution)/shard_map/ppermute | solution.py:57
  113.2 4.1 %convolution_subtract_fusion = f32[512,2048]{1,0:T(8,128)} fusion(f32[512,2048]{1,0:T(8,128)S(1)} %copy-done.1, f32[2048,128]{1,0:T(8,128)S(1)} %constant_dynamic-update-slice_fusion.1, f32[2048,128]{1,0:T(8,128)S(1)} %convolution_subtract_fusion.1, f32[512,128]{1,0:T(8,128)S(1)} %fusion.4, f32[512,128]{1,0:T(8,128)S(1)} %copy-done.2), kind=kOutput, calls=%fused_computation | convolution fusion | flops 1612316672 | bytes 11010048 | tf_op jit(solution)/shard_map/dot_general | solution.py:83
  (44 shorter events, 4.8 us)
Async XLA Ops:
  0.0 103.5 %copy-start = (f32[128,128]{1,0:T(8,128)S(1)}, f32[128,128]{1,0:T(8,128)}, u32[]{:S(2)}) copy-start(f32[128,128]{1,0:T(8,128)} %param.5) | copy-start | bytes 196612
  1.0 7.6 %collective-permute-start.1 = (f32[512,128]{1,0:T(8,128)S(1)}, f32[512,128]{1,0:T(8,128)S(1)}, u32[]{:S(2)}, u32[]{:S(2)}) collective-permute-start(f32[512,128]{1,0:T(8,128)S(1)} %broadcast_select_fusion.1), channel_id=1, source_target_pairs={{0,64},{8,72},{16,80},{24,88},{33,97},{41,105},{49,113},{57,121},{... | collective-permute-start | bytes 786440 | tf_op jit(solution)/shard_map/ppermute | solution.py:45
  4.0 9.9 %collective-permute-start.2 = (f32[512,128]{1,0:T(8,128)S(1)}, f32[512,128]{1,0:T(8,128)S(1)}, u32[]{:S(2)}, u32[]{:S(2)}) collective-permute-start(f32[512,128]{1,0:T(8,128)S(1)} %broadcast_select_fusion.1), channel_id=1, source_target_pairs={{0,96},{8,104},{16,112},{24,120},{33,65},{41,73},{49,81},{57,89},{... | collective-permute-start | bytes 786440 | tf_op jit(solution)/shard_map/ppermute | solution.py:45
  7.3 6.6 %collective-permute-start = (f32[512,128]{1,0:T(8,128)S(1)}, f32[512,128]{1,0:T(8,128)S(1)}, u32[]{:S(2)}, u32[]{:S(2)}) collective-permute-start(f32[512,128]{1,0:T(8,128)S(1)} %broadcast_select_fusion.1), channel_id=1, source_target_pairs={{0,32},{8,40},{16,48},{24,56},{33,1},{41,9},{49,17},{57,25},{66,98... | collective-permute-start | bytes 786440 | tf_op jit(solution)/shard_map/ppermute | solution.py:45
  14.9 4.9 %collective-permute-start.3 = (f32[512,128]{1,0:T(8,128)S(1)}, f32[512,128]{1,0:T(8,128)S(1)}, u32[]{:S(2)}, u32[]{:S(2)}) collective-permute-start(f32[512,128]{1,0:T(8,128)S(1)} %add_add_fusion), channel_id=1, source_target_pairs={{0,128},{1,129},{2,130},{3,131},{8,136},{9,137},{10,138},{11,139},... | collective-permute-start | bytes 786440 | tf_op jit(solution)/shard_map/ppermute | solution.py:45
  20.0 7.1 %collective-permute-start.5 = (f32[512,128]{1,0:T(8,128)S(1)}, f32[512,128]{1,0:T(8,128)S(1)}, u32[]{:S(2)}, u32[]{:S(2)}) collective-permute-start(f32[512,128]{1,0:T(8,128)S(1)} %get-tuple-element.8), channel_id=1, source_target_pairs={{0,16},{8,24},{16,0},{24,8},{32,48},{40,56},{48,32},{56,40},{64,80... | collective-permute-start | bytes 786440 | tf_op jit(solution)/shard_map/ppermute | solution.py:56
  22.7 7.3 %collective-permute-start.4 = (f32[512,128]{1,0:T(8,128)S(1)}, f32[512,128]{1,0:T(8,128)S(1)}, u32[]{:S(2)}, u32[]{:S(2)}) collective-permute-start(f32[512,128]{1,0:T(8,128)S(1)} %get-tuple-element.8), channel_id=1, source_target_pairs={{0,8},{8,0},{16,24},{24,16},{32,40},{40,32},{48,56},{56,48},{64,72... | collective-permute-start | bytes 786440 | tf_op jit(solution)/shard_map/ppermute | solution.py:55
  27.1 4.0 %collective-permute-start.6 = (f32[512,128]{1,0:T(8,128)S(1)}, f32[512,128]{1,0:T(8,128)S(1)}, u32[]{:S(2)}, u32[]{:S(2)}) collective-permute-start(f32[512,128]{1,0:T(8,128)S(1)} %collective-permute-done.5), channel_id=1, source_target_pairs={{0,8},{8,0},{16,24},{24,16},{32,40},{40,32},{48,56},{56,48},{64,72... | collective-permute-start | bytes 786440 | tf_op jit(solution)/shard_map/ppermute | solution.py:57
  30.0 41.8 %copy-start.2 = (f32[512,128]{1,0:T(8,128)S(1)}, f32[512,128]{1,0:T(8,128)}, u32[]{:S(2)}) copy-start(f32[512,128]{1,0:T(8,128)} %param.4) | copy-start | bytes 786436
  72.3 7.5 %collective-permute-start.7 = (f32[640,128]{1,0:T(8,128)S(1)}, f32[640,128]{1,0:T(8,128)S(1)}, u32[]{:S(2)}, u32[]{:S(2)}) collective-permute-start(f32[640,128]{1,0:T(8,128)S(1)} %pad_maximum_fusion), channel_id=1, source_target_pairs={{0,32},{1,33},{2,34},{3,35},{4,36},{5,37},{6,38},{7,39},{8,40},{9,... | collective-permute-start | bytes 983048 | tf_op jit(solution)/shard_map/ppermute | solution.py:45
  79.9 6.0 %collective-permute-start.8 = (f32[640,128]{1,0:T(8,128)S(1)}, f32[640,128]{1,0:T(8,128)S(1)}, u32[]{:S(2)}, u32[]{:S(2)}) collective-permute-start(f32[640,128]{1,0:T(8,128)S(1)} %pad_maximum_fusion.1), channel_id=1, source_target_pairs={{0,64},{1,65},{2,66},{3,67},{4,68},{5,69},{6,70},{7,71},{8,72},{9,... | collective-permute-start | bytes 983048 | tf_op jit(solution)/shard_map/ppermute | solution.py:45
  86.0 7.9 %collective-permute-start.9 = (f32[640,128]{1,0:T(8,128)S(1)}, f32[640,128]{1,0:T(8,128)S(1)}, u32[]{:S(2)}, u32[]{:S(2)}) collective-permute-start(f32[640,128]{1,0:T(8,128)S(1)} %pad_maximum_fusion.2), channel_id=1, source_target_pairs={{0,128},{1,129},{2,130},{3,131},{4,132},{5,133},{6,134},{7,135},{8... | collective-permute-start | bytes 983048 | tf_op jit(solution)/shard_map/ppermute | solution.py:45
  94.0 9.8 %collective-permute-start.11 = (f32[640,128]{1,0:T(8,128)S(1)}, f32[640,128]{1,0:T(8,128)S(1)}, u32[]{:S(2)}, u32[]{:S(2)}) collective-permute-start(f32[640,128]{1,0:T(8,128)S(1)} %pad_maximum_fusion.3), channel_id=1, source_target_pairs={{0,16},{8,24},{16,0},{24,8},{32,48},{40,56},{48,32},{56,40},{64,80... | collective-permute-start | bytes 983048 | tf_op jit(solution)/shard_map/ppermute | solution.py:56
  94.5 15.5 %collective-permute-start.10 = (f32[640,128]{1,0:T(8,128)S(1)}, f32[640,128]{1,0:T(8,128)S(1)}, u32[]{:S(2)}, u32[]{:S(2)}) collective-permute-start(f32[640,128]{1,0:T(8,128)S(1)} %pad_maximum_fusion.3), channel_id=1, source_target_pairs={{0,8},{8,0},{16,24},{24,16},{32,40},{40,32},{48,56},{56,48},{64,72... | collective-permute-start | bytes 983048 | tf_op jit(solution)/shard_map/ppermute | solution.py:55
  103.8 7.4 %collective-permute-start.12 = (f32[640,128]{1,0:T(8,128)S(1)}, f32[640,128]{1,0:T(8,128)S(1)}, u32[]{:S(2)}, u32[]{:S(2)}) collective-permute-start(f32[640,128]{1,0:T(8,128)S(1)} %collective-permute-done.11), channel_id=1, source_target_pairs={{0,8},{8,0},{16,24},{24,16},{32,40},{40,32},{48,56},{56,48},{64,72... | collective-permute-start | bytes 983048 | tf_op jit(solution)/shard_map/ppermute | solution.py:57
  110.0 3.2 %copy-start.1 = (f32[512,2048]{1,0:T(8,128)S(1)}, f32[512,2048]{1,0:T(8,128)}, u32[]{:S(2)}) copy-start(f32[512,2048]{1,0:T(8,128)} %param.3) | copy-start | bytes 12582916

commit v19 on v14

--- a/solution.py
+++ b/solution.py
@@ -30,23 +30,26 @@
     known = 1
     while known < col_count:
         width = 4 if col_count % (known * 4) == 0 else 2
-        sent = mine if extra is None else jnp.concatenate([mine, extra], axis=0)
         arrived = []
         for digit in range(1, width):
             mask = digit * known
             pairs = []
+            every = []
             for src_high in range(col_count):
                 for src_low in range(per):
                     for src_col in range(col_count):
-                        if extra is not None or (src_high ^ src_col) < known:
-                            src = (per * src_high + src_low) * col_count + src_col
-                            dst = (per * (src_high ^ mask) + src_low) * col_count + src_col
+                        src = (per * src_high + src_low) * col_count + src_col
+                        dst = (per * (src_high ^ mask) + src_low) * col_count + src_col
+                        every.append((src, dst))
+                        if (src_high ^ src_col) < known:
                             pairs.append((src, dst))
-            arrived.append(lax.ppermute(sent, ("row", "col"), pairs))
-        for got in arrived:
-            mine = mine + got[:rows_here]
+            block = lax.ppermute(mine, ("row", "col"), pairs)
+            summand = None if extra is None else lax.ppermute(extra, ("row", "col"), every)
+            arrived.append((block, summand))
+        for block, summand in arrived:
+            mine = mine + block
             if extra is not None:
-                extra = extra + got[rows_here:]
+                extra = extra + summand
         known *= width
     gathered = jnp.zeros((per * rows_here,) + panel_rows.shape[1:], panel_rows.dtype)
     gathered = lax.dynamic_update_slice_in_dim(gathered, mine, low * rows_here, 0)

time: 118 us -> 115 us (0.975)
  waiting for transfers between devices: 39.7 us -> 22.3 us
  starting transfers between devices: 27.5 us -> 41.6 us
    ppermute x8 -> x12, waiting for transfers between devices: 31.8 us -> 18 us  [the longest x8 9.68 us: to_columns(): block = lax.ppermute(mine, ('row', 'col'), pairs)]
    ppermute x8 -> x12, starting transfers between devices: 13.2 us -> 20.2 us  [the longest x8 15.9 us: to_columns(): block = lax.ppermute(mine, ('row', 'col'), pairs)]
    ppermute x2, starting transfers between devices: 5.22 us -> 9.36 us  [to_columns(): other = lax.ppermute(sent, 'row', core_pairs)]
    ppermute x2, waiting for transfers between devices: 5.63 us -> 1.96 us  [to_columns(): across = lax.ppermute(sent, 'row', [(i, i ^ 2) for i in range(row_count)])]
    ppermute x2, starting transfers between devices: 6.26 us -> 9.16 us  [to_columns(): diagonal = lax.ppermute(across, 'row', core_pairs)]
  transfers between devices with their start and end apart: 14 -> 18, of which waited for: 10 -> 8; matrix products, arithmetic and copies ran while one was open for 0% -> 1% of each run, Pallas kernels for 0% -> 0%
where the time goes in v19:
time: 115 us; the launch traced here: 114 us
  starting transfers between devices  41.6 us (36%)
  blocking collectives  36.1 us (31%)
  waiting for transfers between devices  22.3 us (19%)
  matrix products  11.1 us (10%)
  other arithmetic  2.22 us (2%)
    all_to_all x1, blocking collectives, col_sum_rows(): total = jnp.sum(lax.all_to_all(pieces, 'col', 0, 0, tiled=True), axis=0)  24.1 us
    ppermute x8, starting transfers between devices, to_columns(): block = lax.ppermute(mine, ('row', 'col'), pairs)  15.9 us
    all_to_all x1, blocking collectives, col_sum_rows(): lax.all_to_all(spread, 'col', 0, 0, tiled=True).reshape(partial.shape)  12.1 us
    ppermute x8, waiting for transfers between devices, to_columns(): block = lax.ppermute(mine, ('row', 'col'), pairs)  9.68 us
    ppermute x2, starting transfers between devices, to_columns(): other = lax.ppermute(sent, 'row', core_pairs)  9.36 us
    ppermute x2, starting transfers between devices, to_columns(): diagonal = lax.ppermute(across, 'row', core_pairs)  9.16 us
    ppermute x4, waiting for transfers between devices, to_columns(): lax.ppermute(extra, ('row', 'col'), every)  8.34 us
    dot_general x6, matrix products, product(): jnp.dot(left, right, precision=lax.Precision.HIGH, preferred_element_type...  6.38 us
  transfers between devices with their start and end apart: 18, of which 8 were waited for; matrix products, arithmetic and copies ran while one was open for 1% of the time, Pallas kernels for 0%

profile of v19, /device:TPU:1, one launch (start us, length us, event | category | flops | bytes accessed | tf_op | source)
XLA Modules:
  0.0 114.1 jit_solution(10028020613015784555)
XLA Ops:
  1.0 3.0 %collective-permute-start.1 = (f32[512,128]{1,0:T(8,128)S(1)}, f32[512,128]{1,0:T(8,128)S(1)}, u32[]{:S(2)}, u32[]{:S(2)}) collective-permute-start(f32[512,128]{1,0:T(8,128)S(1)} %broadcast_select_fusion.1), channel_id=1, source_target_pairs={{0,64},{8,72},{16,80},{24,88},{33,97},{41,105},{49,113},{57,121},{... | collective-permute-start | bytes 786440 | tf_op jit(solution)/shard_map/ppermute | solution.py:46
  4.0 3.3 %collective-permute-start.2 = (f32[512,128]{1,0:T(8,128)S(1)}, f32[512,128]{1,0:T(8,128)S(1)}, u32[]{:S(2)}, u32[]{:S(2)}) collective-permute-start(f32[512,128]{1,0:T(8,128)S(1)} %broadcast_select_fusion.1), channel_id=1, source_target_pairs={{0,96},{8,104},{16,112},{24,120},{33,65},{41,73},{49,81},{57,89},{... | collective-permute-start | bytes 786440 | tf_op jit(solution)/shard_map/ppermute | solution.py:46
  7.3 1.3 %collective-permute-start = (f32[512,128]{1,0:T(8,128)S(1)}, f32[512,128]{1,0:T(8,128)S(1)}, u32[]{:S(2)}, u32[]{:S(2)}) collective-permute-start(f32[512,128]{1,0:T(8,128)S(1)} %broadcast_select_fusion.1), channel_id=1, source_target_pairs={{0,32},{8,40},{16,48},{24,56},{33,1},{41,9},{49,17},{57,25},{66,98... | collective-permute-start | bytes 786440 | tf_op jit(solution)/shard_map/ppermute | solution.py:46
  8.6 5.3 %collective-permute-done.2 = f32[512,128]{1,0:T(8,128)S(1)} collective-permute-done((f32[512,128]{1,0:T(8,128)S(1)}, f32[512,128]{1,0:T(8,128)S(1)}, u32[]{:S(2)}, u32[]{:S(2)}) %collective-permute-start.2) | collective-permute-done | bytes 262176 | tf_op jit(solution)/shard_map/ppermute | solution.py:46
  14.9 1.3 %collective-permute-start.3 = (f32[512,128]{1,0:T(8,128)S(1)}, f32[512,128]{1,0:T(8,128)S(1)}, u32[]{:S(2)}, u32[]{:S(2)}) collective-permute-start(f32[512,128]{1,0:T(8,128)S(1)} %add_add_fusion.1), channel_id=1, source_target_pairs={{0,128},{1,129},{2,130},{3,131},{8,136},{9,137},{10,138},{11,139},... | collective-permute-start | bytes 786440 | tf_op jit(solution)/shard_map/ppermute | solution.py:46
  16.2 3.6 %collective-permute-done.3 = f32[512,128]{1,0:T(8,128)S(1)} collective-permute-done((f32[512,128]{1,0:T(8,128)S(1)}, f32[512,128]{1,0:T(8,128)S(1)}, u32[]{:S(2)}, u32[]{:S(2)}) %collective-permute-start.3) | collective-permute-done | bytes 262176 | tf_op jit(solution)/shard_map/ppermute | solution.py:46
  20.0 2.7 %collective-permute-start.5 = (f32[512,128]{1,0:T(8,128)S(1)}, f32[512,128]{1,0:T(8,128)S(1)}, u32[]{:S(2)}, u32[]{:S(2)}) collective-permute-start(f32[512,128]{1,0:T(8,128)S(1)} %get-tuple-element.8), channel_id=1, source_target_pairs={{0,16},{8,24},{16,0},{24,8},{32,48},{40,56},{48,32},{56,40},{64,80... | collective-permute-start | bytes 786440 | tf_op jit(solution)/shard_map/ppermute | solution.py:59
  22.7 2.5 %collective-permute-start.4 = (f32[512,128]{1,0:T(8,128)S(1)}, f32[512,128]{1,0:T(8,128)S(1)}, u32[]{:S(2)}, u32[]{:S(2)}) collective-permute-start(f32[512,128]{1,0:T(8,128)S(1)} %get-tuple-element.8), channel_id=1, source_target_pairs={{0,8},{8,0},{16,24},{24,16},{32,40},{40,32},{48,56},{56,48},{64,72... | collective-permute-start | bytes 786440 | tf_op jit(solution)/shard_map/ppermute | solution.py:58
  25.1 2.0 %collective-permute-done.5 = f32[512,128]{1,0:T(8,128)S(1)} collective-permute-done((f32[512,128]{1,0:T(8,128)S(1)}, f32[512,128]{1,0:T(8,128)S(1)}, u32[]{:S(2)}, u32[]{:S(2)}) %collective-permute-start.5) | collective-permute-done | bytes 262176 | tf_op jit(solution)/shard_map/ppermute | solution.py:59
  27.1 2.8 %collective-permute-start.6 = (f32[512,128]{1,0:T(8,128)S(1)}, f32[512,128]{1,0:T(8,128)S(1)}, u32[]{:S(2)}, u32[]{:S(2)}) collective-permute-start(f32[512,128]{1,0:T(8,128)S(1)} %collective-permute-done.5), channel_id=1, source_target_pairs={{0,8},{8,0},{16,24},{24,16},{32,40},{40,32},{48,56},{56,48},{64,72... | collective-permute-start | bytes 786440 | tf_op jit(solution)/shard_map/ppermute | solution.py:60
  31.1 4.5 %convolution_bitcast_fusion = f32[512,128]{0,1:T(8,128)S(1)} fusion(f32[2048,128]{1,0:T(8,128)S(1)} %constant_dynamic-update-slice_fusion.1, f32[512,2048]{1,0:T(8,128)} %param.3), kind=kOutput, calls=%fused_computation.9 | convolution fusion | flops 805306368 | bytes 5505024 | tf_op jit(solution)/shard_map/dot_general | solution.py:8
  35.8 24.1 %all_to_all.11 = f32[8,64,128]{2,1,0:T(8,128)S(1)} all-to-all(f32[8,64,128]{2,1,0:T(8,128)S(1)} %bitcast.30), channel_id=1, replica_groups=mesh['row'=32,'col'=8] {'col'}, dimensions={0} | all-to-all | bytes 524288 | tf_op jit(solution)/shard_map/all_to_all | solution.py:72
  59.9 12.1 %all_to_all.10 = f32[8,64,128]{2,1,0:T(8,128)S(1)} all-to-all(f32[8,64,128]{2,1,0:T(8,128)S(1)} %broadcast_in_dim.2), channel_id=1, replica_groups=mesh['row'=32,'col'=8] {'col'}, dimensions={0} | all-to-all | bytes 524288 | tf_op jit(solution)/shard_map/all_to_all | solution.py:74
  72.0 3.1 %collective-permute-start.12 = (f32[512,128]{1,0:T(8,128)S(1)}, f32[512,128]{1,0:T(8,128)S(1)}, u32[]{:S(2)}, u32[]{:S(2)}) collective-permute-start(f32[512,128]{1,0:T(8,128)S(1)} %broadcast_select_fusion), channel_id=1, source_target_pairs={{0,64},{8,72},{16,80},{24,88},{33,97},{41,105},{49,113},{57,121},{... | collective-permute-start | bytes 786440 | tf_op jit(solution)/shard_map/ppermute | solution.py:46
  75.1 1.3 %collective-permute-start.13 = (f32[512,128]{1,0:T(8,128)S(1)}, f32[512,128]{1,0:T(8,128)S(1)}, u32[]{:S(2)}, u32[]{:S(2)}) collective-permute-start(f32[512,128]{1,0:T(8,128)S(1)} %broadcast_select_fusion), channel_id=1, source_target_pairs={{0,96},{8,104},{16,112},{24,120},{33,65},{41,73},{49,81},{57,89},{... | collective-permute-start | bytes 786440 | tf_op jit(solution)/shard_map/ppermute | solution.py:46
  76.4 1.3 %collective-permute-start.11 = (f32[512,128]{1,0:T(8,128)S(1)}, f32[512,128]{1,0:T(8,128)S(1)}, u32[]{:S(2)}, u32[]{:S(2)}) collective-permute-start(f32[512,128]{1,0:T(8,128)S(1)} %broadcast_select_fusion), channel_id=1, source_target_pairs={{0,32},{8,40},{16,48},{24,56},{33,1},{41,9},{49,17},{57,25},{66,98... | collective-permute-start | bytes 786440 | tf_op jit(solution)/shard_map/ppermute | solution.py:46
  78.4 4.0 %collective-permute-start.7 = (f32[128,128]{1,0:T(8,128)S(1)}, f32[128,128]{1,0:T(8,128)S(1)}, u32[]{:S(2)}, u32[]{:S(2)}) collective-permute-start(f32[128,128]{1,0:T(8,128)S(1)} %convolution_bitcast_fusion.1), channel_id=1, source_target_pairs={{0,32},{1,33},{2,34},{3,35},{4,36},{5,37},{6,38},{7,39},{8,40},{9,... | collective-permute-start | bytes 196616 | tf_op jit(solution)/shard_map/ppermute | solution.py:47
  83.2 1.3 %collective-permute-start.14 = (f32[512,128]{1,0:T(8,128)S(1)}, f32[512,128]{1,0:T(8,128)S(1)}, u32[]{:S(2)}, u32[]{:S(2)}) collective-permute-start(f32[512,128]{1,0:T(8,128)S(1)} %add_add_fusion), channel_id=1, source_target_pairs={{0,128},{1,129},{2,130},{3,131},{8,136},{9,137},{10,138},{11,139},... | collective-permute-start | bytes 786440 | tf_op jit(solution)/shard_map/ppermute | solution.py:46
  84.5 1.4 %collective-permute-done.8 = f32[128,128]{1,0:T(8,128)S(1)} collective-permute-done((f32[128,128]{1,0:T(8,128)S(1)}, f32[128,128]{1,0:T(8,128)S(1)}, u32[]{:S(2)}, u32[]{:S(2)}) %collective-permute-start.8) | collective-permute-done | bytes 65568 | tf_op jit(solution)/shard_map/ppermute | solution.py:47
  86.1 6.9 %collective-permute-done.10 = f32[128,128]{1,0:T(8,128)S(1)} collective-permute-done((f32[128,128]{1,0:T(8,128)S(1)}, f32[128,128]{1,0:T(8,128)S(1)}, u32[]{:S(2)}, u32[]{:S(2)}) %collective-permute-start.10) | collective-permute-done | bytes 65568 | tf_op jit(solution)/shard_map/ppermute | solution.py:47
  93.3 6.9 %collective-permute-start.15 = (f32[640,128]{1,0:T(8,128)S(1)}, f32[640,128]{1,0:T(8,128)S(1)}, u32[]{:S(2)}, u32[]{:S(2)}) collective-permute-start(f32[640,128]{1,0:T(8,128)S(1)} %pad_maximum_fusion), channel_id=1, source_target_pairs={{0,8},{8,0},{16,24},{24,16},{32,40},{40,32},{48,56},{56,48},{64,72... | collective-permute-start | bytes 983048 | tf_op jit(solution)/shard_map/ppermute | solution.py:58
  100.4 6.3 %collective-permute-start.17 = (f32[640,128]{1,0:T(8,128)S(1)}, f32[640,128]{1,0:T(8,128)S(1)}, u32[]{:S(2)}, u32[]{:S(2)}) collective-permute-start(f32[640,128]{1,0:T(8,128)S(1)} %collective-permute-done.16), channel_id=1, source_target_pairs={{0,8},{8,0},{16,24},{24,16},{32,40},{40,32},{48,56},{56,48},{64,72... | collective-permute-start | bytes 983048 | tf_op jit(solution)/shard_map/ppermute | solution.py:60
  106.8 1.2 %collective-permute-done.17 = f32[640,128]{1,0:T(8,128)S(1)} collective-permute-done((f32[640,128]{1,0:T(8,128)S(1)}, f32[640,128]{1,0:T(8,128)S(1)}, u32[]{:S(2)}, u32[]{:S(2)}) %collective-permute-start.17) | collective-permute-done | bytes 327712 | tf_op jit(solution)/shard_map/ppermute | solution.py:60
  110.0 4.1 %convolution_subtract_fusion = f32[512,2048]{1,0:T(8,128)} fusion(f32[512,2048]{1,0:T(8,128)S(1)} %copy-done.1, f32[2048,128]{1,0:T(8,128)S(1)} %constant_dynamic-update-slice_fusion.1, f32[2048,128]{1,0:T(8,128)S(1)} %convolution_subtract_fusion.1, f32[512,128]{1,0:T(8,128)S(1)} %fusion.4, f32[512,128]{1,0:T(8,128)S(1)} %copy-done.2), kind=kOutput, calls=%fused_computation | convolution fusion | flops 1612316672 | bytes 11010048 | tf_op jit(solution)/shard_map/dot_general | solution.py:86
  (49 shorter events, 7.5 us)
Async XLA Ops:
  0.0 100.2 %copy-start = (f32[128,128]{1,0:T(8,128)S(1)}, f32[128,128]{1,0:T(8,128)}, u32[]{:S(2)}) copy-start(f32[128,128]{1,0:T(8,128)} %param.5) | copy-start | bytes 196612
  1.0 7.6 %collective-permute-start.1 = (f32[512,128]{1,0:T(8,128)S(1)}, f32[512,128]{1,0:T(8,128)S(1)}, u32[]{:S(2)}, u32[]{:S(2)}) collective-permute-start(f32[512,128]{1,0:T(8,128)S(1)} %broadcast_select_fusion.1), channel_id=1, source_target_pairs={{0,64},{8,72},{16,80},{24,88},{33,97},{41,105},{49,113},{57,121},{... | collective-permute-start | bytes 786440 | tf_op jit(solution)/shard_map/ppermute | solution.py:46
  4.0 9.9 %collective-permute-start.2 = (f32[512,128]{1,0:T(8,128)S(1)}, f32[512,128]{1,0:T(8,128)S(1)}, u32[]{:S(2)}, u32[]{:S(2)}) collective-permute-start(f32[512,128]{1,0:T(8,128)S(1)} %broadcast_select_fusion.1), channel_id=1, source_target_pairs={{0,96},{8,104},{16,112},{24,120},{33,65},{41,73},{49,81},{57,89},{... | collective-permute-start | bytes 786440 | tf_op jit(solution)/shard_map/ppermute | solution.py:46
  7.3 6.6 %collective-permute-start = (f32[512,128]{1,0:T(8,128)S(1)}, f32[512,128]{1,0:T(8,128)S(1)}, u32[]{:S(2)}, u32[]{:S(2)}) collective-permute-start(f32[512,128]{1,0:T(8,128)S(1)} %broadcast_select_fusion.1), channel_id=1, source_target_pairs={{0,32},{8,40},{16,48},{24,56},{33,1},{41,9},{49,17},{57,25},{66,98... | collective-permute-start | bytes 786440 | tf_op jit(solution)/shard_map/ppermute | solution.py:46
  14.9 4.9 %collective-permute-start.3 = (f32[512,128]{1,0:T(8,128)S(1)}, f32[512,128]{1,0:T(8,128)S(1)}, u32[]{:S(2)}, u32[]{:S(2)}) collective-permute-start(f32[512,128]{1,0:T(8,128)S(1)} %add_add_fusion.1), channel_id=1, source_target_pairs={{0,128},{1,129},{2,130},{3,131},{8,136},{9,137},{10,138},{11,139},... | collective-permute-start | bytes 786440 | tf_op jit(solution)/shard_map/ppermute | solution.py:46
  20.0 7.1 %collective-permute-start.5 = (f32[512,128]{1,0:T(8,128)S(1)}, f32[512,128]{1,0:T(8,128)S(1)}, u32[]{:S(2)}, u32[]{:S(2)}) collective-permute-start(f32[512,128]{1,0:T(8,128)S(1)} %get-tuple-element.8), channel_id=1, source_target_pairs={{0,16},{8,24},{16,0},{24,8},{32,48},{40,56},{48,32},{56,40},{64,80... | collective-permute-start | bytes 786440 | tf_op jit(solution)/shard_map/ppermute | solution.py:59
  22.7 7.3 %collective-permute-start.4 = (f32[512,128]{1,0:T(8,128)S(1)}, f32[512,128]{1,0:T(8,128)S(1)}, u32[]{:S(2)}, u32[]{:S(2)}) collective-permute-start(f32[512,128]{1,0:T(8,128)S(1)} %get-tuple-element.8), channel_id=1, source_target_pairs={{0,8},{8,0},{16,24},{24,16},{32,40},{40,32},{48,56},{56,48},{64,72... | collective-permute-start | bytes 786440 | tf_op jit(solution)/shard_map/ppermute | solution.py:58
  27.1 4.0 %collective-permute-start.6 = (f32[512,128]{1,0:T(8,128)S(1)}, f32[512,128]{1,0:T(8,128)S(1)}, u32[]{:S(2)}, u32[]{:S(2)}) collective-permute-start(f32[512,128]{1,0:T(8,128)S(1)} %collective-permute-done.5), channel_id=1, source_target_pairs={{0,8},{8,0},{16,24},{24,16},{32,40},{40,32},{48,56},{56,48},{64,72... | collective-permute-start | bytes 786440 | tf_op jit(solution)/shard_map/ppermute | solution.py:60
  31.1 46.6 %copy-start.2 = (f32[512,128]{1,0:T(8,128)S(1)}, f32[512,128]{1,0:T(8,128)}, u32[]{:S(2)}) copy-start(f32[512,128]{1,0:T(8,128)} %param.4) | copy-start | bytes 786436
  72.0 6.4 %collective-permute-start.12 = (f32[512,128]{1,0:T(8,128)S(1)}, f32[512,128]{1,0:T(8,128)S(1)}, u32[]{:S(2)}, u32[]{:S(2)}) collective-permute-start(f32[512,128]{1,0:T(8,128)S(1)} %broadcast_select_fusion), channel_id=1, source_target_pairs={{0,64},{8,72},{16,80},{24,88},{33,97},{41,105},{49,113},{57,121},{... | collective-permute-start | bytes 786440 | tf_op jit(solution)/shard_map/ppermute | solution.py:46
  75.1 8.0 %collective-permute-start.13 = (f32[512,128]{1,0:T(8,128)S(1)}, f32[512,128]{1,0:T(8,128)S(1)}, u32[]{:S(2)}, u32[]{:S(2)}) collective-permute-start(f32[512,128]{1,0:T(8,128)S(1)} %broadcast_select_fusion), channel_id=1, source_target_pairs={{0,96},{8,104},{16,112},{24,120},{33,65},{41,73},{49,81},{57,89},{... | collective-permute-start | bytes 786440 | tf_op jit(solution)/shard_map/ppermute | solution.py:46
  76.4 6.7 %collective-permute-start.11 = (f32[512,128]{1,0:T(8,128)S(1)}, f32[512,128]{1,0:T(8,128)S(1)}, u32[]{:S(2)}, u32[]{:S(2)}) collective-permute-start(f32[512,128]{1,0:T(8,128)S(1)} %broadcast_select_fusion), channel_id=1, source_target_pairs={{0,32},{8,40},{16,48},{24,56},{33,1},{41,9},{49,17},{57,25},{66,98... | collective-permute-start | bytes 786440 | tf_op jit(solution)/shard_map/ppermute | solution.py:46
  78.1 6.4 %collective-permute-start.9 = (f32[128,128]{1,0:T(8,128)S(1)}, f32[128,128]{1,0:T(8,128)S(1)}, u32[]{:S(2)}, u32[]{:S(2)}) collective-permute-start(f32[128,128]{1,0:T(8,128)S(1)} %convolution_bitcast_fusion.1), channel_id=1, source_target_pairs={{0,96},{1,97},{2,98},{3,99},{4,100},{5,101},{6,102},{7,103},{8,104... | collective-permute-start | bytes 196616 | tf_op jit(solution)/shard_map/ppermute | solution.py:47
  78.2 7.7 %collective-permute-start.8 = (f32[128,128]{1,0:T(8,128)S(1)}, f32[128,128]{1,0:T(8,128)S(1)}, u32[]{:S(2)}, u32[]{:S(2)}) collective-permute-start(f32[128,128]{1,0:T(8,128)S(1)} %convolution_bitcast_fusion.1), channel_id=1, source_target_pairs={{0,64},{1,65},{2,66},{3,67},{4,68},{5,69},{6,70},{7,71},{8,72},{9,... | collective-permute-start | bytes 196616 | tf_op jit(solution)/shard_map/ppermute | solution.py:47
  78.4 7.6 %collective-permute-start.7 = (f32[128,128]{1,0:T(8,128)S(1)}, f32[128,128]{1,0:T(8,128)S(1)}, u32[]{:S(2)}, u32[]{:S(2)}) collective-permute-start(f32[128,128]{1,0:T(8,128)S(1)} %convolution_bitcast_fusion.1), channel_id=1, source_target_pairs={{0,32},{1,33},{2,34},{3,35},{4,36},{5,37},{6,38},{7,39},{8,40},{9,... | collective-permute-start | bytes 196616 | tf_op jit(solution)/shard_map/ppermute | solution.py:47
  83.2 9.8 %collective-permute-start.14 = (f32[512,128]{1,0:T(8,128)S(1)}, f32[512,128]{1,0:T(8,128)S(1)}, u32[]{:S(2)}, u32[]{:S(2)}) collective-permute-start(f32[512,128]{1,0:T(8,128)S(1)} %add_add_fusion), channel_id=1, source_target_pairs={{0,128},{1,129},{2,130},{3,131},{8,136},{9,137},{10,138},{11,139},... | collective-permute-start | bytes 786440 | tf_op jit(solution)/shard_map/ppermute | solution.py:46
  86.0 7.0 %collective-permute-start.10 = (f32[128,128]{1,0:T(8,128)S(1)}, f32[128,128]{1,0:T(8,128)S(1)}, u32[]{:S(2)}, u32[]{:S(2)}) collective-permute-start(f32[128,128]{1,0:T(8,128)S(1)} %add_add_fusion.2), channel_id=1, source_target_pairs={{0,128},{1,129},{2,130},{3,131},{4,132},{5,133},{6,134},{7,135},{8... | collective-permute-start | bytes 196616 | tf_op jit(solution)/shard_map/ppermute | solution.py:47
  93.1 7.3 %collective-permute-start.16 = (f32[640,128]{1,0:T(8,128)S(1)}, f32[640,128]{1,0:T(8,128)S(1)}, u32[]{:S(2)}, u32[]{:S(2)}) collective-permute-start(f32[640,128]{1,0:T(8,128)S(1)} %pad_maximum_fusion), channel_id=1, source_target_pairs={{0,16},{8,24},{16,0},{24,8},{32,48},{40,56},{48,32},{56,40},{64,80... | collective-permute-start | bytes 983048 | tf_op jit(solution)/shard_map/ppermute | solution.py:59
  93.3 13.5 %collective-permute-start.15 = (f32[640,128]{1,0:T(8,128)S(1)}, f32[640,128]{1,0:T(8,128)S(1)}, u32[]{:S(2)}, u32[]{:S(2)}) collective-permute-start(f32[640,128]{1,0:T(8,128)S(1)} %pad_maximum_fusion), channel_id=1, source_target_pairs={{0,8},{8,0},{16,24},{24,16},{32,40},{40,32},{48,56},{56,48},{64,72... | collective-permute-start | bytes 983048 | tf_op jit(solution)/shard_map/ppermute | solution.py:58
  100.4 7.6 %collective-permute-start.17 = (f32[640,128]{1,0:T(8,128)S(1)}, f32[640,128]{1,0:T(8,128)S(1)}, u32[]{:S(2)}, u32[]{:S(2)}) collective-permute-start(f32[640,128]{1,0:T(8,128)S(1)} %collective-permute-done.16), channel_id=1, source_target_pairs={{0,8},{8,0},{16,24},{24,16},{32,40},{40,32},{48,56},{56,48},{64,72... | collective-permute-start | bytes 983048 | tf_op jit(solution)/shard_map/ppermute | solution.py:60
  106.8 3.2 %copy-start.1 = (f32[512,2048]{1,0:T(8,128)S(1)}, f32[512,2048]{1,0:T(8,128)}, u32[]{:S(2)}) copy-start(f32[512,2048]{1,0:T(8,128)} %param.3) | copy-start | bytes 12582916

commit v20 on v19

--- a/solution.py
+++ b/solution.py
@@ -54,15 +54,16 @@
     gathered = jnp.zeros((per * rows_here,) + panel_rows.shape[1:], panel_rows.dtype)
     gathered = lax.dynamic_update_slice_in_dim(gathered, mine, low * rows_here, 0)
     core_pairs = [(i, i ^ 1) for i in range(row_count)]
-    sent = mine if extra is None else jnp.concatenate([mine, extra], axis=0)
-    other = lax.ppermute(sent, "row", core_pairs)
-    across = lax.ppermute(sent, "row", [(i, i ^ 2) for i in range(row_count)])
+    other = lax.ppermute(mine, "row", core_pairs)
+    across = lax.ppermute(mine, "row", [(i, i ^ 2) for i in range(row_count)])
     diagonal = lax.ppermute(across, "row", core_pairs)
     for mask, block in ((1, other), (2, across), (3, diagonal)):
         gathered = lax.dynamic_update_slice_in_dim(gathered, block[:rows_here], (low ^ mask) * rows_here, 0)
     if extra is None:
         return gathered, None
-    total = extra + other[rows_here:] + across[rows_here:] + diagonal[rows_here:]
+    total = extra
+    for mask in range(1, per):
+        total = total + lax.ppermute(extra, "row", [(i, i ^ mask) for i in range(row_count)])
     return gathered, total
 
 

time: 115 us -> 122 us (1.061)
  waiting for transfers between devices: 22.3 us -> 29.6 us
    ppermute x4 -> x7, waiting for transfers between devices: 1.97 us -> 8.75 us  [the longest x2 8.74 us: to_columns(): across = lax.ppermute(mine, 'row', [(i, i ^ 2) for i in range(row_count)])]
    ppermute x2, starting transfers between devices: 9.16 us -> 3.7 us  [to_columns(): diagonal = lax.ppermute(across, 'row', core_pairs)]
    ppermute x8, starting transfers between devices: 15.9 us -> 20.4 us  [to_columns(): block = lax.ppermute(mine, ('row', 'col'), pairs)]
    ppermute x8, waiting for transfers between devices: 9.68 us -> 13.5 us  [to_columns(): block = lax.ppermute(mine, ('row', 'col'), pairs)]
    ppermute x4, waiting for transfers between devices: 8.34 us -> 5.52 us  [to_columns(): lax.ppermute(extra, ('row', 'col'), every)]
    ppermute x4 -> x7, starting transfers between devices: 12.2 us -> 13.5 us  [the longest x3 6.37 us: to_columns(): lax.ppermute(extra, 'row', [(i, i ^ mask) for i in range(row_count)])]
  transfers between devices with their start and end apart: 18 -> 21, of which waited for: 8 -> 8; matrix products, arithmetic and copies ran while one was open for 1% -> 2% of each run, Pallas kernels for 0% -> 0%
where the time goes in v20:
time: 122 us
  starting transfers between devices  41.9 us (34%)
  blocking collectives  36 us (30%)
  waiting for transfers between devices  29.6 us (24%)
  matrix products  11.1 us (9%)
  other arithmetic  2.2 us (2%)
    all_to_all x1, blocking collectives, col_sum_rows(): total = jnp.sum(lax.all_to_all(pieces, 'col', 0, 0, tiled=True), axis=0)  24 us
    ppermute x8, starting transfers between devices, to_columns(): block = lax.ppermute(mine, ('row', 'col'), pairs)  20.4 us
    ppermute x8, waiting for transfers between devices, to_columns(): block = lax.ppermute(mine, ('row', 'col'), pairs)  13.5 us
    all_to_all x1, blocking collectives, col_sum_rows(): lax.all_to_all(spread, 'col', 0, 0, tiled=True).reshape(partial.shape)  12 us
    ppermute x2, waiting for transfers between devices, to_columns(): across = lax.ppermute(mine, 'row', [(i, i ^ 2) for i in range(row_count)])  8.74 us
    dot_general x6, matrix products, product(): jnp.dot(left, right, precision=lax.Precision.HIGH, preferred_element_type...  6.41 us
    ppermute x3, starting transfers between devices, to_columns(): lax.ppermute(extra, 'row', [(i, i ^ mask) for i in range(row_count)])  6.37 us
    ppermute x4, waiting for transfers between devices, to_columns(): lax.ppermute(extra, ('row', 'col'), every)  5.52 us
  transfers between devices with their start and end apart: 21, of which 8 were waited for; matrix products, arithmetic and copies ran while one was open for 2% of the time, Pallas kernels for 0%

profile of v20, /device:TPU:1, one launch (start us, length us, event | category | flops | bytes accessed | tf_op | source)
XLA Modules:
  0.0 121.7 jit_solution(15166269889411282470)
XLA Ops:
  1.0 3.0 %collective-permute-start.1 = (f32[512,128]{1,0:T(8,128)S(1)}, f32[512,128]{1,0:T(8,128)S(1)}, u32[]{:S(2)}, u32[]{:S(2)}) collective-permute-start(f32[512,128]{1,0:T(8,128)S(1)} %broadcast_select_fusion.1), channel_id=1, source_target_pairs={{0,64},{8,72},{16,80},{24,88},{33,97},{41,105},{49,113},{57,121},{... | collective-permute-start | bytes 786440 | tf_op jit(solution)/shard_map/ppermute | solution.py:46
  4.0 3.3 %collective-permute-start.2 = (f32[512,128]{1,0:T(8,128)S(1)}, f32[512,128]{1,0:T(8,128)S(1)}, u32[]{:S(2)}, u32[]{:S(2)}) collective-permute-start(f32[512,128]{1,0:T(8,128)S(1)} %broadcast_select_fusion.1), channel_id=1, source_target_pairs={{0,96},{8,104},{16,112},{24,120},{33,65},{41,73},{49,81},{57,89},{... | collective-permute-start | bytes 786440 | tf_op jit(solution)/shard_map/ppermute | solution.py:46
  7.3 1.3 %collective-permute-start = (f32[512,128]{1,0:T(8,128)S(1)}, f32[512,128]{1,0:T(8,128)S(1)}, u32[]{:S(2)}, u32[]{:S(2)}) collective-permute-start(f32[512,128]{1,0:T(8,128)S(1)} %broadcast_select_fusion.1), channel_id=1, source_target_pairs={{0,32},{8,40},{16,48},{24,56},{33,1},{41,9},{49,17},{57,25},{66,98... | collective-permute-start | bytes 786440 | tf_op jit(solution)/shard_map/ppermute | solution.py:46
  8.6 5.3 %collective-permute-done.2 = f32[512,128]{1,0:T(8,128)S(1)} collective-permute-done((f32[512,128]{1,0:T(8,128)S(1)}, f32[512,128]{1,0:T(8,128)S(1)}, u32[]{:S(2)}, u32[]{:S(2)}) %collective-permute-start.2) | collective-permute-done | bytes 262176 | tf_op jit(solution)/shard_map/ppermute | solution.py:46
  14.9 1.3 %collective-permute-start.3 = (f32[512,128]{1,0:T(8,128)S(1)}, f32[512,128]{1,0:T(8,128)S(1)}, u32[]{:S(2)}, u32[]{:S(2)}) collective-permute-start(f32[512,128]{1,0:T(8,128)S(1)} %add_add_fusion.1), channel_id=1, source_target_pairs={{0,128},{1,129},{2,130},{3,131},{8,136},{9,137},{10,138},{11,139},... | collective-permute-start | bytes 786440 | tf_op jit(solution)/shard_map/ppermute | solution.py:46
  16.2 3.6 %collective-permute-done.3 = f32[512,128]{1,0:T(8,128)S(1)} collective-permute-done((f32[512,128]{1,0:T(8,128)S(1)}, f32[512,128]{1,0:T(8,128)S(1)}, u32[]{:S(2)}, u32[]{:S(2)}) %collective-permute-start.3) | collective-permute-done | bytes 262176 | tf_op jit(solution)/shard_map/ppermute | solution.py:46
  20.0 2.7 %collective-permute-start.5 = (f32[512,128]{1,0:T(8,128)S(1)}, f32[512,128]{1,0:T(8,128)S(1)}, u32[]{:S(2)}, u32[]{:S(2)}) collective-permute-start(f32[512,128]{1,0:T(8,128)S(1)} %get-tuple-element.8), channel_id=1, source_target_pairs={{0,16},{8,24},{16,0},{24,8},{32,48},{40,56},{48,32},{56,40},{64,80... | collective-permute-start | bytes 786440 | tf_op jit(solution)/shard_map/ppermute | solution.py:58
  22.7 2.5 %collective-permute-start.4 = (f32[512,128]{1,0:T(8,128)S(1)}, f32[512,128]{1,0:T(8,128)S(1)}, u32[]{:S(2)}, u32[]{:S(2)}) collective-permute-start(f32[512,128]{1,0:T(8,128)S(1)} %get-tuple-element.8), channel_id=1, source_target_pairs={{0,8},{8,0},{16,24},{24,16},{32,40},{40,32},{48,56},{56,48},{64,72... | collective-permute-start | bytes 786440 | tf_op jit(solution)/shard_map/ppermute | solution.py:57
  25.1 2.0 %collective-permute-done.5 = f32[512,128]{1,0:T(8,128)S(1)} collective-permute-done((f32[512,128]{1,0:T(8,128)S(1)}, f32[512,128]{1,0:T(8,128)S(1)}, u32[]{:S(2)}, u32[]{:S(2)}) %collective-permute-start.5) | collective-permute-done | bytes 262176 | tf_op jit(solution)/shard_map/ppermute | solution.py:58
  27.1 2.8 %collective-permute-start.6 = (f32[512,128]{1,0:T(8,128)S(1)}, f32[512,128]{1,0:T(8,128)S(1)}, u32[]{:S(2)}, u32[]{:S(2)}) collective-permute-start(f32[512,128]{1,0:T(8,128)S(1)} %collective-permute-done.5), channel_id=1, source_target_pairs={{0,8},{8,0},{16,24},{24,16},{32,40},{40,32},{48,56},{56,48},{64,72... | collective-permute-start | bytes 786440 | tf_op jit(solution)/shard_map/ppermute | solution.py:59
  31.1 4.5 %convolution_bitcast_fusion = f32[512,128]{0,1:T(8,128)S(1)} fusion(f32[2048,128]{1,0:T(8,128)S(1)} %constant_dynamic-update-slice_fusion.4, f32[512,2048]{1,0:T(8,128)} %param.3), kind=kOutput, calls=%fused_computation.9 | convolution fusion | flops 805306368 | bytes 5505024 | tf_op jit(solution)/shard_map/dot_general | solution.py:8
  35.7 24.0 %all_to_all.11 = f32[8,64,128]{2,1,0:T(8,128)S(1)} all-to-all(f32[8,64,128]{2,1,0:T(8,128)S(1)} %bitcast.30), channel_id=1, replica_groups=mesh['row'=32,'col'=8] {'col'}, dimensions={0} | all-to-all | bytes 524288 | tf_op jit(solution)/shard_map/all_to_all | solution.py:73
  59.8 12.0 %all_to_all.10 = f32[8,64,128]{2,1,0:T(8,128)S(1)} all-to-all(f32[8,64,128]{2,1,0:T(8,128)S(1)} %broadcast_in_dim.2), channel_id=1, replica_groups=mesh['row'=32,'col'=8] {'col'}, dimensions={0} | all-to-all | bytes 524288 | tf_op jit(solution)/shard_map/all_to_all | solution.py:75
  72.2 2.0 %collective-permute-start.9 = (f32[128,128]{0,1:T(8,128)S(1)}, f32[128,128]{0,1:T(8,128)S(1)}, u32[]{:S(2)}, u32[]{:S(2)}) collective-permute-start(f32[128,128]{0,1:T(8,128)S(1)} %convolution_bitcast_fusion.1), channel_id=1, source_target_pairs={{0,96},{1,97},{2,98},{3,99},{4,100},{5,101},{6,102},{7,103},{8,104... | collective-permute-start | bytes 196616 | tf_op jit(solution)/shard_map/ppermute | solution.py:47
  74.5 1.9 %collective-permute-start.7 = (f32[128,128]{0,1:T(8,128)S(1)}, f32[128,128]{0,1:T(8,128)S(1)}, u32[]{:S(2)}, u32[]{:S(2)}) collective-permute-start(f32[128,128]{0,1:T(8,128)S(1)} %convolution_bitcast_fusion.1), channel_id=1, source_target_pairs={{0,32},{1,33},{2,34},{3,35},{4,36},{5,37},{6,38},{7,39},{8,40},{9,... | collective-permute-start | bytes 196616 | tf_op jit(solution)/shard_map/ppermute | solution.py:47
  76.5 3.2 %collective-permute-start.15 = (f32[512,128]{1,0:T(8,128)S(1)}, f32[512,128]{1,0:T(8,128)S(1)}, u32[]{:S(2)}, u32[]{:S(2)}) collective-permute-start(f32[512,128]{1,0:T(8,128)S(1)} %broadcast_select_fusion), channel_id=1, source_target_pairs={{0,64},{8,72},{16,80},{24,88},{33,97},{41,105},{49,113},{57,121},{... | collective-permute-start | bytes 786440 | tf_op jit(solution)/shard_map/ppermute | solution.py:46
  79.7 1.3 %collective-permute-start.16 = (f32[512,128]{1,0:T(8,128)S(1)}, f32[512,128]{1,0:T(8,128)S(1)}, u32[]{:S(2)}, u32[]{:S(2)}) collective-permute-start(f32[512,128]{1,0:T(8,128)S(1)} %broadcast_select_fusion), channel_id=1, source_target_pairs={{0,96},{8,104},{16,112},{24,120},{33,65},{41,73},{49,81},{57,89},{... | collective-permute-start | bytes 786440 | tf_op jit(solution)/shard_map/ppermute | solution.py:46
  82.8 5.5 %collective-permute-done.10 = f32[128,128]{0,1:T(8,128)S(1)} collective-permute-done((f32[128,128]{0,1:T(8,128)S(1)}, f32[128,128]{0,1:T(8,128)S(1)}, u32[]{:S(2)}, u32[]{:S(2)}) %collective-permute-start.10) | collective-permute-done | bytes 65568 | tf_op jit(solution)/shard_map/ppermute | solution.py:47
  88.3 5.3 %collective-permute-start.13 = (f32[128,128]{0,1:T(8,128)S(1)}, f32[128,128]{0,1:T(8,128)S(1)}, u32[]{:S(2)}, u32[]{:S(2)}) collective-permute-start(f32[128,128]{0,1:T(8,128)S(1)} %add.79), channel_id=1, source_target_pairs={{0,24},{8,16},{16,8},{24,0},{32,56},{40,48},{48,40},{56,32},{64,88... | collective-permute-start | bytes 196616 | tf_op jit(solution)/shard_map/ppermute | solution.py:66
  94.7 5.6 %collective-permute-start.17 = (f32[512,128]{1,0:T(8,128)S(1)}, f32[512,128]{1,0:T(8,128)S(1)}, u32[]{:S(2)}, u32[]{:S(2)}) collective-permute-start(f32[512,128]{1,0:T(8,128)S(1)} %add_add_fusion), channel_id=1, source_target_pairs={{0,128},{1,129},{2,130},{3,131},{8,136},{9,137},{10,138},{11,139},... | collective-permute-start | bytes 786440 | tf_op jit(solution)/shard_map/ppermute | solution.py:46
  100.9 4.6 %collective-permute-done.17 = f32[512,128]{1,0:T(8,128)S(1)} collective-permute-done((f32[512,128]{1,0:T(8,128)S(1)}, f32[512,128]{1,0:T(8,128)S(1)}, u32[]{:S(2)}, u32[]{:S(2)}) %collective-permute-start.17) | collective-permute-done | bytes 262176 | tf_op jit(solution)/shard_map/ppermute | solution.py:46
  105.6 1.4 %collective-permute-start.18 = (f32[512,128]{1,0:T(8,128)S(1)}, f32[512,128]{1,0:T(8,128)S(1)}, u32[]{:S(2)}, u32[]{:S(2)}) collective-permute-start(f32[512,128]{1,0:T(8,128)S(1)} %get-tuple-element.6), channel_id=1, source_target_pairs={{0,8},{8,0},{16,24},{24,16},{32,40},{40,32},{48,56},{56,48},{64,72... | collective-permute-start | bytes 786440 | tf_op jit(solution)/shard_map/ppermute | solution.py:57
  108.2 6.8 %collective-permute-done.19 = f32[512,128]{1,0:T(8,128)S(1)} collective-permute-done((f32[512,128]{1,0:T(8,128)S(1)}, f32[512,128]{1,0:T(8,128)S(1)}, u32[]{:S(2)}, u32[]{:S(2)}) %collective-permute-start.19) | collective-permute-done | bytes 262176 | tf_op jit(solution)/shard_map/ppermute | solution.py:58
  117.6 4.1 %convolution_subtract_fusion = f32[512,2048]{1,0:T(8,128)} fusion(f32[512,2048]{1,0:T(8,128)S(1)} %copy-done.1, f32[2048,128]{1,0:T(8,128)S(1)} %constant_dynamic-update-slice_fusion.4, f32[2048,128]{1,0:T(8,128)S(1)} %convolution_subtract_fusion.1, f32[512,128]{1,0:T(8,128)S(1)} %fusion.4, f32[512,128]{1,0:T(8,128)S(1)} %copy-done.2), kind=kOutput, calls=%fused_computation | convolution fusion | flops 1612316672 | bytes 11010048 | tf_op jit(solution)/shard_map/dot_general | solution.py:87
  (54 shorter events, 11.3 us)
Async XLA Ops:
  0.0 82.5 %copy-start = (f32[128,128]{1,0:T(8,128)S(1)}, f32[128,128]{1,0:T(8,128)}, u32[]{:S(2)}) copy-start(f32[128,128]{1,0:T(8,128)} %param.5) | copy-start | bytes 196612
  1.0 7.6 %collective-permute-start.1 = (f32[512,128]{1,0:T(8,128)S(1)}, f32[512,128]{1,0:T(8,128)S(1)}, u32[]{:S(2)}, u32[]{:S(2)}) collective-permute-start(f32[512,128]{1,0:T(8,128)S(1)} %broadcast_select_fusion.1), channel_id=1, source_target_pairs={{0,64},{8,72},{16,80},{24,88},{33,97},{41,105},{49,113},{57,121},{... | collective-permute-start | bytes 786440 | tf_op jit(solution)/shard_map/ppermute | solution.py:46
  4.0 9.9 %collective-permute-start.2 = (f32[512,128]{1,0:T(8,128)S(1)}, f32[512,128]{1,0:T(8,128)S(1)}, u32[]{:S(2)}, u32[]{:S(2)}) collective-permute-start(f32[512,128]{1,0:T(8,128)S(1)} %broadcast_select_fusion.1), channel_id=1, source_target_pairs={{0,96},{8,104},{16,112},{24,120},{33,65},{41,73},{49,81},{57,89},{... | collective-permute-start | bytes 786440 | tf_op jit(solution)/shard_map/ppermute | solution.py:46
  7.3 6.6 %collective-permute-start = (f32[512,128]{1,0:T(8,128)S(1)}, f32[512,128]{1,0:T(8,128)S(1)}, u32[]{:S(2)}, u32[]{:S(2)}) collective-permute-start(f32[512,128]{1,0:T(8,128)S(1)} %broadcast_select_fusion.1), channel_id=1, source_target_pairs={{0,32},{8,40},{16,48},{24,56},{33,1},{41,9},{49,17},{57,25},{66,98... | collective-permute-start | bytes 786440 | tf_op jit(solution)/shard_map/ppermute | solution.py:46
  14.9 4.9 %collective-permute-start.3 = (f32[512,128]{1,0:T(8,128)S(1)}, f32[512,128]{1,0:T(8,128)S(1)}, u32[]{:S(2)}, u32[]{:S(2)}) collective-permute-start(f32[512,128]{1,0:T(8,128)S(1)} %add_add_fusion.1), channel_id=1, source_target_pairs={{0,128},{1,129},{2,130},{3,131},{8,136},{9,137},{10,138},{11,139},... | collective-permute-start | bytes 786440 | tf_op jit(solution)/shard_map/ppermute | solution.py:46
  20.0 7.1 %collective-permute-start.5 = (f32[512,128]{1,0:T(8,128)S(1)}, f32[512,128]{1,0:T(8,128)S(1)}, u32[]{:S(2)}, u32[]{:S(2)}) collective-permute-start(f32[512,128]{1,0:T(8,128)S(1)} %get-tuple-element.8), channel_id=1, source_target_pairs={{0,16},{8,24},{16,0},{24,8},{32,48},{40,56},{48,32},{56,40},{64,80... | collective-permute-start | bytes 786440 | tf_op jit(solution)/shard_map/ppermute | solution.py:58
  22.7 7.3 %collective-permute-start.4 = (f32[512,128]{1,0:T(8,128)S(1)}, f32[512,128]{1,0:T(8,128)S(1)}, u32[]{:S(2)}, u32[]{:S(2)}) collective-permute-start(f32[512,128]{1,0:T(8,128)S(1)} %get-tuple-element.8), channel_id=1, source_target_pairs={{0,8},{8,0},{16,24},{24,16},{32,40},{40,32},{48,56},{56,48},{64,72... | collective-permute-start | bytes 786440 | tf_op jit(solution)/shard_map/ppermute | solution.py:57
  27.1 4.0 %collective-permute-start.6 = (f32[512,128]{1,0:T(8,128)S(1)}, f32[512,128]{1,0:T(8,128)S(1)}, u32[]{:S(2)}, u32[]{:S(2)}) collective-permute-start(f32[512,128]{1,0:T(8,128)S(1)} %collective-permute-done.5), channel_id=1, source_target_pairs={{0,8},{8,0},{16,24},{24,16},{32,40},{40,32},{48,56},{56,48},{64,72... | collective-permute-start | bytes 786440 | tf_op jit(solution)/shard_map/ppermute | solution.py:59
  30.0 41.8 %copy-start.2 = (f32[512,128]{1,0:T(8,128)S(1)}, f32[512,128]{1,0:T(8,128)}, u32[]{:S(2)}) copy-start(f32[512,128]{1,0:T(8,128)} %param.4) | copy-start | bytes 786436
  72.2 8.8 %collective-permute-start.9 = (f32[128,128]{0,1:T(8,128)S(1)}, f32[128,128]{0,1:T(8,128)S(1)}, u32[]{:S(2)}, u32[]{:S(2)}) collective-permute-start(f32[128,128]{0,1:T(8,128)S(1)} %convolution_bitcast_fusion.1), channel_id=1, source_target_pairs={{0,96},{1,97},{2,98},{3,99},{4,100},{5,101},{6,102},{7,103},{8,104... | collective-permute-start | bytes 196616 | tf_op jit(solution)/shard_map/ppermute | solution.py:47
  74.2 8.1 %collective-permute-start.8 = (f32[128,128]{0,1:T(8,128)S(1)}, f32[128,128]{0,1:T(8,128)S(1)}, u32[]{:S(2)}, u32[]{:S(2)}) collective-permute-start(f32[128,128]{0,1:T(8,128)S(1)} %convolution_bitcast_fusion.1), channel_id=1, source_target_pairs={{0,64},{1,65},{2,66},{3,67},{4,68},{5,69},{6,70},{7,71},{8,72},{9,... | collective-permute-start | bytes 196616 | tf_op jit(solution)/shard_map/ppermute | solution.py:47
  74.5 7.9 %collective-permute-start.7 = (f32[128,128]{0,1:T(8,128)S(1)}, f32[128,128]{0,1:T(8,128)S(1)}, u32[]{:S(2)}, u32[]{:S(2)}) collective-permute-start(f32[128,128]{0,1:T(8,128)S(1)} %convolution_bitcast_fusion.1), channel_id=1, source_target_pairs={{0,32},{1,33},{2,34},{3,35},{4,36},{5,37},{6,38},{7,39},{8,40},{9,... | collective-permute-start | bytes 196616 | tf_op jit(solution)/shard_map/ppermute | solution.py:47
  76.5 18.2 %collective-permute-start.15 = (f32[512,128]{1,0:T(8,128)S(1)}, f32[512,128]{1,0:T(8,128)S(1)}, u32[]{:S(2)}, u32[]{:S(2)}) collective-permute-start(f32[512,128]{1,0:T(8,128)S(1)} %broadcast_select_fusion), channel_id=1, source_target_pairs={{0,64},{8,72},{16,80},{24,88},{33,97},{41,105},{49,113},{57,121},{... | collective-permute-start | bytes 786440 | tf_op jit(solution)/shard_map/ppermute | solution.py:46
  79.7 15.0 %collective-permute-start.16 = (f32[512,128]{1,0:T(8,128)S(1)}, f32[512,128]{1,0:T(8,128)S(1)}, u32[]{:S(2)}, u32[]{:S(2)}) collective-permute-start(f32[512,128]{1,0:T(8,128)S(1)} %broadcast_select_fusion), channel_id=1, source_target_pairs={{0,96},{8,104},{16,112},{24,120},{33,65},{41,73},{49,81},{57,89},{... | collective-permute-start | bytes 786440 | tf_op jit(solution)/shard_map/ppermute | solution.py:46
  81.0 13.6 %collective-permute-start.14 = (f32[512,128]{1,0:T(8,128)S(1)}, f32[512,128]{1,0:T(8,128)S(1)}, u32[]{:S(2)}, u32[]{:S(2)}) collective-permute-start(f32[512,128]{1,0:T(8,128)S(1)} %broadcast_select_fusion), channel_id=1, source_target_pairs={{0,32},{8,40},{16,48},{24,56},{33,1},{41,9},{49,17},{57,25},{66,98... | collective-permute-start | bytes 786440 | tf_op jit(solution)/shard_map/ppermute | solution.py:46
  82.4 5.9 %collective-permute-start.10 = (f32[128,128]{0,1:T(8,128)S(1)}, f32[128,128]{0,1:T(8,128)S(1)}, u32[]{:S(2)}, u32[]{:S(2)}) collective-permute-start(f32[128,128]{0,1:T(8,128)S(1)} %add_add_fusion.2), channel_id=1, source_target_pairs={{0,128},{1,129},{2,130},{3,131},{4,132},{5,133},{6,134},{7,135},{8... | collective-permute-start | bytes 196616 | tf_op jit(solution)/shard_map/ppermute | solution.py:47
  88.3 12.1 %collective-permute-start.13 = (f32[128,128]{0,1:T(8,128)S(1)}, f32[128,128]{0,1:T(8,128)S(1)}, u32[]{:S(2)}, u32[]{:S(2)}) collective-permute-start(f32[128,128]{0,1:T(8,128)S(1)} %add.79), channel_id=1, source_target_pairs={{0,24},{8,16},{16,8},{24,0},{32,56},{40,48},{48,40},{56,32},{64,88... | collective-permute-start | bytes 196616 | tf_op jit(solution)/shard_map/ppermute | solution.py:66
  93.6 6.8 %collective-permute-start.12 = (f32[128,128]{0,1:T(8,128)S(1)}, f32[128,128]{0,1:T(8,128)S(1)}, u32[]{:S(2)}, u32[]{:S(2)}) collective-permute-start(f32[128,128]{0,1:T(8,128)S(1)} %add.79), channel_id=1, source_target_pairs={{0,16},{8,24},{16,0},{24,8},{32,48},{40,56},{48,32},{56,40},{64,80... | collective-permute-start | bytes 196616 | tf_op jit(solution)/shard_map/ppermute | solution.py:66
  94.7 5.7 %collective-permute-start.11 = (f32[128,128]{0,1:T(8,128)S(1)}, f32[128,128]{0,1:T(8,128)S(1)}, u32[]{:S(2)}, u32[]{:S(2)}) collective-permute-start(f32[128,128]{0,1:T(8,128)S(1)} %add.79), channel_id=1, source_target_pairs={{0,8},{8,0},{16,24},{24,16},{32,40},{40,32},{48,56},{56,48},{64,72... | collective-permute-start | bytes 196616 | tf_op jit(solution)/shard_map/ppermute | solution.py:66
  94.7 10.8 %collective-permute-start.17 = (f32[512,128]{1,0:T(8,128)S(1)}, f32[512,128]{1,0:T(8,128)S(1)}, u32[]{:S(2)}, u32[]{:S(2)}) collective-permute-start(f32[512,128]{1,0:T(8,128)S(1)} %add_add_fusion), channel_id=1, source_target_pairs={{0,128},{1,129},{2,130},{3,131},{8,136},{9,137},{10,138},{11,139},... | collective-permute-start | bytes 786440 | tf_op jit(solution)/shard_map/ppermute | solution.py:46
  105.6 12.0 %copy-start.1 = (f32[512,2048]{1,0:T(8,128)S(1)}, f32[512,2048]{1,0:T(8,128)}, u32[]{:S(2)}) copy-start(f32[512,2048]{1,0:T(8,128)} %param.3) | copy-start | bytes 12582916
  105.6 10.5 %collective-permute-start.18 = (f32[512,128]{1,0:T(8,128)S(1)}, f32[512,128]{1,0:T(8,128)S(1)}, u32[]{:S(2)}, u32[]{:S(2)}) collective-permute-start(f32[512,128]{1,0:T(8,128)S(1)} %get-tuple-element.6), channel_id=1, source_target_pairs={{0,8},{8,0},{16,24},{24,16},{32,40},{40,32},{48,56},{56,48},{64,72... | collective-permute-start | bytes 786440 | tf_op jit(solution)/shard_map/ppermute | solution.py:57
  107.1 7.9 %collective-permute-start.19 = (f32[512,128]{1,0:T(8,128)S(1)}, f32[512,128]{1,0:T(8,128)S(1)}, u32[]{:S(2)}, u32[]{:S(2)}) collective-permute-start(f32[512,128]{1,0:T(8,128)S(1)} %get-tuple-element.6), channel_id=1, source_target_pairs={{0,16},{8,24},{16,0},{24,8},{32,48},{40,56},{48,32},{56,40},{64,80... | collective-permute-start | bytes 786440 | tf_op jit(solution)/shard_map/ppermute | solution.py:58
  114.9 2.0 %collective-permute-start.20 = (f32[512,128]{1,0:T(8,128)S(1)}, f32[512,128]{1,0:T(8,128)S(1)}, u32[]{:S(2)}, u32[]{:S(2)}) collective-permute-start(f32[512,128]{1,0:T(8,128)S(1)} %collective-permute-done.19), channel_id=1, source_target_pairs={{0,8},{8,0},{16,24},{24,16},{32,40},{40,32},{48,56},{56,48},{64,72... | collective-permute-start | bytes 786440 | tf_op jit(solution)/shard_map/ppermute | solution.py:59

commit v21 on v19

--- a/solution.py
+++ b/solution.py
@@ -5,7 +5,7 @@
 
 
 def product(left, right):
-    return jnp.dot(left, right, precision=lax.Precision.HIGH, preferred_element_type=jnp.float32)
+    return jnp.dot(left, right, precision=lax.Precision.HIGHEST, preferred_element_type=jnp.float32)
 
 
 def inner_product(left, right):
@@ -13,7 +13,7 @@
         left,
         right,
         (((0,), (0,)), ((), ())),
-        precision=lax.Precision.HIGH,
+        precision=lax.Precision.HIGHEST,
         preferred_element_type=jnp.float32,
     )
 
@@ -85,7 +85,7 @@
     right = jnp.concatenate([w_cols, vec_cols], axis=1)
     return matrix - lax.dot_general(
         left, right, (((1,), (1,)), ((), ())),
-        precision=lax.Precision.HIGH, preferred_element_type=jnp.float32,
+        precision=lax.Precision.HIGHEST, preferred_element_type=jnp.float32,
     )
 
 

time: 115 us -> 119 us (1.035)
  matrix products: 11.1 us -> 15.8 us
    dot_general x6, matrix products: 6.38 us -> 9.58 us  [product(): jnp.dot(left, right, precision=lax.Precision.HIGHEST, preferred_element_t...]
    dot_general x1, matrix products: 4.1 us -> 5.35 us  [shards(): lax.dot_general(left, right, (((1,), (1,)), ((), ())), precision=lax.Prec...]
where the time goes in v21:
time: 119 us; the launch traced here: 118 us
  starting transfers between devices  41.5 us (35%)
  blocking collectives  36.1 us (30%)
  waiting for transfers between devices  21.9 us (18%)
  matrix products  15.8 us (13%)
  other arithmetic  2.22 us (2%)
    all_to_all x1, blocking collectives, col_sum_rows(): total = jnp.sum(lax.all_to_all(pieces, 'col', 0, 0, tiled=True), axis=0)  24.1 us
    ppermute x8, starting transfers between devices, to_columns(): block = lax.ppermute(mine, ('row', 'col'), pairs)  15.7 us
    all_to_all x1, blocking collectives, col_sum_rows(): lax.all_to_all(spread, 'col', 0, 0, tiled=True).reshape(partial.shape)  12.1 us
    dot_general x6, matrix products, product(): jnp.dot(left, right, precision=lax.Precision.HIGHEST, preferred_element_t...  9.58 us
    ppermute x2, starting transfers between devices, to_columns(): other = lax.ppermute(sent, 'row', core_pairs)  9.36 us
    ppermute x8, waiting for transfers between devices, to_columns(): block = lax.ppermute(mine, ('row', 'col'), pairs)  9.26 us
    ppermute x2, starting transfers between devices, to_columns(): diagonal = lax.ppermute(across, 'row', core_pairs)  8.85 us
    ppermute x4, waiting for transfers between devices, to_columns(): lax.ppermute(extra, ('row', 'col'), every)  8.34 us
  transfers between devices with their start and end apart: 18, of which 8 were waited for; matrix products, arithmetic and copies ran while one was open for 1% of the time, Pallas kernels for 0%

profile of v21, /device:TPU:1, one launch (start us, length us, event | category | flops | bytes accessed | tf_op | source)
XLA Modules:
  0.0 118.2 jit_solution(16730615467076442674)
XLA Ops:
  1.0 3.0 %collective-permute-start.1 = (f32[512,128]{1,0:T(8,128)S(1)}, f32[512,128]{1,0:T(8,128)S(1)}, u32[]{:S(2)}, u32[]{:S(2)}) collective-permute-start(f32[512,128]{1,0:T(8,128)S(1)} %broadcast_select_fusion.1), channel_id=1, source_target_pairs={{0,64},{8,72},{16,80},{24,88},{33,97},{41,105},{49,113},{57,121},{... | collective-permute-start | bytes 786440 | tf_op jit(solution)/shard_map/ppermute | solution.py:46
  4.0 3.3 %collective-permute-start.2 = (f32[512,128]{1,0:T(8,128)S(1)}, f32[512,128]{1,0:T(8,128)S(1)}, u32[]{:S(2)}, u32[]{:S(2)}) collective-permute-start(f32[512,128]{1,0:T(8,128)S(1)} %broadcast_select_fusion.1), channel_id=1, source_target_pairs={{0,96},{8,104},{16,112},{24,120},{33,65},{41,73},{49,81},{57,89},{... | collective-permute-start | bytes 786440 | tf_op jit(solution)/shard_map/ppermute | solution.py:46
  7.3 1.3 %collective-permute-start = (f32[512,128]{1,0:T(8,128)S(1)}, f32[512,128]{1,0:T(8,128)S(1)}, u32[]{:S(2)}, u32[]{:S(2)}) collective-permute-start(f32[512,128]{1,0:T(8,128)S(1)} %broadcast_select_fusion.1), channel_id=1, source_target_pairs={{0,32},{8,40},{16,48},{24,56},{33,1},{41,9},{49,17},{57,25},{66,98... | collective-permute-start | bytes 786440 | tf_op jit(solution)/shard_map/ppermute | solution.py:46
  8.6 5.3 %collective-permute-done.2 = f32[512,128]{1,0:T(8,128)S(1)} collective-permute-done((f32[512,128]{1,0:T(8,128)S(1)}, f32[512,128]{1,0:T(8,128)S(1)}, u32[]{:S(2)}, u32[]{:S(2)}) %collective-permute-start.2) | collective-permute-done | bytes 262176 | tf_op jit(solution)/shard_map/ppermute | solution.py:46
  14.9 1.3 %collective-permute-start.3 = (f32[512,128]{1,0:T(8,128)S(1)}, f32[512,128]{1,0:T(8,128)S(1)}, u32[]{:S(2)}, u32[]{:S(2)}) collective-permute-start(f32[512,128]{1,0:T(8,128)S(1)} %add_add_fusion.1), channel_id=1, source_target_pairs={{0,128},{1,129},{2,130},{3,131},{8,136},{9,137},{10,138},{11,139},... | collective-permute-start | bytes 786440 | tf_op jit(solution)/shard_map/ppermute | solution.py:46
  16.2 3.6 %collective-permute-done.3 = f32[512,128]{1,0:T(8,128)S(1)} collective-permute-done((f32[512,128]{1,0:T(8,128)S(1)}, f32[512,128]{1,0:T(8,128)S(1)}, u32[]{:S(2)}, u32[]{:S(2)}) %collective-permute-start.3) | collective-permute-done | bytes 262176 | tf_op jit(solution)/shard_map/ppermute | solution.py:46
  20.0 2.7 %collective-permute-start.5 = (f32[512,128]{1,0:T(8,128)S(1)}, f32[512,128]{1,0:T(8,128)S(1)}, u32[]{:S(2)}, u32[]{:S(2)}) collective-permute-start(f32[512,128]{1,0:T(8,128)S(1)} %get-tuple-element.8), channel_id=1, source_target_pairs={{0,16},{8,24},{16,0},{24,8},{32,48},{40,56},{48,32},{56,40},{64,80... | collective-permute-start | bytes 786440 | tf_op jit(solution)/shard_map/ppermute | solution.py:59
  22.7 2.5 %collective-permute-start.4 = (f32[512,128]{1,0:T(8,128)S(1)}, f32[512,128]{1,0:T(8,128)S(1)}, u32[]{:S(2)}, u32[]{:S(2)}) collective-permute-start(f32[512,128]{1,0:T(8,128)S(1)} %get-tuple-element.8), channel_id=1, source_target_pairs={{0,8},{8,0},{16,24},{24,16},{32,40},{40,32},{48,56},{56,48},{64,72... | collective-permute-start | bytes 786440 | tf_op jit(solution)/shard_map/ppermute | solution.py:58
  25.1 2.0 %collective-permute-done.5 = f32[512,128]{1,0:T(8,128)S(1)} collective-permute-done((f32[512,128]{1,0:T(8,128)S(1)}, f32[512,128]{1,0:T(8,128)S(1)}, u32[]{:S(2)}, u32[]{:S(2)}) %collective-permute-start.5) | collective-permute-done | bytes 262176 | tf_op jit(solution)/shard_map/ppermute | solution.py:59
  27.1 2.8 %collective-permute-start.6 = (f32[512,128]{1,0:T(8,128)S(1)}, f32[512,128]{1,0:T(8,128)S(1)}, u32[]{:S(2)}, u32[]{:S(2)}) collective-permute-start(f32[512,128]{1,0:T(8,128)S(1)} %collective-permute-done.5), channel_id=1, source_target_pairs={{0,8},{8,0},{16,24},{24,16},{32,40},{40,32},{48,56},{56,48},{64,72... | collective-permute-start | bytes 786440 | tf_op jit(solution)/shard_map/ppermute | solution.py:60
  31.1 6.7 %convolution_bitcast_fusion = f32[512,128]{0,1:T(8,128)S(1)} fusion(f32[2048,128]{1,0:T(8,128)S(1)} %constant_dynamic-update-slice_fusion.1, f32[512,2048]{1,0:T(8,128)} %param.3), kind=kOutput, calls=%fused_computation.9 | convolution fusion | flops 1610612736 | bytes 5505024 | tf_op jit(solution)/shard_map/dot_general | solution.py:8
  38.0 24.1 %all_to_all.11 = f32[8,64,128]{2,1,0:T(8,128)S(1)} all-to-all(f32[8,64,128]{2,1,0:T(8,128)S(1)} %bitcast.30), channel_id=1, replica_groups=mesh['row'=32,'col'=8] {'col'}, dimensions={0} | all-to-all | bytes 524288 | tf_op jit(solution)/shard_map/all_to_all | solution.py:72
  62.1 12.1 %all_to_all.10 = f32[8,64,128]{2,1,0:T(8,128)S(1)} all-to-all(f32[8,64,128]{2,1,0:T(8,128)S(1)} %broadcast_in_dim.2), channel_id=1, replica_groups=mesh['row'=32,'col'=8] {'col'}, dimensions={0} | all-to-all | bytes 524288 | tf_op jit(solution)/shard_map/all_to_all | solution.py:74
  74.2 2.9 %collective-permute-start.12 = (f32[512,128]{1,0:T(8,128)S(1)}, f32[512,128]{1,0:T(8,128)S(1)}, u32[]{:S(2)}, u32[]{:S(2)}) collective-permute-start(f32[512,128]{1,0:T(8,128)S(1)} %broadcast_select_fusion), channel_id=1, source_target_pairs={{0,64},{8,72},{16,80},{24,88},{33,97},{41,105},{49,113},{57,121},{... | collective-permute-start | bytes 786440 | tf_op jit(solution)/shard_map/ppermute | solution.py:46
  77.1 1.3 %collective-permute-start.13 = (f32[512,128]{1,0:T(8,128)S(1)}, f32[512,128]{1,0:T(8,128)S(1)}, u32[]{:S(2)}, u32[]{:S(2)}) collective-permute-start(f32[512,128]{1,0:T(8,128)S(1)} %broadcast_select_fusion), channel_id=1, source_target_pairs={{0,96},{8,104},{16,112},{24,120},{33,65},{41,73},{49,81},{57,89},{... | collective-permute-start | bytes 786440 | tf_op jit(solution)/shard_map/ppermute | solution.py:46
  78.4 1.3 %collective-permute-start.11 = (f32[512,128]{1,0:T(8,128)S(1)}, f32[512,128]{1,0:T(8,128)S(1)}, u32[]{:S(2)}, u32[]{:S(2)}) collective-permute-start(f32[512,128]{1,0:T(8,128)S(1)} %broadcast_select_fusion), channel_id=1, source_target_pairs={{0,32},{8,40},{16,48},{24,56},{33,1},{41,9},{49,17},{57,25},{66,98... | collective-permute-start | bytes 786440 | tf_op jit(solution)/shard_map/ppermute | solution.py:46
  80.5 4.0 %collective-permute-start.7 = (f32[128,128]{1,0:T(8,128)S(1)}, f32[128,128]{1,0:T(8,128)S(1)}, u32[]{:S(2)}, u32[]{:S(2)}) collective-permute-start(f32[128,128]{1,0:T(8,128)S(1)} %convolution_bitcast_fusion.1), channel_id=1, source_target_pairs={{0,32},{1,33},{2,34},{3,35},{4,36},{5,37},{6,38},{7,39},{8,40},{9,... | collective-permute-start | bytes 196616 | tf_op jit(solution)/shard_map/ppermute | solution.py:47
  85.0 1.3 %collective-permute-start.14 = (f32[512,128]{1,0:T(8,128)S(1)}, f32[512,128]{1,0:T(8,128)S(1)}, u32[]{:S(2)}, u32[]{:S(2)}) collective-permute-start(f32[512,128]{1,0:T(8,128)S(1)} %add_add_fusion), channel_id=1, source_target_pairs={{0,128},{1,129},{2,130},{3,131},{8,136},{9,137},{10,138},{11,139},... | collective-permute-start | bytes 786440 | tf_op jit(solution)/shard_map/ppermute | solution.py:46
  86.3 1.4 %collective-permute-done.8 = f32[128,128]{1,0:T(8,128)S(1)} collective-permute-done((f32[128,128]{1,0:T(8,128)S(1)}, f32[128,128]{1,0:T(8,128)S(1)}, u32[]{:S(2)}, u32[]{:S(2)}) %collective-permute-start.8) | collective-permute-done | bytes 65568 | tf_op jit(solution)/shard_map/ppermute | solution.py:47
  87.9 6.9 %collective-permute-done.10 = f32[128,128]{1,0:T(8,128)S(1)} collective-permute-done((f32[128,128]{1,0:T(8,128)S(1)}, f32[128,128]{1,0:T(8,128)S(1)}, u32[]{:S(2)}, u32[]{:S(2)}) %collective-permute-start.10) | collective-permute-done | bytes 65568 | tf_op jit(solution)/shard_map/ppermute | solution.py:47
  95.4 6.9 %collective-permute-start.15 = (f32[640,128]{1,0:T(8,128)S(1)}, f32[640,128]{1,0:T(8,128)S(1)}, u32[]{:S(2)}, u32[]{:S(2)}) collective-permute-start(f32[640,128]{1,0:T(8,128)S(1)} %pad_maximum_fusion), channel_id=1, source_target_pairs={{0,8},{8,0},{16,24},{24,16},{32,40},{40,32},{48,56},{56,48},{64,72... | collective-permute-start | bytes 983048 | tf_op jit(solution)/shard_map/ppermute | solution.py:58
  102.7 6.0 %collective-permute-start.17 = (f32[640,128]{1,0:T(8,128)S(1)}, f32[640,128]{1,0:T(8,128)S(1)}, u32[]{:S(2)}, u32[]{:S(2)}) collective-permute-start(f32[640,128]{1,0:T(8,128)S(1)} %collective-permute-done.16), channel_id=1, source_target_pairs={{0,8},{8,0},{16,24},{24,16},{32,40},{40,32},{48,56},{56,48},{64,72... | collective-permute-start | bytes 983048 | tf_op jit(solution)/shard_map/ppermute | solution.py:60
  108.8 1.2 %collective-permute-done.17 = f32[640,128]{1,0:T(8,128)S(1)} collective-permute-done((f32[640,128]{1,0:T(8,128)S(1)}, f32[640,128]{1,0:T(8,128)S(1)}, u32[]{:S(2)}, u32[]{:S(2)}) %collective-permute-start.17) | collective-permute-done | bytes 327712 | tf_op jit(solution)/shard_map/ppermute | solution.py:60
  112.9 5.3 %convolution_subtract_fusion = f32[512,2048]{1,0:T(8,128)} fusion(f32[512,2048]{1,0:T(8,128)S(1)} %copy-done.1, f32[2048,128]{1,0:T(8,128)S(1)} %constant_dynamic-update-slice_fusion.1, f32[2048,128]{1,0:T(8,128)S(1)} %convolution_subtract_fusion.1, f32[512,128]{1,0:T(8,128)S(1)} %fusion.4, f32[512,128]{1,0:T(8,128)S(1)} %copy-done.2), kind=kOutput, calls=%fused_computation | convolution fusion | flops 3222929408 | bytes 11010048 | tf_op jit(solution)/shard_map/dot_general | solution.py:86
  (49 shorter events, 8.7 us)
Async XLA Ops:
  0.0 102.3 %copy-start = (f32[128,128]{1,0:T(8,128)S(1)}, f32[128,128]{1,0:T(8,128)}, u32[]{:S(2)}) copy-start(f32[128,128]{1,0:T(8,128)} %param.5) | copy-start | bytes 196612
  1.0 7.6 %collective-permute-start.1 = (f32[512,128]{1,0:T(8,128)S(1)}, f32[512,128]{1,0:T(8,128)S(1)}, u32[]{:S(2)}, u32[]{:S(2)}) collective-permute-start(f32[512,128]{1,0:T(8,128)S(1)} %broadcast_select_fusion.1), channel_id=1, source_target_pairs={{0,64},{8,72},{16,80},{24,88},{33,97},{41,105},{49,113},{57,121},{... | collective-permute-start | bytes 786440 | tf_op jit(solution)/shard_map/ppermute | solution.py:46
  4.0 9.9 %collective-permute-start.2 = (f32[512,128]{1,0:T(8,128)S(1)}, f32[512,128]{1,0:T(8,128)S(1)}, u32[]{:S(2)}, u32[]{:S(2)}) collective-permute-start(f32[512,128]{1,0:T(8,128)S(1)} %broadcast_select_fusion.1), channel_id=1, source_target_pairs={{0,96},{8,104},{16,112},{24,120},{33,65},{41,73},{49,81},{57,89},{... | collective-permute-start | bytes 786440 | tf_op jit(solution)/shard_map/ppermute | solution.py:46
  7.3 6.6 %collective-permute-start = (f32[512,128]{1,0:T(8,128)S(1)}, f32[512,128]{1,0:T(8,128)S(1)}, u32[]{:S(2)}, u32[]{:S(2)}) collective-permute-start(f32[512,128]{1,0:T(8,128)S(1)} %broadcast_select_fusion.1), channel_id=1, source_target_pairs={{0,32},{8,40},{16,48},{24,56},{33,1},{41,9},{49,17},{57,25},{66,98... | collective-permute-start | bytes 786440 | tf_op jit(solution)/shard_map/ppermute | solution.py:46
  14.9 4.9 %collective-permute-start.3 = (f32[512,128]{1,0:T(8,128)S(1)}, f32[512,128]{1,0:T(8,128)S(1)}, u32[]{:S(2)}, u32[]{:S(2)}) collective-permute-start(f32[512,128]{1,0:T(8,128)S(1)} %add_add_fusion.1), channel_id=1, source_target_pairs={{0,128},{1,129},{2,130},{3,131},{8,136},{9,137},{10,138},{11,139},... | collective-permute-start | bytes 786440 | tf_op jit(solution)/shard_map/ppermute | solution.py:46
  20.0 7.1 %collective-permute-start.5 = (f32[512,128]{1,0:T(8,128)S(1)}, f32[512,128]{1,0:T(8,128)S(1)}, u32[]{:S(2)}, u32[]{:S(2)}) collective-permute-start(f32[512,128]{1,0:T(8,128)S(1)} %get-tuple-element.8), channel_id=1, source_target_pairs={{0,16},{8,24},{16,0},{24,8},{32,48},{40,56},{48,32},{56,40},{64,80... | collective-permute-start | bytes 786440 | tf_op jit(solution)/shard_map/ppermute | solution.py:59
  22.7 7.3 %collective-permute-start.4 = (f32[512,128]{1,0:T(8,128)S(1)}, f32[512,128]{1,0:T(8,128)S(1)}, u32[]{:S(2)}, u32[]{:S(2)}) collective-permute-start(f32[512,128]{1,0:T(8,128)S(1)} %get-tuple-element.8), channel_id=1, source_target_pairs={{0,8},{8,0},{16,24},{24,16},{32,40},{40,32},{48,56},{56,48},{64,72... | collective-permute-start | bytes 786440 | tf_op jit(solution)/shard_map/ppermute | solution.py:58
  27.1 4.0 %collective-permute-start.6 = (f32[512,128]{1,0:T(8,128)S(1)}, f32[512,128]{1,0:T(8,128)S(1)}, u32[]{:S(2)}, u32[]{:S(2)}) collective-permute-start(f32[512,128]{1,0:T(8,128)S(1)} %collective-permute-done.5), channel_id=1, source_target_pairs={{0,8},{8,0},{16,24},{24,16},{32,40},{40,32},{48,56},{56,48},{64,72... | collective-permute-start | bytes 786440 | tf_op jit(solution)/shard_map/ppermute | solution.py:60
  31.1 48.6 %copy-start.2 = (f32[512,128]{1,0:T(8,128)S(1)}, f32[512,128]{1,0:T(8,128)}, u32[]{:S(2)}) copy-start(f32[512,128]{1,0:T(8,128)} %param.4) | copy-start | bytes 786436
  74.2 6.4 %collective-permute-start.12 = (f32[512,128]{1,0:T(8,128)S(1)}, f32[512,128]{1,0:T(8,128)S(1)}, u32[]{:S(2)}, u32[]{:S(2)}) collective-permute-start(f32[512,128]{1,0:T(8,128)S(1)} %broadcast_select_fusion), channel_id=1, source_target_pairs={{0,64},{8,72},{16,80},{24,88},{33,97},{41,105},{49,113},{57,121},{... | collective-permute-start | bytes 786440 | tf_op jit(solution)/shard_map/ppermute | solution.py:46
  77.1 7.9 %collective-permute-start.13 = (f32[512,128]{1,0:T(8,128)S(1)}, f32[512,128]{1,0:T(8,128)S(1)}, u32[]{:S(2)}, u32[]{:S(2)}) collective-permute-start(f32[512,128]{1,0:T(8,128)S(1)} %broadcast_select_fusion), channel_id=1, source_target_pairs={{0,96},{8,104},{16,112},{24,120},{33,65},{41,73},{49,81},{57,89},{... | collective-permute-start | bytes 786440 | tf_op jit(solution)/shard_map/ppermute | solution.py:46
  78.4 6.5 %collective-permute-start.11 = (f32[512,128]{1,0:T(8,128)S(1)}, f32[512,128]{1,0:T(8,128)S(1)}, u32[]{:S(2)}, u32[]{:S(2)}) collective-permute-start(f32[512,128]{1,0:T(8,128)S(1)} %broadcast_select_fusion), channel_id=1, source_target_pairs={{0,32},{8,40},{16,48},{24,56},{33,1},{41,9},{49,17},{57,25},{66,98... | collective-permute-start | bytes 786440 | tf_op jit(solution)/shard_map/ppermute | solution.py:46
  80.3 6.0 %collective-permute-start.9 = (f32[128,128]{1,0:T(8,128)S(1)}, f32[128,128]{1,0:T(8,128)S(1)}, u32[]{:S(2)}, u32[]{:S(2)}) collective-permute-start(f32[128,128]{1,0:T(8,128)S(1)} %convolution_bitcast_fusion.1), channel_id=1, source_target_pairs={{0,96},{1,97},{2,98},{3,99},{4,100},{5,101},{6,102},{7,103},{8,104... | collective-permute-start | bytes 196616 | tf_op jit(solution)/shard_map/ppermute | solution.py:47
  80.4 7.3 %collective-permute-start.8 = (f32[128,128]{1,0:T(8,128)S(1)}, f32[128,128]{1,0:T(8,128)S(1)}, u32[]{:S(2)}, u32[]{:S(2)}) collective-permute-start(f32[128,128]{1,0:T(8,128)S(1)} %convolution_bitcast_fusion.1), channel_id=1, source_target_pairs={{0,64},{1,65},{2,66},{3,67},{4,68},{5,69},{6,70},{7,71},{8,72},{9,... | collective-permute-start | bytes 196616 | tf_op jit(solution)/shard_map/ppermute | solution.py:47
  80.5 7.2 %collective-permute-start.7 = (f32[128,128]{1,0:T(8,128)S(1)}, f32[128,128]{1,0:T(8,128)S(1)}, u32[]{:S(2)}, u32[]{:S(2)}) collective-permute-start(f32[128,128]{1,0:T(8,128)S(1)} %convolution_bitcast_fusion.1), channel_id=1, source_target_pairs={{0,32},{1,33},{2,34},{3,35},{4,36},{5,37},{6,38},{7,39},{8,40},{9,... | collective-permute-start | bytes 196616 | tf_op jit(solution)/shard_map/ppermute | solution.py:47
  85.0 9.8 %collective-permute-start.14 = (f32[512,128]{1,0:T(8,128)S(1)}, f32[512,128]{1,0:T(8,128)S(1)}, u32[]{:S(2)}, u32[]{:S(2)}) collective-permute-start(f32[512,128]{1,0:T(8,128)S(1)} %add_add_fusion), channel_id=1, source_target_pairs={{0,128},{1,129},{2,130},{3,131},{8,136},{9,137},{10,138},{11,139},... | collective-permute-start | bytes 786440 | tf_op jit(solution)/shard_map/ppermute | solution.py:46
  87.8 7.0 %collective-permute-start.10 = (f32[128,128]{1,0:T(8,128)S(1)}, f32[128,128]{1,0:T(8,128)S(1)}, u32[]{:S(2)}, u32[]{:S(2)}) collective-permute-start(f32[128,128]{1,0:T(8,128)S(1)} %add_add_fusion.2), channel_id=1, source_target_pairs={{0,128},{1,129},{2,130},{3,131},{4,132},{5,133},{6,134},{7,135},{8... | collective-permute-start | bytes 196616 | tf_op jit(solution)/shard_map/ppermute | solution.py:47
  95.0 7.7 %collective-permute-start.16 = (f32[640,128]{1,0:T(8,128)S(1)}, f32[640,128]{1,0:T(8,128)S(1)}, u32[]{:S(2)}, u32[]{:S(2)}) collective-permute-start(f32[640,128]{1,0:T(8,128)S(1)} %pad_maximum_fusion), channel_id=1, source_target_pairs={{0,16},{8,24},{16,0},{24,8},{32,48},{40,56},{48,32},{56,40},{64,80... | collective-permute-start | bytes 983048 | tf_op jit(solution)/shard_map/ppermute | solution.py:59
  95.4 13.3 %collective-permute-start.15 = (f32[640,128]{1,0:T(8,128)S(1)}, f32[640,128]{1,0:T(8,128)S(1)}, u32[]{:S(2)}, u32[]{:S(2)}) collective-permute-start(f32[640,128]{1,0:T(8,128)S(1)} %pad_maximum_fusion), channel_id=1, source_target_pairs={{0,8},{8,0},{16,24},{24,16},{32,40},{40,32},{48,56},{56,48},{64,72... | collective-permute-start | bytes 983048 | tf_op jit(solution)/shard_map/ppermute | solution.py:58
  102.7 7.3 %collective-permute-start.17 = (f32[640,128]{1,0:T(8,128)S(1)}, f32[640,128]{1,0:T(8,128)S(1)}, u32[]{:S(2)}, u32[]{:S(2)}) collective-permute-start(f32[640,128]{1,0:T(8,128)S(1)} %collective-permute-done.16), channel_id=1, source_target_pairs={{0,8},{8,0},{16,24},{24,16},{32,40},{40,32},{48,56},{56,48},{64,72... | collective-permute-start | bytes 983048 | tf_op jit(solution)/shard_map/ppermute | solution.py:60
  108.7 4.2 %copy-start.1 = (f32[512,2048]{1,0:T(8,128)S(1)}, f32[512,2048]{1,0:T(8,128)}, u32[]{:S(2)}) copy-start(f32[512,2048]{1,0:T(8,128)} %param.3) | copy-start | bytes 12582916

commit v22 on v19

--- a/solution.py
+++ b/solution.py
@@ -29,7 +29,7 @@
     mine = jnp.where(high == col, panel_rows, jnp.zeros_like(panel_rows))
     known = 1
     while known < col_count:
-        width = 4 if col_count % (known * 4) == 0 else 2
+        width = 4 if extra is None and col_count % (known * 4) == 0 else 2
         arrived = []
         for digit in range(1, width):
             mask = digit * known

time: 115 us -> 124 us (1.078)
  waiting for transfers between devices: 22.3 us -> 27.8 us
  starting transfers between devices: 41.6 us -> 45.4 us
    ppermute x8 -> x7, waiting for transfers between devices: 9.68 us -> 15.4 us  [to_columns(): block = lax.ppermute(mine, ('row', 'col'), pairs)]
    ppermute x2, starting transfers between devices: 9.36 us -> 13.5 us  [to_columns(): other = lax.ppermute(sent, 'row', core_pairs)]
    ppermute x8 -> x7, starting transfers between devices: 15.9 us -> 14.4 us  [to_columns(): block = lax.ppermute(mine, ('row', 'col'), pairs)]
    ppermute x4 -> x3, starting transfers between devices: 4.27 us -> 5.58 us  [to_columns(): lax.ppermute(extra, ('row', 'col'), every)]
    ppermute x4 -> x3, waiting for transfers between devices: 8.34 us -> 8.08 us  [to_columns(): lax.ppermute(extra, ('row', 'col'), every)]
  transfers between devices with their start and end apart: 18 -> 16, of which waited for: 8 -> 10; matrix products, arithmetic and copies ran while one was open for 1% -> 1% of each run, Pallas kernels for 0% -> 0%
where the time goes in v22:
time: 124 us; the launch traced here: 123 us
  starting transfers between devices  45.4 us (37%)
  blocking collectives  36.1 us (29%)
  waiting for transfers between devices  27.8 us (22%)
  matrix products  11.1 us (9%)
  other arithmetic  2.23 us (2%)
    all_to_all x1, blocking collectives, col_sum_rows(): total = jnp.sum(lax.all_to_all(pieces, 'col', 0, 0, tiled=True), axis=0)  24.1 us
    ppermute x7, waiting for transfers between devices, to_columns(): block = lax.ppermute(mine, ('row', 'col'), pairs)  15.4 us
    ppermute x7, starting transfers between devices, to_columns(): block = lax.ppermute(mine, ('row', 'col'), pairs)  14.4 us
    ppermute x2, starting transfers between devices, to_columns(): other = lax.ppermute(sent, 'row', core_pairs)  13.5 us
    all_to_all x1, blocking collectives, col_sum_rows(): lax.all_to_all(spread, 'col', 0, 0, tiled=True).reshape(partial.shape)  12.1 us
    ppermute x2, starting transfers between devices, to_columns(): diagonal = lax.ppermute(across, 'row', core_pairs)  8.43 us
    ppermute x3, waiting for transfers between devices, to_columns(): lax.ppermute(extra, ('row', 'col'), every)  8.08 us
    dot_general x6, matrix products, product(): jnp.dot(left, right, precision=lax.Precision.HIGH, preferred_element_type...  6.38 us
  transfers between devices with their start and end apart: 16, of which 10 were waited for; matrix products, arithmetic and copies ran while one was open for 1% of the time, Pallas kernels for 0%

profile of v22, /device:TPU:1, one launch (start us, length us, event | category | flops | bytes accessed | tf_op | source)
XLA Modules:
  0.0 123.4 jit_solution(5166043888714409563)
XLA Ops:
  1.0 3.0 %collective-permute-start.1 = (f32[512,128]{1,0:T(8,128)S(1)}, f32[512,128]{1,0:T(8,128)S(1)}, u32[]{:S(2)}, u32[]{:S(2)}) collective-permute-start(f32[512,128]{1,0:T(8,128)S(1)} %broadcast_select_fusion.1), channel_id=1, source_target_pairs={{0,64},{8,72},{16,80},{24,88},{33,97},{41,105},{49,113},{57,121},{... | collective-permute-start | bytes 786440 | tf_op jit(solution)/shard_map/ppermute | solution.py:46
  4.0 3.3 %collective-permute-start.2 = (f32[512,128]{1,0:T(8,128)S(1)}, f32[512,128]{1,0:T(8,128)S(1)}, u32[]{:S(2)}, u32[]{:S(2)}) collective-permute-start(f32[512,128]{1,0:T(8,128)S(1)} %broadcast_select_fusion.1), channel_id=1, source_target_pairs={{0,96},{8,104},{16,112},{24,120},{33,65},{41,73},{49,81},{57,89},{... | collective-permute-start | bytes 786440 | tf_op jit(solution)/shard_map/ppermute | solution.py:46
  8.6 5.3 %collective-permute-done.2 = f32[512,128]{1,0:T(8,128)S(1)} collective-permute-done((f32[512,128]{1,0:T(8,128)S(1)}, f32[512,128]{1,0:T(8,128)S(1)}, u32[]{:S(2)}, u32[]{:S(2)}) %collective-permute-start.2) | collective-permute-done | bytes 262176 | tf_op jit(solution)/shard_map/ppermute | solution.py:46
  14.9 1.3 %collective-permute-start.3 = (f32[512,128]{1,0:T(8,128)S(1)}, f32[512,128]{1,0:T(8,128)S(1)}, u32[]{:S(2)}, u32[]{:S(2)}) collective-permute-start(f32[512,128]{1,0:T(8,128)S(1)} %add_add_fusion), channel_id=1, source_target_pairs={{0,128},{1,129},{2,130},{3,131},{8,136},{9,137},{10,138},{11,139},... | collective-permute-start | bytes 786440 | tf_op jit(solution)/shard_map/ppermute | solution.py:46
  16.2 3.6 %collective-permute-done.3 = f32[512,128]{1,0:T(8,128)S(1)} collective-permute-done((f32[512,128]{1,0:T(8,128)S(1)}, f32[512,128]{1,0:T(8,128)S(1)}, u32[]{:S(2)}, u32[]{:S(2)}) %collective-permute-start.3) | collective-permute-done | bytes 262176 | tf_op jit(solution)/shard_map/ppermute | solution.py:46
  20.0 2.7 %collective-permute-start.5 = (f32[512,128]{1,0:T(8,128)S(1)}, f32[512,128]{1,0:T(8,128)S(1)}, u32[]{:S(2)}, u32[]{:S(2)}) collective-permute-start(f32[512,128]{1,0:T(8,128)S(1)} %get-tuple-element.8), channel_id=1, source_target_pairs={{0,16},{8,24},{16,0},{24,8},{32,48},{40,56},{48,32},{56,40},{64,80... | collective-permute-start | bytes 786440 | tf_op jit(solution)/shard_map/ppermute | solution.py:59
  22.7 2.5 %collective-permute-start.4 = (f32[512,128]{1,0:T(8,128)S(1)}, f32[512,128]{1,0:T(8,128)S(1)}, u32[]{:S(2)}, u32[]{:S(2)}) collective-permute-start(f32[512,128]{1,0:T(8,128)S(1)} %get-tuple-element.8), channel_id=1, source_target_pairs={{0,8},{8,0},{16,24},{24,16},{32,40},{40,32},{48,56},{56,48},{64,72... | collective-permute-start | bytes 786440 | tf_op jit(solution)/shard_map/ppermute | solution.py:58
  25.1 2.0 %collective-permute-done.5 = f32[512,128]{1,0:T(8,128)S(1)} collective-permute-done((f32[512,128]{1,0:T(8,128)S(1)}, f32[512,128]{1,0:T(8,128)S(1)}, u32[]{:S(2)}, u32[]{:S(2)}) %collective-permute-start.5) | collective-permute-done | bytes 262176 | tf_op jit(solution)/shard_map/ppermute | solution.py:59
  27.1 2.8 %collective-permute-start.6 = (f32[512,128]{1,0:T(8,128)S(1)}, f32[512,128]{1,0:T(8,128)S(1)}, u32[]{:S(2)}, u32[]{:S(2)}) collective-permute-start(f32[512,128]{1,0:T(8,128)S(1)} %collective-permute-done.5), channel_id=1, source_target_pairs={{0,8},{8,0},{16,24},{24,16},{32,40},{40,32},{48,56},{56,48},{64,72... | collective-permute-start | bytes 786440 | tf_op jit(solution)/shard_map/ppermute | solution.py:60
  31.1 4.5 %convolution_bitcast_fusion = f32[512,128]{0,1:T(8,128)S(1)} fusion(f32[2048,128]{1,0:T(8,128)S(1)} %constant_dynamic-update-slice_fusion.1, f32[512,2048]{1,0:T(8,128)} %param.3), kind=kOutput, calls=%fused_computation.9 | convolution fusion | flops 805306368 | bytes 5505024 | tf_op jit(solution)/shard_map/dot_general | solution.py:8
  35.8 24.1 %all_to_all.11 = f32[8,64,128]{2,1,0:T(8,128)S(1)} all-to-all(f32[8,64,128]{2,1,0:T(8,128)S(1)} %bitcast.30), channel_id=1, replica_groups=mesh['row'=32,'col'=8] {'col'}, dimensions={0} | all-to-all | bytes 524288 | tf_op jit(solution)/shard_map/all_to_all | solution.py:72
  59.9 12.1 %all_to_all.10 = f32[8,64,128]{2,1,0:T(8,128)S(1)} all-to-all(f32[8,64,128]{2,1,0:T(8,128)S(1)} %broadcast_in_dim.2), channel_id=1, replica_groups=mesh['row'=32,'col'=8] {'col'}, dimensions={0} | all-to-all | bytes 524288 | tf_op jit(solution)/shard_map/all_to_all | solution.py:74
  72.0 2.8 %collective-permute-start.10 = (f32[512,128]{1,0:T(8,128)S(1)}, f32[512,128]{1,0:T(8,128)S(1)}, u32[]{:S(2)}, u32[]{:S(2)}) collective-permute-start(f32[512,128]{1,0:T(8,128)S(1)} %broadcast_select_fusion), channel_id=1, source_target_pairs={{0,32},{8,40},{16,48},{24,56},{33,1},{41,9},{49,17},{57,25},{66,98... | collective-permute-start | bytes 786440 | tf_op jit(solution)/shard_map/ppermute | solution.py:46
  74.8 3.3 %collective-permute-done.10 = f32[512,128]{1,0:T(8,128)S(1)} collective-permute-done((f32[512,128]{1,0:T(8,128)S(1)}, f32[512,128]{1,0:T(8,128)S(1)}, u32[]{:S(2)}, u32[]{:S(2)}) %collective-permute-start.10) | collective-permute-done | bytes 262176 | tf_op jit(solution)/shard_map/ppermute | solution.py:46
  78.2 1.3 %collective-permute-start.11 = (f32[512,128]{1,0:T(8,128)S(1)}, f32[512,128]{1,0:T(8,128)S(1)}, u32[]{:S(2)}, u32[]{:S(2)}) collective-permute-start(f32[512,128]{1,0:T(8,128)S(1)} %fusion.27), channel_id=1, source_target_pairs={{0,64},{1,65},{8,72},{9,73},{16,80},{17,81},{24,88},{25,89},{32,96... | collective-permute-start | bytes 786440 | tf_op jit(solution)/shard_map/ppermute | solution.py:46
  79.5 3.3 %collective-permute-done.11 = f32[512,128]{1,0:T(8,128)S(1)} collective-permute-done((f32[512,128]{1,0:T(8,128)S(1)}, f32[512,128]{1,0:T(8,128)S(1)}, u32[]{:S(2)}, u32[]{:S(2)}) %collective-permute-start.11) | collective-permute-done | bytes 262176 | tf_op jit(solution)/shard_map/ppermute | solution.py:46
  84.5 3.5 %collective-permute-start.7 = (f32[128,128]{1,0:T(8,128)S(1)}, f32[128,128]{1,0:T(8,128)S(1)}, u32[]{:S(2)}, u32[]{:S(2)}) collective-permute-start(f32[128,128]{1,0:T(8,128)S(1)} %convolution_bitcast_fusion.1), channel_id=1, source_target_pairs={{0,32},{1,33},{2,34},{3,35},{4,36},{5,37},{6,38},{7,39},{8,40},{9,... | collective-permute-start | bytes 196616 | tf_op jit(solution)/shard_map/ppermute | solution.py:47
  88.0 1.7 %collective-permute-done.7 = f32[128,128]{1,0:T(8,128)S(1)} collective-permute-done((f32[128,128]{1,0:T(8,128)S(1)}, f32[128,128]{1,0:T(8,128)S(1)}, u32[]{:S(2)}, u32[]{:S(2)}) %collective-permute-start.7) | collective-permute-done | bytes 65568 | tf_op jit(solution)/shard_map/ppermute | solution.py:47
  89.7 2.0 %collective-permute-start.8 = (f32[128,128]{1,0:T(8,128)S(1)}, f32[128,128]{1,0:T(8,128)S(1)}, u32[]{:S(2)}, u32[]{:S(2)}) collective-permute-start(f32[128,128]{1,0:T(8,128)S(1)} %add.70), channel_id=1, source_target_pairs={{0,64},{1,65},{2,66},{3,67},{4,68},{5,69},{6,70},{7,71},{8,72},{9,... | collective-permute-start | bytes 196616 | tf_op jit(solution)/shard_map/ppermute | solution.py:47
  91.7 1.8 %collective-permute-done.8 = f32[128,128]{1,0:T(8,128)S(1)} collective-permute-done((f32[128,128]{1,0:T(8,128)S(1)}, f32[128,128]{1,0:T(8,128)S(1)}, u32[]{:S(2)}, u32[]{:S(2)}) %collective-permute-start.8) | collective-permute-done | bytes 65568 | tf_op jit(solution)/shard_map/ppermute | solution.py:47
  93.6 4.6 %collective-permute-done.9 = f32[128,128]{1,0:T(8,128)S(1)} collective-permute-done((f32[128,128]{1,0:T(8,128)S(1)}, f32[128,128]{1,0:T(8,128)S(1)}, u32[]{:S(2)}, u32[]{:S(2)}) %collective-permute-start.9) | collective-permute-done | bytes 65568 | tf_op jit(solution)/shard_map/ppermute | solution.py:47
  99.2 11.0 %collective-permute-start.13 = (f32[640,128]{1,0:T(8,128)S(1)}, f32[640,128]{1,0:T(8,128)S(1)}, u32[]{:S(2)}, u32[]{:S(2)}) collective-permute-start(f32[640,128]{1,0:T(8,128)S(1)} %pad_maximum_fusion), channel_id=1, source_target_pairs={{0,8},{8,0},{16,24},{24,16},{32,40},{40,32},{48,56},{56,48},{64,72... | collective-permute-start | bytes 983048 | tf_op jit(solution)/shard_map/ppermute | solution.py:58
  110.5 5.6 %collective-permute-start.15 = (f32[640,128]{1,0:T(8,128)S(1)}, f32[640,128]{1,0:T(8,128)S(1)}, u32[]{:S(2)}, u32[]{:S(2)}) collective-permute-start(f32[640,128]{1,0:T(8,128)S(1)} %collective-permute-done.14), channel_id=1, source_target_pairs={{0,8},{8,0},{16,24},{24,16},{32,40},{40,32},{48,56},{56,48},{64,72... | collective-permute-start | bytes 983048 | tf_op jit(solution)/shard_map/ppermute | solution.py:60
  119.3 4.1 %convolution_subtract_fusion = f32[512,2048]{1,0:T(8,128)} fusion(f32[512,2048]{1,0:T(8,128)S(1)} %copy-done.1, f32[2048,128]{1,0:T(8,128)S(1)} %constant_dynamic-update-slice_fusion.1, f32[2048,128]{1,0:T(8,128)S(1)} %convolution_subtract_fusion.1, f32[512,128]{1,0:T(8,128)S(1)} %fusion.4, f32[512,128]{1,0:T(8,128)S(1)} %copy-done.2), kind=kOutput, calls=%fused_computation | convolution fusion | flops 1612316672 | bytes 11010048 | tf_op jit(solution)/shard_map/dot_general | solution.py:86
  (47 shorter events, 11.0 us)
Async XLA Ops:
  0.0 110.2 %copy-start = (f32[128,128]{1,0:T(8,128)S(1)}, f32[128,128]{1,0:T(8,128)}, u32[]{:S(2)}) copy-start(f32[128,128]{1,0:T(8,128)} %param.5) | copy-start | bytes 196612
  1.0 7.6 %collective-permute-start.1 = (f32[512,128]{1,0:T(8,128)S(1)}, f32[512,128]{1,0:T(8,128)S(1)}, u32[]{:S(2)}, u32[]{:S(2)}) collective-permute-start(f32[512,128]{1,0:T(8,128)S(1)} %broadcast_select_fusion.1), channel_id=1, source_target_pairs={{0,64},{8,72},{16,80},{24,88},{33,97},{41,105},{49,113},{57,121},{... | collective-permute-start | bytes 786440 | tf_op jit(solution)/shard_map/ppermute | solution.py:46
  4.0 9.9 %collective-permute-start.2 = (f32[512,128]{1,0:T(8,128)S(1)}, f32[512,128]{1,0:T(8,128)S(1)}, u32[]{:S(2)}, u32[]{:S(2)}) collective-permute-start(f32[512,128]{1,0:T(8,128)S(1)} %broadcast_select_fusion.1), channel_id=1, source_target_pairs={{0,96},{8,104},{16,112},{24,120},{33,65},{41,73},{49,81},{57,89},{... | collective-permute-start | bytes 786440 | tf_op jit(solution)/shard_map/ppermute | solution.py:46
  7.3 6.6 %collective-permute-start = (f32[512,128]{1,0:T(8,128)S(1)}, f32[512,128]{1,0:T(8,128)S(1)}, u32[]{:S(2)}, u32[]{:S(2)}) collective-permute-start(f32[512,128]{1,0:T(8,128)S(1)} %broadcast_select_fusion.1), channel_id=1, source_target_pairs={{0,32},{8,40},{16,48},{24,56},{33,1},{41,9},{49,17},{57,25},{66,98... | collective-permute-start | bytes 786440 | tf_op jit(solution)/shard_map/ppermute | solution.py:46
  14.9 4.9 %collective-permute-start.3 = (f32[512,128]{1,0:T(8,128)S(1)}, f32[512,128]{1,0:T(8,128)S(1)}, u32[]{:S(2)}, u32[]{:S(2)}) collective-permute-start(f32[512,128]{1,0:T(8,128)S(1)} %add_add_fusion), channel_id=1, source_target_pairs={{0,128},{1,129},{2,130},{3,131},{8,136},{9,137},{10,138},{11,139},... | collective-permute-start | bytes 786440 | tf_op jit(solution)/shard_map/ppermute | solution.py:46
  20.0 7.1 %collective-permute-start.5 = (f32[512,128]{1,0:T(8,128)S(1)}, f32[512,128]{1,0:T(8,128)S(1)}, u32[]{:S(2)}, u32[]{:S(2)}) collective-permute-start(f32[512,128]{1,0:T(8,128)S(1)} %get-tuple-element.8), channel_id=1, source_target_pairs={{0,16},{8,24},{16,0},{24,8},{32,48},{40,56},{48,32},{56,40},{64,80... | collective-permute-start | bytes 786440 | tf_op jit(solution)/shard_map/ppermute | solution.py:59
  22.7 7.3 %collective-permute-start.4 = (f32[512,128]{1,0:T(8,128)S(1)}, f32[512,128]{1,0:T(8,128)S(1)}, u32[]{:S(2)}, u32[]{:S(2)}) collective-permute-start(f32[512,128]{1,0:T(8,128)S(1)} %get-tuple-element.8), channel_id=1, source_target_pairs={{0,8},{8,0},{16,24},{24,16},{32,40},{40,32},{48,56},{56,48},{64,72... | collective-permute-start | bytes 786440 | tf_op jit(solution)/shard_map/ppermute | solution.py:58
  27.1 4.0 %collective-permute-start.6 = (f32[512,128]{1,0:T(8,128)S(1)}, f32[512,128]{1,0:T(8,128)S(1)}, u32[]{:S(2)}, u32[]{:S(2)}) collective-permute-start(f32[512,128]{1,0:T(8,128)S(1)} %collective-permute-done.5), channel_id=1, source_target_pairs={{0,8},{8,0},{16,24},{24,16},{32,40},{40,32},{48,56},{56,48},{64,72... | collective-permute-start | bytes 786440 | tf_op jit(solution)/shard_map/ppermute | solution.py:60
  31.1 53.0 %copy-start.2 = (f32[512,128]{1,0:T(8,128)S(1)}, f32[512,128]{1,0:T(8,128)}, u32[]{:S(2)}) copy-start(f32[512,128]{1,0:T(8,128)} %param.4) | copy-start | bytes 786436
  72.0 6.1 %collective-permute-start.10 = (f32[512,128]{1,0:T(8,128)S(1)}, f32[512,128]{1,0:T(8,128)S(1)}, u32[]{:S(2)}, u32[]{:S(2)}) collective-permute-start(f32[512,128]{1,0:T(8,128)S(1)} %broadcast_select_fusion), channel_id=1, source_target_pairs={{0,32},{8,40},{16,48},{24,56},{33,1},{41,9},{49,17},{57,25},{66,98... | collective-permute-start | bytes 786440 | tf_op jit(solution)/shard_map/ppermute | solution.py:46
  78.2 4.6 %collective-permute-start.11 = (f32[512,128]{1,0:T(8,128)S(1)}, f32[512,128]{1,0:T(8,128)S(1)}, u32[]{:S(2)}, u32[]{:S(2)}) collective-permute-start(f32[512,128]{1,0:T(8,128)S(1)} %fusion.27), channel_id=1, source_target_pairs={{0,64},{1,65},{8,72},{9,73},{16,80},{17,81},{24,88},{25,89},{32,96... | collective-permute-start | bytes 786440 | tf_op jit(solution)/shard_map/ppermute | solution.py:46
  82.8 15.4 %collective-permute-start.12 = (f32[512,128]{1,0:T(8,128)S(1)}, f32[512,128]{1,0:T(8,128)S(1)}, u32[]{:S(2)}, u32[]{:S(2)}) collective-permute-start(f32[512,128]{1,0:T(8,128)S(1)} %add.74), channel_id=1, source_target_pairs={{0,128},{1,129},{2,130},{3,131},{8,136},{9,137},{10,138},{11,139},... | collective-permute-start | bytes 786440 | tf_op jit(solution)/shard_map/ppermute | solution.py:46
  84.5 5.2 %collective-permute-start.7 = (f32[128,128]{1,0:T(8,128)S(1)}, f32[128,128]{1,0:T(8,128)S(1)}, u32[]{:S(2)}, u32[]{:S(2)}) collective-permute-start(f32[128,128]{1,0:T(8,128)S(1)} %convolution_bitcast_fusion.1), channel_id=1, source_target_pairs={{0,32},{1,33},{2,34},{3,35},{4,36},{5,37},{6,38},{7,39},{8,40},{9,... | collective-permute-start | bytes 196616 | tf_op jit(solution)/shard_map/ppermute | solution.py:47
  89.7 3.8 %collective-permute-start.8 = (f32[128,128]{1,0:T(8,128)S(1)}, f32[128,128]{1,0:T(8,128)S(1)}, u32[]{:S(2)}, u32[]{:S(2)}) collective-permute-start(f32[128,128]{1,0:T(8,128)S(1)} %add.70), channel_id=1, source_target_pairs={{0,64},{1,65},{2,66},{3,67},{4,68},{5,69},{6,70},{7,71},{8,72},{9,... | collective-permute-start | bytes 196616 | tf_op jit(solution)/shard_map/ppermute | solution.py:47
  93.5 4.7 %collective-permute-start.9 = (f32[128,128]{1,0:T(8,128)S(1)}, f32[128,128]{1,0:T(8,128)S(1)}, u32[]{:S(2)}, u32[]{:S(2)}) collective-permute-start(f32[128,128]{1,0:T(8,128)S(1)} %add.71), channel_id=1, source_target_pairs={{0,128},{1,129},{2,130},{3,131},{4,132},{5,133},{6,134},{7,135},{8... | collective-permute-start | bytes 196616 | tf_op jit(solution)/shard_map/ppermute | solution.py:47
  98.4 12.1 %collective-permute-start.14 = (f32[640,128]{1,0:T(8,128)S(1)}, f32[640,128]{1,0:T(8,128)S(1)}, u32[]{:S(2)}, u32[]{:S(2)}) collective-permute-start(f32[640,128]{1,0:T(8,128)S(1)} %pad_maximum_fusion), channel_id=1, source_target_pairs={{0,16},{8,24},{16,0},{24,8},{32,48},{40,56},{48,32},{56,40},{64,80... | collective-permute-start | bytes 983048 | tf_op jit(solution)/shard_map/ppermute | solution.py:59
  99.2 16.9 %collective-permute-start.13 = (f32[640,128]{1,0:T(8,128)S(1)}, f32[640,128]{1,0:T(8,128)S(1)}, u32[]{:S(2)}, u32[]{:S(2)}) collective-permute-start(f32[640,128]{1,0:T(8,128)S(1)} %pad_maximum_fusion), channel_id=1, source_target_pairs={{0,8},{8,0},{16,24},{24,16},{32,40},{40,32},{48,56},{56,48},{64,72... | collective-permute-start | bytes 983048 | tf_op jit(solution)/shard_map/ppermute | solution.py:58
  110.5 6.9 %collective-permute-start.15 = (f32[640,128]{1,0:T(8,128)S(1)}, f32[640,128]{1,0:T(8,128)S(1)}, u32[]{:S(2)}, u32[]{:S(2)}) collective-permute-start(f32[640,128]{1,0:T(8,128)S(1)} %collective-permute-done.14), channel_id=1, source_target_pairs={{0,8},{8,0},{16,24},{24,16},{32,40},{40,32},{48,56},{56,48},{64,72... | collective-permute-start | bytes 983048 | tf_op jit(solution)/shard_map/ppermute | solution.py:60
  116.1 3.2 %copy-start.1 = (f32[512,2048]{1,0:T(8,128)S(1)}, f32[512,2048]{1,0:T(8,128)}, u32[]{:S(2)}) copy-start(f32[512,2048]{1,0:T(8,128)} %param.3) | copy-start | bytes 12582916

commit v23 on v22

--- a/solution.py
+++ b/solution.py
@@ -27,12 +27,14 @@
     low = lax.axis_index("row") % per
     col = lax.axis_index("col")
     mine = jnp.where(high == col, panel_rows, jnp.zeros_like(panel_rows))
-    known = 1
-    while known < col_count:
-        width = 4 if extra is None and col_count % (known * 4) == 0 else 2
+    if col_count == 8:
+        rounds = [(2, 4, 6), (1,)]
+    else:
+        rounds = [(1 << k,) for k in range(col_count.bit_length() - 1)]
+    reached = {0}
+    for masks in rounds:
         arrived = []
-        for digit in range(1, width):
-            mask = digit * known
+        for mask in masks:
             pairs = []
             every = []
             for src_high in range(col_count):
@@ -41,7 +43,7 @@
                         src = (per * src_high + src_low) * col_count + src_col
                         dst = (per * (src_high ^ mask) + src_low) * col_count + src_col
                         every.append((src, dst))
-                        if (src_high ^ src_col) < known:
+                        if (src_high ^ src_col) in reached:
                             pairs.append((src, dst))
             block = lax.ppermute(mine, ("row", "col"), pairs)
             summand = None if extra is None else lax.ppermute(extra, ("row", "col"), every)
@@ -50,7 +52,7 @@
             mine = mine + block
             if extra is not None:
                 extra = extra + summand
-        known *= width
+        reached = reached | {r ^ mask for r in reached for mask in masks}
     gathered = jnp.zeros((per * rows_here,) + panel_rows.shape[1:], panel_rows.dtype)
     gathered = lax.dynamic_update_slice_in_dim(gathered, mine, low * rows_here, 0)
     core_pairs = [(i, i ^ 1) for i in range(row_count)]

time: 124 us -> 113 us (0.911); the launches traced: 123 us -> 111 us
  starting transfers between devices: 45.4 us -> 40 us
  blocking collectives: 36.1 us -> 31.4 us
  waiting for transfers between devices: 27.8 us -> 25.5 us
    all_to_all x1, blocking collectives: 24.1 us -> 19.4 us  [col_sum_rows(): total = jnp.sum(lax.all_to_all(pieces, 'col', 0, 0, tiled=True), axis=0)]
    ppermute x2, starting transfers between devices: 13.5 us -> 9.58 us  [to_columns(): other = lax.ppermute(sent, 'row', core_pairs)]
    ppermute x7 -> x8, starting transfers between devices: 14.4 us -> 17.2 us  [to_columns(): block = lax.ppermute(mine, ('row', 'col'), pairs)]
    ppermute x3 -> x4, starting transfers between devices: 5.58 us -> 3.33 us  [to_columns(): lax.ppermute(extra, ('row', 'col'), every)]
    ppermute x3 -> x4, waiting for transfers between devices: 8.08 us -> 6.04 us  [to_columns(): lax.ppermute(extra, ('row', 'col'), every)]
    ppermute x2, starting transfers between devices: 3.53 us -> 2.06 us  [to_columns(): across = lax.ppermute(sent, 'row', [(i, i ^ 2) for i in range(row_count)])]
    ppermute x7 -> x8, waiting for transfers between devices: 15.4 us -> 14 us  [to_columns(): block = lax.ppermute(mine, ('row', 'col'), pairs)]
  transfers between devices with their start and end apart: 16 -> 18, of which waited for: 10 -> 12; matrix products, arithmetic and copies ran while one was open for 1% -> 1% of each run, Pallas kernels for 0% -> 0%
where the time goes in v23:
time: 113 us; the launch traced here: 111 us
  starting transfers between devices  40 us (35%)
  blocking collectives  31.4 us (28%)
  waiting for transfers between devices  25.5 us (23%)
  matrix products  11.1 us (10%)
  other arithmetic  2.22 us (2%)
    all_to_all x1, blocking collectives, col_sum_rows(): total = jnp.sum(lax.all_to_all(pieces, 'col', 0, 0, tiled=True), axis=0)  19.4 us
    ppermute x8, starting transfers between devices, to_columns(): block = lax.ppermute(mine, ('row', 'col'), pairs)  17.2 us
    ppermute x8, waiting for transfers between devices, to_columns(): block = lax.ppermute(mine, ('row', 'col'), pairs)  14 us
    all_to_all x1, blocking collectives, col_sum_rows(): lax.all_to_all(spread, 'col', 0, 0, tiled=True).reshape(partial.shape)  12.1 us
    ppermute x2, starting transfers between devices, to_columns(): other = lax.ppermute(sent, 'row', core_pairs)  9.58 us
    ppermute x2, starting transfers between devices, to_columns(): diagonal = lax.ppermute(across, 'row', core_pairs)  7.76 us
    dot_general x6, matrix products, product(): jnp.dot(left, right, precision=lax.Precision.HIGH, preferred_element_type...  6.37 us
    ppermute x4, waiting for transfers between devices, to_columns(): lax.ppermute(extra, ('row', 'col'), every)  6.04 us
  transfers between devices with their start and end apart: 18, of which 12 were waited for; matrix products, arithmetic and copies ran while one was open for 1% of the time, Pallas kernels for 0%

profile of v23, /device:TPU:1, one launch (start us, length us, event | category | flops | bytes accessed | tf_op | source)
XLA Modules:
  0.0 110.9 jit_solution(10513558233020438407)
XLA Ops:
  1.0 4.5 %collective-permute-start.1 = (f32[512,128]{1,0:T(8,128)S(1)}, f32[512,128]{1,0:T(8,128)S(1)}, u32[]{:S(2)}, u32[]{:S(2)}) collective-permute-start(f32[512,128]{1,0:T(8,128)S(1)} %broadcast_select_fusion.1), channel_id=1, source_target_pairs={{0,128},{8,136},{16,144},{24,152},{33,161},{41,169},{49,177},{57,1... | collective-permute-start | bytes 786440 | tf_op jit(solution)/shard_map/ppermute | solution.py:48
  5.5 1.3 %collective-permute-start.2 = (f32[512,128]{1,0:T(8,128)S(1)}, f32[512,128]{1,0:T(8,128)S(1)}, u32[]{:S(2)}, u32[]{:S(2)}) collective-permute-start(f32[512,128]{1,0:T(8,128)S(1)} %broadcast_select_fusion.1), channel_id=1, source_target_pairs={{0,192},{8,200},{16,208},{24,216},{33,225},{41,233},{49,241},{57,2... | collective-permute-start | bytes 786440 | tf_op jit(solution)/shard_map/ppermute | solution.py:48
  8.2 2.3 %collective-permute-done.1 = f32[512,128]{1,0:T(8,128)S(1)} collective-permute-done((f32[512,128]{1,0:T(8,128)S(1)}, f32[512,128]{1,0:T(8,128)S(1)}, u32[]{:S(2)}, u32[]{:S(2)}) %collective-permute-start.1) | collective-permute-done | bytes 262176 | tf_op jit(solution)/shard_map/ppermute | solution.py:48
  10.5 1.3 %collective-permute-done.2 = f32[512,128]{1,0:T(8,128)S(1)} collective-permute-done((f32[512,128]{1,0:T(8,128)S(1)}, f32[512,128]{1,0:T(8,128)S(1)}, u32[]{:S(2)}, u32[]{:S(2)}) %collective-permute-start.2) | collective-permute-done | bytes 262176 | tf_op jit(solution)/shard_map/ppermute | solution.py:48
  11.8 4.3 %collective-permute-done = f32[512,128]{1,0:T(8,128)S(1)} collective-permute-done((f32[512,128]{1,0:T(8,128)S(1)}, f32[512,128]{1,0:T(8,128)S(1)}, u32[]{:S(2)}, u32[]{:S(2)}) %collective-permute-start) | collective-permute-done | bytes 262176 | tf_op jit(solution)/shard_map/ppermute | solution.py:48
  18.4 4.3 %collective-permute-done.3 = f32[512,128]{1,0:T(8,128)S(1)} collective-permute-done((f32[512,128]{1,0:T(8,128)S(1)}, f32[512,128]{1,0:T(8,128)S(1)}, u32[]{:S(2)}, u32[]{:S(2)}) %collective-permute-start.3) | collective-permute-done | bytes 262176 | tf_op jit(solution)/shard_map/ppermute | solution.py:48
  22.8 1.4 %collective-permute-start.5 = (f32[512,128]{1,0:T(8,128)S(1)}, f32[512,128]{1,0:T(8,128)S(1)}, u32[]{:S(2)}, u32[]{:S(2)}) collective-permute-start(f32[512,128]{1,0:T(8,128)S(1)} %get-tuple-element.8), channel_id=1, source_target_pairs={{0,16},{8,24},{16,0},{24,8},{32,48},{40,56},{48,32},{56,40},{64,80... | collective-permute-start | bytes 786440 | tf_op jit(solution)/shard_map/ppermute | solution.py:61
  24.2 3.3 %collective-permute-start.4 = (f32[512,128]{1,0:T(8,128)S(1)}, f32[512,128]{1,0:T(8,128)S(1)}, u32[]{:S(2)}, u32[]{:S(2)}) collective-permute-start(f32[512,128]{1,0:T(8,128)S(1)} %get-tuple-element.8), channel_id=1, source_target_pairs={{0,8},{8,0},{16,24},{24,16},{32,40},{40,32},{48,56},{56,48},{64,72... | collective-permute-start | bytes 786440 | tf_op jit(solution)/shard_map/ppermute | solution.py:60
  27.5 2.4 %collective-permute-done.5 = f32[512,128]{1,0:T(8,128)S(1)} collective-permute-done((f32[512,128]{1,0:T(8,128)S(1)}, f32[512,128]{1,0:T(8,128)S(1)}, u32[]{:S(2)}, u32[]{:S(2)}) %collective-permute-start.5) | collective-permute-done | bytes 262176 | tf_op jit(solution)/shard_map/ppermute | solution.py:61
  29.9 2.6 %collective-permute-start.6 = (f32[512,128]{1,0:T(8,128)S(1)}, f32[512,128]{1,0:T(8,128)S(1)}, u32[]{:S(2)}, u32[]{:S(2)}) collective-permute-start(f32[512,128]{1,0:T(8,128)S(1)} %collective-permute-done.5), channel_id=1, source_target_pairs={{0,8},{8,0},{16,24},{24,16},{32,40},{40,32},{48,56},{56,48},{64,72... | collective-permute-start | bytes 786440 | tf_op jit(solution)/shard_map/ppermute | solution.py:62
  33.7 4.5 %convolution_bitcast_fusion = f32[512,128]{0,1:T(8,128)S(1)} fusion(f32[2048,128]{1,0:T(8,128)S(1)} %constant_dynamic-update-slice_fusion.1, f32[512,2048]{1,0:T(8,128)} %param.3), kind=kOutput, calls=%fused_computation.9 | convolution fusion | flops 805306368 | bytes 5505024 | tf_op jit(solution)/shard_map/dot_general | solution.py:8
  38.4 19.4 %all_to_all.11 = f32[8,64,128]{2,1,0:T(8,128)S(1)} all-to-all(f32[8,64,128]{2,1,0:T(8,128)S(1)} %bitcast.30), channel_id=1, replica_groups=mesh['row'=32,'col'=8] {'col'}, dimensions={0} | all-to-all | bytes 524288 | tf_op jit(solution)/shard_map/all_to_all | solution.py:74
  57.8 12.1 %all_to_all.10 = f32[8,64,128]{2,1,0:T(8,128)S(1)} all-to-all(f32[8,64,128]{2,1,0:T(8,128)S(1)} %broadcast_in_dim.2), channel_id=1, replica_groups=mesh['row'=32,'col'=8] {'col'}, dimensions={0} | all-to-all | bytes 524288 | tf_op jit(solution)/shard_map/all_to_all | solution.py:76
  69.9 4.9 %collective-permute-start.12 = (f32[512,128]{1,0:T(8,128)S(1)}, f32[512,128]{1,0:T(8,128)S(1)}, u32[]{:S(2)}, u32[]{:S(2)}) collective-permute-start(f32[512,128]{1,0:T(8,128)S(1)} %broadcast_select_fusion), channel_id=1, source_target_pairs={{0,128},{8,136},{16,144},{24,152},{33,161},{41,169},{49,177},{57,1... | collective-permute-start | bytes 786440 | tf_op jit(solution)/shard_map/ppermute | solution.py:48
  74.8 1.3 %collective-permute-start.13 = (f32[512,128]{1,0:T(8,128)S(1)}, f32[512,128]{1,0:T(8,128)S(1)}, u32[]{:S(2)}, u32[]{:S(2)}) collective-permute-start(f32[512,128]{1,0:T(8,128)S(1)} %broadcast_select_fusion), channel_id=1, source_target_pairs={{0,192},{8,200},{16,208},{24,216},{33,225},{41,233},{49,241},{57,2... | collective-permute-start | bytes 786440 | tf_op jit(solution)/shard_map/ppermute | solution.py:48
  76.1 1.3 %collective-permute-start.11 = (f32[512,128]{1,0:T(8,128)S(1)}, f32[512,128]{1,0:T(8,128)S(1)}, u32[]{:S(2)}, u32[]{:S(2)}) collective-permute-start(f32[512,128]{1,0:T(8,128)S(1)} %broadcast_select_fusion), channel_id=1, source_target_pairs={{0,64},{8,72},{16,80},{24,88},{33,97},{41,105},{49,113},{57,121},{... | collective-permute-start | bytes 786440 | tf_op jit(solution)/shard_map/ppermute | solution.py:48
  78.1 3.1 %collective-permute-start.7 = (f32[128,128]{1,0:T(8,128)S(1)}, f32[128,128]{1,0:T(8,128)S(1)}, u32[]{:S(2)}, u32[]{:S(2)}) collective-permute-start(f32[128,128]{1,0:T(8,128)S(1)} %convolution_bitcast_fusion.1), channel_id=1, source_target_pairs={{0,64},{1,65},{2,66},{3,67},{4,68},{5,69},{6,70},{7,71},{8,72},{9,... | collective-permute-start | bytes 196616 | tf_op jit(solution)/shard_map/ppermute | solution.py:49
  81.1 1.7 %collective-permute-done.11 = f32[512,128]{1,0:T(8,128)S(1)} collective-permute-done((f32[512,128]{1,0:T(8,128)S(1)}, f32[512,128]{1,0:T(8,128)S(1)}, u32[]{:S(2)}, u32[]{:S(2)}) %collective-permute-start.11) | collective-permute-done | bytes 262176 | tf_op jit(solution)/shard_map/ppermute | solution.py:48
  82.9 1.3 %collective-permute-start.14 = (f32[512,128]{1,0:T(8,128)S(1)}, f32[512,128]{1,0:T(8,128)S(1)}, u32[]{:S(2)}, u32[]{:S(2)}) collective-permute-start(f32[512,128]{1,0:T(8,128)S(1)} %add_add_fusion), channel_id=1, source_target_pairs={{0,32},{2,34},{4,36},{6,38},{8,40},{10,42},{12,44},{14,46},{16,48}... | collective-permute-start | bytes 786440 | tf_op jit(solution)/shard_map/ppermute | solution.py:48
  84.3 1.4 %collective-permute-done.7 = f32[128,128]{1,0:T(8,128)S(1)} collective-permute-done((f32[128,128]{1,0:T(8,128)S(1)}, f32[128,128]{1,0:T(8,128)S(1)}, u32[]{:S(2)}, u32[]{:S(2)}) %collective-permute-start.7) | collective-permute-done | bytes 65568 | tf_op jit(solution)/shard_map/ppermute | solution.py:49
  85.8 4.6 %collective-permute-done.10 = f32[128,128]{1,0:T(8,128)S(1)} collective-permute-done((f32[128,128]{1,0:T(8,128)S(1)}, f32[128,128]{1,0:T(8,128)S(1)}, u32[]{:S(2)}, u32[]{:S(2)}) %collective-permute-start.10) | collective-permute-done | bytes 65568 | tf_op jit(solution)/shard_map/ppermute | solution.py:49
  91.3 6.3 %collective-permute-start.15 = (f32[640,128]{1,0:T(8,128)S(1)}, f32[640,128]{1,0:T(8,128)S(1)}, u32[]{:S(2)}, u32[]{:S(2)}) collective-permute-start(f32[640,128]{1,0:T(8,128)S(1)} %pad_maximum_fusion), channel_id=1, source_target_pairs={{0,8},{8,0},{16,24},{24,16},{32,40},{40,32},{48,56},{56,48},{64,72... | collective-permute-start | bytes 983048 | tf_op jit(solution)/shard_map/ppermute | solution.py:60
  98.5 5.2 %collective-permute-start.17 = (f32[640,128]{1,0:T(8,128)S(1)}, f32[640,128]{1,0:T(8,128)S(1)}, u32[]{:S(2)}, u32[]{:S(2)}) collective-permute-start(f32[640,128]{1,0:T(8,128)S(1)} %collective-permute-done.16), channel_id=1, source_target_pairs={{0,8},{8,0},{16,24},{24,16},{32,40},{40,32},{48,56},{56,48},{64,72... | collective-permute-start | bytes 983048 | tf_op jit(solution)/shard_map/ppermute | solution.py:62
  106.8 4.1 %convolution_subtract_fusion = f32[512,2048]{1,0:T(8,128)} fusion(f32[512,2048]{1,0:T(8,128)S(1)} %copy-done.1, f32[2048,128]{1,0:T(8,128)S(1)} %constant_dynamic-update-slice_fusion.1, f32[2048,128]{1,0:T(8,128)S(1)} %convolution_subtract_fusion.1, f32[512,128]{1,0:T(8,128)S(1)} %fusion.4, f32[512,128]{1,0:T(8,128)S(1)} %copy-done.2), kind=kOutput, calls=%fused_computation | convolution fusion | flops 1612316672 | bytes 11010048 | tf_op jit(solution)/shard_map/dot_general | solution.py:88
  (49 shorter events, 11.8 us)
Async XLA Ops:
  0.0 97.5 %copy-start = (f32[128,128]{1,0:T(8,128)S(1)}, f32[128,128]{1,0:T(8,128)}, u32[]{:S(2)}) copy-start(f32[128,128]{1,0:T(8,128)} %param.5) | copy-start | bytes 196612
  1.0 9.5 %collective-permute-start.1 = (f32[512,128]{1,0:T(8,128)S(1)}, f32[512,128]{1,0:T(8,128)S(1)}, u32[]{:S(2)}, u32[]{:S(2)}) collective-permute-start(f32[512,128]{1,0:T(8,128)S(1)} %broadcast_select_fusion.1), channel_id=1, source_target_pairs={{0,128},{8,136},{16,144},{24,152},{33,161},{41,169},{49,177},{57,1... | collective-permute-start | bytes 786440 | tf_op jit(solution)/shard_map/ppermute | solution.py:48
  5.5 6.3 %collective-permute-start.2 = (f32[512,128]{1,0:T(8,128)S(1)}, f32[512,128]{1,0:T(8,128)S(1)}, u32[]{:S(2)}, u32[]{:S(2)}) collective-permute-start(f32[512,128]{1,0:T(8,128)S(1)} %broadcast_select_fusion.1), channel_id=1, source_target_pairs={{0,192},{8,200},{16,208},{24,216},{33,225},{41,233},{49,241},{57,2... | collective-permute-start | bytes 786440 | tf_op jit(solution)/shard_map/ppermute | solution.py:48
  6.8 9.2 %collective-permute-start = (f32[512,128]{1,0:T(8,128)S(1)}, f32[512,128]{1,0:T(8,128)S(1)}, u32[]{:S(2)}, u32[]{:S(2)}) collective-permute-start(f32[512,128]{1,0:T(8,128)S(1)} %broadcast_select_fusion.1), channel_id=1, source_target_pairs={{0,64},{8,72},{16,80},{24,88},{33,97},{41,105},{49,113},{57,121},{... | collective-permute-start | bytes 786440 | tf_op jit(solution)/shard_map/ppermute | solution.py:48
  17.1 5.6 %collective-permute-start.3 = (f32[512,128]{1,0:T(8,128)S(1)}, f32[512,128]{1,0:T(8,128)S(1)}, u32[]{:S(2)}, u32[]{:S(2)}) collective-permute-start(f32[512,128]{1,0:T(8,128)S(1)} %add_add_fusion.1), channel_id=1, source_target_pairs={{0,32},{2,34},{4,36},{6,38},{8,40},{10,42},{12,44},{14,46},{16,48}... | collective-permute-start | bytes 786440 | tf_op jit(solution)/shard_map/ppermute | solution.py:48
  22.8 7.1 %collective-permute-start.5 = (f32[512,128]{1,0:T(8,128)S(1)}, f32[512,128]{1,0:T(8,128)S(1)}, u32[]{:S(2)}, u32[]{:S(2)}) collective-permute-start(f32[512,128]{1,0:T(8,128)S(1)} %get-tuple-element.8), channel_id=1, source_target_pairs={{0,16},{8,24},{16,0},{24,8},{32,48},{40,56},{48,32},{56,40},{64,80... | collective-permute-start | bytes 786440 | tf_op jit(solution)/shard_map/ppermute | solution.py:61
  24.2 8.3 %collective-permute-start.4 = (f32[512,128]{1,0:T(8,128)S(1)}, f32[512,128]{1,0:T(8,128)S(1)}, u32[]{:S(2)}, u32[]{:S(2)}) collective-permute-start(f32[512,128]{1,0:T(8,128)S(1)} %get-tuple-element.8), channel_id=1, source_target_pairs={{0,8},{8,0},{16,24},{24,16},{32,40},{40,32},{48,56},{56,48},{64,72... | collective-permute-start | bytes 786440 | tf_op jit(solution)/shard_map/ppermute | solution.py:60
  29.9 3.8 %collective-permute-start.6 = (f32[512,128]{1,0:T(8,128)S(1)}, f32[512,128]{1,0:T(8,128)S(1)}, u32[]{:S(2)}, u32[]{:S(2)}) collective-permute-start(f32[512,128]{1,0:T(8,128)S(1)} %collective-permute-done.5), channel_id=1, source_target_pairs={{0,8},{8,0},{16,24},{24,16},{32,40},{40,32},{48,56},{56,48},{64,72... | collective-permute-start | bytes 786440 | tf_op jit(solution)/shard_map/ppermute | solution.py:62
  33.7 43.7 %copy-start.2 = (f32[512,128]{1,0:T(8,128)S(1)}, f32[512,128]{1,0:T(8,128)}, u32[]{:S(2)}) copy-start(f32[512,128]{1,0:T(8,128)} %param.4) | copy-start | bytes 786436
  69.9 8.2 %collective-permute-start.12 = (f32[512,128]{1,0:T(8,128)S(1)}, f32[512,128]{1,0:T(8,128)S(1)}, u32[]{:S(2)}, u32[]{:S(2)}) collective-permute-start(f32[512,128]{1,0:T(8,128)S(1)} %broadcast_select_fusion), channel_id=1, source_target_pairs={{0,128},{8,136},{16,144},{24,152},{33,161},{41,169},{49,177},{57,1... | collective-permute-start | bytes 786440 | tf_op jit(solution)/shard_map/ppermute | solution.py:48
  74.8 6.4 %collective-permute-start.13 = (f32[512,128]{1,0:T(8,128)S(1)}, f32[512,128]{1,0:T(8,128)S(1)}, u32[]{:S(2)}, u32[]{:S(2)}) collective-permute-start(f32[512,128]{1,0:T(8,128)S(1)} %broadcast_select_fusion), channel_id=1, source_target_pairs={{0,192},{8,200},{16,208},{24,216},{33,225},{41,233},{49,241},{57,2... | collective-permute-start | bytes 786440 | tf_op jit(solution)/shard_map/ppermute | solution.py:48
  76.1 6.8 %collective-permute-start.11 = (f32[512,128]{1,0:T(8,128)S(1)}, f32[512,128]{1,0:T(8,128)S(1)}, u32[]{:S(2)}, u32[]{:S(2)}) collective-permute-start(f32[512,128]{1,0:T(8,128)S(1)} %broadcast_select_fusion), channel_id=1, source_target_pairs={{0,64},{8,72},{16,80},{24,88},{33,97},{41,105},{49,113},{57,121},{... | collective-permute-start | bytes 786440 | tf_op jit(solution)/shard_map/ppermute | solution.py:48
  77.8 6.4 %collective-permute-start.9 = (f32[128,128]{1,0:T(8,128)S(1)}, f32[128,128]{1,0:T(8,128)S(1)}, u32[]{:S(2)}, u32[]{:S(2)}) collective-permute-start(f32[128,128]{1,0:T(8,128)S(1)} %convolution_bitcast_fusion.1), channel_id=1, source_target_pairs={{0,192},{1,193},{2,194},{3,195},{4,196},{5,197},{6,198},{7,199},{8... | collective-permute-start | bytes 196616 | tf_op jit(solution)/shard_map/ppermute | solution.py:49
  77.9 6.4 %collective-permute-start.8 = (f32[128,128]{1,0:T(8,128)S(1)}, f32[128,128]{1,0:T(8,128)S(1)}, u32[]{:S(2)}, u32[]{:S(2)}) collective-permute-start(f32[128,128]{1,0:T(8,128)S(1)} %convolution_bitcast_fusion.1), channel_id=1, source_target_pairs={{0,128},{1,129},{2,130},{3,131},{4,132},{5,133},{6,134},{7,135},{8... | collective-permute-start | bytes 196616 | tf_op jit(solution)/shard_map/ppermute | solution.py:49
  78.1 7.6 %collective-permute-start.7 = (f32[128,128]{1,0:T(8,128)S(1)}, f32[128,128]{1,0:T(8,128)S(1)}, u32[]{:S(2)}, u32[]{:S(2)}) collective-permute-start(f32[128,128]{1,0:T(8,128)S(1)} %convolution_bitcast_fusion.1), channel_id=1, source_target_pairs={{0,64},{1,65},{2,66},{3,67},{4,68},{5,69},{6,70},{7,71},{8,72},{9,... | collective-permute-start | bytes 196616 | tf_op jit(solution)/shard_map/ppermute | solution.py:49
  82.9 7.5 %collective-permute-start.14 = (f32[512,128]{1,0:T(8,128)S(1)}, f32[512,128]{1,0:T(8,128)S(1)}, u32[]{:S(2)}, u32[]{:S(2)}) collective-permute-start(f32[512,128]{1,0:T(8,128)S(1)} %add_add_fusion), channel_id=1, source_target_pairs={{0,32},{2,34},{4,36},{6,38},{8,40},{10,42},{12,44},{14,46},{16,48}... | collective-permute-start | bytes 786440 | tf_op jit(solution)/shard_map/ppermute | solution.py:48
  85.7 4.7 %collective-permute-start.10 = (f32[128,128]{1,0:T(8,128)S(1)}, f32[128,128]{1,0:T(8,128)S(1)}, u32[]{:S(2)}, u32[]{:S(2)}) collective-permute-start(f32[128,128]{1,0:T(8,128)S(1)} %add_add_fusion.2), channel_id=1, source_target_pairs={{0,32},{1,33},{2,34},{3,35},{4,36},{5,37},{6,38},{7,39},{8,40},{9,... | collective-permute-start | bytes 196616 | tf_op jit(solution)/shard_map/ppermute | solution.py:49
  90.6 7.9 %collective-permute-start.16 = (f32[640,128]{1,0:T(8,128)S(1)}, f32[640,128]{1,0:T(8,128)S(1)}, u32[]{:S(2)}, u32[]{:S(2)}) collective-permute-start(f32[640,128]{1,0:T(8,128)S(1)} %pad_maximum_fusion), channel_id=1, source_target_pairs={{0,16},{8,24},{16,0},{24,8},{32,48},{40,56},{48,32},{56,40},{64,80... | collective-permute-start | bytes 983048 | tf_op jit(solution)/shard_map/ppermute | solution.py:61
  91.3 12.4 %collective-permute-start.15 = (f32[640,128]{1,0:T(8,128)S(1)}, f32[640,128]{1,0:T(8,128)S(1)}, u32[]{:S(2)}, u32[]{:S(2)}) collective-permute-start(f32[640,128]{1,0:T(8,128)S(1)} %pad_maximum_fusion), channel_id=1, source_target_pairs={{0,8},{8,0},{16,24},{24,16},{32,40},{40,32},{48,56},{56,48},{64,72... | collective-permute-start | bytes 983048 | tf_op jit(solution)/shard_map/ppermute | solution.py:60
  98.5 6.4 %collective-permute-start.17 = (f32[640,128]{1,0:T(8,128)S(1)}, f32[640,128]{1,0:T(8,128)S(1)}, u32[]{:S(2)}, u32[]{:S(2)}) collective-permute-start(f32[640,128]{1,0:T(8,128)S(1)} %collective-permute-done.16), channel_id=1, source_target_pairs={{0,8},{8,0},{16,24},{24,16},{32,40},{40,32},{48,56},{56,48},{64,72... | collective-permute-start | bytes 983048 | tf_op jit(solution)/shard_map/ppermute | solution.py:62
  103.6 3.2 %copy-start.1 = (f32[512,2048]{1,0:T(8,128)S(1)}, f32[512,2048]{1,0:T(8,128)}, u32[]{:S(2)}) copy-start(f32[512,2048]{1,0:T(8,128)} %param.3) | copy-start | bytes 12582916

commit v24 on v23

--- a/solution.py
+++ b/solution.py
@@ -28,7 +28,7 @@
     col = lax.axis_index("col")
     mine = jnp.where(high == col, panel_rows, jnp.zeros_like(panel_rows))
     if col_count == 8:
-        rounds = [(2, 4, 6), (1,)]
+        rounds = [(1,), (2, 4, 6)]
     else:
         rounds = [(1 << k,) for k in range(col_count.bit_length() - 1)]
     reached = {0}

time: 113 us -> 115 us (1.018); the launches traced: 111 us -> 114 us
  waiting for transfers between devices: 25.5 us -> 29.3 us
    ppermute x8, waiting for transfers between devices: 14 us -> 19.6 us  [to_columns(): block = lax.ppermute(mine, ('row', 'col'), pairs)]
    ppermute x2, starting transfers between devices: 7.76 us -> 9.5 us  [to_columns(): diagonal = lax.ppermute(across, 'row', core_pairs)]
    ppermute x2, starting transfers between devices: 2.06 us -> 0.58 us  [to_columns(): across = lax.ppermute(sent, 'row', [(i, i ^ 2) for i in range(row_count)])]
    ppermute x4, waiting for transfers between devices: 6.04 us -> 4.61 us  [to_columns(): lax.ppermute(extra, ('row', 'col'), every)]
    ppermute x2, starting transfers between devices: 9.58 us -> 8.23 us  [to_columns(): other = lax.ppermute(sent, 'row', core_pairs)]
  transfers between devices with their start and end apart: 18 -> 18, of which waited for: 12 -> 11; matrix products, arithmetic and copies ran while one was open for 1% -> 1% of each run, Pallas kernels for 0% -> 0%
where the time goes in v24:
time: 115 us; the launch traced here: 114 us
  starting transfers between devices  39.5 us (34%)
  blocking collectives  31.3 us (27%)
  waiting for transfers between devices  29.3 us (25%)
  matrix products  11.1 us (10%)
  other arithmetic  2.24 us (2%)
    ppermute x8, waiting for transfers between devices, to_columns(): block = lax.ppermute(mine, ('row', 'col'), pairs)  19.6 us
    all_to_all x1, blocking collectives, col_sum_rows(): total = jnp.sum(lax.all_to_all(pieces, 'col', 0, 0, tiled=True), axis=0)  19.3 us
    ppermute x8, starting transfers between devices, to_columns(): block = lax.ppermute(mine, ('row', 'col'), pairs)  17.7 us
    all_to_all x1, blocking collectives, col_sum_rows(): lax.all_to_all(spread, 'col', 0, 0, tiled=True).reshape(partial.shape)  12.1 us
    ppermute x2, starting transfers between devices, to_columns(): diagonal = lax.ppermute(across, 'row', core_pairs)  9.5 us
    ppermute x2, starting transfers between devices, to_columns(): other = lax.ppermute(sent, 'row', core_pairs)  8.23 us
    dot_general x6, matrix products, product(): jnp.dot(left, right, precision=lax.Precision.HIGH, preferred_element_type...  6.37 us
    ppermute x4, waiting for transfers between devices, to_columns(): lax.ppermute(extra, ('row', 'col'), every)  4.61 us
  transfers between devices with their start and end apart: 18, of which 11 were waited for; matrix products, arithmetic and copies ran while one was open for 1% of the time, Pallas kernels for 0%

profile of v24, /device:TPU:1, one launch (start us, length us, event | category | flops | bytes accessed | tf_op | source)
XLA Modules:
  0.0 114.2 jit_solution(17880026602830302136)
XLA Ops:
  1.0 4.7 %collective-permute-start = (f32[512,128]{1,0:T(8,128)S(1)}, f32[512,128]{1,0:T(8,128)S(1)}, u32[]{:S(2)}, u32[]{:S(2)}) collective-permute-start(f32[512,128]{1,0:T(8,128)S(1)} %broadcast_select_fusion.1), channel_id=1, source_target_pairs={{0,32},{8,40},{16,48},{24,56},{33,1},{41,9},{49,17},{57,25},{66,98... | collective-permute-start | bytes 786440 | tf_op jit(solution)/shard_map/ppermute | solution.py:48
  5.7 4.9 %collective-permute-done = f32[512,128]{1,0:T(8,128)S(1)} collective-permute-done((f32[512,128]{1,0:T(8,128)S(1)}, f32[512,128]{1,0:T(8,128)S(1)}, u32[]{:S(2)}, u32[]{:S(2)}) %collective-permute-start) | collective-permute-done | bytes 262176 | tf_op jit(solution)/shard_map/ppermute | solution.py:48
  11.6 1.3 %collective-permute-start.3 = (f32[512,128]{1,0:T(8,128)S(1)}, f32[512,128]{1,0:T(8,128)S(1)}, u32[]{:S(2)}, u32[]{:S(2)}) collective-permute-start(f32[512,128]{1,0:T(8,128)S(1)} %fusion.28), channel_id=1, source_target_pairs={{0,192},{1,193},{8,200},{9,201},{16,208},{17,209},{24,216},{25,217... | collective-permute-start | bytes 786440 | tf_op jit(solution)/shard_map/ppermute | solution.py:48
  12.9 1.3 %collective-permute-start.2 = (f32[512,128]{1,0:T(8,128)S(1)}, f32[512,128]{1,0:T(8,128)S(1)}, u32[]{:S(2)}, u32[]{:S(2)}) collective-permute-start(f32[512,128]{1,0:T(8,128)S(1)} %fusion.28), channel_id=1, source_target_pairs={{0,128},{1,129},{8,136},{9,137},{16,144},{17,145},{24,152},{25,153... | collective-permute-start | bytes 786440 | tf_op jit(solution)/shard_map/ppermute | solution.py:48
  14.2 1.3 %collective-permute-start.1 = (f32[512,128]{1,0:T(8,128)S(1)}, f32[512,128]{1,0:T(8,128)S(1)}, u32[]{:S(2)}, u32[]{:S(2)}) collective-permute-start(f32[512,128]{1,0:T(8,128)S(1)} %fusion.28), channel_id=1, source_target_pairs={{0,64},{1,65},{8,72},{9,73},{16,80},{17,81},{24,88},{25,89},{32,96... | collective-permute-start | bytes 786440 | tf_op jit(solution)/shard_map/ppermute | solution.py:48
  15.6 1.7 %collective-permute-done.3 = f32[512,128]{1,0:T(8,128)S(1)} collective-permute-done((f32[512,128]{1,0:T(8,128)S(1)}, f32[512,128]{1,0:T(8,128)S(1)}, u32[]{:S(2)}, u32[]{:S(2)}) %collective-permute-start.3) | collective-permute-done | bytes 262176 | tf_op jit(solution)/shard_map/ppermute | solution.py:48
  17.2 1.3 %collective-permute-done.2 = f32[512,128]{1,0:T(8,128)S(1)} collective-permute-done((f32[512,128]{1,0:T(8,128)S(1)}, f32[512,128]{1,0:T(8,128)S(1)}, u32[]{:S(2)}, u32[]{:S(2)}) %collective-permute-start.2) | collective-permute-done | bytes 262176 | tf_op jit(solution)/shard_map/ppermute | solution.py:48
  18.5 5.6 %collective-permute-done.1 = f32[512,128]{1,0:T(8,128)S(1)} collective-permute-done((f32[512,128]{1,0:T(8,128)S(1)}, f32[512,128]{1,0:T(8,128)S(1)}, u32[]{:S(2)}, u32[]{:S(2)}) %collective-permute-start.1) | collective-permute-done | bytes 262176 | tf_op jit(solution)/shard_map/ppermute | solution.py:48
  24.8 2.5 %collective-permute-start.4 = (f32[512,128]{1,0:T(8,128)S(1)}, f32[512,128]{1,0:T(8,128)S(1)}, u32[]{:S(2)}, u32[]{:S(2)}) collective-permute-start(f32[512,128]{1,0:T(8,128)S(1)} %get-tuple-element.8), channel_id=1, source_target_pairs={{0,8},{8,0},{16,24},{24,16},{32,40},{40,32},{48,56},{56,48},{64,72... | collective-permute-start | bytes 786440 | tf_op jit(solution)/shard_map/ppermute | solution.py:60
  27.3 2.7 %collective-permute-done.5 = f32[512,128]{1,0:T(8,128)S(1)} collective-permute-done((f32[512,128]{1,0:T(8,128)S(1)}, f32[512,128]{1,0:T(8,128)S(1)}, u32[]{:S(2)}, u32[]{:S(2)}) %collective-permute-start.5) | collective-permute-done | bytes 262176 | tf_op jit(solution)/shard_map/ppermute | solution.py:61
  30.0 3.1 %collective-permute-start.6 = (f32[512,128]{1,0:T(8,128)S(1)}, f32[512,128]{1,0:T(8,128)S(1)}, u32[]{:S(2)}, u32[]{:S(2)}) collective-permute-start(f32[512,128]{1,0:T(8,128)S(1)} %collective-permute-done.5), channel_id=1, source_target_pairs={{0,8},{8,0},{16,24},{24,16},{32,40},{40,32},{48,56},{56,48},{64,72... | collective-permute-start | bytes 786440 | tf_op jit(solution)/shard_map/ppermute | solution.py:62
  34.3 4.5 %convolution_bitcast_fusion = f32[512,128]{0,1:T(8,128)S(1)} fusion(f32[2048,128]{1,0:T(8,128)S(1)} %constant_dynamic-update-slice_fusion.1, f32[512,2048]{1,0:T(8,128)} %param.3), kind=kOutput, calls=%fused_computation.9 | convolution fusion | flops 805306368 | bytes 5505024 | tf_op jit(solution)/shard_map/dot_general | solution.py:8
  38.9 19.3 %all_to_all.11 = f32[8,64,128]{2,1,0:T(8,128)S(1)} all-to-all(f32[8,64,128]{2,1,0:T(8,128)S(1)} %bitcast.30), channel_id=1, replica_groups=mesh['row'=32,'col'=8] {'col'}, dimensions={0} | all-to-all | bytes 524288 | tf_op jit(solution)/shard_map/all_to_all | solution.py:74
  58.3 12.1 %all_to_all.10 = f32[8,64,128]{2,1,0:T(8,128)S(1)} all-to-all(f32[8,64,128]{2,1,0:T(8,128)S(1)} %broadcast_in_dim.2), channel_id=1, replica_groups=mesh['row'=32,'col'=8] {'col'}, dimensions={0} | all-to-all | bytes 524288 | tf_op jit(solution)/shard_map/all_to_all | solution.py:76
  70.4 4.0 %collective-permute-start.11 = (f32[512,128]{1,0:T(8,128)S(1)}, f32[512,128]{1,0:T(8,128)S(1)}, u32[]{:S(2)}, u32[]{:S(2)}) collective-permute-start(f32[512,128]{1,0:T(8,128)S(1)} %broadcast_select_fusion), channel_id=1, source_target_pairs={{0,32},{8,40},{16,48},{24,56},{33,1},{41,9},{49,17},{57,25},{66,98... | collective-permute-start | bytes 786440 | tf_op jit(solution)/shard_map/ppermute | solution.py:48
  74.9 4.6 %collective-permute-done.7 = f32[128,128]{1,0:T(8,128)S(1)} collective-permute-done((f32[128,128]{1,0:T(8,128)S(1)}, f32[128,128]{1,0:T(8,128)S(1)}, u32[]{:S(2)}, u32[]{:S(2)}) %collective-permute-start.7) | collective-permute-done | bytes 65568 | tf_op jit(solution)/shard_map/ppermute | solution.py:49
  80.2 2.6 %collective-permute-start.8 = (f32[128,128]{1,0:T(8,128)S(1)}, f32[128,128]{1,0:T(8,128)S(1)}, u32[]{:S(2)}, u32[]{:S(2)}) collective-permute-start(f32[128,128]{1,0:T(8,128)S(1)} %add.76), channel_id=1, source_target_pairs={{0,64},{1,65},{2,66},{3,67},{4,68},{5,69},{6,70},{7,71},{8,72},{9,... | collective-permute-start | bytes 196616 | tf_op jit(solution)/shard_map/ppermute | solution.py:49
  82.9 2.5 %collective-permute-start.14 = (f32[512,128]{1,0:T(8,128)S(1)}, f32[512,128]{1,0:T(8,128)S(1)}, u32[]{:S(2)}, u32[]{:S(2)}) collective-permute-start(f32[512,128]{1,0:T(8,128)S(1)} %fusion.27), channel_id=1, source_target_pairs={{0,192},{1,193},{8,200},{9,201},{16,208},{17,209},{24,216},{25,217... | collective-permute-start | bytes 786440 | tf_op jit(solution)/shard_map/ppermute | solution.py:48
  86.7 1.3 %collective-permute-start.12 = (f32[512,128]{1,0:T(8,128)S(1)}, f32[512,128]{1,0:T(8,128)S(1)}, u32[]{:S(2)}, u32[]{:S(2)}) collective-permute-start(f32[512,128]{1,0:T(8,128)S(1)} %fusion.27), channel_id=1, source_target_pairs={{0,64},{1,65},{8,72},{9,73},{16,80},{17,81},{24,88},{25,89},{32,96... | collective-permute-start | bytes 786440 | tf_op jit(solution)/shard_map/ppermute | solution.py:48
  88.1 1.6 %collective-permute-done.14 = f32[512,128]{1,0:T(8,128)S(1)} collective-permute-done((f32[512,128]{1,0:T(8,128)S(1)}, f32[512,128]{1,0:T(8,128)S(1)}, u32[]{:S(2)}, u32[]{:S(2)}) %collective-permute-start.14) | collective-permute-done | bytes 262176 | tf_op jit(solution)/shard_map/ppermute | solution.py:48
  90.7 3.5 %collective-permute-done.12 = f32[512,128]{1,0:T(8,128)S(1)} collective-permute-done((f32[512,128]{1,0:T(8,128)S(1)}, f32[512,128]{1,0:T(8,128)S(1)}, u32[]{:S(2)}, u32[]{:S(2)}) %collective-permute-start.12) | collective-permute-done | bytes 262176 | tf_op jit(solution)/shard_map/ppermute | solution.py:48
  94.4 5.8 %collective-permute-start.15 = (f32[640,128]{1,0:T(8,128)S(1)}, f32[640,128]{1,0:T(8,128)S(1)}, u32[]{:S(2)}, u32[]{:S(2)}) collective-permute-start(f32[640,128]{1,0:T(8,128)S(1)} %pad_maximum_fusion), channel_id=1, source_target_pairs={{0,8},{8,0},{16,24},{24,16},{32,40},{40,32},{48,56},{56,48},{64,72... | collective-permute-start | bytes 983048 | tf_op jit(solution)/shard_map/ppermute | solution.py:60
  100.5 6.4 %collective-permute-start.17 = (f32[640,128]{1,0:T(8,128)S(1)}, f32[640,128]{1,0:T(8,128)S(1)}, u32[]{:S(2)}, u32[]{:S(2)}) collective-permute-start(f32[640,128]{1,0:T(8,128)S(1)} %collective-permute-done.16), channel_id=1, source_target_pairs={{0,8},{8,0},{16,24},{24,16},{32,40},{40,32},{48,56},{56,48},{64,72... | collective-permute-start | bytes 983048 | tf_op jit(solution)/shard_map/ppermute | solution.py:62
  110.1 4.1 %convolution_subtract_fusion = f32[512,2048]{1,0:T(8,128)} fusion(f32[512,2048]{1,0:T(8,128)S(1)} %copy-done.1, f32[2048,128]{1,0:T(8,128)S(1)} %constant_dynamic-update-slice_fusion.1, f32[2048,128]{1,0:T(8,128)S(1)} %convolution_subtract_fusion.1, f32[512,128]{1,0:T(8,128)S(1)} %fusion.4, f32[512,128]{1,0:T(8,128)S(1)} %copy-done.2), kind=kOutput, calls=%fused_computation | convolution fusion | flops 1612316672 | bytes 11010048 | tf_op jit(solution)/shard_map/dot_general | solution.py:88
  (49 shorter events, 11.2 us)
Async XLA Ops:
  0.0 100.2 %copy-start = (f32[128,128]{1,0:T(8,128)S(1)}, f32[128,128]{1,0:T(8,128)}, u32[]{:S(2)}) copy-start(f32[128,128]{1,0:T(8,128)} %param.5) | copy-start | bytes 196612
  1.0 9.6 %collective-permute-start = (f32[512,128]{1,0:T(8,128)S(1)}, f32[512,128]{1,0:T(8,128)S(1)}, u32[]{:S(2)}, u32[]{:S(2)}) collective-permute-start(f32[512,128]{1,0:T(8,128)S(1)} %broadcast_select_fusion.1), channel_id=1, source_target_pairs={{0,32},{8,40},{16,48},{24,56},{33,1},{41,9},{49,17},{57,25},{66,98... | collective-permute-start | bytes 786440 | tf_op jit(solution)/shard_map/ppermute | solution.py:48
  11.6 5.6 %collective-permute-start.3 = (f32[512,128]{1,0:T(8,128)S(1)}, f32[512,128]{1,0:T(8,128)S(1)}, u32[]{:S(2)}, u32[]{:S(2)}) collective-permute-start(f32[512,128]{1,0:T(8,128)S(1)} %fusion.28), channel_id=1, source_target_pairs={{0,192},{1,193},{8,200},{9,201},{16,208},{17,209},{24,216},{25,217... | collective-permute-start | bytes 786440 | tf_op jit(solution)/shard_map/ppermute | solution.py:48
  12.9 5.6 %collective-permute-start.2 = (f32[512,128]{1,0:T(8,128)S(1)}, f32[512,128]{1,0:T(8,128)S(1)}, u32[]{:S(2)}, u32[]{:S(2)}) collective-permute-start(f32[512,128]{1,0:T(8,128)S(1)} %fusion.28), channel_id=1, source_target_pairs={{0,128},{1,129},{8,136},{9,137},{16,144},{17,145},{24,152},{25,153... | collective-permute-start | bytes 786440 | tf_op jit(solution)/shard_map/ppermute | solution.py:48
  14.2 9.9 %collective-permute-start.1 = (f32[512,128]{1,0:T(8,128)S(1)}, f32[512,128]{1,0:T(8,128)S(1)}, u32[]{:S(2)}, u32[]{:S(2)}) collective-permute-start(f32[512,128]{1,0:T(8,128)S(1)} %fusion.28), channel_id=1, source_target_pairs={{0,64},{1,65},{8,72},{9,73},{16,80},{17,81},{24,88},{25,89},{32,96... | collective-permute-start | bytes 786440 | tf_op jit(solution)/shard_map/ppermute | solution.py:48
  24.3 5.7 %collective-permute-start.5 = (f32[512,128]{1,0:T(8,128)S(1)}, f32[512,128]{1,0:T(8,128)S(1)}, u32[]{:S(2)}, u32[]{:S(2)}) collective-permute-start(f32[512,128]{1,0:T(8,128)S(1)} %get-tuple-element.8), channel_id=1, source_target_pairs={{0,16},{8,24},{16,0},{24,8},{32,48},{40,56},{48,32},{56,40},{64,80... | collective-permute-start | bytes 786440 | tf_op jit(solution)/shard_map/ppermute | solution.py:61
  24.8 8.3 %collective-permute-start.4 = (f32[512,128]{1,0:T(8,128)S(1)}, f32[512,128]{1,0:T(8,128)S(1)}, u32[]{:S(2)}, u32[]{:S(2)}) collective-permute-start(f32[512,128]{1,0:T(8,128)S(1)} %get-tuple-element.8), channel_id=1, source_target_pairs={{0,8},{8,0},{16,24},{24,16},{32,40},{40,32},{48,56},{56,48},{64,72... | collective-permute-start | bytes 786440 | tf_op jit(solution)/shard_map/ppermute | solution.py:60
  30.0 4.3 %collective-permute-start.6 = (f32[512,128]{1,0:T(8,128)S(1)}, f32[512,128]{1,0:T(8,128)S(1)}, u32[]{:S(2)}, u32[]{:S(2)}) collective-permute-start(f32[512,128]{1,0:T(8,128)S(1)} %collective-permute-done.5), channel_id=1, source_target_pairs={{0,8},{8,0},{16,24},{24,16},{32,40},{40,32},{48,56},{56,48},{64,72... | collective-permute-start | bytes 786440 | tf_op jit(solution)/shard_map/ppermute | solution.py:62
  34.3 40.1 %copy-start.2 = (f32[512,128]{1,0:T(8,128)S(1)}, f32[512,128]{1,0:T(8,128)}, u32[]{:S(2)}) copy-start(f32[512,128]{1,0:T(8,128)} %param.4) | copy-start | bytes 786436
  70.4 12.5 %collective-permute-start.11 = (f32[512,128]{1,0:T(8,128)S(1)}, f32[512,128]{1,0:T(8,128)S(1)}, u32[]{:S(2)}, u32[]{:S(2)}) collective-permute-start(f32[512,128]{1,0:T(8,128)S(1)} %broadcast_select_fusion), channel_id=1, source_target_pairs={{0,32},{8,40},{16,48},{24,56},{33,1},{41,9},{49,17},{57,25},{66,98... | collective-permute-start | bytes 786440 | tf_op jit(solution)/shard_map/ppermute | solution.py:48
  74.8 4.7 %collective-permute-start.7 = (f32[128,128]{1,0:T(8,128)S(1)}, f32[128,128]{1,0:T(8,128)S(1)}, u32[]{:S(2)}, u32[]{:S(2)}) collective-permute-start(f32[128,128]{1,0:T(8,128)S(1)} %convolution_bitcast_fusion.1), channel_id=1, source_target_pairs={{0,32},{1,33},{2,34},{3,35},{4,36},{5,37},{6,38},{7,39},{8,40},{9,... | collective-permute-start | bytes 196616 | tf_op jit(solution)/shard_map/ppermute | solution.py:49
  79.5 7.2 %collective-permute-start.10 = (f32[128,128]{1,0:T(8,128)S(1)}, f32[128,128]{1,0:T(8,128)S(1)}, u32[]{:S(2)}, u32[]{:S(2)}) collective-permute-start(f32[128,128]{1,0:T(8,128)S(1)} %add.76), channel_id=1, source_target_pairs={{0,192},{1,193},{2,194},{3,195},{4,196},{5,197},{6,198},{7,199},{8... | collective-permute-start | bytes 196616 | tf_op jit(solution)/shard_map/ppermute | solution.py:49
  80.2 7.9 %collective-permute-start.9 = (f32[128,128]{1,0:T(8,128)S(1)}, f32[128,128]{1,0:T(8,128)S(1)}, u32[]{:S(2)}, u32[]{:S(2)}) collective-permute-start(f32[128,128]{1,0:T(8,128)S(1)} %add.76), channel_id=1, source_target_pairs={{0,128},{1,129},{2,130},{3,131},{4,132},{5,133},{6,134},{7,135},{8... | collective-permute-start | bytes 196616 | tf_op jit(solution)/shard_map/ppermute | solution.py:49
  80.2 7.9 %collective-permute-start.8 = (f32[128,128]{1,0:T(8,128)S(1)}, f32[128,128]{1,0:T(8,128)S(1)}, u32[]{:S(2)}, u32[]{:S(2)}) collective-permute-start(f32[128,128]{1,0:T(8,128)S(1)} %add.76), channel_id=1, source_target_pairs={{0,64},{1,65},{2,66},{3,67},{4,68},{5,69},{6,70},{7,71},{8,72},{9,... | collective-permute-start | bytes 196616 | tf_op jit(solution)/shard_map/ppermute | solution.py:49
  82.9 6.8 %collective-permute-start.14 = (f32[512,128]{1,0:T(8,128)S(1)}, f32[512,128]{1,0:T(8,128)S(1)}, u32[]{:S(2)}, u32[]{:S(2)}) collective-permute-start(f32[512,128]{1,0:T(8,128)S(1)} %fusion.27), channel_id=1, source_target_pairs={{0,192},{1,193},{8,200},{9,201},{16,208},{17,209},{24,216},{25,217... | collective-permute-start | bytes 786440 | tf_op jit(solution)/shard_map/ppermute | solution.py:48
  85.4 5.3 %collective-permute-start.13 = (f32[512,128]{1,0:T(8,128)S(1)}, f32[512,128]{1,0:T(8,128)S(1)}, u32[]{:S(2)}, u32[]{:S(2)}) collective-permute-start(f32[512,128]{1,0:T(8,128)S(1)} %fusion.27), channel_id=1, source_target_pairs={{0,128},{1,129},{8,136},{9,137},{16,144},{17,145},{24,152},{25,153... | collective-permute-start | bytes 786440 | tf_op jit(solution)/shard_map/ppermute | solution.py:48
  86.7 7.4 %collective-permute-start.12 = (f32[512,128]{1,0:T(8,128)S(1)}, f32[512,128]{1,0:T(8,128)S(1)}, u32[]{:S(2)}, u32[]{:S(2)}) collective-permute-start(f32[512,128]{1,0:T(8,128)S(1)} %fusion.27), channel_id=1, source_target_pairs={{0,64},{1,65},{8,72},{9,73},{16,80},{17,81},{24,88},{25,89},{32,96... | collective-permute-start | bytes 786440 | tf_op jit(solution)/shard_map/ppermute | solution.py:48
  94.3 6.1 %collective-permute-start.16 = (f32[640,128]{1,0:T(8,128)S(1)}, f32[640,128]{1,0:T(8,128)S(1)}, u32[]{:S(2)}, u32[]{:S(2)}) collective-permute-start(f32[640,128]{1,0:T(8,128)S(1)} %pad_maximum_fusion), channel_id=1, source_target_pairs={{0,16},{8,24},{16,0},{24,8},{32,48},{40,56},{48,32},{56,40},{64,80... | collective-permute-start | bytes 983048 | tf_op jit(solution)/shard_map/ppermute | solution.py:61
  94.4 12.4 %collective-permute-start.15 = (f32[640,128]{1,0:T(8,128)S(1)}, f32[640,128]{1,0:T(8,128)S(1)}, u32[]{:S(2)}, u32[]{:S(2)}) collective-permute-start(f32[640,128]{1,0:T(8,128)S(1)} %pad_maximum_fusion), channel_id=1, source_target_pairs={{0,8},{8,0},{16,24},{24,16},{32,40},{40,32},{48,56},{56,48},{64,72... | collective-permute-start | bytes 983048 | tf_op jit(solution)/shard_map/ppermute | solution.py:60
  100.5 7.7 %collective-permute-start.17 = (f32[640,128]{1,0:T(8,128)S(1)}, f32[640,128]{1,0:T(8,128)S(1)}, u32[]{:S(2)}, u32[]{:S(2)}) collective-permute-start(f32[640,128]{1,0:T(8,128)S(1)} %collective-permute-done.16), channel_id=1, source_target_pairs={{0,8},{8,0},{16,24},{24,16},{32,40},{40,32},{48,56},{56,48},{64,72... | collective-permute-start | bytes 983048 | tf_op jit(solution)/shard_map/ppermute | solution.py:62
  106.9 3.2 %copy-start.1 = (f32[512,2048]{1,0:T(8,128)S(1)}, f32[512,2048]{1,0:T(8,128)}, u32[]{:S(2)}) copy-start(f32[512,2048]{1,0:T(8,128)} %param.3) | copy-start | bytes 12582916

commit v25 on v24

--- a/solution.py
+++ b/solution.py
@@ -28,7 +28,7 @@
     col = lax.axis_index("col")
     mine = jnp.where(high == col, panel_rows, jnp.zeros_like(panel_rows))
     if col_count == 8:
-        rounds = [(1,), (2, 4, 6)]
+        rounds = [(2, 4, 6), (1,)] if extra is not None else [(1, 2, 3), (4,)]
     else:
         rounds = [(1 << k,) for k in range(col_count.bit_length() - 1)]
     reached = {0}

time: 115 us -> 111 us (0.965)
  waiting for transfers between devices: 29.3 us -> 22 us
  blocking collectives: 31.3 us -> 36.1 us
  starting transfers between devices: 39.5 us -> 37.6 us
    ppermute x8, waiting for transfers between devices: 19.6 us -> 11 us  [to_columns(): block = lax.ppermute(mine, ('row', 'col'), pairs)]
    all_to_all x1, blocking collectives: 19.3 us -> 24.1 us  [col_sum_rows(): total = jnp.sum(lax.all_to_all(pieces, 'col', 0, 0, tiled=True), axis=0)]
    ppermute x8, starting transfers between devices: 17.7 us -> 14.7 us  [to_columns(): block = lax.ppermute(mine, ('row', 'col'), pairs)]
    ppermute x2, starting transfers between devices: 0.58 us -> 2.8 us  [to_columns(): across = lax.ppermute(sent, 'row', [(i, i ^ 2) for i in range(row_count)])]
    ppermute x4, waiting for transfers between devices: 4.61 us -> 6.04 us  [to_columns(): lax.ppermute(extra, ('row', 'col'), every)]
  transfers between devices with their start and end apart: 18 -> 18, of which waited for: 11 -> 9; matrix products, arithmetic and copies ran while one was open for 1% -> 1% of each run, Pallas kernels for 0% -> 0%
where the time goes in v25:
time: 111 us; the launch traced here: 110 us
  starting transfers between devices  37.6 us (34%)
  blocking collectives  36.1 us (33%)
  waiting for transfers between devices  22 us (20%)
  matrix products  11.1 us (10%)
  other arithmetic  2.22 us (2%)
    all_to_all x1, blocking collectives, col_sum_rows(): total = jnp.sum(lax.all_to_all(pieces, 'col', 0, 0, tiled=True), axis=0)  24.1 us
    ppermute x8, starting transfers between devices, to_columns(): block = lax.ppermute(mine, ('row', 'col'), pairs)  14.7 us
    all_to_all x1, blocking collectives, col_sum_rows(): lax.all_to_all(spread, 'col', 0, 0, tiled=True).reshape(partial.shape)  12.1 us
    ppermute x8, waiting for transfers between devices, to_columns(): block = lax.ppermute(mine, ('row', 'col'), pairs)  11 us
    ppermute x2, starting transfers between devices, to_columns(): diagonal = lax.ppermute(across, 'row', core_pairs)  8.48 us
    ppermute x2, starting transfers between devices, to_columns(): other = lax.ppermute(sent, 'row', core_pairs)  8.24 us
    dot_general x6, matrix products, product(): jnp.dot(left, right, precision=lax.Precision.HIGH, preferred_element_type...  6.37 us
    ppermute x4, waiting for transfers between devices, to_columns(): lax.ppermute(extra, ('row', 'col'), every)  6.04 us
  transfers between devices with their start and end apart: 18, of which 9 were waited for; matrix products, arithmetic and copies ran while one was open for 1% of the time, Pallas kernels for 0%

profile of v25, /device:TPU:1, one launch (start us, length us, event | category | flops | bytes accessed | tf_op | source)
XLA Modules:
  0.0 109.8 jit_solution(12471741416027490817)
XLA Ops:
  1.0 3.0 %collective-permute-start.1 = (f32[512,128]{1,0:T(8,128)S(1)}, f32[512,128]{1,0:T(8,128)S(1)}, u32[]{:S(2)}, u32[]{:S(2)}) collective-permute-start(f32[512,128]{1,0:T(8,128)S(1)} %broadcast_select_fusion.1), channel_id=1, source_target_pairs={{0,64},{8,72},{16,80},{24,88},{33,97},{41,105},{49,113},{57,121},{... | collective-permute-start | bytes 786440 | tf_op jit(solution)/shard_map/ppermute | solution.py:48
  4.0 3.3 %collective-permute-start.2 = (f32[512,128]{1,0:T(8,128)S(1)}, f32[512,128]{1,0:T(8,128)S(1)}, u32[]{:S(2)}, u32[]{:S(2)}) collective-permute-start(f32[512,128]{1,0:T(8,128)S(1)} %broadcast_select_fusion.1), channel_id=1, source_target_pairs={{0,96},{8,104},{16,112},{24,120},{33,65},{41,73},{49,81},{57,89},{... | collective-permute-start | bytes 786440 | tf_op jit(solution)/shard_map/ppermute | solution.py:48
  7.3 1.3 %collective-permute-start = (f32[512,128]{1,0:T(8,128)S(1)}, f32[512,128]{1,0:T(8,128)S(1)}, u32[]{:S(2)}, u32[]{:S(2)}) collective-permute-start(f32[512,128]{1,0:T(8,128)S(1)} %broadcast_select_fusion.1), channel_id=1, source_target_pairs={{0,32},{8,40},{16,48},{24,56},{33,1},{41,9},{49,17},{57,25},{66,98... | collective-permute-start | bytes 786440 | tf_op jit(solution)/shard_map/ppermute | solution.py:48
  8.6 5.3 %collective-permute-done.2 = f32[512,128]{1,0:T(8,128)S(1)} collective-permute-done((f32[512,128]{1,0:T(8,128)S(1)}, f32[512,128]{1,0:T(8,128)S(1)}, u32[]{:S(2)}, u32[]{:S(2)}) %collective-permute-start.2) | collective-permute-done | bytes 262176 | tf_op jit(solution)/shard_map/ppermute | solution.py:48
  14.9 1.3 %collective-permute-start.3 = (f32[512,128]{1,0:T(8,128)S(1)}, f32[512,128]{1,0:T(8,128)S(1)}, u32[]{:S(2)}, u32[]{:S(2)}) collective-permute-start(f32[512,128]{1,0:T(8,128)S(1)} %add_add_fusion.1), channel_id=1, source_target_pairs={{0,128},{1,129},{2,130},{3,131},{8,136},{9,137},{10,138},{11,139},... | collective-permute-start | bytes 786440 | tf_op jit(solution)/shard_map/ppermute | solution.py:48
  16.2 3.6 %collective-permute-done.3 = f32[512,128]{1,0:T(8,128)S(1)} collective-permute-done((f32[512,128]{1,0:T(8,128)S(1)}, f32[512,128]{1,0:T(8,128)S(1)}, u32[]{:S(2)}, u32[]{:S(2)}) %collective-permute-start.3) | collective-permute-done | bytes 262176 | tf_op jit(solution)/shard_map/ppermute | solution.py:48
  20.0 2.7 %collective-permute-start.5 = (f32[512,128]{1,0:T(8,128)S(1)}, f32[512,128]{1,0:T(8,128)S(1)}, u32[]{:S(2)}, u32[]{:S(2)}) collective-permute-start(f32[512,128]{1,0:T(8,128)S(1)} %get-tuple-element.8), channel_id=1, source_target_pairs={{0,16},{8,24},{16,0},{24,8},{32,48},{40,56},{48,32},{56,40},{64,80... | collective-permute-start | bytes 786440 | tf_op jit(solution)/shard_map/ppermute | solution.py:61
  22.7 2.5 %collective-permute-start.4 = (f32[512,128]{1,0:T(8,128)S(1)}, f32[512,128]{1,0:T(8,128)S(1)}, u32[]{:S(2)}, u32[]{:S(2)}) collective-permute-start(f32[512,128]{1,0:T(8,128)S(1)} %get-tuple-element.8), channel_id=1, source_target_pairs={{0,8},{8,0},{16,24},{24,16},{32,40},{40,32},{48,56},{56,48},{64,72... | collective-permute-start | bytes 786440 | tf_op jit(solution)/shard_map/ppermute | solution.py:60
  25.1 2.0 %collective-permute-done.5 = f32[512,128]{1,0:T(8,128)S(1)} collective-permute-done((f32[512,128]{1,0:T(8,128)S(1)}, f32[512,128]{1,0:T(8,128)S(1)}, u32[]{:S(2)}, u32[]{:S(2)}) %collective-permute-start.5) | collective-permute-done | bytes 262176 | tf_op jit(solution)/shard_map/ppermute | solution.py:61
  27.1 2.8 %collective-permute-start.6 = (f32[512,128]{1,0:T(8,128)S(1)}, f32[512,128]{1,0:T(8,128)S(1)}, u32[]{:S(2)}, u32[]{:S(2)}) collective-permute-start(f32[512,128]{1,0:T(8,128)S(1)} %collective-permute-done.5), channel_id=1, source_target_pairs={{0,8},{8,0},{16,24},{24,16},{32,40},{40,32},{48,56},{56,48},{64,72... | collective-permute-start | bytes 786440 | tf_op jit(solution)/shard_map/ppermute | solution.py:62
  31.1 4.5 %convolution_bitcast_fusion = f32[512,128]{0,1:T(8,128)S(1)} fusion(f32[2048,128]{1,0:T(8,128)S(1)} %constant_dynamic-update-slice_fusion.1, f32[512,2048]{1,0:T(8,128)} %param.3), kind=kOutput, calls=%fused_computation.9 | convolution fusion | flops 805306368 | bytes 5505024 | tf_op jit(solution)/shard_map/dot_general | solution.py:8
  35.8 24.1 %all_to_all.11 = f32[8,64,128]{2,1,0:T(8,128)S(1)} all-to-all(f32[8,64,128]{2,1,0:T(8,128)S(1)} %bitcast.30), channel_id=1, replica_groups=mesh['row'=32,'col'=8] {'col'}, dimensions={0} | all-to-all | bytes 524288 | tf_op jit(solution)/shard_map/all_to_all | solution.py:74
  59.9 12.1 %all_to_all.10 = f32[8,64,128]{2,1,0:T(8,128)S(1)} all-to-all(f32[8,64,128]{2,1,0:T(8,128)S(1)} %broadcast_in_dim.2), channel_id=1, replica_groups=mesh['row'=32,'col'=8] {'col'}, dimensions={0} | all-to-all | bytes 524288 | tf_op jit(solution)/shard_map/all_to_all | solution.py:76
  72.0 1.3 %collective-permute-start.12 = (f32[512,128]{1,0:T(8,128)S(1)}, f32[512,128]{1,0:T(8,128)S(1)}, u32[]{:S(2)}, u32[]{:S(2)}) collective-permute-start(f32[512,128]{1,0:T(8,128)S(1)} %broadcast_select_fusion), channel_id=1, source_target_pairs={{0,128},{8,136},{16,144},{24,152},{33,161},{41,169},{49,177},{57,1... | collective-permute-start | bytes 786440 | tf_op jit(solution)/shard_map/ppermute | solution.py:48
  73.3 1.3 %collective-permute-start.13 = (f32[512,128]{1,0:T(8,128)S(1)}, f32[512,128]{1,0:T(8,128)S(1)}, u32[]{:S(2)}, u32[]{:S(2)}) collective-permute-start(f32[512,128]{1,0:T(8,128)S(1)} %broadcast_select_fusion), channel_id=1, source_target_pairs={{0,192},{8,200},{16,208},{24,216},{33,225},{41,233},{49,241},{57,2... | collective-permute-start | bytes 786440 | tf_op jit(solution)/shard_map/ppermute | solution.py:48
  74.6 1.9 %collective-permute-start.11 = (f32[512,128]{1,0:T(8,128)S(1)}, f32[512,128]{1,0:T(8,128)S(1)}, u32[]{:S(2)}, u32[]{:S(2)}) collective-permute-start(f32[512,128]{1,0:T(8,128)S(1)} %broadcast_select_fusion), channel_id=1, source_target_pairs={{0,64},{8,72},{16,80},{24,88},{33,97},{41,105},{49,113},{57,121},{... | collective-permute-start | bytes 786440 | tf_op jit(solution)/shard_map/ppermute | solution.py:48
  78.1 2.1 %collective-permute-start.7 = (f32[128,128]{1,0:T(8,128)S(1)}, f32[128,128]{1,0:T(8,128)S(1)}, u32[]{:S(2)}, u32[]{:S(2)}) collective-permute-start(f32[128,128]{1,0:T(8,128)S(1)} %convolution_bitcast_fusion.1), channel_id=1, source_target_pairs={{0,64},{1,65},{2,66},{3,67},{4,68},{5,69},{6,70},{7,71},{8,72},{9,... | collective-permute-start | bytes 196616 | tf_op jit(solution)/shard_map/ppermute | solution.py:49
  80.2 2.1 %collective-permute-done.11 = f32[512,128]{1,0:T(8,128)S(1)} collective-permute-done((f32[512,128]{1,0:T(8,128)S(1)}, f32[512,128]{1,0:T(8,128)S(1)}, u32[]{:S(2)}, u32[]{:S(2)}) %collective-permute-start.11) | collective-permute-done | bytes 262176 | tf_op jit(solution)/shard_map/ppermute | solution.py:48
  82.4 1.3 %collective-permute-start.14 = (f32[512,128]{1,0:T(8,128)S(1)}, f32[512,128]{1,0:T(8,128)S(1)}, u32[]{:S(2)}, u32[]{:S(2)}) collective-permute-start(f32[512,128]{1,0:T(8,128)S(1)} %add_add_fusion), channel_id=1, source_target_pairs={{0,32},{2,34},{4,36},{6,38},{8,40},{10,42},{12,44},{14,46},{16,48}... | collective-permute-start | bytes 786440 | tf_op jit(solution)/shard_map/ppermute | solution.py:48
  83.7 1.4 %collective-permute-done.7 = f32[128,128]{1,0:T(8,128)S(1)} collective-permute-done((f32[128,128]{1,0:T(8,128)S(1)}, f32[128,128]{1,0:T(8,128)S(1)}, u32[]{:S(2)}, u32[]{:S(2)}) %collective-permute-start.7) | collective-permute-done | bytes 65568 | tf_op jit(solution)/shard_map/ppermute | solution.py:49
  85.2 4.6 %collective-permute-done.10 = f32[128,128]{1,0:T(8,128)S(1)} collective-permute-done((f32[128,128]{1,0:T(8,128)S(1)}, f32[128,128]{1,0:T(8,128)S(1)}, u32[]{:S(2)}, u32[]{:S(2)}) %collective-permute-start.10) | collective-permute-done | bytes 65568 | tf_op jit(solution)/shard_map/ppermute | solution.py:49
  90.1 5.8 %collective-permute-start.15 = (f32[640,128]{1,0:T(8,128)S(1)}, f32[640,128]{1,0:T(8,128)S(1)}, u32[]{:S(2)}, u32[]{:S(2)}) collective-permute-start(f32[640,128]{1,0:T(8,128)S(1)} %pad_maximum_fusion), channel_id=1, source_target_pairs={{0,8},{8,0},{16,24},{24,16},{32,40},{40,32},{48,56},{56,48},{64,72... | collective-permute-start | bytes 983048 | tf_op jit(solution)/shard_map/ppermute | solution.py:60
  96.8 5.7 %collective-permute-start.17 = (f32[640,128]{1,0:T(8,128)S(1)}, f32[640,128]{1,0:T(8,128)S(1)}, u32[]{:S(2)}, u32[]{:S(2)}) collective-permute-start(f32[640,128]{1,0:T(8,128)S(1)} %collective-permute-done.16), channel_id=1, source_target_pairs={{0,8},{8,0},{16,24},{24,16},{32,40},{40,32},{48,56},{56,48},{64,72... | collective-permute-start | bytes 983048 | tf_op jit(solution)/shard_map/ppermute | solution.py:62
  105.7 4.1 %convolution_subtract_fusion = f32[512,2048]{1,0:T(8,128)} fusion(f32[512,2048]{1,0:T(8,128)S(1)} %copy-done.1, f32[2048,128]{1,0:T(8,128)S(1)} %constant_dynamic-update-slice_fusion.1, f32[2048,128]{1,0:T(8,128)S(1)} %convolution_subtract_fusion.1, f32[512,128]{1,0:T(8,128)S(1)} %fusion.4, f32[512,128]{1,0:T(8,128)S(1)} %copy-done.2), kind=kOutput, calls=%fused_computation | convolution fusion | flops 1612316672 | bytes 11010048 | tf_op jit(solution)/shard_map/dot_general | solution.py:88
  (49 shorter events, 9.6 us)
Async XLA Ops:
  0.0 95.9 %copy-start = (f32[128,128]{1,0:T(8,128)S(1)}, f32[128,128]{1,0:T(8,128)}, u32[]{:S(2)}) copy-start(f32[128,128]{1,0:T(8,128)} %param.5) | copy-start | bytes 196612
  1.0 7.6 %collective-permute-start.1 = (f32[512,128]{1,0:T(8,128)S(1)}, f32[512,128]{1,0:T(8,128)S(1)}, u32[]{:S(2)}, u32[]{:S(2)}) collective-permute-start(f32[512,128]{1,0:T(8,128)S(1)} %broadcast_select_fusion.1), channel_id=1, source_target_pairs={{0,64},{8,72},{16,80},{24,88},{33,97},{41,105},{49,113},{57,121},{... | collective-permute-start | bytes 786440 | tf_op jit(solution)/shard_map/ppermute | solution.py:48
  4.0 9.9 %collective-permute-start.2 = (f32[512,128]{1,0:T(8,128)S(1)}, f32[512,128]{1,0:T(8,128)S(1)}, u32[]{:S(2)}, u32[]{:S(2)}) collective-permute-start(f32[512,128]{1,0:T(8,128)S(1)} %broadcast_select_fusion.1), channel_id=1, source_target_pairs={{0,96},{8,104},{16,112},{24,120},{33,65},{41,73},{49,81},{57,89},{... | collective-permute-start | bytes 786440 | tf_op jit(solution)/shard_map/ppermute | solution.py:48
  7.3 6.6 %collective-permute-start = (f32[512,128]{1,0:T(8,128)S(1)}, f32[512,128]{1,0:T(8,128)S(1)}, u32[]{:S(2)}, u32[]{:S(2)}) collective-permute-start(f32[512,128]{1,0:T(8,128)S(1)} %broadcast_select_fusion.1), channel_id=1, source_target_pairs={{0,32},{8,40},{16,48},{24,56},{33,1},{41,9},{49,17},{57,25},{66,98... | collective-permute-start | bytes 786440 | tf_op jit(solution)/shard_map/ppermute | solution.py:48
  14.9 4.9 %collective-permute-start.3 = (f32[512,128]{1,0:T(8,128)S(1)}, f32[512,128]{1,0:T(8,128)S(1)}, u32[]{:S(2)}, u32[]{:S(2)}) collective-permute-start(f32[512,128]{1,0:T(8,128)S(1)} %add_add_fusion.1), channel_id=1, source_target_pairs={{0,128},{1,129},{2,130},{3,131},{8,136},{9,137},{10,138},{11,139},... | collective-permute-start | bytes 786440 | tf_op jit(solution)/shard_map/ppermute | solution.py:48
  20.0 7.1 %collective-permute-start.5 = (f32[512,128]{1,0:T(8,128)S(1)}, f32[512,128]{1,0:T(8,128)S(1)}, u32[]{:S(2)}, u32[]{:S(2)}) collective-permute-start(f32[512,128]{1,0:T(8,128)S(1)} %get-tuple-element.8), channel_id=1, source_target_pairs={{0,16},{8,24},{16,0},{24,8},{32,48},{40,56},{48,32},{56,40},{64,80... | collective-permute-start | bytes 786440 | tf_op jit(solution)/shard_map/ppermute | solution.py:61
  22.7 7.3 %collective-permute-start.4 = (f32[512,128]{1,0:T(8,128)S(1)}, f32[512,128]{1,0:T(8,128)S(1)}, u32[]{:S(2)}, u32[]{:S(2)}) collective-permute-start(f32[512,128]{1,0:T(8,128)S(1)} %get-tuple-element.8), channel_id=1, source_target_pairs={{0,8},{8,0},{16,24},{24,16},{32,40},{40,32},{48,56},{56,48},{64,72... | collective-permute-start | bytes 786440 | tf_op jit(solution)/shard_map/ppermute | solution.py:60
  27.1 4.0 %collective-permute-start.6 = (f32[512,128]{1,0:T(8,128)S(1)}, f32[512,128]{1,0:T(8,128)S(1)}, u32[]{:S(2)}, u32[]{:S(2)}) collective-permute-start(f32[512,128]{1,0:T(8,128)S(1)} %collective-permute-done.5), channel_id=1, source_target_pairs={{0,8},{8,0},{16,24},{24,16},{32,40},{40,32},{48,56},{56,48},{64,72... | collective-permute-start | bytes 786440 | tf_op jit(solution)/shard_map/ppermute | solution.py:62
  31.1 45.4 %copy-start.2 = (f32[512,128]{1,0:T(8,128)S(1)}, f32[512,128]{1,0:T(8,128)}, u32[]{:S(2)}) copy-start(f32[512,128]{1,0:T(8,128)} %param.4) | copy-start | bytes 786436
  72.0 6.2 %collective-permute-start.12 = (f32[512,128]{1,0:T(8,128)S(1)}, f32[512,128]{1,0:T(8,128)S(1)}, u32[]{:S(2)}, u32[]{:S(2)}) collective-permute-start(f32[512,128]{1,0:T(8,128)S(1)} %broadcast_select_fusion), channel_id=1, source_target_pairs={{0,128},{8,136},{16,144},{24,152},{33,161},{41,169},{49,177},{57,1... | collective-permute-start | bytes 786440 | tf_op jit(solution)/shard_map/ppermute | solution.py:48
  73.3 6.9 %collective-permute-start.13 = (f32[512,128]{1,0:T(8,128)S(1)}, f32[512,128]{1,0:T(8,128)S(1)}, u32[]{:S(2)}, u32[]{:S(2)}) collective-permute-start(f32[512,128]{1,0:T(8,128)S(1)} %broadcast_select_fusion), channel_id=1, source_target_pairs={{0,192},{8,200},{16,208},{24,216},{33,225},{41,233},{49,241},{57,2... | collective-permute-start | bytes 786440 | tf_op jit(solution)/shard_map/ppermute | solution.py:48
  74.6 7.7 %collective-permute-start.11 = (f32[512,128]{1,0:T(8,128)S(1)}, f32[512,128]{1,0:T(8,128)S(1)}, u32[]{:S(2)}, u32[]{:S(2)}) collective-permute-start(f32[512,128]{1,0:T(8,128)S(1)} %broadcast_select_fusion), channel_id=1, source_target_pairs={{0,64},{8,72},{16,80},{24,88},{33,97},{41,105},{49,113},{57,121},{... | collective-permute-start | bytes 786440 | tf_op jit(solution)/shard_map/ppermute | solution.py:48
  76.9 6.8 %collective-permute-start.9 = (f32[128,128]{1,0:T(8,128)S(1)}, f32[128,128]{1,0:T(8,128)S(1)}, u32[]{:S(2)}, u32[]{:S(2)}) collective-permute-start(f32[128,128]{1,0:T(8,128)S(1)} %convolution_bitcast_fusion.1), channel_id=1, source_target_pairs={{0,192},{1,193},{2,194},{3,195},{4,196},{5,197},{6,198},{7,199},{8... | collective-permute-start | bytes 196616 | tf_op jit(solution)/shard_map/ppermute | solution.py:49
  77.0 6.7 %collective-permute-start.8 = (f32[128,128]{1,0:T(8,128)S(1)}, f32[128,128]{1,0:T(8,128)S(1)}, u32[]{:S(2)}, u32[]{:S(2)}) collective-permute-start(f32[128,128]{1,0:T(8,128)S(1)} %convolution_bitcast_fusion.1), channel_id=1, source_target_pairs={{0,128},{1,129},{2,130},{3,131},{4,132},{5,133},{6,134},{7,135},{8... | collective-permute-start | bytes 196616 | tf_op jit(solution)/shard_map/ppermute | solution.py:49
  78.1 7.0 %collective-permute-start.7 = (f32[128,128]{1,0:T(8,128)S(1)}, f32[128,128]{1,0:T(8,128)S(1)}, u32[]{:S(2)}, u32[]{:S(2)}) collective-permute-start(f32[128,128]{1,0:T(8,128)S(1)} %convolution_bitcast_fusion.1), channel_id=1, source_target_pairs={{0,64},{1,65},{2,66},{3,67},{4,68},{5,69},{6,70},{7,71},{8,72},{9,... | collective-permute-start | bytes 196616 | tf_op jit(solution)/shard_map/ppermute | solution.py:49
  82.4 7.5 %collective-permute-start.14 = (f32[512,128]{1,0:T(8,128)S(1)}, f32[512,128]{1,0:T(8,128)S(1)}, u32[]{:S(2)}, u32[]{:S(2)}) collective-permute-start(f32[512,128]{1,0:T(8,128)S(1)} %add_add_fusion), channel_id=1, source_target_pairs={{0,32},{2,34},{4,36},{6,38},{8,40},{10,42},{12,44},{14,46},{16,48}... | collective-permute-start | bytes 786440 | tf_op jit(solution)/shard_map/ppermute | solution.py:48
  85.1 4.7 %collective-permute-start.10 = (f32[128,128]{1,0:T(8,128)S(1)}, f32[128,128]{1,0:T(8,128)S(1)}, u32[]{:S(2)}, u32[]{:S(2)}) collective-permute-start(f32[128,128]{1,0:T(8,128)S(1)} %add_add_fusion.2), channel_id=1, source_target_pairs={{0,32},{1,33},{2,34},{3,35},{4,36},{5,37},{6,38},{7,39},{8,40},{9,... | collective-permute-start | bytes 196616 | tf_op jit(solution)/shard_map/ppermute | solution.py:49
  90.0 6.8 %collective-permute-start.16 = (f32[640,128]{1,0:T(8,128)S(1)}, f32[640,128]{1,0:T(8,128)S(1)}, u32[]{:S(2)}, u32[]{:S(2)}) collective-permute-start(f32[640,128]{1,0:T(8,128)S(1)} %pad_maximum_fusion), channel_id=1, source_target_pairs={{0,16},{8,24},{16,0},{24,8},{32,48},{40,56},{48,32},{56,40},{64,80... | collective-permute-start | bytes 983048 | tf_op jit(solution)/shard_map/ppermute | solution.py:61
  90.1 12.4 %collective-permute-start.15 = (f32[640,128]{1,0:T(8,128)S(1)}, f32[640,128]{1,0:T(8,128)S(1)}, u32[]{:S(2)}, u32[]{:S(2)}) collective-permute-start(f32[640,128]{1,0:T(8,128)S(1)} %pad_maximum_fusion), channel_id=1, source_target_pairs={{0,8},{8,0},{16,24},{24,16},{32,40},{40,32},{48,56},{56,48},{64,72... | collective-permute-start | bytes 983048 | tf_op jit(solution)/shard_map/ppermute | solution.py:60
  96.8 6.9 %collective-permute-start.17 = (f32[640,128]{1,0:T(8,128)S(1)}, f32[640,128]{1,0:T(8,128)S(1)}, u32[]{:S(2)}, u32[]{:S(2)}) collective-permute-start(f32[640,128]{1,0:T(8,128)S(1)} %collective-permute-done.16), channel_id=1, source_target_pairs={{0,8},{8,0},{16,24},{24,16},{32,40},{40,32},{48,56},{56,48},{64,72... | collective-permute-start | bytes 983048 | tf_op jit(solution)/shard_map/ppermute | solution.py:62
  102.5 3.2 %copy-start.1 = (f32[512,2048]{1,0:T(8,128)S(1)}, f32[512,2048]{1,0:T(8,128)}, u32[]{:S(2)}) copy-start(f32[512,2048]{1,0:T(8,128)} %param.3) | copy-start | bytes 12582916
